TPU v7x, 128 devices: a whole 4x4x4 slice. The times are simulated.
128 devices in a mesh: gx: 8 (over z, x_lo), gy: 8 (over y, x_hi), gz: 2 (over core).
Axes of the slice: x: 4 (x_hi: 2, x_lo: 2; x = x_hi * 2 + x_lo), y: 4, z: 4, core: 2. Of those that a mesh axis runs over, the one named last changes fastest.
Arguments:
- populations: float32 [19, 64, 16, 1024], P(None, 'gx', 'gz', 'gy'), may hold values from 0.01 to 0.2
- le_shift: int32 [2], replicated, may hold values from 0 to 1023
- le_frac: int32 [2], replicated, may hold values from 0 to 255
- links: int32 [64, 16, 256], P('gx', 'gz', 'gy'), may hold values from 1 to 19455, as said below
Outputs:
- final_states: float32 [19, 64, 16, 1024], P(None, 'gx', 'gz', 'gy')
- final_density: float32 [64, 16, 1024], P('gx', 'gz', 'gy')
Inputs may be any that keep to these rules, and one draw needn't show every extreme that they name: `links`: each entry is y * 19 + m with m from 1 to 18; the entries in columns b * 32 to (b + 1) * 32 - 1 have y from b * 128 to (b + 1) * 128 - 1.
All inputs are finite; a program needn't handle non-finite values.
Results may differ from a plain program's by a relative error of at most 0.00002.
Values sent between devices are 32-bit elements; how exact they have to be, the bound alone decides.
No kernel may reach another device: no remote copies, remote signals or barrier semaphores. Data moves between devices by JAX's collectives and lax.ppermute only.
A program may use at most 64 MiB of HBM per device.

v0:
```python
import jax
import jax.numpy as jnp
import numpy as np
from jax import lax
from jax.sharding import PartitionSpec as P

STEPS = 2


velocity_table = (
    (0, 0, 0),
    (1, 0, 0),
    (-1, 0, 0),
    (0, 1, 0),
    (0, -1, 0),
    (0, 0, 1),
    (0, 0, -1),
    (1, 1, 0),
    (-1, -1, 0),
    (1, -1, 0),
    (-1, 1, 0),
    (1, 0, 1),
    (-1, 0, -1),
    (1, 0, -1),
    (-1, 0, 1),
    (0, 1, 1),
    (0, -1, -1),
    (0, 1, -1),
    (0, -1, 1),
)
weight_table = (1.0 / 3.0,) + (1.0 / 18.0,) * 6 + (1.0 / 36.0,) * 12
upward = (1, 7, 9, 11, 13)
downward = (2, 8, 10, 12, 14)
relax_rate = 1.25
plane_speed = 0.08


def extended_2(cells, sides, width):
    for axis, dim in sides:
        count = lax.axis_size(axis)
        head = lax.slice_in_dim(cells, 0, width, axis=dim)
        tail = lax.slice_in_dim(cells, cells.shape[dim] - width, cells.shape[dim], axis=dim)
        cells = jnp.concatenate(
            [
                lax.ppermute(tail, axis, [(i, (i + 1) % count) for i in range(count)]),
                cells,
                lax.ppermute(head, axis, [((i + 1) % count, i) for i in range(count)]),
            ],
            axis=dim,
        )
    return cells


def in_order(parts, dim):
    parts = jnp.moveaxis(parts, 0, dim)
    dims = parts.shape
    return parts.reshape(*dims[:dim], dims[dim] * dims[dim + 1], *dims[dim + 2 :])


def from_everyone(array, axis):
    copies = jnp.broadcast_to(array, (lax.axis_size(axis), *array.shape))
    return lax.all_to_all(copies, axis, split_axis=0, concat_axis=0, tiled=True)


def gather_directly(array, axis, dim):
    return in_order(from_everyone(array, axis), dim)


def total_density(states):
    density = states[0]
    for member in range(1, 19):
        density = density + states[member]
    return density


def moments(states):
    density = total_density(states)
    velocity = []
    for dim_index in range(3):
        momentum = None
        for member in range(19):
            sign_part = velocity_table[member][dim_index]
            if sign_part == 1:
                momentum = states[member] if momentum is None else momentum + states[member]
            elif sign_part == -1:
                momentum = momentum - states[member]
        velocity.append(momentum / density)
    return (density, velocity)


def speed_square(velocity):
    return velocity[0] * velocity[0] + velocity[1] * velocity[1] + velocity[2] * velocity[2]


def equilibrium(member, density, velocity, speed_sq):
    projected = None
    for dim_index in range(3):
        sign_part = velocity_table[member][dim_index]
        if sign_part != 0:
            summand = velocity[dim_index] if sign_part > 0 else -velocity[dim_index]
            projected = summand if projected is None else projected + summand
    if projected is None:
        return weight_table[member] * density * (1.0 - 1.5 * speed_sq)
    return (
        weight_table[member]
        * density
        * (1.0 + 3.0 * projected + 4.5 * projected * projected - 1.5 * speed_sq)
    )


def relax(states):
    density, velocity = moments(states)
    speed_sq = speed_square(velocity)
    return jnp.stack(
        [
            states[member]
            + relax_rate * (equilibrium(member, density, velocity, speed_sq) - states[member])
            for member in range(19)
        ]
    )


def corrected(plane, members, sign_part):
    density, velocity = moments(plane)
    speed_sq = speed_square(velocity)
    moved = [velocity[0], velocity[1] + sign_part * plane_speed, velocity[2]]
    moved_sq = speed_square(moved)
    return jnp.stack(
        [
            plane[member]
            + equilibrium(member, density, moved, moved_sq)
            - equilibrium(member, density, velocity, speed_sq)
            for member in members
        ]
    )


def bounce_back(read, relaxed, links, anchor):
    row_span = read.shape[3]
    cell_code = (anchor + lax.broadcasted_iota(jnp.int32, (row_span,), 0)) * 19
    result = [read[0]]
    for member in range(1, 19):
        source = member - 1 + 2 * (member % 2)
        target = cell_code + source
        hit = jnp.any(links[:, :, :, None] == target[None, None, None, :], axis=2)
        result.append(jnp.where(hit, relaxed[source], read[member]))
    return jnp.stack(result)


def per_device(populations, le_shift, le_frac, links):
    states = populations
    slab_width = states.shape[1]
    slab_depth = states.shape[2]
    row_span = states.shape[3]
    flow_cycle = lax.axis_size("gy")
    flow_cells = row_span * flow_cycle
    anchor = lax.axis_index("gy") * row_span
    for section in range(STEPS):
        relaxed = relax(states)
        offset = le_shift[section]
        fraction = le_frac[section].astype(jnp.float32) / 256.0
        keep = 1.0 - fraction
        face_pair = jnp.stack(
            [
                corrected(relaxed[:, 0], downward, 1.0),
                corrected(relaxed[:, slab_width - 1], upward, -1.0),
            ]
        )
        bordered = extended_2(face_pair, (("gx", 0),), 1)
        sources = jnp.stack([bordered[0], bordered[3]])
        lag_pair = jnp.stack([offset, flow_cells - 1 - offset])
        everything = gather_directly(sources, "gy", 3)
        joined = jnp.concatenate([everything, everything], axis=3)
        starts = (anchor - lag_pair - 1) % flow_cells
        low_window = lax.dynamic_slice_in_dim(joined[0], starts[0], row_span + 1, 2)
        high_window = lax.dynamic_slice_in_dim(joined[1], starts[1], row_span + 1, 2)
        low_ghost = keep * low_window[:, :, 1:] + fraction * low_window[:, :, :-1]
        high_ghost = fraction * high_window[:, :, 1:] + keep * high_window[:, :, :-1]
        empty = jnp.zeros((19, slab_depth, row_span), jnp.float32)
        low_plane = empty.at[np.array(upward)].set(low_ghost)
        high_plane = empty.at[np.array(downward)].set(high_ghost)
        extended = jnp.concatenate([low_plane[:, None], relaxed, high_plane[:, None]], axis=1)
        side_padded = extended_2(extended[3:], (("gy", 3), ("gz", 2)), 1)
        pulled = []
        for member in range(19):
            step_x, step_y, step_z = velocity_table[member]
            if member < 3:
                pulled.append(extended[member, 1 - step_x : 1 - step_x + slab_width])
            else:
                padded = side_padded[member - 3]
                pulled.append(
                    padded[
                        1 - step_x : 1 - step_x + slab_width,
                        1 - step_z : 1 - step_z + slab_depth,
                        1 - step_y : 1 - step_y + row_span,
                    ]
                )
        read = jnp.stack(pulled)
        states = bounce_back(read, relaxed, links, anchor)
    return (states, total_density(states))


def solution(mesh):
    in_specs = (P(None, "gx", "gz", "gy"), P(), P(), P("gx", "gz", "gy"))
    out_specs = (P(None, "gx", "gz", "gy"), P("gx", "gz", "gy"))
    return jax.shard_map(
        per_device, mesh=mesh, in_specs=in_specs, out_specs=out_specs, check_vma=False
    )
```

profile of v0, /device:TPU:1, one launch (start us, length us, event | category | flops | bytes accessed | tf_op | source)
XLA Modules:
  0.0 111.9 jit_solution(10529114877232067362)
XLA Ops:
  0.7 1.2 %constant_dynamic-update-slice_fusion.28 = (f32[19,8,8,128]{3,2,1,0:T(8,128)S(1)}, f32[1,8,8,128]{3,2,1,0:T(8,128)S(1)}, f32[1,8,8,128]{3,2,1,0:T(8,128)S(1)}, f...) fusion(f32[19,8,8,128]{3,2,1,0:T(8,128)} %param.12), kind=kLoop, calls=%fused_computation.58 | loop fusion | flops 491519 | bytes 851968
  9.4 2.1 %collective-permute-start = (f32[1,5,8,128]{3,2,1,0:T(8,128)S(1)}, f32[1,5,8,128]{3,2,1,0:T(8,128)S(1)}, u32[]{:S(2)}, u32[]{:S(2)}) collective-permute-start(f32[1,5,8,128]{3,2,1,0:T(8,128)S(1)} %bitcast.1437), channel_id=1, source_target_pairs={{0,16},{16,32},{32,48},{48,64},{64,80},{80,96},{96,112},{112,0},{1... | collective-permute-start | bytes 61448 | tf_op jit(solution)/shard_map/ppermute | solution.py:45
  11.6 3.6 %collective-permute-start.1 = (f32[1,5,8,128]{3,2,1,0:T(8,128)S(1)}, f32[1,5,8,128]{3,2,1,0:T(8,128)S(1)}, u32[]{:S(2)}, u32[]{:S(2)}) collective-permute-start(f32[1,5,8,128]{3,2,1,0:T(8,128)S(1)} %bitcast.1435), channel_id=1, source_target_pairs={{16,0},{32,16},{48,32},{64,48},{80,64},{96,80},{112,96},{0,112},{1... | collective-permute-start | bytes 61448 | tf_op jit(solution)/shard_map/ppermute | solution.py:47
  20.0 1.9 %and_select_fusion = (s32[2]{0:T(128)}, s32[2]{0:T(128)S(1)}) fusion(s32[1]{0:T(128)S(6)} %sub.3222, s32[1]{0:T(128)} %get-tuple-element.202, s32[]{:T(128)S(6)} %mul.3256, s32[1]{0:T(128)S(6)} %sub.3071, s32[1]{0:T(128)} %get-tuple-element.203), kind=kLoop, calls=%fused_computation.939 | loop fusion | flops 56 | bytes 36 | tf_op jit(solution)/shard_map/jit(remainder)/select_n | solution.py:174
  29.0 6.4 %all-to-all-start = ((f32[8,2,5,8,128]{4,3,2,1,0:T(8,128)}), f32[8,2,5,8,128]{4,3,2,1,0:T(8,128)S(1)}, u32[]{:S(2)}, u32[]{:S(2)}) async-start(f32[8,2,5,8,128]{4,3,2,1,0:T(8,128)} %broadcast_in_dim.21), calls=%async_computation | async-start | bytes 655360 | tf_op jit(solution)/shard_map/all_to_all | solution.py:62
  37.0 6.4 %all-to-all-done = f32[8,2,5,8,128]{4,3,2,1,0:T(8,128)S(1)} async-done(((f32[8,2,5,8,128]{4,3,2,1,0:T(8,128)}), f32[8,2,5,8,128]{4,3,2,1,0:T(8,128)S(1)}, u32[]{:S(2)}, u32[]{:S(2)}) %all-to-all-start) | async-done | bytes 327712 | tf_op jit(solution)/shard_map/all_to_all | solution.py:62
  45.6 1.2 %copy.92 = f32[16,10,8,1]{0,2,3,1:T(8,128)} copy(f32[16,10,8,1]{3,2,1,0:T(8,128)S(1)} %get-tuple-element.192) | data formatting | bytes 10240 | tf_op jit(solution)/shard_map/slice | solution.py:42
  47.4 1.9 %collective-permute-start.3 = (f32[16,10,8,1]{0,2,3,1:T(8,128)S(1)}, f32[16,10,8,1]{0,2,3,1:T(8,128)}, u32[]{:S(2)}, u32[]{:S(2)}) collective-permute-start(f32[16,10,8,1]{0,2,3,1:T(8,128)S(1)} %copy.93), channel_id=1, source_target_pairs={{2,0},{4,2},{6,4},{8,6},{10,8},{12,10},{14,12},{0,14},{3,1},{5,3},... | collective-permute-start | bytes 15368 | tf_op jit(solution)/shard_map/ppermute | solution.py:47
  49.3 1.1 collective-permute-start.2
  50.4 6.3 %compare_reduce_fusion.17 = (pred[8,8,128]{2,1,0:T(8,128)(4,1)}, pred[8,8,128]{2,1,0:T(8,128)(4,1)}, pred[8,8,128]{2,1,0:T(8,128)(4,1)}, pred[8,8,128]{2,1,0:T(8...) fusion(s32[128]{0:T(128)} %get-tuple-element.225, ...), kind=kLoop, calls=%fused_computation.23 | loop fusion | flops 9289728 | bytes 164864 | tf_op jit(solution)/shard_map/reduce_or | solution.py:145
  57.4 1.3 %copy.95 = f32[16,10,8,1]{3,2,1,0:T(8,128)S(1)} copy(f32[16,10,8,1]{0,2,3,1:T(8,128)} %collective-permute-done.3) | data formatting | bytes 10240 | tf_op jit(solution)/shard_map/ppermute | solution.py:47
  58.7 1.1 %pad_maximum_fusion.9 = (f32[16,10,1,130]{3,2,1,0:T(1,128)S(1)}, f32[16,10,1,130]{3,2,1,0:T(1,128)S(1)}) fusion(f32[16,10,8,1]{3,2,1,0:T(8,128)S(1)} %copy.95, f32[16,10,8,128]{3,2,1,0:T(8,128)S(1)} %slice.1265, f32[16,10,8,1]{3,2,1,0:T(8,128)S(1)} %copy.94), kind=kLoop, calls=%fused_computation.144 | loop fusion | flops 83200 | bytes 832000 | tf_op jit(solution)/shard_map/slice | solution.py:42
  59.8 3.0 %collective-permute-start.4 = (f32[16,10,1,130]{3,2,1,0:T(1,128)S(1)}, f32[16,10,1,130]{3,2,1,0:T(1,128)S(1)}, u32[]{:S(2)}, u32[]{:S(2)}) collective-permute-start(f32[16,10,1,130]{3,2,1,0:T(1,128)S(1)} %get-tuple-element.188), channel_id=1, source_target_pairs={{0,1},{1,0},{2,3},{3,2},{4,5},{5,4},{6,7},{7,6},{8,9},{9,8},{10,11... | collective-permute-start | bytes 249608 | tf_op jit(solution)/shard_map/ppermute | solution.py:45
  64.3 1.3 %pad_maximum_fusion = f32[16,10,10,130]{3,2,1,0:T(8,128)S(1)} fusion(f32[16,10,1,130]{3,2,1,0:T(1,128)S(1)} %collective-permute-done.5, f32[16,10,8,1]{3,2,1,0:T(8,128)S(1)} %copy.95, f32[16,10,8,128]{3,2,1,0:T(8,128)S(1)} %slice.1265, f32[16,10,8,1]{3,2,1,0:T(8,128)S(1)} %copy.94, f32[16,10,1,130]{3,2,1,0:T(1,128)S(1)} %collective-permute-done.4), kind=kLoop, calls=%fused_computation.4 | loop fusion | flops 832000 | bytes 1664000 | tf_op jit(solution)/shard_map/concatenate | solution.py:43
  67.8 1.1 %collective-permute-start.7 = (f32[1,5,8,128]{3,2,1,0:T(8,128)S(1)}, f32[1,5,8,128]{3,2,1,0:T(8,128)S(1)}, u32[]{:S(2)}, u32[]{:S(2)}) collective-permute-start(f32[1,5,8,128]{3,2,1,0:T(8,128)S(1)} %bitcast.1436), channel_id=1, source_target_pairs={{16,0},{32,16},{48,32},{64,48},{80,64},{96,80},{112,96},{0,112},{1... | collective-permute-start | bytes 61448 | tf_op jit(solution)/shard_map/ppermute | solution.py:47
  70.5 3.3 %collective-permute-done.6 = f32[1,5,8,128]{3,2,1,0:T(8,128)S(1)} collective-permute-done((f32[1,5,8,128]{3,2,1,0:T(8,128)S(1)}, f32[1,5,8,128]{3,2,1,0:T(8,128)S(1)}, u32[]{:S(2)}, u32[]{:S(2)}) %collective-permute-start.6) | collective-permute-done | bytes 20512 | tf_op jit(solution)/shard_map/ppermute | solution.py:45
  74.6 5.2 %all-to-all-start.1 = ((f32[8,2,5,8,128]{4,3,2,1,0:T(8,128)}), f32[8,2,5,8,128]{4,3,2,1,0:T(8,128)S(1)}, u32[]{:S(2)}, u32[]{:S(2)}) async-start(f32[8,2,5,8,128]{4,3,2,1,0:T(8,128)} %broadcast_in_dim.26), calls=%async_computation.1 | async-start | bytes 655360 | tf_op jit(solution)/shard_map/all_to_all | solution.py:62
  85.0 3.0 %all-to-all-done.1 = f32[8,2,5,8,128]{4,3,2,1,0:T(8,128)S(1)} async-done(((f32[8,2,5,8,128]{4,3,2,1,0:T(8,128)}), f32[8,2,5,8,128]{4,3,2,1,0:T(8,128)S(1)}, u32[]{:S(2)}, u32[]{:S(2)}) %all-to-all-start.1) | async-done | bytes 327712 | tf_op jit(solution)/shard_map/all_to_all | solution.py:62
  90.3 1.2 %copy.101 = f32[16,10,8,1]{0,2,3,1:T(8,128)} copy(f32[16,10,8,1]{3,2,1,0:T(8,128)S(1)} %get-tuple-element.190) | data formatting | bytes 10240 | tf_op jit(solution)/shard_map/slice | solution.py:42
  92.4 4.8 %collective-permute-start.9 = (f32[16,10,8,1]{0,2,3,1:T(8,128)S(1)}, f32[16,10,8,1]{0,2,3,1:T(8,128)}, u32[]{:S(2)}, u32[]{:S(2)}) collective-permute-start(f32[16,10,8,1]{0,2,3,1:T(8,128)S(1)} %copy.102), channel_id=1, source_target_pairs={{2,0},{4,2},{6,4},{8,6},{10,8},{12,10},{14,12},{0,14},{3,1},{5,3},... | collective-permute-start | bytes 15368 | tf_op jit(solution)/shard_map/ppermute | solution.py:47
  98.7 1.3 %copy.104 = f32[16,10,8,1]{3,2,1,0:T(8,128)S(1)} copy(f32[16,10,8,1]{0,2,3,1:T(8,128)} %collective-permute-done.9) | data formatting | bytes 10240 | tf_op jit(solution)/shard_map/ppermute | solution.py:47
  100.1 1.1 %pad_maximum_fusion.6 = (f32[16,10,1,130]{3,2,1,0:T(1,128)S(1)}, f32[16,10,1,130]{3,2,1,0:T(1,128)S(1)}) fusion(f32[16,10,8,1]{3,2,1,0:T(8,128)S(1)} %copy.104, f32[16,10,8,128]{3,2,1,0:T(8,128)S(1)} %slice.1344, f32[16,10,8,1]{3,2,1,0:T(8,128)S(1)} %copy.103), kind=kLoop, calls=%fused_computation.125 | loop fusion | flops 83200 | bytes 832000 | tf_op jit(solution)/shard_map/slice | solution.py:42
  101.2 4.1 %collective-permute-start.10 = (f32[16,10,1,130]{3,2,1,0:T(1,128)S(1)}, f32[16,10,1,130]{3,2,1,0:T(1,128)S(1)}, u32[]{:S(2)}, u32[]{:S(2)}) collective-permute-start(f32[16,10,1,130]{3,2,1,0:T(1,128)S(1)} %get-tuple-element.186), channel_id=1, source_target_pairs={{0,1},{1,0},{2,3},{3,2},{4,5},{5,4},{6,7},{7,6},{8,9},{9,8},{10,11... | collective-permute-start | bytes 249608 | tf_op jit(solution)/shard_map/ppermute | solution.py:45
  106.7 1.3 %pad_maximum_fusion.1 = f32[16,10,10,130]{3,2,1,0:T(8,128)S(1)} fusion(f32[16,10,1,130]{3,2,1,0:T(1,128)S(1)} %collective-permute-done.11, f32[16,10,8,1]{3,2,1,0:T(8,128)S(1)} %copy.104, f32[16,10,8,128]{3,2,1,0:T(8,128)S(1)} %slice.1344, f32[16,10,8,1]{3,2,1,0:T(8,128)S(1)} %copy.103, f32[16,10,1,130]{3,2,1,0:T(1,128)S(1)} %collective-permute-done.10), kind=kLoop, calls=%fused_computation.5 | loop fusion | flops 832000 | bytes 1664000 | tf_op jit(solution)/shard_map/concatenate | solution.py:43
  (302 shorter events, 34.1 us)
Async XLA Ops:
  0.7 21.8 %copy-start.78 = (s32[2]{0:T(128)S(1)}, s32[2]{0:T(128)}, u32[]{:S(2)}) copy-start(s32[2]{0:T(128)} %param.14) | copy-start | bytes 28
  9.1 34.8 %copy-start.73 = (s32[5]{0:T(128)S(1)}, s32[5]{0:T(128)}, u32[]{:S(2)}) copy-start(s32[5]{0:T(128)} %constant.131) | copy-start | bytes 64
  9.2 35.4 %copy-start.75 = (s32[5]{0:T(128)S(1)}, s32[5]{0:T(128)}, u32[]{:S(2)}) copy-start(s32[5]{0:T(128)} %constant.130) | copy-start | bytes 64
  9.4 18.9 %collective-permute-start = (f32[1,5,8,128]{3,2,1,0:T(8,128)S(1)}, f32[1,5,8,128]{3,2,1,0:T(8,128)S(1)}, u32[]{:S(2)}, u32[]{:S(2)}) collective-permute-start(f32[1,5,8,128]{3,2,1,0:T(8,128)S(1)} %bitcast.1437), channel_id=1, source_target_pairs={{0,16},{16,32},{32,48},{48,64},{64,80},{80,96},{96,112},{112,0},{1... | collective-permute-start | bytes 61448 | tf_op jit(solution)/shard_map/ppermute | solution.py:45
  11.6 16.7 %collective-permute-start.1 = (f32[1,5,8,128]{3,2,1,0:T(8,128)S(1)}, f32[1,5,8,128]{3,2,1,0:T(8,128)S(1)}, u32[]{:S(2)}, u32[]{:S(2)}) collective-permute-start(f32[1,5,8,128]{3,2,1,0:T(8,128)S(1)} %bitcast.1435), channel_id=1, source_target_pairs={{16,0},{32,16},{48,32},{64,48},{80,64},{96,80},{112,96},{0,112},{1... | collective-permute-start | bytes 61448 | tf_op jit(solution)/shard_map/ppermute | solution.py:47
  29.0 14.4 %all-to-all-start = ((f32[8,2,5,8,128]{4,3,2,1,0:T(8,128)}), f32[8,2,5,8,128]{4,3,2,1,0:T(8,128)S(1)}, u32[]{:S(2)}, u32[]{:S(2)}) async-start(f32[8,2,5,8,128]{4,3,2,1,0:T(8,128)} %broadcast_in_dim.21), calls=%async_computation | async-start | bytes 655360 | tf_op jit(solution)/shard_map/all_to_all | solution.py:62
  47.4 10.0 %collective-permute-start.3 = (f32[16,10,8,1]{0,2,3,1:T(8,128)S(1)}, f32[16,10,8,1]{0,2,3,1:T(8,128)}, u32[]{:S(2)}, u32[]{:S(2)}) collective-permute-start(f32[16,10,8,1]{0,2,3,1:T(8,128)S(1)} %copy.93), channel_id=1, source_target_pairs={{2,0},{4,2},{6,4},{8,6},{10,8},{12,10},{14,12},{0,14},{3,1},{5,3},... | collective-permute-start | bytes 15368 | tf_op jit(solution)/shard_map/ppermute | solution.py:47
  49.3 7.5 %collective-permute-start.2 = (f32[16,10,8,1]{0,2,3,1:T(8,128)}, f32[16,10,8,1]{0,2,3,1:T(8,128)S(1)}, u32[]{:S(2)}, u32[]{:S(2)}) collective-permute-start(f32[16,10,8,1]{0,2,3,1:T(8,128)} %copy.92), channel_id=1, source_target_pairs={{0,2},{2,4},{4,6},{6,8},{8,10},{10,12},{12,14},{14,0},{1,3},{3,5},... | collective-permute-start | bytes 15368 | tf_op jit(solution)/shard_map/ppermute | solution.py:45
  59.8 4.1 %collective-permute-start.4 = (f32[16,10,1,130]{3,2,1,0:T(1,128)S(1)}, f32[16,10,1,130]{3,2,1,0:T(1,128)S(1)}, u32[]{:S(2)}, u32[]{:S(2)}) collective-permute-start(f32[16,10,1,130]{3,2,1,0:T(1,128)S(1)} %get-tuple-element.188), channel_id=1, source_target_pairs={{0,1},{1,0},{2,3},{3,2},{4,5},{5,4},{6,7},{7,6},{8,9},{9,8},{10,11... | collective-permute-start | bytes 249608 | tf_op jit(solution)/shard_map/ppermute | solution.py:45
  62.9 1.4 %collective-permute-start.5 = (f32[16,10,1,130]{3,2,1,0:T(1,128)S(1)}, f32[16,10,1,130]{3,2,1,0:T(1,128)S(1)}, u32[]{:S(2)}, u32[]{:S(2)}) collective-permute-start(f32[16,10,1,130]{3,2,1,0:T(1,128)S(1)} %get-tuple-element.189), channel_id=1, source_target_pairs={{1,0},{0,1},{3,2},{2,3},{5,4},{4,5},{7,6},{6,7},{9,8},{8,9},{11,10... | collective-permute-start | bytes 249608 | tf_op jit(solution)/shard_map/ppermute | solution.py:47
  67.0 21.1 %copy-start.34 = (f32[8,8,128]{2,1,0:T(8,128)}, f32[8,8,128]{2,1,0:T(8,128)S(1)}, u32[]{:S(2)}) copy-start(f32[8,8,128]{2,1,0:T(8,128)S(1)} %get-tuple-element.68) | copy-start | bytes 98308
  67.2 21.0 %copy-start.28 = (f32[8,8,128]{2,1,0:T(8,128)}, f32[8,8,128]{2,1,0:T(8,128)S(1)}, u32[]{:S(2)}) copy-start(f32[8,8,128]{2,1,0:T(8,128)S(1)} %get-tuple-element.60) | copy-start | bytes 98308
  67.2 20.9 %copy-start.6 = (f32[8,8,128]{2,1,0:T(8,128)}, f32[8,8,128]{2,1,0:T(8,128)S(1)}, u32[]{:S(2)}) copy-start(f32[8,8,128]{2,1,0:T(8,128)S(1)} %get-tuple-element.56) | copy-start | bytes 98308
  67.3 20.9 %copy-start.8 = (f32[8,8,128]{2,1,0:T(8,128)}, f32[8,8,128]{2,1,0:T(8,128)S(1)}, u32[]{:S(2)}) copy-start(f32[8,8,128]{2,1,0:T(8,128)S(1)} %get-tuple-element.52) | copy-start | bytes 98308
  67.3 20.9 %copy-start.2 = (f32[8,8,128]{2,1,0:T(8,128)}, f32[8,8,128]{2,1,0:T(8,128)S(1)}, u32[]{:S(2)}) copy-start(f32[8,8,128]{2,1,0:T(8,128)S(1)} %get-tuple-element.50) | copy-start | bytes 98308
  67.5 21.1 %copy-start.76 = (s32[5]{0:T(128)S(1)}, s32[5]{0:T(128)}, u32[]{:S(2)}) copy-start(s32[5]{0:T(128)} %constant.130) | copy-start | bytes 64
  67.6 21.8 %copy-start.74 = (s32[5]{0:T(128)S(1)}, s32[5]{0:T(128)}, u32[]{:S(2)}) copy-start(s32[5]{0:T(128)} %constant.131) | copy-start | bytes 64
  67.8 2.7 %collective-permute-start.7 = (f32[1,5,8,128]{3,2,1,0:T(8,128)S(1)}, f32[1,5,8,128]{3,2,1,0:T(8,128)S(1)}, u32[]{:S(2)}, u32[]{:S(2)}) collective-permute-start(f32[1,5,8,128]{3,2,1,0:T(8,128)S(1)} %bitcast.1436), channel_id=1, source_target_pairs={{16,0},{32,16},{48,32},{64,48},{80,64},{96,80},{112,96},{0,112},{1... | collective-permute-start | bytes 61448 | tf_op jit(solution)/shard_map/ppermute | solution.py:47
  69.0 4.8 %collective-permute-start.6 = (f32[1,5,8,128]{3,2,1,0:T(8,128)S(1)}, f32[1,5,8,128]{3,2,1,0:T(8,128)S(1)}, u32[]{:S(2)}, u32[]{:S(2)}) collective-permute-start(f32[1,5,8,128]{3,2,1,0:T(8,128)S(1)} %bitcast.1434), channel_id=1, source_target_pairs={{0,16},{16,32},{32,48},{48,64},{64,80},{80,96},{96,112},{112,0},{1... | collective-permute-start | bytes 61448 | tf_op jit(solution)/shard_map/ppermute | solution.py:45
  74.6 13.5 %all-to-all-start.1 = ((f32[8,2,5,8,128]{4,3,2,1,0:T(8,128)}), f32[8,2,5,8,128]{4,3,2,1,0:T(8,128)S(1)}, u32[]{:S(2)}, u32[]{:S(2)}) async-start(f32[8,2,5,8,128]{4,3,2,1,0:T(8,128)} %broadcast_in_dim.26), calls=%async_computation.1 | async-start | bytes 655360 | tf_op jit(solution)/shard_map/all_to_all | solution.py:62
  91.5 6.7 %collective-permute-start.8 = (f32[16,10,8,1]{0,2,3,1:T(8,128)}, f32[16,10,8,1]{0,2,3,1:T(8,128)S(1)}, u32[]{:S(2)}, u32[]{:S(2)}) collective-permute-start(f32[16,10,8,1]{0,2,3,1:T(8,128)} %copy.101), channel_id=1, source_target_pairs={{0,2},{2,4},{4,6},{6,8},{8,10},{10,12},{12,14},{14,0},{1,3},{3,5},... | collective-permute-start | bytes 15368 | tf_op jit(solution)/shard_map/ppermute | solution.py:45
  92.4 6.4 %collective-permute-start.9 = (f32[16,10,8,1]{0,2,3,1:T(8,128)S(1)}, f32[16,10,8,1]{0,2,3,1:T(8,128)}, u32[]{:S(2)}, u32[]{:S(2)}) collective-permute-start(f32[16,10,8,1]{0,2,3,1:T(8,128)S(1)} %copy.102), channel_id=1, source_target_pairs={{2,0},{4,2},{6,4},{8,6},{10,8},{12,10},{14,12},{0,14},{3,1},{5,3},... | collective-permute-start | bytes 15368 | tf_op jit(solution)/shard_map/ppermute | solution.py:47
  101.2 5.1 %collective-permute-start.10 = (f32[16,10,1,130]{3,2,1,0:T(1,128)S(1)}, f32[16,10,1,130]{3,2,1,0:T(1,128)S(1)}, u32[]{:S(2)}, u32[]{:S(2)}) collective-permute-start(f32[16,10,1,130]{3,2,1,0:T(1,128)S(1)} %get-tuple-element.186), channel_id=1, source_target_pairs={{0,1},{1,0},{2,3},{3,2},{4,5},{5,4},{6,7},{7,6},{8,9},{9,8},{10,11... | collective-permute-start | bytes 249608 | tf_op jit(solution)/shard_map/ppermute | solution.py:45
  105.3 1.4 %collective-permute-start.11 = (f32[16,10,1,130]{3,2,1,0:T(1,128)S(1)}, f32[16,10,1,130]{3,2,1,0:T(1,128)S(1)}, u32[]{:S(2)}, u32[]{:S(2)}) collective-permute-start(f32[16,10,1,130]{3,2,1,0:T(1,128)S(1)} %get-tuple-element.187), channel_id=1, source_target_pairs={{1,0},{0,1},{3,2},{2,3},{5,4},{4,5},{7,6},{6,7},{9,8},{8,9},{11,10... | collective-permute-start | bytes 249608 | tf_op jit(solution)/shard_map/ppermute | solution.py:47
  (69 other events, 338.0 us)
where the time goes:
time: 113 us; the launch traced here: 112 us
  starting transfers between devices  34.4 us (30%)
  other arithmetic  30.5 us (27%)
  local copies, waits for them, and re-layouts  17.5 us (15%)
  waiting for transfers between devices  17 us (15%)
  between operations  12.5 us (11%)
    ppermute x6, starting transfers between devices, extended_2(): lax.ppermute(head, axis, [((i + 1) % count, i) for i in range(count)])  11.8 us
    all_to_all x2, starting transfers between devices, from_everyone(): return lax.all_to_all(copies, axis, split_axis=0, concat_axis=0, tiled=True)  11.5 us
    ppermute x6, starting transfers between devices, extended_2(): lax.ppermute(tail, axis, [(i, (i + 1) % count) for i in range(count)])  11 us
    unnamed x67, other arithmetic  10.5 us
    all_to_all x2, waiting for transfers between devices, from_everyone(): return lax.all_to_all(copies, axis, split_axis=0, concat_axis=0, tiled=True)  9.39 us
    reduce_or x1, other arithmetic, bounce_back(): hit = jnp.any(links[:, :, :, None] == target[None, None, None, :], axis=2)  6.34 us
    ppermute x6, waiting for transfers between devices, extended_2(): lax.ppermute(tail, axis, [(i, (i + 1) % count) for i in range(count)])  5.88 us
    add x9, other arithmetic, bounce_back(): target = cell_code + source  5.2 us
  transfers between devices with their start and end apart: 14, of which 9 were waited for; matrix products, arithmetic and copies ran while one was open for 16% of the time, Pallas kernels for 0%

commit v1 on v0

v1 whole, which is shorter than its diff:
```python
import jax
import jax.numpy as jnp
import numpy as np
from jax import lax
from jax.sharding import PartitionSpec as P

STEPS = 2


velocity_table = (
    (0, 0, 0),
    (1, 0, 0),
    (-1, 0, 0),
    (0, 1, 0),
    (0, -1, 0),
    (0, 0, 1),
    (0, 0, -1),
    (1, 1, 0),
    (-1, -1, 0),
    (1, -1, 0),
    (-1, 1, 0),
    (1, 0, 1),
    (-1, 0, -1),
    (1, 0, -1),
    (-1, 0, 1),
    (0, 1, 1),
    (0, -1, -1),
    (0, 1, -1),
    (0, -1, 1),
)
weight_table = (1.0 / 3.0,) + (1.0 / 18.0,) * 6 + (1.0 / 36.0,) * 12
upward = (1, 7, 9, 11, 13)
downward = (2, 8, 10, 12, 14)
y_plus = tuple(m for m in range(19) if velocity_table[m][1] == 1)
y_minus = tuple(m for m in range(19) if velocity_table[m][1] == -1)
relax_rate = 1.25
plane_speed = 0.08


def total_density(states):
    density = states[0]
    for member in range(1, 19):
        density = density + states[member]
    return density


def moments(states):
    density = total_density(states)
    velocity = []
    for dim_index in range(3):
        momentum = None
        for member in range(19):
            sign_part = velocity_table[member][dim_index]
            if sign_part == 1:
                momentum = states[member] if momentum is None else momentum + states[member]
            elif sign_part == -1:
                momentum = momentum - states[member]
        velocity.append(momentum / density)
    return (density, velocity)


def speed_square(velocity):
    return velocity[0] * velocity[0] + velocity[1] * velocity[1] + velocity[2] * velocity[2]


def equilibrium(member, density, velocity, speed_sq):
    projected = None
    for dim_index in range(3):
        sign_part = velocity_table[member][dim_index]
        if sign_part != 0:
            summand = velocity[dim_index] if sign_part > 0 else -velocity[dim_index]
            projected = summand if projected is None else projected + summand
    if projected is None:
        return weight_table[member] * density * (1.0 - 1.5 * speed_sq)
    return (
        weight_table[member]
        * density
        * (1.0 + 3.0 * projected + 4.5 * projected * projected - 1.5 * speed_sq)
    )


def relax(states):
    density, velocity = moments(states)
    speed_sq = speed_square(velocity)
    return [
        states[member]
        + relax_rate * (equilibrium(member, density, velocity, speed_sq) - states[member])
        for member in range(19)
    ]


def corrected(plane, members, sign_part):
    density, velocity = moments(plane)
    speed_sq = speed_square(velocity)
    moved = [velocity[0], velocity[1] + sign_part * plane_speed, velocity[2]]
    moved_sq = speed_square(moved)
    return jnp.stack(
        [
            plane[member]
            + equilibrium(member, density, moved, moved_sq)
            - equilibrium(member, density, velocity, speed_sq)
            for member in members
        ]
    )


def link_hits(links, anchor, row_span):
    cell_y = links // 19 - anchor
    member = links % 19
    by_member = (member[:, :, None, :] == jnp.arange(19, dtype=jnp.int32)[:, None]).astype(jnp.bfloat16)
    by_cell = (cell_y[:, :, :, None] == jnp.arange(row_span, dtype=jnp.int32)).astype(jnp.bfloat16)
    counts = jnp.einsum("xzml,xzly->mxzy", by_member, by_cell, preferred_element_type=jnp.float32)
    return counts > 0.5


def per_device(populations, le_shift, le_frac, links):
    n_members, slab_width, half_depth, row_span = populations.shape
    flow_cycle = lax.axis_size("gy")
    slab_cycle = lax.axis_size("gx")
    flow_cells = row_span * flow_cycle
    me_y = lax.axis_index("gy")
    me_z = lax.axis_index("gz")
    anchor = me_y * row_span

    size = populations.size
    packed = jnp.concatenate([populations.reshape(-1), links.astype(jnp.float32).reshape(-1)])
    other = lax.ppermute(packed, "gz", [(0, 1), (1, 0)])
    other_states = other[:size].reshape(populations.shape)
    other_links = other[size:].reshape(links.shape).astype(jnp.int32)
    first = me_z == 0
    states = jnp.where(
        first,
        jnp.concatenate([populations, other_states], axis=2),
        jnp.concatenate([other_states, populations], axis=2),
    )
    all_links = jnp.where(
        first, jnp.concatenate([links, other_links], axis=1), jnp.concatenate([other_links, links], axis=1)
    )
    depth = 2 * half_depth
    hits = link_hits(all_links, anchor, row_span)

    peer = lax.broadcasted_iota(jnp.int32, (flow_cycle, 1), 0)
    to_next = peer == (me_y + 1) % flow_cycle
    to_prev = peer == (me_y - 1 + flow_cycle) % flow_cycle
    face_size = 2 * 5 * depth * row_span
    span = row_span + 2

    for section in range(STEPS):
        relaxed = relax([states[m] for m in range(n_members)])
        offset = le_shift[section]
        fraction = le_frac[section].astype(jnp.float32) / 256.0
        keep = 1.0 - fraction
        top = corrected([r[slab_width - 1] for r in relaxed], upward, -1.0)
        bottom = corrected([r[0] for r in relaxed], downward, 1.0)
        faces = jnp.stack([top, bottom]).reshape(1, -1)
        up_rim = jnp.stack([relaxed[m][:, :, row_span - 1] for m in y_plus]).reshape(1, -1)
        down_rim = jnp.stack([relaxed[m][:, :, 0] for m in y_minus]).reshape(1, -1)
        rim = jnp.where(to_next, up_rim, jnp.where(to_prev, down_rim, 0.0))
        chunks = jnp.concatenate([jnp.broadcast_to(faces, (flow_cycle, face_size)), rim], axis=1)
        got = lax.all_to_all(chunks, "gy", 0, 0, tiled=True)
        rim_low = lax.dynamic_index_in_dim(got, (me_y - 1 + flow_cycle) % flow_cycle, 0, keepdims=False)
        rim_high = lax.dynamic_index_in_dim(got, (me_y + 1) % flow_cycle, 0, keepdims=False)
        rim_low = rim_low[face_size:].reshape(5, slab_width, depth)
        rim_high = rim_high[face_size:].reshape(5, slab_width, depth)
        whole = got[:, :face_size].reshape(flow_cycle, 2, 5, depth, row_span)
        whole = jnp.moveaxis(whole, 0, 3).reshape(2, 5, depth, flow_cells)
        whole = jnp.concatenate([whole, whole[..., : span + 1]], axis=3)
        low_start = (anchor - offset - 2 + 2 * flow_cells) % flow_cells
        high_start = (anchor + offset - 1 + flow_cells) % flow_cells
        low_window = lax.dynamic_slice_in_dim(whole[0], low_start, span + 1, 2)
        high_window = lax.dynamic_slice_in_dim(whole[1], high_start, span + 1, 2)
        low_send = keep * low_window[:, :, 1:] + fraction * low_window[:, :, :-1]
        high_send = fraction * high_window[:, :, 1:] + keep * high_window[:, :, :-1]
        low_ghost = lax.ppermute(low_send, "gx", [(i, (i + 1) % slab_cycle) for i in range(slab_cycle)])
        high_ghost = lax.ppermute(high_send, "gx", [(i, (i - 1) % slab_cycle) for i in range(slab_cycle)])

        result = []
        for member in range(n_members):
            step_x, step_y, step_z = velocity_table[member]
            cells = relaxed[member]
            if step_y == 1:
                cells = jnp.concatenate([rim_low[y_plus.index(member)][:, :, None], cells[:, :, : row_span - 1]], axis=2)
            elif step_y == -1:
                cells = jnp.concatenate([cells[:, :, 1:], rim_high[y_minus.index(member)][:, :, None]], axis=2)
            if step_x == 1:
                ghost = low_ghost[upward.index(member), :, 1 - step_y : 1 - step_y + row_span]
                cells = jnp.concatenate([ghost[None], cells[: slab_width - 1]], axis=0)
            elif step_x == -1:
                ghost = high_ghost[downward.index(member), :, 1 - step_y : 1 - step_y + row_span]
                cells = jnp.concatenate([cells[1:], ghost[None]], axis=0)
            if step_z != 0:
                cells = jnp.roll(cells, step_z, axis=1)
            result.append(cells)
        bounced = [result[0]]
        for member in range(1, n_members):
            source = member - 1 + 2 * (member % 2)
            bounced.append(jnp.where(hits[source], relaxed[source], result[member]))
        states = jnp.stack(bounced)

    final = lax.dynamic_slice_in_dim(states, me_z * half_depth, half_depth, axis=2)
    return (final, total_density(final))


def solution(mesh):
    in_specs = (P(None, "gx", "gz", "gy"), P(), P(), P("gx", "gz", "gy"))
    out_specs = (P(None, "gx", "gz", "gy"), P("gx", "gz", "gy"))
    return jax.shard_map(
        per_device, mesh=mesh, in_specs=in_specs, out_specs=out_specs, check_vma=False
    )
```

time: 113 us -> 156 us (1.38)
  the two profiles are of different devices: /device:TPU:1 before, /device:TPU:0 now
where the time goes in v1:
time: 156 us; the launch traced here: 155 us
  local copies, waits for them, and re-layouts  64.8 us (42%)
  other arithmetic  39.2 us (25%)
  waiting for transfers between devices  25.4 us (16%)
  starting transfers between devices  16.8 us (11%)
  between operations  6.97 us (4%)
    all_to_all x2, waiting for transfers between devices, per_device(): got = lax.all_to_all(chunks, 'gy', 0, 0, tiled=True)  19.2 us
    all_to_all x2, starting transfers between devices, per_device(): got = lax.all_to_all(chunks, 'gy', 0, 0, tiled=True)  10.6 us
    another operation x17, local copies, waits for them, and re-layouts, per_device(): rim_high[y_minus.index(member)][:, :, None]  7.68 us
    unnamed x229, local copies, waits for them, and re-layouts  7.42 us
    concatenate x23, other arithmetic, per_device(): cells = jnp.roll(cells, step_z, axis=1)  7.3 us
    another operation x18, local copies, waits for them, and re-layouts, per_device(): rim_low[y_plus.index(member)][:, :, None]  6.9 us
    ppermute x2, waiting for transfers between devices, per_device(): lax.ppermute(low_send, 'gx', [(i, (i + 1) % slab_cycle) for i in range(sl...  6.11 us
    add x7, other arithmetic, relax(): states[member]  5.65 us
  transfers between devices with their start and end apart: 7, of which 4 were waited for; matrix products, arithmetic and copies ran while one was open for 14% of the time, Pallas kernels for 0%

profile of v1, /device:TPU:0, one launch (start us, length us, event | category | flops | bytes accessed | tf_op | source)
XLA Modules:
  0.0 154.5 jit_solution(938290542959230265)
XLA Ops:
  12.5 1.4 fusion
  26.6 1.4 broadcast_in_dim.84
  29.9 1.3 all_to_all.16
  31.2 7.0 %all-to-all-start = ((f32[8,1,21120]{2,1,0:T(1,128)}), f32[8,1,21120]{2,1,0:T(1,128)S(1)}, u32[]{:S(2)}, u32[]{:S(2)}) async-start(f32[8,1,21120]{2,1,0:T(1,128)} %all_to_all.16), calls=%async_computation | async-start | bytes 1351680 | tf_op jit(solution)/shard_map/all_to_all | solution.py:160
  41.0 11.1 %all-to-all-done = f32[8,1,21120]{2,1,0:T(1,128)S(1)} async-done(((f32[8,1,21120]{2,1,0:T(1,128)}), f32[8,1,21120]{2,1,0:T(1,128)S(1)}, u32[]{:S(2)}, u32[]{:S(2)}) %all-to-all-start) | async-done | bytes 675872 | tf_op jit(solution)/shard_map/all_to_all | solution.py:160
  57.8 1.8 %slice_reduce_fusion.19 = (f32[128]{0:T(128)}, f32[128]{0:T(128)S(1)}, f32[128]{0:T(128)}, f32[128]{0:T(128)}, f32[128]{0:T(128)}, /*index=5*/f32[128]{0:T(128)}) fusion(f32[1,21120]{1,0:T(1,128)} %get-tuple-element.140), kind=kLoop, calls=%fused_computation.1022 | loop fusion | bytes 5632 | tf_op jit(solution)/shard_map/slice | solution.py:184
  61.3 1.4 broadcast_in_dim_squeeze.61
  65.6 1.4 broadcast_in_dim_squeeze.59
  72.6 1.3 broadcast_in_dim_squeeze.58
  74.8 1.5 fusion.633
  77.9 1.5 fusion.634
  81.5 4.1 %collective-permute-start.2 = (f32[5,16,130]{2,0,1:T(8,128)}, f32[5,16,130]{2,0,1:T(8,128)}, u32[]{:S(2)}, u32[]{:S(2)}) collective-permute-start(f32[5,16,130]{2,0,1:T(8,128)} %fusion.6), channel_id=1, source_target_pairs={{0,112},{16,0},{32,16},{48,32},{64,48},{80,64},{96,80},{112,96},{1... | collective-permute-start | bytes 124808 | tf_op jit(solution)/shard_map/ppermute | solution.py:175
  89.7 1.9 %fusion.605 = (f32[1,16,128]{2,0,1:T(1,128)S(1)}, f32[1,1,16,128]{3,1,2,0:T(1,128)}, f32[1,1,16,128]{3,1,2,0:T(1,128)}, f32[1,1,16,128]{3,1,2,0:T(1,128)}, f32[1...) fusion(f32[5,16,130]{2,0,1:T(8,128)} %collective-permute-done.2), kind=kLoop, calls=%fused_computation.1047 | loop fusion | bytes 106496 | tf_op jit(solution)/shard_map/slice | solution.py:189
  93.0 4.0 %collective-permute-done.1 = f32[5,16,130]{2,0,1:T(8,128)S(1)} collective-permute-done((f32[5,16,130]{2,0,1:T(8,128)}, f32[5,16,130]{2,0,1:T(8,128)S(1)}, u32[]{:S(2)}, u32[]{:S(2)}) %collective-permute-start.1) | collective-permute-done | bytes 41632 | tf_op jit(solution)/shard_map/ppermute | solution.py:174
  98.5 1.6 %fusion.287 = (f32[8,16,128]{2,0,1:T(8,128)S(1)}, f32[8,16,128]{2,0,1:T(8,128)S(1)}, f32[8,16,128]{2,0,1:T(8,128)S(1)}, f32[8,16,128]{2,0,1:T(8,128)S(1)}, f32[8...) fusion(f32[8,16,128]{2,0,1:T(8,128)} %get-tuple-element.85, ...), kind=kLoop, calls=%fused_computation.461 | loop fusion | flops 1638400 | bytes 4145152 | tf_op jit(solution)/shard_map/add | solution.py:86
  110.3 1.3 all_to_all.19
  111.6 3.5 %all-to-all-start.1 = ((f32[8,1,21120]{2,1,0:T(1,128)}), f32[8,1,21120]{2,1,0:T(1,128)S(1)}, u32[]{:S(2)}, u32[]{:S(2)}) async-start(f32[8,1,21120]{2,1,0:T(1,128)} %all_to_all.19), calls=%async_computation.1 | async-start | bytes 1351680 | tf_op jit(solution)/shard_map/all_to_all | solution.py:160
  115.3 3.2 %fusion.475 = (f32[1,8,16,128]{3,1,2,0:T(8,128)}, f32[1,8,16,128]{3,1,2,0:T(8,128)S(1)}, f32[1,8,16,128]{3,1,2,0:T(8,128)S(1)}, f32[1,8,16,128]{3,1,2,0:T(8,128)...) fusion(f32[1,8,16,128]{3,1,2,0:T(8,128)} %get-tuple-element.87,, ...), kind=kLoop, calls=%fused_computation.649 | loop fusion | flops 4800512 | bytes 4472832 | tf_op jit(solution)/shard_map/add | solution.py:86
  119.2 8.2 %all-to-all-done.1 = f32[8,1,21120]{2,1,0:T(1,128)S(1)} async-done(((f32[8,1,21120]{2,1,0:T(1,128)}), f32[8,1,21120]{2,1,0:T(1,128)S(1)}, u32[]{:S(2)}, u32[]{:S(2)}) %all-to-all-start.1) | async-done | bytes 675872 | tf_op jit(solution)/shard_map/all_to_all | solution.py:160
  129.6 1.3 slice_reduce_fusion.2
  141.6 1.7 %collective-permute-start.3 = (f32[5,16,130]{2,0,1:T(8,128)}, f32[5,16,130]{2,0,1:T(8,128)}, u32[]{:S(2)}, u32[]{:S(2)}) collective-permute-start(f32[5,16,130]{2,0,1:T(8,128)} %fusion.5), channel_id=1, source_target_pairs={{0,16},{16,32},{32,48},{48,64},{64,80},{80,96},{96,112},{112,0},{1... | collective-permute-start | bytes 124808 | tf_op jit(solution)/shard_map/ppermute | solution.py:174
  145.5 1.3 fusion.602
  146.9 2.1 %collective-permute-done.3 = f32[5,16,130]{2,0,1:T(8,128)} collective-permute-done((f32[5,16,130]{2,0,1:T(8,128)}, f32[5,16,130]{2,0,1:T(8,128)}, u32[]{:S(2)}, u32[]{:S(2)}) %collective-permute-start.3) | collective-permute-done | bytes 41632 | tf_op jit(solution)/shard_map/ppermute | solution.py:174
  149.0 1.4 fusion.603
  (514 shorter events, 80.6 us)
Async XLA Ops:
  2.7 6.0 %collective-permute-start = (f32[157696]{0:T(1024)S(1)}, f32[157696]{0:T(1024)S(1)}, u32[]{:S(2)}, u32[]{:S(2)}) collective-permute-start(f32[157696]{0:T(1024)S(1)} %pad_maximum_fusion.2), channel_id=1, source_target_pairs={{0,1},{1,0},{2,3},{3,2},{4,5},{5,4},{6,7},{7,6},{8,9},{9,8},{10,11... | collective-permute-start | bytes 1892360 | tf_op jit(solution)/shard_map/ppermute | solution.py:127
  10.2 18.0 %copy-start.1 = (f32[8,16,128]{2,0,1:T(8,128)}, f32[8,16,128]{2,0,1:T(8,128)S(1)}, u32[]{:S(2)}) copy-start(f32[8,16,128]{2,0,1:T(8,128)S(1)} %get-tuple-element.134) | copy-start | bytes 196612
  10.2 18.3 %copy-start.5 = (f32[8,16,128]{2,0,1:T(8,128)}, f32[8,16,128]{2,0,1:T(8,128)S(1)}, u32[]{:S(2)}) copy-start(f32[8,16,128]{2,0,1:T(8,128)S(1)} %get-tuple-element.136) | copy-start | bytes 196612
  10.3 29.3 %copy-start.3 = (f32[8,16,128]{2,0,1:T(8,128)}, f32[8,16,128]{2,0,1:T(8,128)S(1)}, u32[]{:S(2)}) copy-start(f32[8,16,128]{2,0,1:T(8,128)S(1)} %get-tuple-element.135) | copy-start | bytes 196612
  16.2 12.0 %copy-start.15 = (f32[8,16,128]{2,0,1:T(8,128)}, f32[8,16,128]{2,0,1:T(8,128)S(1)}, u32[]{:S(2)}) copy-start(f32[8,16,128]{2,0,1:T(8,128)S(1)} %get-tuple-element.86) | copy-start | bytes 196612
  31.2 20.9 %all-to-all-start = ((f32[8,1,21120]{2,1,0:T(1,128)}), f32[8,1,21120]{2,1,0:T(1,128)S(1)}, u32[]{:S(2)}, u32[]{:S(2)}) async-start(f32[8,1,21120]{2,1,0:T(1,128)} %all_to_all.16), calls=%async_computation | async-start | bytes 1351680 | tf_op jit(solution)/shard_map/all_to_all | solution.py:160
  61.3 18.1 %copy-start.13 = (f32[8,16,127]{2,0,1:T(8,128)S(1)}, f32[8,16,127]{2,0,1:T(8,128)}, u32[]{:S(2)}) copy-start(f32[8,16,127]{2,0,1:T(8,128)} %slice.1357) | copy-start | bytes 195076
  81.5 8.2 %collective-permute-start.2 = (f32[5,16,130]{2,0,1:T(8,128)}, f32[5,16,130]{2,0,1:T(8,128)}, u32[]{:S(2)}, u32[]{:S(2)}) collective-permute-start(f32[5,16,130]{2,0,1:T(8,128)} %fusion.6), channel_id=1, source_target_pairs={{0,112},{16,0},{32,16},{48,32},{64,48},{80,64},{96,80},{112,96},{1... | collective-permute-start | bytes 124808 | tf_op jit(solution)/shard_map/ppermute | solution.py:175
  87.4 11.0 %copy-start.4 = (f32[8,16,128]{2,0,1:T(8,128)S(1)}, f32[8,16,128]{2,0,1:T(8,128)}, u32[]{:S(2)}) copy-start(f32[8,16,128]{2,0,1:T(8,128)} %copy-done.3) | copy-start | bytes 196612
  87.4 11.0 %copy-start.7 = (f32[8,16,128]{2,0,1:T(8,128)S(1)}, f32[8,16,128]{2,0,1:T(8,128)}, u32[]{:S(2)}) copy-start(f32[8,16,128]{2,0,1:T(8,128)} %copy-done.5) | copy-start | bytes 196612
  87.4 11.0 %copy-start.9 = (f32[8,16,128]{2,0,1:T(8,128)S(1)}, f32[8,16,128]{2,0,1:T(8,128)}, u32[]{:S(2)}) copy-start(f32[8,16,128]{2,0,1:T(8,128)} %copy-done.8) | copy-start | bytes 196612
  87.4 11.0 %copy-start.30 = (f32[7,16,128]{2,0,1:T(8,128)S(1)}, f32[7,16,128]{2,0,1:T(8,128)}, u32[]{:S(2)}) copy-start(f32[7,16,128]{2,0,1:T(8,128)} %pad_maximum_fusion.10) | copy-start | bytes 172036
  87.4 11.0 %copy-start.31 = (f32[7,16,128]{2,0,1:T(8,128)S(1)}, f32[7,16,128]{2,0,1:T(8,128)}, u32[]{:S(2)}) copy-start(f32[7,16,128]{2,0,1:T(8,128)} %pad_maximum_fusion.13) | copy-start | bytes 172036
  87.4 11.0 %copy-start.32 = (f32[7,16,128]{2,0,1:T(8,128)S(1)}, f32[7,16,128]{2,0,1:T(8,128)}, u32[]{:S(2)}) copy-start(f32[7,16,128]{2,0,1:T(8,128)} %pad_maximum_fusion.11) | copy-start | bytes 172036
  87.5 11.0 %copy-start.33 = (f32[7,16,128]{2,0,1:T(8,128)S(1)}, f32[7,16,128]{2,0,1:T(8,128)}, u32[]{:S(2)}) copy-start(f32[7,16,128]{2,0,1:T(8,128)} %pad_maximum_fusion.12) | copy-start | bytes 172036
  87.5 11.0 %copy-start.35 = (f32[7,16,128]{2,0,1:T(8,128)S(1)}, f32[7,16,128]{2,0,1:T(8,128)}, u32[]{:S(2)}) copy-start(f32[7,16,128]{2,0,1:T(8,128)} %get-tuple-element.242) | copy-start | bytes 172036
  87.5 11.0 %copy-start.36 = (f32[7,16,128]{2,0,1:T(8,128)S(1)}, f32[7,16,128]{2,0,1:T(8,128)}, u32[]{:S(2)}) copy-start(f32[7,16,128]{2,0,1:T(8,128)} %get-tuple-element.287) | copy-start | bytes 172036
  87.5 11.0 %copy-start.37 = (f32[8,16,127]{2,0,1:T(8,128)S(1)}, f32[8,16,127]{2,0,1:T(8,128)}, u32[]{:S(2)}) copy-start(f32[8,16,127]{2,0,1:T(8,128)} %get-tuple-element.248) | copy-start | bytes 195076
  87.5 11.0 %copy-start.62 = (f32[8,1,128]{2,0,1:T(8,128)S(1)}, f32[8,1,128]{2,0,1:T(8,128)}, u32[]{:S(2)}) copy-start(f32[8,1,128]{2,0,1:T(8,128)} %pad_maximum_fusion.27) | copy-start | bytes 12292
  87.6 12.6 %copy-start.64 = (f32[8,1,128]{2,0,1:T(8,128)}, f32[8,1,128]{2,0,1:T(8,128)S(1)}, u32[]{:S(2)}) copy-start(f32[8,1,128]{2,0,1:T(8,128)S(1)} %pad_maximum_fusion.28) | copy-start | bytes 12292
  89.7 7.3 %collective-permute-start.1 = (f32[5,16,130]{2,0,1:T(8,128)}, f32[5,16,130]{2,0,1:T(8,128)S(1)}, u32[]{:S(2)}, u32[]{:S(2)}) collective-permute-start(f32[5,16,130]{2,0,1:T(8,128)} %fusion.7), channel_id=1, source_target_pairs={{0,16},{16,32},{32,48},{48,64},{64,80},{80,96},{96,112},{112,0},{1... | collective-permute-start | bytes 124808 | tf_op jit(solution)/shard_map/ppermute | solution.py:174
  111.6 15.8 %all-to-all-start.1 = ((f32[8,1,21120]{2,1,0:T(1,128)}), f32[8,1,21120]{2,1,0:T(1,128)S(1)}, u32[]{:S(2)}, u32[]{:S(2)}) async-start(f32[8,1,21120]{2,1,0:T(1,128)} %all_to_all.19), calls=%async_computation.1 | async-start | bytes 1351680 | tf_op jit(solution)/shard_map/all_to_all | solution.py:160
  139.4 6.1 %collective-permute-start.4 = (f32[5,16,130]{2,0,1:T(8,128)S(1)}, f32[5,16,130]{2,0,1:T(8,128)}, u32[]{:S(2)}, u32[]{:S(2)}) collective-permute-start(f32[5,16,130]{2,0,1:T(8,128)S(1)} %fusion.4), channel_id=1, source_target_pairs={{0,112},{16,0},{32,16},{48,32},{64,48},{80,64},{96,80},{112,96},{1... | collective-permute-start | bytes 124808 | tf_op jit(solution)/shard_map/ppermute | solution.py:175
  141.6 7.4 %collective-permute-start.3 = (f32[5,16,130]{2,0,1:T(8,128)}, f32[5,16,130]{2,0,1:T(8,128)}, u32[]{:S(2)}, u32[]{:S(2)}) collective-permute-start(f32[5,16,130]{2,0,1:T(8,128)} %fusion.5), channel_id=1, source_target_pairs={{0,16},{16,32},{32,48},{48,64},{64,80},{80,96},{96,112},{112,0},{1... | collective-permute-start | bytes 124808 | tf_op jit(solution)/shard_map/ppermute | solution.py:174
  (74 other events, 257.4 us)

commit v2 on v1

v2 whole, which is shorter than its diff:
```python
import jax
import jax.numpy as jnp
import numpy as np
from jax import lax
from jax.sharding import PartitionSpec as P
from jax.experimental import pallas as pl
from jax.experimental.pallas import tpu as pltpu

STEPS = 2


velocity_table = (
    (0, 0, 0),
    (1, 0, 0),
    (-1, 0, 0),
    (0, 1, 0),
    (0, -1, 0),
    (0, 0, 1),
    (0, 0, -1),
    (1, 1, 0),
    (-1, -1, 0),
    (1, -1, 0),
    (-1, 1, 0),
    (1, 0, 1),
    (-1, 0, -1),
    (1, 0, -1),
    (-1, 0, 1),
    (0, 1, 1),
    (0, -1, -1),
    (0, 1, -1),
    (0, -1, 1),
)
weight_table = (1.0 / 3.0,) + (1.0 / 18.0,) * 6 + (1.0 / 36.0,) * 12
upward = (1, 7, 9, 11, 13)
downward = (2, 8, 10, 12, 14)
y_plus = tuple(m for m in range(19) if velocity_table[m][1] == 1)
y_minus = tuple(m for m in range(19) if velocity_table[m][1] == -1)
relax_rate = 1.25
plane_speed = 0.08


def total_density(states):
    density = states[0]
    for member in range(1, 19):
        density = density + states[member]
    return density


def moments(states):
    density = total_density(states)
    velocity = []
    for dim_index in range(3):
        momentum = None
        for member in range(19):
            sign_part = velocity_table[member][dim_index]
            if sign_part == 1:
                momentum = states[member] if momentum is None else momentum + states[member]
            elif sign_part == -1:
                momentum = momentum - states[member]
        velocity.append(momentum / density)
    return (density, velocity)


def speed_square(velocity):
    return velocity[0] * velocity[0] + velocity[1] * velocity[1] + velocity[2] * velocity[2]


def equilibrium(member, density, velocity, speed_sq):
    projected = None
    for dim_index in range(3):
        sign_part = velocity_table[member][dim_index]
        if sign_part != 0:
            summand = velocity[dim_index] if sign_part > 0 else -velocity[dim_index]
            projected = summand if projected is None else projected + summand
    if projected is None:
        return weight_table[member] * density * (1.0 - 1.5 * speed_sq)
    return (
        weight_table[member]
        * density
        * (1.0 + 3.0 * projected + 4.5 * projected * projected - 1.5 * speed_sq)
    )


def relax(states):
    density, velocity = moments(states)
    speed_sq = speed_square(velocity)
    return [
        states[member]
        + relax_rate * (equilibrium(member, density, velocity, speed_sq) - states[member])
        for member in range(19)
    ]


def corrected(plane, members, sign_part):
    density, velocity = moments(plane)
    speed_sq = speed_square(velocity)
    moved = [velocity[0], velocity[1] + sign_part * plane_speed, velocity[2]]
    moved_sq = speed_square(moved)
    return jnp.stack(
        [
            plane[member]
            + equilibrium(member, density, moved, moved_sq)
            - equilibrium(member, density, velocity, speed_sq)
            for member in members
        ]
    )


def link_hits(links, anchor, row_span):
    cell_y = links // 19 - anchor
    member = links % 19
    by_member = (member[:, :, None, :] == jnp.arange(19, dtype=jnp.int32)[:, None]).astype(jnp.bfloat16)
    by_cell = (cell_y[:, :, :, None] == jnp.arange(row_span, dtype=jnp.int32)).astype(jnp.bfloat16)
    return jnp.einsum("xzml,xzly->mxzy", by_member, by_cell, preferred_element_type=jnp.float32)


LANES = 128
FACE_ROWS = 2 * 5


def _roll(t, shift, axis):
    if isinstance(shift, int):
        shift = shift % t.shape[axis]
        if shift == 0:
            return t
    return pltpu.roll(t, shift, axis)


def _z_roll(t, step):
    half = t.shape[0] // 2
    a, b = t[:half], t[half:]
    row = lax.broadcasted_iota(jnp.int32, a.shape, 0)
    if step == 1:
        ra, rb = _roll(a, 1, 0), _roll(b, 1, 0)
        edge = row == 0
    else:
        ra, rb = _roll(a, half - 1, 0), _roll(b, half - 1, 0)
        edge = row == half - 1
    return jnp.concatenate([jnp.where(edge, rb, ra), jnp.where(edge, ra, rb)], axis=0)


def _emit_relax(cells_of_x, slab_width, relaxed_ref, chunk_ref, sc_ref, depth):
    lane = lax.broadcasted_iota(jnp.int32, (depth, LANES), 1)
    up_pack = jnp.zeros((depth, LANES), jnp.float32)
    down_pack = jnp.zeros((depth, LANES), jnp.float32)
    top = bottom = None
    for x in range(slab_width):
        r = relax(cells_of_x(x))
        for m in range(19):
            relaxed_ref[m, x] = r[m]
        if x == slab_width - 1:
            top = corrected(r, upward, -1.0)
        if x == 0:
            bottom = corrected(r, downward, 1.0)
        for i, m in enumerate(y_plus):
            k = i * slab_width + x
            up_pack = jnp.where(lane == k, _roll(r[m], k + 1, 1), up_pack)
        for i, m in enumerate(y_minus):
            k = i * slab_width + x
            down_pack = jnp.where(lane == k, _roll(r[m], k, 1), down_pack)
    faces = jnp.concatenate([top.reshape(5 * depth, LANES), bottom.reshape(5 * depth, LANES)], axis=0)
    to_next = jnp.full((depth, LANES), sc_ref[1], jnp.int32)
    to_prev = jnp.full((depth, LANES), sc_ref[2], jnp.int32)
    peers = chunk_ref.shape[0]
    for p in range(peers):
        chunk_ref[p, : FACE_ROWS * depth] = faces
        chunk_ref[p, FACE_ROWS * depth :] = jnp.where(to_next == p, up_pack, jnp.where(to_prev == p, down_pack, 0.0))


def _streamed(x, slab_width, relaxed_ref, rims_ref, low_ref, high_ref, hits_ref, depth):
    lane = lax.broadcasted_iota(jnp.int32, (depth, LANES), 1)
    out = []
    for n in range(19):
        step_x, step_y, step_z = velocity_table[n]
        xs = x - step_x
        if xs < 0:
            t = low_ref[upward.index(n)]
        elif xs >= slab_width:
            t = high_ref[downward.index(n)]
        else:
            t = relaxed_ref[n, xs]
            if step_y == 1:
                k = y_plus.index(n) * slab_width + xs
                t = jnp.where(lane == 0, _roll(rims_ref[0], LANES - k, 1), _roll(t, 1, 1))
            elif step_y == -1:
                k = y_minus.index(n) * slab_width + xs
                t = jnp.where(lane == LANES - 1, _roll(rims_ref[1], LANES - 1 - k, 1), _roll(t, LANES - 1, 1))
        if step_z != 0:
            t = _z_roll(t, step_z)
        out.append(t)
    result = [out[0]]
    for n in range(1, 19):
        source = n - 1 + 2 * (n % 2)
        result.append(jnp.where(hits_ref[source, x] > 0.5, relaxed_ref[source, x], out[n]))
    return result


def _first_kernel(sc_ref, states_ref, relaxed_ref, chunk_ref):
    slab_width, depth = states_ref.shape[1], states_ref.shape[2]
    _emit_relax(lambda x: [states_ref[m, x] for m in range(19)], slab_width, relaxed_ref, chunk_ref, sc_ref, depth)


def _middle_kernel(sc_ref, relaxed_ref, rims_ref, low_ref, high_ref, hits_ref, next_ref, chunk_ref):
    slab_width, depth = relaxed_ref.shape[1], relaxed_ref.shape[2]
    cells = lambda x: _streamed(x, slab_width, relaxed_ref, rims_ref, low_ref, high_ref, hits_ref, depth)
    _emit_relax(cells, slab_width, next_ref, chunk_ref, sc_ref, depth)


def _last_kernel(sc_ref, relaxed_ref, rims_ref, low_ref, high_ref, hits_ref, out_ref, density_ref):
    slab_width, depth = relaxed_ref.shape[1], relaxed_ref.shape[2]
    half = depth // 2
    lower = jnp.full((half, LANES), sc_ref[3], jnp.int32) == 0
    for x in range(slab_width):
        cells = _streamed(x, slab_width, relaxed_ref, rims_ref, low_ref, high_ref, hits_ref, depth)
        mine = [jnp.where(lower, c[:half], c[half:]) for c in cells]
        for m in range(19):
            out_ref[m, x] = mine[m]
        density_ref[x] = total_density(mine)


def _window_kernel(sc_ref, mix_ref, got_ref, send_ref, rims_ref):
    peers, _, lanes = got_ref.shape
    depth = send_ref.shape[2]
    me_y, offset = sc_ref[0], sc_ref[4]
    fraction, keep = mix_ref[0], mix_ref[1]
    flow_cells = peers * lanes
    anchor = me_y * lanes
    lane = lax.broadcasted_iota(jnp.int32, (depth, lanes), 1)

    def window(row0, start):
        start = (start + 2 * flow_cells) % flow_cells
        block = start // lanes
        off = start % lanes
        after = (block + 1) % peers
        shift = (lanes - off) % lanes
        first = pltpu.roll(got_ref[block, pl.ds(row0, depth), :], shift, 1)
        second = pltpu.roll(got_ref[after, pl.ds(row0, depth), :], shift, 1)
        return jnp.where(lane < lanes - off, first, second)

    for i, m in enumerate(upward):
        step_y = velocity_table[m][1]
        row0 = i * depth
        a = anchor - offset - step_y
        send_ref[0, i] = keep * window(row0, a) + fraction * window(row0, a - 1)
    for i, m in enumerate(downward):
        step_y = velocity_table[m][1]
        row0 = (5 + i) * depth
        c = anchor + offset - step_y
        send_ref[1, i] = fraction * window(row0, c + 1) + keep * window(row0, c)
    rims_ref[0] = got_ref[sc_ref[2], pl.ds(FACE_ROWS * depth, depth), :]
    rims_ref[1] = got_ref[sc_ref[1], pl.ds(FACE_ROWS * depth, depth), :]


def _vmem():
    return pl.BlockSpec(memory_space=pltpu.VMEM)


def _smem():
    return pl.BlockSpec(memory_space=pltpu.SMEM)


def _call(kernel, n_smem, n_vmem, out_shapes):
    return pl.pallas_call(
        kernel,
        out_shape=out_shapes,
        in_specs=[_smem()] * n_smem + [_vmem()] * n_vmem,
        out_specs=tuple(_vmem() for _ in out_shapes),
    )


def per_device(populations, le_shift, le_frac, links):
    n_members, slab_width, half_depth, row_span = populations.shape
    flow_cycle = lax.axis_size("gy")
    slab_cycle = lax.axis_size("gx")
    me_y = lax.axis_index("gy")
    me_z = lax.axis_index("gz")
    anchor = me_y * row_span

    size = populations.size
    packed = jnp.concatenate([populations.reshape(-1), links.astype(jnp.float32).reshape(-1)])
    other = lax.ppermute(packed, "gz", [(0, 1), (1, 0)])
    other_states = other[:size].reshape(populations.shape)
    other_links = other[size:].reshape(links.shape).astype(jnp.int32)
    first = me_z == 0
    states = jnp.where(
        first,
        jnp.concatenate([populations, other_states], axis=2),
        jnp.concatenate([other_states, populations], axis=2),
    )
    all_links = jnp.where(
        first, jnp.concatenate([links, other_links], axis=1), jnp.concatenate([other_links, links], axis=1)
    )
    depth = 2 * half_depth
    hits = link_hits(all_links, anchor, row_span)

    f32 = jnp.float32
    full = jax.ShapeDtypeStruct((n_members, slab_width, depth, row_span), f32)
    chunk = jax.ShapeDtypeStruct((flow_cycle, (FACE_ROWS + 1) * depth, row_span), f32)
    send = jax.ShapeDtypeStruct((2, 5, depth, row_span), f32)
    rims = jax.ShapeDtypeStruct((2, depth, row_span), f32)
    own = jax.ShapeDtypeStruct((n_members, slab_width, half_depth, row_span), f32)
    density = jax.ShapeDtypeStruct((slab_width, half_depth, row_span), f32)

    relaxed, chunks = None, None
    for section in range(STEPS):
        scalars = jnp.stack(
            [me_y, (me_y + 1) % flow_cycle, (me_y - 1 + flow_cycle) % flow_cycle, me_z, le_shift[section]]
        ).astype(jnp.int32)
        fraction = le_frac[section].astype(f32) / 256.0
        mix = jnp.stack([fraction, 1.0 - fraction])
        if section == 0:
            relaxed, chunks = _call(_first_kernel, 1, 1, (full, chunk))(scalars, states)
        got = lax.all_to_all(chunks, "gy", 0, 0, tiled=True)
        sends, rim_pair = _call(_window_kernel, 2, 1, (send, rims))(scalars, mix, got)
        low_ghost = lax.ppermute(sends[0], "gx", [(i, (i + 1) % slab_cycle) for i in range(slab_cycle)])
        high_ghost = lax.ppermute(sends[1], "gx", [(i, (i - 1) % slab_cycle) for i in range(slab_cycle)])
        if section + 1 < STEPS:
            relaxed, chunks = _call(_middle_kernel, 1, 5, (full, chunk))(
                scalars, relaxed, rim_pair, low_ghost, high_ghost, hits
            )
        else:
            final, dens = _call(_last_kernel, 1, 5, (own, density))(
                scalars, relaxed, rim_pair, low_ghost, high_ghost, hits
            )
    return (final, dens)


def solution(mesh):
    in_specs = (P(None, "gx", "gz", "gy"), P(), P(), P("gx", "gz", "gy"))
    out_specs = (P(None, "gx", "gz", "gy"), P("gx", "gz", "gy"))
    return jax.shard_map(
        per_device, mesh=mesh, in_specs=in_specs, out_specs=out_specs, check_vma=False
    )
```

time: 156 us -> 79.9 us (0.51)
  local copies, waits for them, and re-layouts: 64.8 us -> 9.62 us
  other arithmetic: 39.2 us -> 4.42 us
  Pallas kernels: 0 us -> 14.5 us
  waiting for transfers between devices: 25.4 us -> 30.5 us
  between operations: 6.97 us -> 2.1 us
    slice x89 -> x2, local copies, waits for them, and re-layouts: 24.8 us -> 1.24 us  [the longest x1 0.66 us: per_device(): fraction = le_frac[section].astype(f32) / 256.0]
    concatenate x54 -> x0, other arithmetic: 21.3 us -> none  [the longest x23 7.3 us: per_device(): cells = jnp.roll(cells, step_z, axis=1)]
    pallas_call x0 -> x5, Pallas kernels: none -> 14.5 us  [the longest x1 4.33 us: per_device(): _call(_middle_kernel, 1, 5, (full, chunk))]
    another operation x47 -> x2, local copies, waits for them, and re-layouts: 15.2 us -> 2.34 us  [per_device(): jnp.stack([me_y, (me_y + 1) % flow_cycle, (me_y - 1 + flow_cycle) % flow_...]
    concatenate x21 -> x0, local copies, waits for them, and re-layouts: 10.2 us -> none  [the longest x7 4.35 us: per_device(): cells = jnp.roll(cells, step_z, axis=1)]
    add x16 -> x0, other arithmetic: 9.02 us -> none  [the longest x7 5.65 us: relax(): states[member]]
    unnamed x229 -> x20, local copies, waits for them, and re-layouts: 7.42 us -> 2.97 us
    select_n x10 -> x0, other arithmetic: 3.24 us -> none  [the longest x8 3.09 us: per_device(): bounced.append(jnp.where(hits[source], relaxed[source], result[member]))]
  transfers between devices with their start and end apart: 7 -> 7, of which waited for: 4 -> 6; matrix products, arithmetic and copies ran while one was open for 14% -> 10% of each run, Pallas kernels for 0% -> 0%
where the time goes in v2:
time: 79.9 us; the launch traced here: 79.3 us
  waiting for transfers between devices  30.5 us (38%)
  starting transfers between devices  16.8 us (21%)
  Pallas kernels  14.5 us (18%)
  local copies, waits for them, and re-layouts  9.62 us (12%)
  other arithmetic  4.42 us (6%)
  between operations  2.1 us (3%)
  matrix products  1.34 us (2%)
    all_to_all x2, waiting for transfers between devices, per_device(): got = lax.all_to_all(chunks, 'gy', 0, 0, tiled=True)  21.8 us
    all_to_all x2, starting transfers between devices, per_device(): got = lax.all_to_all(chunks, 'gy', 0, 0, tiled=True)  10.6 us
    ppermute x2, waiting for transfers between devices, per_device(): lax.ppermute(sends[0], 'gx', [(i, (i + 1) % slab_cycle) for i in range(sl...  6.56 us
    ppermute x2, starting transfers between devices, per_device(): lax.ppermute(sends[1], 'gx', [(i, (i - 1) % slab_cycle) for i in range(sl...  5.04 us
    pallas_call x1, Pallas kernels, per_device(): _call(_middle_kernel, 1, 5, (full, chunk))  4.33 us
    pallas_call x2, Pallas kernels, per_device(): _call(_window_kernel, 2, 1, (send, rims))(scalars, mix, got)  3.95 us
    pallas_call x1, Pallas kernels, per_device(): relaxed, chunks = _call(_first_kernel, 1, 1, (full, chunk))(scalars, states)  3.29 us
    unnamed x20, local copies, waits for them, and re-layouts  2.97 us
  transfers between devices with their start and end apart: 7, of which 6 were waited for; matrix products, arithmetic and copies ran while one was open for 10% of the time, Pallas kernels for 0%

profile of v2, /device:TPU:0, one launch (start us, length us, event | category | flops | bytes accessed | tf_op | source)
XLA Modules:
  0.0 79.3 jit_solution(2550491989076918007)
XLA Ops:
  1.5 1.2 %pad_maximum_fusion = f32[157696]{0:T(1024)S(1)} fusion(f32[2048]{0:T(1024)S(1)} %reshape.112, f32[155648]{0:T(1024)} %bitcast.19), kind=kLoop, calls=%fused_computation.7 | loop fusion | flops 157696 | bytes 1261568 | tf_op jit(solution)/shard_map/concatenate | solution.py:280
  3.4 1.2 %stack.37.sc_ref = s32[5]{0:T(128)} concatenate(s32[1]{0:T(128)} %bitcast, s32[1]{0:T(128)} %bitcast.1, s32[1]{0:T(128)} %bitcast.2, s32[1]{0:T(128)} %bitcast.3, s32[1]{0:T(128)} %get-tuple-element.26), dimensions={0} | concatenate | bytes 40 | tf_op jit(solution)/shard_map/stack | solution.py:306
  4.9 1.1 %maximum_select_fusion.states_ref = f32[19,8,16,128]{3,2,1,0:T(8,128)} fusion(f32[19,8,8,128]{3,2,1,0:T(8,128)S(1)} %bitcast.20, f32[19,8,8,128]{3,2,1,0:T(8,128)S(1)} %copy-done.2, pred[]{:T(512)S(6)} %eq.36), kind=kLoop, calls=%fused_computation.3 | loop fusion | flops 933888 | bytes 2490369 | tf_op jit(solution)/shard_map/jit(_where)/select_n | solution.py:285
  6.0 3.3 %shard_map.59 = (f32[19,8,16,128]{3,2,1,0:T(8,128)}, f32[8,176,128]{2,1,0:T(8,128)}) custom-call(s32[5]{0:T(128)} %stack.37.sc_ref, f32[19,8,16,128]{3,2,1,0:T(8,128)} %maximum_select_fusion.states_ref), custom_call_target="tpu_custom_call" | custom-call | tf_op jit(solution)/shard_map/pallas_call | solution.py:312
  9.3 7.0 %all-to-all-start = ((f32[8,176,128]{2,1,0:T(8,128)}), f32[8,176,128]{2,1,0:T(8,128)S(1)}, u32[]{:S(2)}, u32[]{:S(2)}) async-start(f32[8,176,128]{2,1,0:T(8,128)} %get-tuple-element.11), calls=%async_computation | async-start | bytes 1441792 | tf_op jit(solution)/shard_map/all_to_all | solution.py:313
  18.5 12.0 %all-to-all-done.got_ref = f32[8,176,128]{2,1,0:T(8,128)S(1)} async-done(((f32[8,176,128]{2,1,0:T(8,128)}), f32[8,176,128]{2,1,0:T(8,128)S(1)}, u32[]{:S(2)}, u32[]{:S(2)}) %all-to-all-start) | async-done | bytes 720928 | tf_op jit(solution)/shard_map/all_to_all | solution.py:313
  30.4 0.9 %copy-done = f32[8,176,128]{2,1,0:T(8,128)} copy-done((f32[8,176,128]{2,1,0:T(8,128)}, f32[8,176,128]{2,1,0:T(8,128)S(1)}, u32[]{:S(2)}) %copy-start) | copy-done | bytes 720920
  31.3 2.0 %shard_map.60 = (f32[2,5,16,128]{3,2,1,0:T(8,128)}, f32[2,16,128]{2,1,0:T(8,128)}) custom-call(s32[5]{0:T(128)} %stack.37.sc_ref, f32[2]{0:T(128)} %pad_maximum_fusion.1.mix_ref, f32[8,176,128]{2,1,0:T(8,128)} %copy-done), custom_call_target="tpu_custom_call" | custom-call | tf_op jit(solution)/shard_map/pallas_call | solution.py:314
  33.3 0.8 %slice_bitcast_fusion.2 = (f32[5,16,128]{2,1,0:T(8,128)S(1)}, f32[5,16,128]{2,1,0:T(8,128)S(1)}) fusion(f32[2,5,16,128]{3,2,1,0:T(8,128)} %get-tuple-element.13), kind=kLoop, calls=%fused_computation.17 | loop fusion | bytes 163840 | tf_op jit(solution)/shard_map/squeeze | solution.py:316
  34.1 4.1 %collective-permute-start.2 = (f32[5,16,128]{2,1,0:T(8,128)S(1)}, f32[5,16,128]{2,1,0:T(8,128)S(1)}, u32[]{:S(2)}, u32[]{:S(2)}) collective-permute-start(f32[5,16,128]{2,1,0:T(8,128)S(1)} %get-tuple-element.20), channel_id=1, source_target_pairs={{0,112},{16,0},{32,16},{48,32},{64,48},{80,64},{96,80},{112,96},{1... | collective-permute-start | bytes 122888 | tf_op jit(solution)/shard_map/ppermute | solution.py:316
  38.2 1.3 %fusion = f32[8,16,128,19]{2,3,1,0:T(8,128)S(1)} fusion(s32[8,16,32]{2,1,0:T(8,128)S(1)} %get-tuple-element.23, s32[8,16,32]{2,1,0:T(8,128)S(1)} %get-tuple-element.22), kind=kOutput, calls=%fused_computation.1 | convolution fusion | flops 20525056 | bytes 1277952 | tf_op jit(solution)/shard_map/xzml,xzly->mxzy/dot_general | solution.py:114
  39.5 1.3 %copy.8 = f32[8,16,128,19]{2,1,0,3:T(8,128)} copy(f32[8,16,128,19]{2,3,1,0:T(8,128)S(1)} %fusion) | data formatting | bytes 2490368 | tf_op jit(solution)/shard_map/xzml,xzly->mxzy/dot_general | solution.py:114
  40.8 3.5 %collective-permute-done.1.low_ref = f32[5,16,128]{2,1,0:T(8,128)S(1)} collective-permute-done((f32[5,16,128]{2,1,0:T(8,128)S(1)}, f32[5,16,128]{2,1,0:T(8,128)S(1)}, u32[]{:S(2)}, u32[]{:S(2)}) %collective-permute-start.1) | collective-permute-done | bytes 40992 | tf_op jit(solution)/shard_map/ppermute | solution.py:315
  44.9 4.3 %shard_map.61 = (f32[19,8,16,128]{3,2,1,0:T(8,128)}, f32[8,176,128]{2,1,0:T(8,128)}) custom-call(s32[5]{0:T(128)} %stack.37.sc_ref, f32[19,8,16,128]{3,2,1,0:T(8,128)} %get-tuple-element.10.relaxed_ref, f32[2,16,128]{2,1,0:T(8,128)} %get-tuple-element.12.rims_ref, f32[5,16,128]{2,1,0:T(8,128)} %copy-done.5, f32[5,16,128]{2,1,0:T(8,128)} %copy-done.4, ...), custom_call_target="tpu_custom_call" | custom-call | tf_op jit(solution)/shard_map/pallas_call | solution.py:318
  49.2 3.5 %all-to-all-start.1 = ((f32[8,176,128]{2,1,0:T(8,128)}), f32[8,176,128]{2,1,0:T(8,128)S(1)}, u32[]{:S(2)}, u32[]{:S(2)}) async-start(f32[8,176,128]{2,1,0:T(8,128)} %get-tuple-element.15), calls=%async_computation.1 | async-start | bytes 1441792 | tf_op jit(solution)/shard_map/all_to_all | solution.py:313
  52.8 1.1 %stack.36.sc_ref = s32[5]{0:T(128)} concatenate(s32[1]{0:T(128)} %bitcast, s32[1]{0:T(128)} %bitcast.1, s32[1]{0:T(128)} %bitcast.2, s32[1]{0:T(128)} %bitcast.3, s32[1]{0:T(128)} %get-tuple-element.27), dimensions={0} | concatenate | bytes 40 | tf_op jit(solution)/shard_map/stack | solution.py:306
  55.2 9.8 %all-to-all-done.1.got_ref = f32[8,176,128]{2,1,0:T(8,128)S(1)} async-done(((f32[8,176,128]{2,1,0:T(8,128)}), f32[8,176,128]{2,1,0:T(8,128)S(1)}, u32[]{:S(2)}, u32[]{:S(2)}) %all-to-all-start.1) | async-done | bytes 720928 | tf_op jit(solution)/shard_map/all_to_all | solution.py:313
  65.0 0.9 %copy-done.1 = f32[8,176,128]{2,1,0:T(8,128)} copy-done((f32[8,176,128]{2,1,0:T(8,128)}, f32[8,176,128]{2,1,0:T(8,128)S(1)}, u32[]{:S(2)}) %copy-start.1) | copy-done | bytes 720920
  65.9 2.0 %shard_map.62 = (f32[2,5,16,128]{3,2,1,0:T(8,128)}, f32[2,16,128]{2,1,0:T(8,128)}) custom-call(s32[5]{0:T(128)} %stack.36.sc_ref, f32[2]{0:T(128)} %pad_maximum_fusion.2.mix_ref, f32[8,176,128]{2,1,0:T(8,128)} %copy-done.1), custom_call_target="tpu_custom_call" | custom-call | tf_op jit(solution)/shard_map/pallas_call | solution.py:314
  68.6 1.0 %collective-permute-start.4 = (f32[5,16,128]{2,1,0:T(8,128)S(1)}, f32[5,16,128]{2,1,0:T(8,128)S(1)}, u32[]{:S(2)}, u32[]{:S(2)}) collective-permute-start(f32[5,16,128]{2,1,0:T(8,128)S(1)} %get-tuple-element.18), channel_id=1, source_target_pairs={{0,112},{16,0},{32,16},{48,32},{64,48},{80,64},{96,80},{112,96},{1... | collective-permute-start | bytes 122888 | tf_op jit(solution)/shard_map/ppermute | solution.py:316
  69.6 1.1 %collective-permute-start.3 = (f32[5,16,128]{2,1,0:T(8,128)S(1)}, f32[5,16,128]{2,1,0:T(8,128)S(1)}, u32[]{:S(2)}, u32[]{:S(2)}) collective-permute-start(f32[5,16,128]{2,1,0:T(8,128)S(1)} %get-tuple-element.19), channel_id=1, source_target_pairs={{0,16},{16,32},{32,48},{48,64},{64,80},{80,96},{96,112},{112,0},{1... | collective-permute-start | bytes 122888 | tf_op jit(solution)/shard_map/ppermute | solution.py:315
  70.7 2.0 %collective-permute-done.4.high_ref = f32[5,16,128]{2,1,0:T(8,128)S(1)} collective-permute-done((f32[5,16,128]{2,1,0:T(8,128)S(1)}, f32[5,16,128]{2,1,0:T(8,128)S(1)}, u32[]{:S(2)}, u32[]{:S(2)}) %collective-permute-start.4) | collective-permute-done | bytes 40992 | tf_op jit(solution)/shard_map/ppermute | solution.py:316
  72.7 3.1 %collective-permute-done.3.low_ref = f32[5,16,128]{2,1,0:T(8,128)S(1)} collective-permute-done((f32[5,16,128]{2,1,0:T(8,128)S(1)}, f32[5,16,128]{2,1,0:T(8,128)S(1)}, u32[]{:S(2)}, u32[]{:S(2)}) %collective-permute-start.3) | collective-permute-done | bytes 40992 | tf_op jit(solution)/shard_map/ppermute | solution.py:315
  76.3 2.9 %shard_map.63 = (f32[19,8,8,128]{3,2,1,0:T(8,128)}, f32[8,8,128]{2,1,0:T(8,128)}) custom-call(s32[5]{0:T(128)} %stack.36.sc_ref, f32[19,8,16,128]{3,2,1,0:T(8,128)} %get-tuple-element.14.relaxed_ref, f32[2,16,128]{2,1,0:T(8,128)} %get-tuple-element.16.rims_ref, f32[5,16,128]{2,1,0:T(8,128)} %copy-done.7, f32[5,16,128]{2,1,0:T(8,128)} %copy-done.6, ...), custom_call_target="tpu_custom_call" | custom-call | tf_op jit(solution)/shard_map/pallas_call | solution.py:322
  (33 shorter events, 5.9 us)
Async XLA Ops:
  0.6 2.2 %copy-start.8 = (s32[2]{0:T(128)S(1)}, s32[2]{0:T(128)}, u32[]{:S(2)}) copy-start(s32[2]{0:T(128)} %param.5) | copy-start | bytes 28
  1.5 3.4 %copy-start.2 = (f32[19,8,8,128]{3,2,1,0:T(8,128)S(1)}, f32[19,8,8,128]{3,2,1,0:T(8,128)}, u32[]{:S(2)}) copy-start(f32[19,8,8,128]{3,2,1,0:T(8,128)} %param.4) | copy-start | bytes 1867780
  2.7 2.1 %collective-permute-start = (f32[157696]{0:T(1024)S(1)}, f32[157696]{0:T(1024)S(1)}, u32[]{:S(2)}, u32[]{:S(2)}) collective-permute-start(f32[157696]{0:T(1024)S(1)} %pad_maximum_fusion), channel_id=1, source_target_pairs={{0,1},{1,0},{2,3},{3,2},{4,5},{5,4},{6,7},{7,6},{8,9},{9,8},{10,11... | collective-permute-start | bytes 1892360 | tf_op jit(solution)/shard_map/ppermute | solution.py:281
  6.0 10.3 %copy-start.9 = (s32[2]{0:T(128)S(1)}, s32[2]{0:T(128)}, u32[]{:S(2)}) copy-start(s32[2]{0:T(128)} %param.6) | copy-start | bytes 28
  6.0 12.4 %copy-start.3 = (s32[8,8,32]{2,1,0:T(8,128)S(1)}, s32[8,8,32]{2,1,0:T(8,128)}, u32[]{:S(2)}) copy-start(s32[8,8,32]{2,1,0:T(8,128)} %param.7) | copy-start | bytes 24580
  9.3 21.1 %all-to-all-start = ((f32[8,176,128]{2,1,0:T(8,128)}), f32[8,176,128]{2,1,0:T(8,128)S(1)}, u32[]{:S(2)}, u32[]{:S(2)}) async-start(f32[8,176,128]{2,1,0:T(8,128)} %get-tuple-element.11), calls=%async_computation | async-start | bytes 1441792 | tf_op jit(solution)/shard_map/all_to_all | solution.py:313
  30.4 0.9 %copy-start = (f32[8,176,128]{2,1,0:T(8,128)}, f32[8,176,128]{2,1,0:T(8,128)S(1)}, u32[]{:S(2)}) copy-start(f32[8,176,128]{2,1,0:T(8,128)S(1)} %all-to-all-done.got_ref) | copy-start | bytes 2162692
  34.1 6.7 %collective-permute-start.2 = (f32[5,16,128]{2,1,0:T(8,128)S(1)}, f32[5,16,128]{2,1,0:T(8,128)S(1)}, u32[]{:S(2)}, u32[]{:S(2)}) collective-permute-start(f32[5,16,128]{2,1,0:T(8,128)S(1)} %get-tuple-element.20), channel_id=1, source_target_pairs={{0,112},{16,0},{32,16},{48,32},{64,48},{80,64},{96,80},{112,96},{1... | collective-permute-start | bytes 122888 | tf_op jit(solution)/shard_map/ppermute | solution.py:316
  38.2 6.1 %collective-permute-start.1 = (f32[5,16,128]{2,1,0:T(8,128)S(1)}, f32[5,16,128]{2,1,0:T(8,128)S(1)}, u32[]{:S(2)}, u32[]{:S(2)}) collective-permute-start(f32[5,16,128]{2,1,0:T(8,128)S(1)} %get-tuple-element.21), channel_id=1, source_target_pairs={{0,16},{16,32},{32,48},{48,64},{64,80},{80,96},{96,112},{112,0},{1... | collective-permute-start | bytes 122888 | tf_op jit(solution)/shard_map/ppermute | solution.py:315
  40.8 3.5 %copy-start.4 = (f32[5,16,128]{2,1,0:T(8,128)}, f32[5,16,128]{2,1,0:T(8,128)S(1)}, u32[]{:S(2)}) copy-start(f32[5,16,128]{2,1,0:T(8,128)S(1)} %collective-permute-done.2.high_ref) | copy-start | bytes 122884
  44.3 0.6 copy-start.5
  49.2 15.8 %all-to-all-start.1 = ((f32[8,176,128]{2,1,0:T(8,128)}), f32[8,176,128]{2,1,0:T(8,128)S(1)}, u32[]{:S(2)}, u32[]{:S(2)}) async-start(f32[8,176,128]{2,1,0:T(8,128)} %get-tuple-element.15), calls=%async_computation.1 | async-start | bytes 1441792 | tf_op jit(solution)/shard_map/all_to_all | solution.py:313
  65.0 0.9 %copy-start.1 = (f32[8,176,128]{2,1,0:T(8,128)}, f32[8,176,128]{2,1,0:T(8,128)S(1)}, u32[]{:S(2)}) copy-start(f32[8,176,128]{2,1,0:T(8,128)S(1)} %all-to-all-done.1.got_ref) | copy-start | bytes 2162692
  68.6 4.0 %collective-permute-start.4 = (f32[5,16,128]{2,1,0:T(8,128)S(1)}, f32[5,16,128]{2,1,0:T(8,128)S(1)}, u32[]{:S(2)}, u32[]{:S(2)}) collective-permute-start(f32[5,16,128]{2,1,0:T(8,128)S(1)} %get-tuple-element.18), channel_id=1, source_target_pairs={{0,112},{16,0},{32,16},{48,32},{64,48},{80,64},{96,80},{112,96},{1... | collective-permute-start | bytes 122888 | tf_op jit(solution)/shard_map/ppermute | solution.py:316
  69.6 6.1 %collective-permute-start.3 = (f32[5,16,128]{2,1,0:T(8,128)S(1)}, f32[5,16,128]{2,1,0:T(8,128)S(1)}, u32[]{:S(2)}, u32[]{:S(2)}) collective-permute-start(f32[5,16,128]{2,1,0:T(8,128)S(1)} %get-tuple-element.19), channel_id=1, source_target_pairs={{0,16},{16,32},{32,48},{48,64},{64,80},{80,96},{96,112},{112,0},{1... | collective-permute-start | bytes 122888 | tf_op jit(solution)/shard_map/ppermute | solution.py:315
  72.7 3.1 %copy-start.6 = (f32[5,16,128]{2,1,0:T(8,128)}, f32[5,16,128]{2,1,0:T(8,128)S(1)}, u32[]{:S(2)}) copy-start(f32[5,16,128]{2,1,0:T(8,128)S(1)} %collective-permute-done.4.high_ref) | copy-start | bytes 122884
  75.7 0.6 copy-start.7

commit v3 on v2

--- a/solution.py
+++ b/solution.py
@@ -1,3 +1,5 @@
+import functools
+
 import jax
 import jax.numpy as jnp
 import numpy as np
@@ -139,7 +141,13 @@
     return jnp.concatenate([jnp.where(edge, rb, ra), jnp.where(edge, ra, rb)], axis=0)
 
 
-def _emit_relax(cells_of_x, slab_width, relaxed_ref, chunk_ref, sc_ref, depth):
+def _positions():
+    flow_cycle = lax.axis_size("gy")
+    me_y = lax.axis_index("gy")
+    return me_y, (me_y + 1) % flow_cycle, (me_y - 1 + flow_cycle) % flow_cycle, lax.axis_index("gz")
+
+
+def _emit_relax(cells_of_x, slab_width, relaxed_ref, chunk_ref, depth):
     lane = lax.broadcasted_iota(jnp.int32, (depth, LANES), 1)
     up_pack = jnp.zeros((depth, LANES), jnp.float32)
     down_pack = jnp.zeros((depth, LANES), jnp.float32)
@@ -159,8 +167,9 @@
             k = i * slab_width + x
             down_pack = jnp.where(lane == k, _roll(r[m], k, 1), down_pack)
     faces = jnp.concatenate([top.reshape(5 * depth, LANES), bottom.reshape(5 * depth, LANES)], axis=0)
-    to_next = jnp.full((depth, LANES), sc_ref[1], jnp.int32)
-    to_prev = jnp.full((depth, LANES), sc_ref[2], jnp.int32)
+    _, after, before, _ = _positions()
+    to_next = jnp.full((depth, LANES), after, jnp.int32)
+    to_prev = jnp.full((depth, LANES), before, jnp.int32)
     peers = chunk_ref.shape[0]
     for p in range(peers):
         chunk_ref[p, : FACE_ROWS * depth] = faces
@@ -195,21 +204,31 @@
     return result
 
 
-def _first_kernel(sc_ref, states_ref, relaxed_ref, chunk_ref):
-    slab_width, depth = states_ref.shape[1], states_ref.shape[2]
-    _emit_relax(lambda x: [states_ref[m, x] for m in range(19)], slab_width, relaxed_ref, chunk_ref, sc_ref, depth)
-
-
-def _middle_kernel(sc_ref, relaxed_ref, rims_ref, low_ref, high_ref, hits_ref, next_ref, chunk_ref):
+def _first_kernel(mine_ref, other_ref, relaxed_ref, chunk_ref):
+    slab_width, half = mine_ref.shape[1], mine_ref.shape[2]
+    depth = 2 * half
+    lower = jnp.full((half, LANES), _positions()[3], jnp.int32) == 0
+
+    def cells(x):
+        out = []
+        for m in range(19):
+            a, b = mine_ref[m, x], other_ref[m, x]
+            out.append(jnp.concatenate([jnp.where(lower, a, b), jnp.where(lower, b, a)], axis=0))
+        return out
+
+    _emit_relax(cells, slab_width, relaxed_ref, chunk_ref, depth)
+
+
+def _middle_kernel(relaxed_ref, rims_ref, low_ref, high_ref, hits_ref, next_ref, chunk_ref):
     slab_width, depth = relaxed_ref.shape[1], relaxed_ref.shape[2]
     cells = lambda x: _streamed(x, slab_width, relaxed_ref, rims_ref, low_ref, high_ref, hits_ref, depth)
-    _emit_relax(cells, slab_width, next_ref, chunk_ref, sc_ref, depth)
-
-
-def _last_kernel(sc_ref, relaxed_ref, rims_ref, low_ref, high_ref, hits_ref, out_ref, density_ref):
+    _emit_relax(cells, slab_width, next_ref, chunk_ref, depth)
+
+
+def _last_kernel(relaxed_ref, rims_ref, low_ref, high_ref, hits_ref, out_ref, density_ref):
     slab_width, depth = relaxed_ref.shape[1], relaxed_ref.shape[2]
     half = depth // 2
-    lower = jnp.full((half, LANES), sc_ref[3], jnp.int32) == 0
+    lower = jnp.full((half, LANES), _positions()[3], jnp.int32) == 0
     for x in range(slab_width):
         cells = _streamed(x, slab_width, relaxed_ref, rims_ref, low_ref, high_ref, hits_ref, depth)
         mine = [jnp.where(lower, c[:half], c[half:]) for c in cells]
@@ -218,11 +237,13 @@
         density_ref[x] = total_density(mine)
 
 
-def _window_kernel(sc_ref, mix_ref, got_ref, send_ref, rims_ref):
+def _window_kernel(section, shift_ref, frac_ref, got_ref, low_ref, high_ref, rims_ref):
     peers, _, lanes = got_ref.shape
-    depth = send_ref.shape[2]
-    me_y, offset = sc_ref[0], sc_ref[4]
-    fraction, keep = mix_ref[0], mix_ref[1]
+    depth = low_ref.shape[1]
+    me_y, after, before, _ = _positions()
+    offset = shift_ref[section]
+    fraction = jnp.full((depth, lanes), frac_ref[section], jnp.int32).astype(jnp.float32) / 256.0
+    keep = 1.0 - fraction
     flow_cells = peers * lanes
     anchor = me_y * lanes
     lane = lax.broadcasted_iota(jnp.int32, (depth, lanes), 1)
@@ -241,14 +262,14 @@
         step_y = velocity_table[m][1]
         row0 = i * depth
         a = anchor - offset - step_y
-        send_ref[0, i] = keep * window(row0, a) + fraction * window(row0, a - 1)
+        low_ref[i] = keep * window(row0, a) + fraction * window(row0, a - 1)
     for i, m in enumerate(downward):
         step_y = velocity_table[m][1]
         row0 = (5 + i) * depth
         c = anchor + offset - step_y
-        send_ref[1, i] = fraction * window(row0, c + 1) + keep * window(row0, c)
-    rims_ref[0] = got_ref[sc_ref[2], pl.ds(FACE_ROWS * depth, depth), :]
-    rims_ref[1] = got_ref[sc_ref[1], pl.ds(FACE_ROWS * depth, depth), :]
+        high_ref[i] = fraction * window(row0, c + 1) + keep * window(row0, c)
+    rims_ref[0] = got_ref[before, pl.ds(FACE_ROWS * depth, depth), :]
+    rims_ref[1] = got_ref[after, pl.ds(FACE_ROWS * depth, depth), :]
 
 
 def _vmem():
@@ -276,19 +297,10 @@
     me_z = lax.axis_index("gz")
     anchor = me_y * row_span
 
-    size = populations.size
-    packed = jnp.concatenate([populations.reshape(-1), links.astype(jnp.float32).reshape(-1)])
-    other = lax.ppermute(packed, "gz", [(0, 1), (1, 0)])
-    other_states = other[:size].reshape(populations.shape)
-    other_links = other[size:].reshape(links.shape).astype(jnp.int32)
-    first = me_z == 0
-    states = jnp.where(
-        first,
-        jnp.concatenate([populations, other_states], axis=2),
-        jnp.concatenate([other_states, populations], axis=2),
-    )
+    other_states = lax.ppermute(populations, "gz", [(0, 1), (1, 0)])
+    other_links = lax.ppermute(links, "gz", [(0, 1), (1, 0)])
     all_links = jnp.where(
-        first, jnp.concatenate([links, other_links], axis=1), jnp.concatenate([other_links, links], axis=1)
+        me_z == 0, jnp.concatenate([links, other_links], axis=1), jnp.concatenate([other_links, links], axis=1)
     )
     depth = 2 * half_depth
     hits = link_hits(all_links, anchor, row_span)
@@ -296,32 +308,23 @@
     f32 = jnp.float32
     full = jax.ShapeDtypeStruct((n_members, slab_width, depth, row_span), f32)
     chunk = jax.ShapeDtypeStruct((flow_cycle, (FACE_ROWS + 1) * depth, row_span), f32)
-    send = jax.ShapeDtypeStruct((2, 5, depth, row_span), f32)
+    ghost = jax.ShapeDtypeStruct((5, depth, row_span), f32)
     rims = jax.ShapeDtypeStruct((2, depth, row_span), f32)
     own = jax.ShapeDtypeStruct((n_members, slab_width, half_depth, row_span), f32)
     density = jax.ShapeDtypeStruct((slab_width, half_depth, row_span), f32)
 
-    relaxed, chunks = None, None
+    relaxed, chunks = _call(_first_kernel, 0, 2, (full, chunk))(populations, other_states)
     for section in range(STEPS):
-        scalars = jnp.stack(
-            [me_y, (me_y + 1) % flow_cycle, (me_y - 1 + flow_cycle) % flow_cycle, me_z, le_shift[section]]
-        ).astype(jnp.int32)
-        fraction = le_frac[section].astype(f32) / 256.0
-        mix = jnp.stack([fraction, 1.0 - fraction])
-        if section == 0:
-            relaxed, chunks = _call(_first_kernel, 1, 1, (full, chunk))(scalars, states)
         got = lax.all_to_all(chunks, "gy", 0, 0, tiled=True)
-        sends, rim_pair = _call(_window_kernel, 2, 1, (send, rims))(scalars, mix, got)
-        low_ghost = lax.ppermute(sends[0], "gx", [(i, (i + 1) % slab_cycle) for i in range(slab_cycle)])
-        high_ghost = lax.ppermute(sends[1], "gx", [(i, (i - 1) % slab_cycle) for i in range(slab_cycle)])
+        low_send, high_send, rim_pair = _call(functools.partial(_window_kernel, section), 2, 1, (ghost, ghost, rims))(
+            le_shift, le_frac, got
+        )
+        low_ghost = lax.ppermute(low_send, "gx", [(i, (i + 1) % slab_cycle) for i in range(slab_cycle)])
+        high_ghost = lax.ppermute(high_send, "gx", [(i, (i - 1) % slab_cycle) for i in range(slab_cycle)])
         if section + 1 < STEPS:
-            relaxed, chunks = _call(_middle_kernel, 1, 5, (full, chunk))(
-                scalars, relaxed, rim_pair, low_ghost, high_ghost, hits
-            )
+            relaxed, chunks = _call(_middle_kernel, 0, 5, (full, chunk))(relaxed, rim_pair, low_ghost, high_ghost, hits)
         else:
-            final, dens = _call(_last_kernel, 1, 5, (own, density))(
-                scalars, relaxed, rim_pair, low_ghost, high_ghost, hits
-            )
+            final, dens = _call(_last_kernel, 0, 5, (own, density))(relaxed, rim_pair, low_ghost, high_ghost, hits)
     return (final, dens)
 
 

time: 79.9 us -> 71.9 us (0.90)
  blocking collectives: 0 us -> 16.9 us
  waiting for transfers between devices: 30.5 us -> 18.2 us
  local copies, waits for them, and re-layouts: 9.62 us -> 4.22 us
  other arithmetic: 4.42 us -> 0.08 us
  between operations: 2.1 us -> 0.7 us
  starting transfers between devices: 16.8 us -> 15.5 us
    all_to_all x0 -> x1, blocking collectives: none -> 16.9 us  [per_device(): got = lax.all_to_all(chunks, 'gy', 0, 0, tiled=True)]
    all_to_all x2 -> x1, waiting for transfers between devices: 21.8 us -> 12.6 us  [per_device(): got = lax.all_to_all(chunks, 'gy', 0, 0, tiled=True)]
    all_to_all x2 -> x1, starting transfers between devices: 10.6 us -> 7.04 us  [per_device(): got = lax.all_to_all(chunks, 'gy', 0, 0, tiled=True)]
    ppermute x5 -> x6, waiting for transfers between devices: 8.76 us -> 5.63 us  [the longest x1 2.25 us: per_device(): other_states = lax.ppermute(populations, 'gz', [(0, 1), (1, 0)])]
    another operation x2 -> x0, local copies, waits for them, and re-layouts: 2.34 us -> none  [per_device(): jnp.stack([me_y, (me_y + 1) % flow_cycle, (me_y - 1 + flow_cycle) % flow_...]
    ppermute x5 -> x6, starting transfers between devices: 6.18 us -> 8.44 us  [the longest x2 7.06 us: per_device(): lax.ppermute(high_send, 'gx', [(i, (i - 1) % slab_cycle) for i in range(s...]
    squeeze x2 -> x0, local copies, waits for them, and re-layouts: 1.61 us -> none  [per_device(): sends[1]]
    slice x3 -> x0, local copies, waits for them, and re-layouts: 1.28 us -> none  [the longest x1 0.66 us: per_device(): fraction = le_frac[section].astype(f32) / 256.0]
  transfers between devices with their start and end apart: 7 -> 7, of which waited for: 6 -> 4; matrix products, arithmetic and copies ran while one was open for 10% -> 4% of each run, Pallas kernels for 0% -> 0%
where the time goes in v3:
time: 71.9 us; the launch traced here: 71.5 us
  waiting for transfers between devices  18.2 us (25%)
  blocking collectives  16.9 us (24%)
  starting transfers between devices  15.5 us (22%)
  Pallas kernels  14.5 us (20%)
  local copies, waits for them, and re-layouts  4.22 us (6%)
  matrix products  1.34 us (2%)
    all_to_all x1, blocking collectives, per_device(): got = lax.all_to_all(chunks, 'gy', 0, 0, tiled=True)  16.9 us
    all_to_all x1, waiting for transfers between devices, per_device(): got = lax.all_to_all(chunks, 'gy', 0, 0, tiled=True)  12.6 us
    ppermute x2, starting transfers between devices, per_device(): lax.ppermute(high_send, 'gx', [(i, (i - 1) % slab_cycle) for i in range(s...  7.06 us
    all_to_all x1, starting transfers between devices, per_device(): got = lax.all_to_all(chunks, 'gy', 0, 0, tiled=True)  7.04 us
    pallas_call x1, Pallas kernels, per_device(): _call(_middle_kernel, 0, 5, (full, chunk))  4.36 us
    pallas_call x2, Pallas kernels, per_device(): _call(functools.partial(_window_kernel, section), 2, 1, (ghost, ghost, ri...  3.93 us
    pallas_call x1, Pallas kernels, per_device(): _call(_first_kernel, 0, 2, (full, chunk))(populations, other_states)  3.29 us
    unnamed x14, local copies, waits for them, and re-layouts  2.94 us
  transfers between devices with their start and end apart: 7, of which 4 were waited for; matrix products, arithmetic and copies ran while one was open for 4% of the time, Pallas kernels for 0%

profile of v3, /device:TPU:0, one launch (start us, length us, event | category | flops | bytes accessed | tf_op | source)
XLA Modules:
  0.0 71.5 jit_solution(16662858303439138089)
XLA Ops:
  0.6 0.1 collective-permute-start
  0.7 2.2 %collective-permute-done.other_ref = f32[19,8,8,128]{3,2,1,0:T(8,128)S(1)} collective-permute-done((f32[19,8,8,128]{3,2,1,0:T(8,128)}, f32[19,8,8,128]{3,2,1,0:T(8,128)S(1)}, u32[]{:S(2)}, u32[]{:S(2)}) %collective-permute-start) | collective-permute-done | bytes 622624 | tf_op jit(solution)/shard_map/ppermute | solution.py:300
  3.0 0.8 %copy-done.1 = f32[19,8,8,128]{3,2,1,0:T(8,128)} copy-done((f32[19,8,8,128]{3,2,1,0:T(8,128)}, f32[19,8,8,128]{3,2,1,0:T(8,128)S(1)}, u32[]{:S(2)}) %copy-start.1) | copy-done | bytes 622616
  3.8 3.3 %shard_map.59 = (f32[19,8,16,128]{3,2,1,0:T(8,128)}, f32[8,176,128]{2,1,0:T(8,128)}) custom-call(f32[19,8,8,128]{3,2,1,0:T(8,128)} %mine_ref.1, f32[19,8,8,128]{3,2,1,0:T(8,128)} %copy-done.1), custom_call_target="tpu_custom_call" | custom-call | tf_op jit(solution)/shard_map/pallas_call | solution.py:316
  7.1 7.0 %all-to-all-start = ((f32[8,176,128]{2,1,0:T(8,128)}), f32[8,176,128]{2,1,0:T(8,128)S(1)}, u32[]{:S(2)}, u32[]{:S(2)}) async-start(f32[8,176,128]{2,1,0:T(8,128)} %get-tuple-element.13), calls=%async_computation | async-start | bytes 1441792 | tf_op jit(solution)/shard_map/all_to_all | solution.py:318
  14.1 0.1 collective-permute-start.3
  14.2 1.2 %collective-permute-done.3 = s32[8,8,32]{2,1,0:T(8,128)S(1)} collective-permute-done((s32[8,8,32]{2,1,0:T(8,128)S(1)}, s32[8,8,32]{2,1,0:T(8,128)S(1)}, u32[]{:S(2)}, u32[]{:S(2)}) %collective-permute-start.3) | collective-permute-done | bytes 8224 | tf_op jit(solution)/shard_map/ppermute | solution.py:301
  15.4 0.1 add_select_fusion
  15.5 12.6 %all-to-all-done.got_ref = f32[8,176,128]{2,1,0:T(8,128)S(1)} async-done(((f32[8,176,128]{2,1,0:T(8,128)}), f32[8,176,128]{2,1,0:T(8,128)S(1)}, u32[]{:S(2)}, u32[]{:S(2)}) %all-to-all-start) | async-done | bytes 720928 | tf_op jit(solution)/shard_map/all_to_all | solution.py:318
  28.1 0.9 %copy-done = f32[8,176,128]{2,1,0:T(8,128)} copy-done((f32[8,176,128]{2,1,0:T(8,128)}, f32[8,176,128]{2,1,0:T(8,128)S(1)}, u32[]{:S(2)}) %copy-start) | copy-done | bytes 720920
  29.0 2.0 %shard_map.60 = (f32[5,16,128]{2,1,0:T(8,128)}, f32[5,16,128]{2,1,0:T(8,128)}, f32[2,16,128]{2,1,0:T(8,128)}) custom-call(s32[2]{0:T(128)} %shift_ref.3, s32[2]{0:T(128)} %frac_ref.3, f32[8,176,128]{2,1,0:T(8,128)} %copy-done), custom_call_target="tpu_custom_call" | custom-call | tf_op jit(solution)/shard_map/pallas_call | solution.py:319
  31.0 0.6 collective-permute-start.1
  31.6 3.5 %collective-permute-start.2 = (f32[5,16,128]{2,1,0:T(8,128)}, f32[5,16,128]{2,1,0:T(8,128)S(1)}, u32[]{:S(2)}, u32[]{:S(2)}) collective-permute-start(f32[5,16,128]{2,1,0:T(8,128)} %get-tuple-element.16), channel_id=1, source_target_pairs={{0,112},{16,0},{32,16},{48,32},{64,48},{80,64},{96,80},{112,96},{1... | collective-permute-start | bytes 122888 | tf_op jit(solution)/shard_map/ppermute | solution.py:323
  35.1 1.3 %fusion = f32[8,16,128,19]{2,3,1,0:T(8,128)S(1)} fusion(s32[8,16,32]{2,1,0:T(8,128)S(1)} %get-tuple-element.23, s32[8,16,32]{2,1,0:T(8,128)S(1)} %get-tuple-element.22), kind=kOutput, calls=%fused_computation.1 | convolution fusion | flops 20525056 | bytes 1277952 | tf_op jit(solution)/shard_map/xzml,xzly->mxzy/dot_general | solution.py:116
  36.5 1.3 %copy.8 = f32[8,16,128,19]{2,1,0,3:T(8,128)} copy(f32[8,16,128,19]{2,3,1,0:T(8,128)S(1)} %fusion) | data formatting | bytes 2490368 | tf_op jit(solution)/shard_map/xzml,xzly->mxzy/dot_general | solution.py:116
  37.8 0.6 copy-done.2
  38.4 4.4 %shard_map.61 = (f32[19,8,16,128]{3,2,1,0:T(8,128)}, f32[8,176,128]{2,1,0:T(8,128)}) custom-call(f32[19,8,16,128]{3,2,1,0:T(8,128)} %get-tuple-element.12.relaxed_ref, f32[2,16,128]{2,1,0:T(8,128)} %get-tuple-element.14.rims_ref, f32[5,16,128]{2,1,0:T(8,128)} %copy-done.2, f32[5,16,128]{2,1,0:T(8,128)} %copy-done.3, f32[19,8,16,128]{3,2,1,0:T(8,128)} %bitcast.3), custom_call_target="tpu_custom_call" | custom-call | tf_op jit(solution)/shard_map/pallas_call | solution.py:325
  42.7 16.9 %all_to_all.10.got_ref = f32[8,176,128]{2,1,0:T(8,128)} all-to-all(f32[8,176,128]{2,1,0:T(8,128)} %get-tuple-element.18), channel_id=1, replica_groups=mesh['gx'=8,'gy'=8,'gz'=2] {'gy'}, dimensions={0} | all-to-all | bytes 1441792 | tf_op jit(solution)/shard_map/all_to_all | solution.py:318
  59.7 2.0 %shard_map.62 = (f32[5,16,128]{2,1,0:T(8,128)}, f32[5,16,128]{2,1,0:T(8,128)}, f32[2,16,128]{2,1,0:T(8,128)}) custom-call(s32[2]{0:T(128)} %shift_ref.3, s32[2]{0:T(128)} %frac_ref.3, f32[8,176,128]{2,1,0:T(8,128)} %all_to_all.10.got_ref), custom_call_target="tpu_custom_call" | custom-call | tf_op jit(solution)/shard_map/pallas_call | solution.py:319
  61.6 0.6 collective-permute-start.4
  62.2 3.5 %collective-permute-start.5 = (f32[5,16,128]{2,1,0:T(8,128)}, f32[5,16,128]{2,1,0:T(8,128)S(1)}, u32[]{:S(2)}, u32[]{:S(2)}) collective-permute-start(f32[5,16,128]{2,1,0:T(8,128)} %get-tuple-element.21), channel_id=1, source_target_pairs={{0,112},{16,0},{32,16},{48,32},{64,48},{80,64},{96,80},{112,96},{1... | collective-permute-start | bytes 122888 | tf_op jit(solution)/shard_map/ppermute | solution.py:323
  65.8 2.2 %collective-permute-done.4.low_ref = f32[5,16,128]{2,1,0:T(8,128)S(1)} collective-permute-done((f32[5,16,128]{2,1,0:T(8,128)}, f32[5,16,128]{2,1,0:T(8,128)S(1)}, u32[]{:S(2)}, u32[]{:S(2)}) %collective-permute-start.4) | collective-permute-done | bytes 40992 | tf_op jit(solution)/shard_map/ppermute | solution.py:322
  68.0 0.6 copy-done.4
  68.6 2.9 %shard_map.63 = (f32[19,8,8,128]{3,2,1,0:T(8,128)}, f32[8,8,128]{2,1,0:T(8,128)}) custom-call(f32[19,8,16,128]{3,2,1,0:T(8,128)} %get-tuple-element.17.relaxed_ref, f32[2,16,128]{2,1,0:T(8,128)} %get-tuple-element.19.rims_ref, f32[5,16,128]{2,1,0:T(8,128)} %copy-done.4, f32[5,16,128]{2,1,0:T(8,128)} %copy-done.5, f32[19,8,16,128]{3,2,1,0:T(8,128)} %bitcast.4), custom_call_target="tpu_custom_call" | custom-call | tf_op jit(solution)/shard_map/pallas_call | solution.py:327
  (13 shorter events, 0.0 us)
Async XLA Ops:
  0.6 13.5 %copy-start.6 = (s32[8,8,32]{2,1,0:T(8,128)S(1)}, s32[8,8,32]{2,1,0:T(8,128)}, u32[]{:S(2)}) copy-start(s32[8,8,32]{2,1,0:T(8,128)} %param.7) | copy-start | bytes 24580
  0.6 2.3 %collective-permute-start = (f32[19,8,8,128]{3,2,1,0:T(8,128)}, f32[19,8,8,128]{3,2,1,0:T(8,128)S(1)}, u32[]{:S(2)}, u32[]{:S(2)}) collective-permute-start(f32[19,8,8,128]{3,2,1,0:T(8,128)} %mine_ref.1), channel_id=1, source_target_pairs={{0,1},{1,0},{2,3},{3,2},{4,5},{5,4},{6,7},{7,6},{8,9},{9,8},{10,11... | collective-permute-start | bytes 1867784 | tf_op jit(solution)/shard_map/ppermute | solution.py:300
  3.0 0.8 %copy-start.1 = (f32[19,8,8,128]{3,2,1,0:T(8,128)}, f32[19,8,8,128]{3,2,1,0:T(8,128)S(1)}, u32[]{:S(2)}) copy-start(f32[19,8,8,128]{3,2,1,0:T(8,128)S(1)} %collective-permute-done.other_ref) | copy-start | bytes 1867780
  7.1 21.0 %all-to-all-start = ((f32[8,176,128]{2,1,0:T(8,128)}), f32[8,176,128]{2,1,0:T(8,128)S(1)}, u32[]{:S(2)}, u32[]{:S(2)}) async-start(f32[8,176,128]{2,1,0:T(8,128)} %get-tuple-element.13), calls=%async_computation | async-start | bytes 1441792 | tf_op jit(solution)/shard_map/all_to_all | solution.py:318
  14.1 1.3 %collective-permute-start.3 = (s32[8,8,32]{2,1,0:T(8,128)S(1)}, s32[8,8,32]{2,1,0:T(8,128)S(1)}, u32[]{:S(2)}, u32[]{:S(2)}) collective-permute-start(s32[8,8,32]{2,1,0:T(8,128)S(1)} %copy-done.6), channel_id=1, source_target_pairs={{0,1},{1,0},{2,3},{3,2},{4,5},{5,4},{6,7},{7,6},{8,9},{9,8},{10,11... | collective-permute-start | bytes 24584 | tf_op jit(solution)/shard_map/ppermute | solution.py:301
  28.1 0.9 %copy-start = (f32[8,176,128]{2,1,0:T(8,128)}, f32[8,176,128]{2,1,0:T(8,128)S(1)}, u32[]{:S(2)}) copy-start(f32[8,176,128]{2,1,0:T(8,128)S(1)} %all-to-all-done.got_ref) | copy-start | bytes 2162692
  31.0 6.8 %collective-permute-start.1 = (f32[5,16,128]{2,1,0:T(8,128)}, f32[5,16,128]{2,1,0:T(8,128)S(1)}, u32[]{:S(2)}, u32[]{:S(2)}) collective-permute-start(f32[5,16,128]{2,1,0:T(8,128)} %get-tuple-element.15), channel_id=1, source_target_pairs={{0,16},{16,32},{32,48},{48,64},{64,80},{80,96},{96,112},{112,0},{1... | collective-permute-start | bytes 122888 | tf_op jit(solution)/shard_map/ppermute | solution.py:322
  31.6 6.2 %collective-permute-start.2 = (f32[5,16,128]{2,1,0:T(8,128)}, f32[5,16,128]{2,1,0:T(8,128)S(1)}, u32[]{:S(2)}, u32[]{:S(2)}) collective-permute-start(f32[5,16,128]{2,1,0:T(8,128)} %get-tuple-element.16), channel_id=1, source_target_pairs={{0,112},{16,0},{32,16},{48,32},{64,48},{80,64},{96,80},{112,96},{1... | collective-permute-start | bytes 122888 | tf_op jit(solution)/shard_map/ppermute | solution.py:323
  37.7 0.6 copy-start.2
  37.8 0.6 copy-start.3
  61.6 6.3 %collective-permute-start.4 = (f32[5,16,128]{2,1,0:T(8,128)}, f32[5,16,128]{2,1,0:T(8,128)S(1)}, u32[]{:S(2)}, u32[]{:S(2)}) collective-permute-start(f32[5,16,128]{2,1,0:T(8,128)} %get-tuple-element.20), channel_id=1, source_target_pairs={{0,16},{16,32},{32,48},{48,64},{64,80},{80,96},{96,112},{112,0},{1... | collective-permute-start | bytes 122888 | tf_op jit(solution)/shard_map/ppermute | solution.py:322
  62.2 5.7 %collective-permute-start.5 = (f32[5,16,128]{2,1,0:T(8,128)}, f32[5,16,128]{2,1,0:T(8,128)S(1)}, u32[]{:S(2)}, u32[]{:S(2)}) collective-permute-start(f32[5,16,128]{2,1,0:T(8,128)} %get-tuple-element.21), channel_id=1, source_target_pairs={{0,112},{16,0},{32,16},{48,32},{64,48},{80,64},{96,80},{112,96},{1... | collective-permute-start | bytes 122888 | tf_op jit(solution)/shard_map/ppermute | solution.py:323
  68.0 0.6 copy-start.4
  68.0 0.6 copy-start.5

commit v4 on v3

--- a/solution.py
+++ b/solution.py
@@ -2,11 +2,11 @@
 
 import jax
 import jax.numpy as jnp
-import numpy as np
 from jax import lax
 from jax.sharding import PartitionSpec as P
 from jax.experimental import pallas as pl
 from jax.experimental.pallas import tpu as pltpu
+
 
 STEPS = 2
 
@@ -289,7 +289,7 @@
     )
 
 
-def per_device(populations, le_shift, le_frac, links):
+def _per_device(populations, le_shift, le_frac, links):
     n_members, slab_width, half_depth, row_span = populations.shape
     flow_cycle = lax.axis_size("gy")
     slab_cycle = lax.axis_size("gx")
@@ -331,6 +331,4 @@
 def solution(mesh):
     in_specs = (P(None, "gx", "gz", "gy"), P(), P(), P("gx", "gz", "gy"))
     out_specs = (P(None, "gx", "gz", "gy"), P("gx", "gz", "gy"))
-    return jax.shard_map(
-        per_device, mesh=mesh, in_specs=in_specs, out_specs=out_specs, check_vma=False
-    )
+    return jax.shard_map(_per_device, mesh=mesh, in_specs=in_specs, out_specs=out_specs, check_vma=False)

time: 71.9 us -> 71.9 us (level)
  no operation moved by 1% of the time
where the time goes in v4:
time: 71.9 us; the launch traced here: 71.5 us
  waiting for transfers between devices  18.2 us (25%)
  blocking collectives  16.9 us (24%)
  starting transfers between devices  15.5 us (22%)
  Pallas kernels  14.5 us (20%)
  local copies, waits for them, and re-layouts  4.22 us (6%)
  matrix products  1.34 us (2%)
    all_to_all x1, blocking collectives, _per_device(): got = lax.all_to_all(chunks, 'gy', 0, 0, tiled=True)  16.9 us
    all_to_all x1, waiting for transfers between devices, _per_device(): got = lax.all_to_all(chunks, 'gy', 0, 0, tiled=True)  12.6 us
    ppermute x2, starting transfers between devices, _per_device(): lax.ppermute(high_send, 'gx', [(i, (i - 1) % slab_cycle) for i in range(s...  7.06 us
    all_to_all x1, starting transfers between devices, _per_device(): got = lax.all_to_all(chunks, 'gy', 0, 0, tiled=True)  7.04 us
    pallas_call x1, Pallas kernels, _per_device(): _call(_middle_kernel, 0, 5, (full, chunk))  4.36 us
    pallas_call x2, Pallas kernels, _per_device(): _call(functools.partial(_window_kernel, section), 2, 1, (ghost, ghost, ri...  3.93 us
    pallas_call x1, Pallas kernels, _per_device(): _call(_first_kernel, 0, 2, (full, chunk))(populations, other_states)  3.29 us
    unnamed x14, local copies, waits for them, and re-layouts  2.94 us
  transfers between devices with their start and end apart: 7, of which 4 were waited for; matrix products, arithmetic and copies ran while one was open for 4% of the time, Pallas kernels for 0%

profile of v4, /device:TPU:0, one launch (start us, length us, event | category | flops | bytes accessed | tf_op | source)
XLA Modules:
  0.0 71.5 jit_solution(16662858303439138089)
XLA Ops:
  0.6 0.1 collective-permute-start
  0.7 2.2 %collective-permute-done.other_ref = f32[19,8,8,128]{3,2,1,0:T(8,128)S(1)} collective-permute-done((f32[19,8,8,128]{3,2,1,0:T(8,128)}, f32[19,8,8,128]{3,2,1,0:T(8,128)S(1)}, u32[]{:S(2)}, u32[]{:S(2)}) %collective-permute-start) | collective-permute-done | bytes 622624 | tf_op jit(solution)/shard_map/ppermute | solution.py:300
  3.0 0.8 %copy-done.1 = f32[19,8,8,128]{3,2,1,0:T(8,128)} copy-done((f32[19,8,8,128]{3,2,1,0:T(8,128)}, f32[19,8,8,128]{3,2,1,0:T(8,128)S(1)}, u32[]{:S(2)}) %copy-start.1) | copy-done | bytes 622616
  3.8 3.3 %shard_map.59 = (f32[19,8,16,128]{3,2,1,0:T(8,128)}, f32[8,176,128]{2,1,0:T(8,128)}) custom-call(f32[19,8,8,128]{3,2,1,0:T(8,128)} %mine_ref.1, f32[19,8,8,128]{3,2,1,0:T(8,128)} %copy-done.1), custom_call_target="tpu_custom_call" | custom-call | tf_op jit(solution)/shard_map/pallas_call | solution.py:316
  7.1 7.0 %all-to-all-start = ((f32[8,176,128]{2,1,0:T(8,128)}), f32[8,176,128]{2,1,0:T(8,128)S(1)}, u32[]{:S(2)}, u32[]{:S(2)}) async-start(f32[8,176,128]{2,1,0:T(8,128)} %get-tuple-element.13), calls=%async_computation | async-start | bytes 1441792 | tf_op jit(solution)/shard_map/all_to_all | solution.py:318
  14.1 0.1 collective-permute-start.3
  14.2 1.2 %collective-permute-done.3 = s32[8,8,32]{2,1,0:T(8,128)S(1)} collective-permute-done((s32[8,8,32]{2,1,0:T(8,128)S(1)}, s32[8,8,32]{2,1,0:T(8,128)S(1)}, u32[]{:S(2)}, u32[]{:S(2)}) %collective-permute-start.3) | collective-permute-done | bytes 8224 | tf_op jit(solution)/shard_map/ppermute | solution.py:301
  15.4 0.1 add_select_fusion
  15.5 12.6 %all-to-all-done.got_ref = f32[8,176,128]{2,1,0:T(8,128)S(1)} async-done(((f32[8,176,128]{2,1,0:T(8,128)}), f32[8,176,128]{2,1,0:T(8,128)S(1)}, u32[]{:S(2)}, u32[]{:S(2)}) %all-to-all-start) | async-done | bytes 720928 | tf_op jit(solution)/shard_map/all_to_all | solution.py:318
  28.1 0.9 %copy-done = f32[8,176,128]{2,1,0:T(8,128)} copy-done((f32[8,176,128]{2,1,0:T(8,128)}, f32[8,176,128]{2,1,0:T(8,128)S(1)}, u32[]{:S(2)}) %copy-start) | copy-done | bytes 720920
  29.0 2.0 %shard_map.60 = (f32[5,16,128]{2,1,0:T(8,128)}, f32[5,16,128]{2,1,0:T(8,128)}, f32[2,16,128]{2,1,0:T(8,128)}) custom-call(s32[2]{0:T(128)} %shift_ref.3, s32[2]{0:T(128)} %frac_ref.3, f32[8,176,128]{2,1,0:T(8,128)} %copy-done), custom_call_target="tpu_custom_call" | custom-call | tf_op jit(solution)/shard_map/pallas_call | solution.py:319
  31.0 0.6 collective-permute-start.1
  31.6 3.5 %collective-permute-start.2 = (f32[5,16,128]{2,1,0:T(8,128)}, f32[5,16,128]{2,1,0:T(8,128)S(1)}, u32[]{:S(2)}, u32[]{:S(2)}) collective-permute-start(f32[5,16,128]{2,1,0:T(8,128)} %get-tuple-element.16), channel_id=1, source_target_pairs={{0,112},{16,0},{32,16},{48,32},{64,48},{80,64},{96,80},{112,96},{1... | collective-permute-start | bytes 122888 | tf_op jit(solution)/shard_map/ppermute | solution.py:323
  35.1 1.3 %fusion = f32[8,16,128,19]{2,3,1,0:T(8,128)S(1)} fusion(s32[8,16,32]{2,1,0:T(8,128)S(1)} %get-tuple-element.23, s32[8,16,32]{2,1,0:T(8,128)S(1)} %get-tuple-element.22), kind=kOutput, calls=%fused_computation.1 | convolution fusion | flops 20525056 | bytes 1277952 | tf_op jit(solution)/shard_map/xzml,xzly->mxzy/dot_general | solution.py:116
  36.5 1.3 %copy.8 = f32[8,16,128,19]{2,1,0,3:T(8,128)} copy(f32[8,16,128,19]{2,3,1,0:T(8,128)S(1)} %fusion) | data formatting | bytes 2490368 | tf_op jit(solution)/shard_map/xzml,xzly->mxzy/dot_general | solution.py:116
  37.8 0.6 copy-done.2
  38.4 4.4 %shard_map.61 = (f32[19,8,16,128]{3,2,1,0:T(8,128)}, f32[8,176,128]{2,1,0:T(8,128)}) custom-call(f32[19,8,16,128]{3,2,1,0:T(8,128)} %get-tuple-element.12.relaxed_ref, f32[2,16,128]{2,1,0:T(8,128)} %get-tuple-element.14.rims_ref, f32[5,16,128]{2,1,0:T(8,128)} %copy-done.2, f32[5,16,128]{2,1,0:T(8,128)} %copy-done.3, f32[19,8,16,128]{3,2,1,0:T(8,128)} %bitcast.3), custom_call_target="tpu_custom_call" | custom-call | tf_op jit(solution)/shard_map/pallas_call | solution.py:325
  42.7 16.9 %all_to_all.10.got_ref = f32[8,176,128]{2,1,0:T(8,128)} all-to-all(f32[8,176,128]{2,1,0:T(8,128)} %get-tuple-element.18), channel_id=1, replica_groups=mesh['gx'=8,'gy'=8,'gz'=2] {'gy'}, dimensions={0} | all-to-all | bytes 1441792 | tf_op jit(solution)/shard_map/all_to_all | solution.py:318
  59.7 2.0 %shard_map.62 = (f32[5,16,128]{2,1,0:T(8,128)}, f32[5,16,128]{2,1,0:T(8,128)}, f32[2,16,128]{2,1,0:T(8,128)}) custom-call(s32[2]{0:T(128)} %shift_ref.3, s32[2]{0:T(128)} %frac_ref.3, f32[8,176,128]{2,1,0:T(8,128)} %all_to_all.10.got_ref), custom_call_target="tpu_custom_call" | custom-call | tf_op jit(solution)/shard_map/pallas_call | solution.py:319
  61.6 0.6 collective-permute-start.4
  62.2 3.5 %collective-permute-start.5 = (f32[5,16,128]{2,1,0:T(8,128)}, f32[5,16,128]{2,1,0:T(8,128)S(1)}, u32[]{:S(2)}, u32[]{:S(2)}) collective-permute-start(f32[5,16,128]{2,1,0:T(8,128)} %get-tuple-element.21), channel_id=1, source_target_pairs={{0,112},{16,0},{32,16},{48,32},{64,48},{80,64},{96,80},{112,96},{1... | collective-permute-start | bytes 122888 | tf_op jit(solution)/shard_map/ppermute | solution.py:323
  65.8 2.2 %collective-permute-done.4.low_ref = f32[5,16,128]{2,1,0:T(8,128)S(1)} collective-permute-done((f32[5,16,128]{2,1,0:T(8,128)}, f32[5,16,128]{2,1,0:T(8,128)S(1)}, u32[]{:S(2)}, u32[]{:S(2)}) %collective-permute-start.4) | collective-permute-done | bytes 40992 | tf_op jit(solution)/shard_map/ppermute | solution.py:322
  68.0 0.6 copy-done.4
  68.6 2.9 %shard_map.63 = (f32[19,8,8,128]{3,2,1,0:T(8,128)}, f32[8,8,128]{2,1,0:T(8,128)}) custom-call(f32[19,8,16,128]{3,2,1,0:T(8,128)} %get-tuple-element.17.relaxed_ref, f32[2,16,128]{2,1,0:T(8,128)} %get-tuple-element.19.rims_ref, f32[5,16,128]{2,1,0:T(8,128)} %copy-done.4, f32[5,16,128]{2,1,0:T(8,128)} %copy-done.5, f32[19,8,16,128]{3,2,1,0:T(8,128)} %bitcast.4), custom_call_target="tpu_custom_call" | custom-call | tf_op jit(solution)/shard_map/pallas_call | solution.py:327
  (13 shorter events, 0.0 us)
Async XLA Ops:
  0.6 13.5 %copy-start.6 = (s32[8,8,32]{2,1,0:T(8,128)S(1)}, s32[8,8,32]{2,1,0:T(8,128)}, u32[]{:S(2)}) copy-start(s32[8,8,32]{2,1,0:T(8,128)} %param.7) | copy-start | bytes 24580
  0.6 2.3 %collective-permute-start = (f32[19,8,8,128]{3,2,1,0:T(8,128)}, f32[19,8,8,128]{3,2,1,0:T(8,128)S(1)}, u32[]{:S(2)}, u32[]{:S(2)}) collective-permute-start(f32[19,8,8,128]{3,2,1,0:T(8,128)} %mine_ref.1), channel_id=1, source_target_pairs={{0,1},{1,0},{2,3},{3,2},{4,5},{5,4},{6,7},{7,6},{8,9},{9,8},{10,11... | collective-permute-start | bytes 1867784 | tf_op jit(solution)/shard_map/ppermute | solution.py:300
  3.0 0.8 %copy-start.1 = (f32[19,8,8,128]{3,2,1,0:T(8,128)}, f32[19,8,8,128]{3,2,1,0:T(8,128)S(1)}, u32[]{:S(2)}) copy-start(f32[19,8,8,128]{3,2,1,0:T(8,128)S(1)} %collective-permute-done.other_ref) | copy-start | bytes 1867780
  7.1 21.0 %all-to-all-start = ((f32[8,176,128]{2,1,0:T(8,128)}), f32[8,176,128]{2,1,0:T(8,128)S(1)}, u32[]{:S(2)}, u32[]{:S(2)}) async-start(f32[8,176,128]{2,1,0:T(8,128)} %get-tuple-element.13), calls=%async_computation | async-start | bytes 1441792 | tf_op jit(solution)/shard_map/all_to_all | solution.py:318
  14.1 1.3 %collective-permute-start.3 = (s32[8,8,32]{2,1,0:T(8,128)S(1)}, s32[8,8,32]{2,1,0:T(8,128)S(1)}, u32[]{:S(2)}, u32[]{:S(2)}) collective-permute-start(s32[8,8,32]{2,1,0:T(8,128)S(1)} %copy-done.6), channel_id=1, source_target_pairs={{0,1},{1,0},{2,3},{3,2},{4,5},{5,4},{6,7},{7,6},{8,9},{9,8},{10,11... | collective-permute-start | bytes 24584 | tf_op jit(solution)/shard_map/ppermute | solution.py:301
  28.1 0.9 %copy-start = (f32[8,176,128]{2,1,0:T(8,128)}, f32[8,176,128]{2,1,0:T(8,128)S(1)}, u32[]{:S(2)}) copy-start(f32[8,176,128]{2,1,0:T(8,128)S(1)} %all-to-all-done.got_ref) | copy-start | bytes 2162692
  31.0 6.8 %collective-permute-start.1 = (f32[5,16,128]{2,1,0:T(8,128)}, f32[5,16,128]{2,1,0:T(8,128)S(1)}, u32[]{:S(2)}, u32[]{:S(2)}) collective-permute-start(f32[5,16,128]{2,1,0:T(8,128)} %get-tuple-element.15), channel_id=1, source_target_pairs={{0,16},{16,32},{32,48},{48,64},{64,80},{80,96},{96,112},{112,0},{1... | collective-permute-start | bytes 122888 | tf_op jit(solution)/shard_map/ppermute | solution.py:322
  31.6 6.2 %collective-permute-start.2 = (f32[5,16,128]{2,1,0:T(8,128)}, f32[5,16,128]{2,1,0:T(8,128)S(1)}, u32[]{:S(2)}, u32[]{:S(2)}) collective-permute-start(f32[5,16,128]{2,1,0:T(8,128)} %get-tuple-element.16), channel_id=1, source_target_pairs={{0,112},{16,0},{32,16},{48,32},{64,48},{80,64},{96,80},{112,96},{1... | collective-permute-start | bytes 122888 | tf_op jit(solution)/shard_map/ppermute | solution.py:323
  37.7 0.6 copy-start.2
  37.8 0.6 copy-start.3
  61.6 6.3 %collective-permute-start.4 = (f32[5,16,128]{2,1,0:T(8,128)}, f32[5,16,128]{2,1,0:T(8,128)S(1)}, u32[]{:S(2)}, u32[]{:S(2)}) collective-permute-start(f32[5,16,128]{2,1,0:T(8,128)} %get-tuple-element.20), channel_id=1, source_target_pairs={{0,16},{16,32},{32,48},{48,64},{64,80},{80,96},{96,112},{112,0},{1... | collective-permute-start | bytes 122888 | tf_op jit(solution)/shard_map/ppermute | solution.py:322
  62.2 5.7 %collective-permute-start.5 = (f32[5,16,128]{2,1,0:T(8,128)}, f32[5,16,128]{2,1,0:T(8,128)S(1)}, u32[]{:S(2)}, u32[]{:S(2)}) collective-permute-start(f32[5,16,128]{2,1,0:T(8,128)} %get-tuple-element.21), channel_id=1, source_target_pairs={{0,112},{16,0},{32,16},{48,32},{64,48},{80,64},{96,80},{112,96},{1... | collective-permute-start | bytes 122888 | tf_op jit(solution)/shard_map/ppermute | solution.py:323
  68.0 0.6 copy-start.4
  68.0 0.6 copy-start.5

commit v5 on v4

--- a/solution.py
+++ b/solution.py
@@ -183,9 +183,9 @@
         step_x, step_y, step_z = velocity_table[n]
         xs = x - step_x
         if xs < 0:
-            t = low_ref[upward.index(n)]
+            t = low_ref(upward.index(n))
         elif xs >= slab_width:
-            t = high_ref[downward.index(n)]
+            t = high_ref(downward.index(n))
         else:
             t = relaxed_ref[n, xs]
             if step_y == 1:
@@ -219,14 +219,23 @@
     _emit_relax(cells, slab_width, relaxed_ref, chunk_ref, depth)
 
 
-def _middle_kernel(relaxed_ref, rims_ref, low_ref, high_ref, hits_ref, next_ref, chunk_ref):
+def _ghost_pair(cross_ref, swap_ref):
+    lower = _positions()[3] == 0
+    low = lambda i: jnp.where(lower, cross_ref[i], swap_ref[i])
+    high = lambda i: jnp.where(lower, swap_ref[i], cross_ref[i])
+    return low, high
+
+
+def _middle_kernel(relaxed_ref, rims_ref, cross_ref, swap_ref, hits_ref, next_ref, chunk_ref):
     slab_width, depth = relaxed_ref.shape[1], relaxed_ref.shape[2]
+    low_ref, high_ref = _ghost_pair(cross_ref, swap_ref)
     cells = lambda x: _streamed(x, slab_width, relaxed_ref, rims_ref, low_ref, high_ref, hits_ref, depth)
     _emit_relax(cells, slab_width, next_ref, chunk_ref, depth)
 
 
-def _last_kernel(relaxed_ref, rims_ref, low_ref, high_ref, hits_ref, out_ref, density_ref):
+def _last_kernel(relaxed_ref, rims_ref, cross_ref, swap_ref, hits_ref, out_ref, density_ref):
     slab_width, depth = relaxed_ref.shape[1], relaxed_ref.shape[2]
+    low_ref, high_ref = _ghost_pair(cross_ref, swap_ref)
     half = depth // 2
     lower = jnp.full((half, LANES), _positions()[3], jnp.int32) == 0
     for x in range(slab_width):
@@ -237,10 +246,10 @@
         density_ref[x] = total_density(mine)
 
 
-def _window_kernel(section, shift_ref, frac_ref, got_ref, low_ref, high_ref, rims_ref):
+def _window_kernel(section, shift_ref, frac_ref, got_ref, ghost_ref, rims_ref):
     peers, _, lanes = got_ref.shape
-    depth = low_ref.shape[1]
-    me_y, after, before, _ = _positions()
+    depth = ghost_ref.shape[1]
+    me_y, after, before, me_z = _positions()
     offset = shift_ref[section]
     fraction = jnp.full((depth, lanes), frac_ref[section], jnp.int32).astype(jnp.float32) / 256.0
     keep = 1.0 - fraction
@@ -258,16 +267,22 @@
         second = pltpu.roll(got_ref[after, pl.ds(row0, depth), :], shift, 1)
         return jnp.where(lane < lanes - off, first, second)
 
-    for i, m in enumerate(upward):
-        step_y = velocity_table[m][1]
-        row0 = i * depth
-        a = anchor - offset - step_y
-        low_ref[i] = keep * window(row0, a) + fraction * window(row0, a - 1)
-    for i, m in enumerate(downward):
-        step_y = velocity_table[m][1]
-        row0 = (5 + i) * depth
-        c = anchor + offset - step_y
-        high_ref[i] = fraction * window(row0, c + 1) + keep * window(row0, c)
+    @pl.when(me_z == 0)
+    def _():
+        for i, m in enumerate(upward):
+            step_y = velocity_table[m][1]
+            row0 = i * depth
+            a = anchor - offset - step_y
+            ghost_ref[i] = keep * window(row0, a) + fraction * window(row0, a - 1)
+
+    @pl.when(me_z != 0)
+    def _():
+        for i, m in enumerate(downward):
+            step_y = velocity_table[m][1]
+            row0 = (5 + i) * depth
+            c = anchor + offset - step_y
+            ghost_ref[i] = fraction * window(row0, c + 1) + keep * window(row0, c)
+
     rims_ref[0] = got_ref[before, pl.ds(FACE_ROWS * depth, depth), :]
     rims_ref[1] = got_ref[after, pl.ds(FACE_ROWS * depth, depth), :]
 
@@ -313,14 +328,23 @@
     own = jax.ShapeDtypeStruct((n_members, slab_width, half_depth, row_span), f32)
     density = jax.ShapeDtypeStruct((slab_width, half_depth, row_span), f32)
 
+    cores = lax.axis_size("gz")
+    slab_pairs = []
+    for a in range(slab_cycle):
+        for b in range(flow_cycle):
+            slab_pairs.append(((a * flow_cycle + b) * cores, (((a + 1) % slab_cycle) * flow_cycle + b) * cores))
+            slab_pairs.append(
+                ((a * flow_cycle + b) * cores + 1, (((a - 1) % slab_cycle) * flow_cycle + b) * cores + 1)
+            )
     relaxed, chunks = _call(_first_kernel, 0, 2, (full, chunk))(populations, other_states)
     for section in range(STEPS):
         got = lax.all_to_all(chunks, "gy", 0, 0, tiled=True)
-        low_send, high_send, rim_pair = _call(functools.partial(_window_kernel, section), 2, 1, (ghost, ghost, rims))(
+        ghost_send, rim_pair = _call(functools.partial(_window_kernel, section), 2, 1, (ghost, rims))(
             le_shift, le_frac, got
         )
-        low_ghost = lax.ppermute(low_send, "gx", [(i, (i + 1) % slab_cycle) for i in range(slab_cycle)])
-        high_ghost = lax.ppermute(high_send, "gx", [(i, (i - 1) % slab_cycle) for i in range(slab_cycle)])
+        cross = lax.ppermute(ghost_send, ("gx", "gy", "gz"), slab_pairs)
+        low_ghost = cross
+        high_ghost = lax.ppermute(cross, "gz", [(0, 1), (1, 0)])
         if section + 1 < STEPS:
             relaxed, chunks = _call(_middle_kernel, 0, 5, (full, chunk))(relaxed, rim_pair, low_ghost, high_ghost, hits)
         else:

time: 71.9 us -> 78.1 us (1.086); the launches traced: 71.5 us -> 76.7 us
  waiting for transfers between devices: 18.2 us -> 29.3 us
  starting transfers between devices: 15.5 us -> 7.81 us
  blocking collectives: 16.9 us -> 18.8 us
    ppermute x4, waiting for transfers between devices: 2.19 us -> 13.2 us  [the longest x2 12 us: _per_device(): cross = lax.ppermute(ghost_send, ('gx', 'gy', 'gz'), slab_pairs)]
    ppermute x4, starting transfers between devices: 8.27 us -> 0.6 us  [the longest x2 0.59 us: _per_device(): cross = lax.ppermute(ghost_send, ('gx', 'gy', 'gz'), slab_pairs)]
    all_to_all x1, blocking collectives: 16.9 us -> 18.8 us  [_per_device(): got = lax.all_to_all(chunks, 'gy', 0, 0, tiled=True)]
    all_to_all x1, waiting for transfers between devices: 12.6 us -> 13.9 us  [_per_device(): got = lax.all_to_all(chunks, 'gy', 0, 0, tiled=True)]
    ppermute x1, waiting for transfers between devices: 1.19 us -> 0.01 us  [_per_device(): other_links = lax.ppermute(links, 'gz', [(0, 1), (1, 0)])]
  transfers between devices with their start and end apart: 7 -> 7, of which waited for: 4 -> 5; matrix products, arithmetic and copies ran while one was open for 4% -> 4% of each run, Pallas kernels for 0% -> 2%
where the time goes in v5:
time: 78.1 us; the launch traced here: 76.7 us
  waiting for transfers between devices  29.3 us (38%)
  blocking collectives  18.8 us (24%)
  Pallas kernels  14.4 us (18%)
  starting transfers between devices  7.81 us (10%)
  local copies, waits for them, and re-layouts  4.21 us (5%)
  matrix products  1.34 us (2%)
    all_to_all x1, blocking collectives, _per_device(): got = lax.all_to_all(chunks, 'gy', 0, 0, tiled=True)  18.8 us
    all_to_all x1, waiting for transfers between devices, _per_device(): got = lax.all_to_all(chunks, 'gy', 0, 0, tiled=True)  13.9 us
    ppermute x2, waiting for transfers between devices, _per_device(): cross = lax.ppermute(ghost_send, ('gx', 'gy', 'gz'), slab_pairs)  12 us
    all_to_all x1, starting transfers between devices, _per_device(): got = lax.all_to_all(chunks, 'gy', 0, 0, tiled=True)  7.04 us
    pallas_call x1, Pallas kernels, _per_device(): _call(_middle_kernel, 0, 5, (full, chunk))  4.36 us
    pallas_call x2, Pallas kernels, _per_device(): _call(functools.partial(_window_kernel, section), 2, 1, (ghost, rims))  3.83 us
    pallas_call x1, Pallas kernels, _per_device(): _call(_first_kernel, 0, 2, (full, chunk))(populations, other_states)  3.29 us
    pallas_call x1, Pallas kernels, _per_device(): _call(_last_kernel, 0, 5, (own, density))  2.94 us
  transfers between devices with their start and end apart: 7, of which 5 were waited for; matrix products, arithmetic and copies ran while one was open for 4% of the time, Pallas kernels for 2%

profile of v5, /device:TPU:0, one launch (start us, length us, event | category | flops | bytes accessed | tf_op | source)
XLA Modules:
  0.0 76.7 jit_solution(8581856556984855273)
XLA Ops:
  0.6 0.1 collective-permute-start
  0.7 2.2 %collective-permute-done.other_ref = f32[19,8,8,128]{3,2,1,0:T(8,128)S(1)} collective-permute-done((f32[19,8,8,128]{3,2,1,0:T(8,128)}, f32[19,8,8,128]{3,2,1,0:T(8,128)S(1)}, u32[]{:S(2)}, u32[]{:S(2)}) %collective-permute-start) | collective-permute-done | bytes 622624 | tf_op jit(solution)/shard_map/ppermute | solution.py:315
  3.0 0.8 %copy-done.1 = f32[19,8,8,128]{3,2,1,0:T(8,128)} copy-done((f32[19,8,8,128]{3,2,1,0:T(8,128)}, f32[19,8,8,128]{3,2,1,0:T(8,128)S(1)}, u32[]{:S(2)}) %copy-start.1) | copy-done | bytes 622616
  3.8 3.3 %shard_map.59 = (f32[19,8,16,128]{3,2,1,0:T(8,128)}, f32[8,176,128]{2,1,0:T(8,128)}) custom-call(f32[19,8,8,128]{3,2,1,0:T(8,128)} %mine_ref.1, f32[19,8,8,128]{3,2,1,0:T(8,128)} %copy-done.1), custom_call_target="tpu_custom_call" | custom-call | tf_op jit(solution)/shard_map/pallas_call | solution.py:339
  7.1 7.0 %all-to-all-start = ((f32[8,176,128]{2,1,0:T(8,128)}), f32[8,176,128]{2,1,0:T(8,128)S(1)}, u32[]{:S(2)}, u32[]{:S(2)}) async-start(f32[8,176,128]{2,1,0:T(8,128)} %get-tuple-element.11), calls=%async_computation | async-start | bytes 1441792 | tf_op jit(solution)/shard_map/all_to_all | solution.py:341
  14.1 0.1 collective-permute-start.3
  14.2 13.9 %all-to-all-done.got_ref = f32[8,176,128]{2,1,0:T(8,128)S(1)} async-done(((f32[8,176,128]{2,1,0:T(8,128)}), f32[8,176,128]{2,1,0:T(8,128)S(1)}, u32[]{:S(2)}, u32[]{:S(2)}) %all-to-all-start) | async-done | bytes 720928 | tf_op jit(solution)/shard_map/all_to_all | solution.py:341
  28.1 0.9 %copy-done = f32[8,176,128]{2,1,0:T(8,128)} copy-done((f32[8,176,128]{2,1,0:T(8,128)}, f32[8,176,128]{2,1,0:T(8,128)S(1)}, u32[]{:S(2)}) %copy-start) | copy-done | bytes 720920
  29.0 1.9 %shard_map.60 = (f32[5,16,128]{2,1,0:T(8,128)}, f32[2,16,128]{2,1,0:T(8,128)}) custom-call(s32[2]{0:T(128)} %shift_ref.3, s32[2]{0:T(128)} %frac_ref.3, f32[8,176,128]{2,1,0:T(8,128)} %copy-done), custom_call_target="tpu_custom_call" | custom-call | tf_op jit(solution)/shard_map/pallas_call | solution.py:342
  30.9 0.6 collective-permute-start.1
  31.5 0.0 collective-permute-done.3
  31.5 0.1 add_select_fusion
  31.6 5.6 %collective-permute-done.1.cross_ref = f32[5,16,128]{2,1,0:T(8,128)S(1)} collective-permute-done((f32[5,16,128]{2,1,0:T(8,128)}, f32[5,16,128]{2,1,0:T(8,128)S(1)}, u32[]{:S(2)}, u32[]{:S(2)}) %collective-permute-start.1) | collective-permute-done | bytes 40992 | tf_op jit(solution)/shard_map/ppermute | solution.py:345
  37.3 0.0 collective-permute-start.2
  37.3 1.3 %fusion = f32[8,16,128,19]{2,3,1,0:T(8,128)S(1)} fusion(s32[8,16,32]{2,1,0:T(8,128)S(1)} %get-tuple-element.19, s32[8,16,32]{2,1,0:T(8,128)S(1)} %get-tuple-element.18), kind=kOutput, calls=%fused_computation.1 | convolution fusion | flops 20525056 | bytes 1277952 | tf_op jit(solution)/shard_map/xzml,xzly->mxzy/dot_general | solution.py:116
  38.6 1.3 %copy.8 = f32[8,16,128,19]{2,1,0,3:T(8,128)} copy(f32[8,16,128,19]{2,3,1,0:T(8,128)S(1)} %fusion) | data formatting | bytes 2490368 | tf_op jit(solution)/shard_map/xzml,xzly->mxzy/dot_general | solution.py:116
  39.9 0.6 copy-done.4
  40.5 4.4 %shard_map.61 = (f32[19,8,16,128]{3,2,1,0:T(8,128)}, f32[8,176,128]{2,1,0:T(8,128)}) custom-call(f32[19,8,16,128]{3,2,1,0:T(8,128)} %get-tuple-element.10.relaxed_ref, f32[2,16,128]{2,1,0:T(8,128)} %get-tuple-element.12.rims_ref, f32[5,16,128]{2,1,0:T(8,128)} %copy-done.2, f32[5,16,128]{2,1,0:T(8,128)} %copy-done.4, f32[19,8,16,128]{3,2,1,0:T(8,128)} %bitcast.3), custom_call_target="tpu_custom_call" | custom-call | tf_op jit(solution)/shard_map/pallas_call | solution.py:349
  44.9 18.8 %all_to_all.10.got_ref = f32[8,176,128]{2,1,0:T(8,128)} all-to-all(f32[8,176,128]{2,1,0:T(8,128)} %get-tuple-element.15), channel_id=1, replica_groups=mesh['gx'=8,'gy'=8,'gz'=2] {'gy'}, dimensions={0} | all-to-all | bytes 1441792 | tf_op jit(solution)/shard_map/all_to_all | solution.py:341
  63.7 1.9 %shard_map.62 = (f32[5,16,128]{2,1,0:T(8,128)}, f32[2,16,128]{2,1,0:T(8,128)}) custom-call(s32[2]{0:T(128)} %shift_ref.3, s32[2]{0:T(128)} %frac_ref.3, f32[8,176,128]{2,1,0:T(8,128)} %all_to_all.10.got_ref), custom_call_target="tpu_custom_call" | custom-call | tf_op jit(solution)/shard_map/pallas_call | solution.py:342
  65.6 6.3 %collective-permute-done.4.cross_ref = f32[5,16,128]{2,1,0:T(8,128)S(1)} collective-permute-done((f32[5,16,128]{2,1,0:T(8,128)}, f32[5,16,128]{2,1,0:T(8,128)S(1)}, u32[]{:S(2)}, u32[]{:S(2)}) %collective-permute-start.4) | collective-permute-done | bytes 40992 | tf_op jit(solution)/shard_map/ppermute | solution.py:345
  71.9 1.2 %collective-permute-done.5.swap_ref = f32[5,16,128]{2,1,0:T(8,128)S(1)} collective-permute-done((f32[5,16,128]{2,1,0:T(8,128)S(1)}, f32[5,16,128]{2,1,0:T(8,128)S(1)}, u32[]{:S(2)}, u32[]{:S(2)}) %collective-permute-start.5) | collective-permute-done | bytes 40992 | tf_op jit(solution)/shard_map/ppermute | solution.py:347
  73.2 0.6 copy-done.5
  73.8 2.9 %shard_map.63 = (f32[19,8,8,128]{3,2,1,0:T(8,128)}, f32[8,8,128]{2,1,0:T(8,128)}) custom-call(f32[19,8,16,128]{3,2,1,0:T(8,128)} %get-tuple-element.14.relaxed_ref, f32[2,16,128]{2,1,0:T(8,128)} %get-tuple-element.16.rims_ref, f32[5,16,128]{2,1,0:T(8,128)} %copy-done.3, f32[5,16,128]{2,1,0:T(8,128)} %copy-done.5, f32[19,8,16,128]{3,2,1,0:T(8,128)} %bitcast.4), custom_call_target="tpu_custom_call" | custom-call | tf_op jit(solution)/shard_map/pallas_call | solution.py:351
  (13 shorter events, 0.0 us)
Async XLA Ops:
  0.6 13.5 %copy-start.6 = (s32[8,8,32]{2,1,0:T(8,128)S(1)}, s32[8,8,32]{2,1,0:T(8,128)}, u32[]{:S(2)}) copy-start(s32[8,8,32]{2,1,0:T(8,128)} %param.7) | copy-start | bytes 24580
  0.6 2.3 %collective-permute-start = (f32[19,8,8,128]{3,2,1,0:T(8,128)}, f32[19,8,8,128]{3,2,1,0:T(8,128)S(1)}, u32[]{:S(2)}, u32[]{:S(2)}) collective-permute-start(f32[19,8,8,128]{3,2,1,0:T(8,128)} %mine_ref.1), channel_id=1, source_target_pairs={{0,1},{1,0},{2,3},{3,2},{4,5},{5,4},{6,7},{7,6},{8,9},{9,8},{10,11... | collective-permute-start | bytes 1867784 | tf_op jit(solution)/shard_map/ppermute | solution.py:315
  3.0 0.8 %copy-start.1 = (f32[19,8,8,128]{3,2,1,0:T(8,128)}, f32[19,8,8,128]{3,2,1,0:T(8,128)S(1)}, u32[]{:S(2)}) copy-start(f32[19,8,8,128]{3,2,1,0:T(8,128)S(1)} %collective-permute-done.other_ref) | copy-start | bytes 1867780
  7.1 21.0 %all-to-all-start = ((f32[8,176,128]{2,1,0:T(8,128)}), f32[8,176,128]{2,1,0:T(8,128)S(1)}, u32[]{:S(2)}, u32[]{:S(2)}) async-start(f32[8,176,128]{2,1,0:T(8,128)} %get-tuple-element.11), calls=%async_computation | async-start | bytes 1441792 | tf_op jit(solution)/shard_map/all_to_all | solution.py:341
  14.1 17.4 %collective-permute-start.3 = (s32[8,8,32]{2,1,0:T(8,128)S(1)}, s32[8,8,32]{2,1,0:T(8,128)S(1)}, u32[]{:S(2)}, u32[]{:S(2)}) collective-permute-start(s32[8,8,32]{2,1,0:T(8,128)S(1)} %copy-done.6), channel_id=1, source_target_pairs={{0,1},{1,0},{2,3},{3,2},{4,5},{5,4},{6,7},{7,6},{8,9},{9,8},{10,11... | collective-permute-start | bytes 24584 | tf_op jit(solution)/shard_map/ppermute | solution.py:316
  28.1 0.9 %copy-start = (f32[8,176,128]{2,1,0:T(8,128)}, f32[8,176,128]{2,1,0:T(8,128)S(1)}, u32[]{:S(2)}) copy-start(f32[8,176,128]{2,1,0:T(8,128)S(1)} %all-to-all-done.got_ref) | copy-start | bytes 2162692
  30.9 6.3 %collective-permute-start.1 = (f32[5,16,128]{2,1,0:T(8,128)}, f32[5,16,128]{2,1,0:T(8,128)S(1)}, u32[]{:S(2)}, u32[]{:S(2)}) collective-permute-start(f32[5,16,128]{2,1,0:T(8,128)} %get-tuple-element.13), channel_id=1, source_target_pairs={{0,16},{1,113},{2,18},{3,115},{4,20},{5,117},{6,22},{7,119},{8,24}... | collective-permute-start | bytes 122888 | tf_op jit(solution)/shard_map/ppermute | solution.py:345
  37.3 2.6 %copy-start.2 = (f32[5,16,128]{2,1,0:T(8,128)}, f32[5,16,128]{2,1,0:T(8,128)S(1)}, u32[]{:S(2)}) copy-start(f32[5,16,128]{2,1,0:T(8,128)S(1)} %collective-permute-done.1.cross_ref) | copy-start | bytes 122884
  37.3 2.6 %collective-permute-start.2 = (f32[5,16,128]{2,1,0:T(8,128)S(1)}, f32[5,16,128]{2,1,0:T(8,128)S(1)}, u32[]{:S(2)}, u32[]{:S(2)}) collective-permute-start(f32[5,16,128]{2,1,0:T(8,128)S(1)} %collective-permute-done.1.cross_ref), channel_id=1, source_target_pairs={{0,1},{1,0},{2,3},{3,2},{4,5},{5,4},{6,7},{7,6},{8,9},{9,8},{10,11... | collective-permute-start | bytes 122888 | tf_op jit(solution)/shard_map/ppermute | solution.py:347
  39.9 0.6 copy-start.4
  65.6 6.3 %collective-permute-start.4 = (f32[5,16,128]{2,1,0:T(8,128)}, f32[5,16,128]{2,1,0:T(8,128)S(1)}, u32[]{:S(2)}, u32[]{:S(2)}) collective-permute-start(f32[5,16,128]{2,1,0:T(8,128)} %get-tuple-element.17), channel_id=1, source_target_pairs={{0,16},{1,113},{2,18},{3,115},{4,20},{5,117},{6,22},{7,119},{8,24}... | collective-permute-start | bytes 122888 | tf_op jit(solution)/shard_map/ppermute | solution.py:345
  71.9 1.2 %copy-start.3 = (f32[5,16,128]{2,1,0:T(8,128)}, f32[5,16,128]{2,1,0:T(8,128)S(1)}, u32[]{:S(2)}) copy-start(f32[5,16,128]{2,1,0:T(8,128)S(1)} %collective-permute-done.4.cross_ref) | copy-start | bytes 122884
  71.9 1.2 %collective-permute-start.5 = (f32[5,16,128]{2,1,0:T(8,128)S(1)}, f32[5,16,128]{2,1,0:T(8,128)S(1)}, u32[]{:S(2)}, u32[]{:S(2)}) collective-permute-start(f32[5,16,128]{2,1,0:T(8,128)S(1)} %collective-permute-done.4.cross_ref), channel_id=1, source_target_pairs={{0,1},{1,0},{2,3},{3,2},{4,5},{5,4},{6,7},{7,6},{8,9},{9,8},{10,11... | collective-permute-start | bytes 122888 | tf_op jit(solution)/shard_map/ppermute | solution.py:347
  73.2 0.6 copy-start.5

commit v6 on v4

--- a/solution.py
+++ b/solution.py
@@ -152,8 +152,12 @@
     up_pack = jnp.zeros((depth, LANES), jnp.float32)
     down_pack = jnp.zeros((depth, LANES), jnp.float32)
     top = bottom = None
+    half = depth // 2
     for x in range(slab_width):
-        r = relax(cells_of_x(x))
+        cells = cells_of_x(x)
+        lower = relax([c[:half] for c in cells])
+        upper = relax([c[half:] for c in cells])
+        r = [jnp.concatenate([a, b], axis=0) for a, b in zip(lower, upper)]
         for m in range(19):
             relaxed_ref[m, x] = r[m]
         if x == slab_width - 1:

time: 71.9 us -> 71.9 us (level)
  no operation moved by 1% of the time
where the time goes in v6:
time: 71.9 us; the launch traced here: 71.5 us
  waiting for transfers between devices  18.2 us (25%)
  blocking collectives  16.9 us (24%)
  starting transfers between devices  15.5 us (22%)
  Pallas kernels  14.5 us (20%)
  local copies, waits for them, and re-layouts  4.22 us (6%)
  matrix products  1.34 us (2%)
    all_to_all x1, blocking collectives, _per_device(): got = lax.all_to_all(chunks, 'gy', 0, 0, tiled=True)  16.9 us
    all_to_all x1, waiting for transfers between devices, _per_device(): got = lax.all_to_all(chunks, 'gy', 0, 0, tiled=True)  12.6 us
    ppermute x2, starting transfers between devices, _per_device(): lax.ppermute(high_send, 'gx', [(i, (i - 1) % slab_cycle) for i in range(s...  7.06 us
    all_to_all x1, starting transfers between devices, _per_device(): got = lax.all_to_all(chunks, 'gy', 0, 0, tiled=True)  7.04 us
    pallas_call x1, Pallas kernels, _per_device(): _call(_middle_kernel, 0, 5, (full, chunk))  4.35 us
    pallas_call x2, Pallas kernels, _per_device(): _call(functools.partial(_window_kernel, section), 2, 1, (ghost, ghost, ri...  3.93 us
    pallas_call x1, Pallas kernels, _per_device(): _call(_first_kernel, 0, 2, (full, chunk))(populations, other_states)  3.29 us
    unnamed x14, local copies, waits for them, and re-layouts  2.94 us
  transfers between devices with their start and end apart: 7, of which 4 were waited for; matrix products, arithmetic and copies ran while one was open for 4% of the time, Pallas kernels for 0%

profile of v6, /device:TPU:0, one launch (start us, length us, event | category | flops | bytes accessed | tf_op | source)
XLA Modules:
  0.0 71.5 jit_solution(18108064558919764253)
XLA Ops:
  0.6 0.1 collective-permute-start
  0.7 2.2 %collective-permute-done.other_ref = f32[19,8,8,128]{3,2,1,0:T(8,128)S(1)} collective-permute-done((f32[19,8,8,128]{3,2,1,0:T(8,128)}, f32[19,8,8,128]{3,2,1,0:T(8,128)S(1)}, u32[]{:S(2)}, u32[]{:S(2)}) %collective-permute-start) | collective-permute-done | bytes 622624 | tf_op jit(solution)/shard_map/ppermute | solution.py:304
  3.0 0.8 %copy-done.1 = f32[19,8,8,128]{3,2,1,0:T(8,128)} copy-done((f32[19,8,8,128]{3,2,1,0:T(8,128)}, f32[19,8,8,128]{3,2,1,0:T(8,128)S(1)}, u32[]{:S(2)}) %copy-start.1) | copy-done | bytes 622616
  3.8 3.3 %shard_map.59 = (f32[19,8,16,128]{3,2,1,0:T(8,128)}, f32[8,176,128]{2,1,0:T(8,128)}) custom-call(f32[19,8,8,128]{3,2,1,0:T(8,128)} %mine_ref.1, f32[19,8,8,128]{3,2,1,0:T(8,128)} %copy-done.1), custom_call_target="tpu_custom_call" | custom-call | tf_op jit(solution)/shard_map/pallas_call | solution.py:320
  7.1 7.0 %all-to-all-start = ((f32[8,176,128]{2,1,0:T(8,128)}), f32[8,176,128]{2,1,0:T(8,128)S(1)}, u32[]{:S(2)}, u32[]{:S(2)}) async-start(f32[8,176,128]{2,1,0:T(8,128)} %get-tuple-element.13), calls=%async_computation | async-start | bytes 1441792 | tf_op jit(solution)/shard_map/all_to_all | solution.py:322
  14.1 0.1 collective-permute-start.3
  14.2 1.2 %collective-permute-done.3 = s32[8,8,32]{2,1,0:T(8,128)S(1)} collective-permute-done((s32[8,8,32]{2,1,0:T(8,128)S(1)}, s32[8,8,32]{2,1,0:T(8,128)S(1)}, u32[]{:S(2)}, u32[]{:S(2)}) %collective-permute-start.3) | collective-permute-done | bytes 8224 | tf_op jit(solution)/shard_map/ppermute | solution.py:305
  15.4 0.1 add_select_fusion
  15.5 12.6 %all-to-all-done.got_ref = f32[8,176,128]{2,1,0:T(8,128)S(1)} async-done(((f32[8,176,128]{2,1,0:T(8,128)}), f32[8,176,128]{2,1,0:T(8,128)S(1)}, u32[]{:S(2)}, u32[]{:S(2)}) %all-to-all-start) | async-done | bytes 720928 | tf_op jit(solution)/shard_map/all_to_all | solution.py:322
  28.1 0.9 %copy-done = f32[8,176,128]{2,1,0:T(8,128)} copy-done((f32[8,176,128]{2,1,0:T(8,128)}, f32[8,176,128]{2,1,0:T(8,128)S(1)}, u32[]{:S(2)}) %copy-start) | copy-done | bytes 720920
  29.0 2.0 %shard_map.60 = (f32[5,16,128]{2,1,0:T(8,128)}, f32[5,16,128]{2,1,0:T(8,128)}, f32[2,16,128]{2,1,0:T(8,128)}) custom-call(s32[2]{0:T(128)} %shift_ref.3, s32[2]{0:T(128)} %frac_ref.3, f32[8,176,128]{2,1,0:T(8,128)} %copy-done), custom_call_target="tpu_custom_call" | custom-call | tf_op jit(solution)/shard_map/pallas_call | solution.py:323
  31.0 0.6 collective-permute-start.1
  31.6 3.5 %collective-permute-start.2 = (f32[5,16,128]{2,1,0:T(8,128)}, f32[5,16,128]{2,1,0:T(8,128)S(1)}, u32[]{:S(2)}, u32[]{:S(2)}) collective-permute-start(f32[5,16,128]{2,1,0:T(8,128)} %get-tuple-element.16), channel_id=1, source_target_pairs={{0,112},{16,0},{32,16},{48,32},{64,48},{80,64},{96,80},{112,96},{1... | collective-permute-start | bytes 122888 | tf_op jit(solution)/shard_map/ppermute | solution.py:327
  35.1 1.3 %fusion = f32[8,16,128,19]{2,3,1,0:T(8,128)S(1)} fusion(s32[8,16,32]{2,1,0:T(8,128)S(1)} %get-tuple-element.23, s32[8,16,32]{2,1,0:T(8,128)S(1)} %get-tuple-element.22), kind=kOutput, calls=%fused_computation.1 | convolution fusion | flops 20525056 | bytes 1277952 | tf_op jit(solution)/shard_map/xzml,xzly->mxzy/dot_general | solution.py:116
  36.5 1.3 %copy.8 = f32[8,16,128,19]{2,1,0,3:T(8,128)} copy(f32[8,16,128,19]{2,3,1,0:T(8,128)S(1)} %fusion) | data formatting | bytes 2490368 | tf_op jit(solution)/shard_map/xzml,xzly->mxzy/dot_general | solution.py:116
  37.8 0.6 copy-done.2
  38.4 4.4 %shard_map.61 = (f32[19,8,16,128]{3,2,1,0:T(8,128)}, f32[8,176,128]{2,1,0:T(8,128)}) custom-call(f32[19,8,16,128]{3,2,1,0:T(8,128)} %get-tuple-element.12.relaxed_ref, f32[2,16,128]{2,1,0:T(8,128)} %get-tuple-element.14.rims_ref, f32[5,16,128]{2,1,0:T(8,128)} %copy-done.2, f32[5,16,128]{2,1,0:T(8,128)} %copy-done.3, f32[19,8,16,128]{3,2,1,0:T(8,128)} %bitcast.3), custom_call_target="tpu_custom_call" | custom-call | tf_op jit(solution)/shard_map/pallas_call | solution.py:329
  42.7 16.9 %all_to_all.10.got_ref = f32[8,176,128]{2,1,0:T(8,128)} all-to-all(f32[8,176,128]{2,1,0:T(8,128)} %get-tuple-element.18), channel_id=1, replica_groups=mesh['gx'=8,'gy'=8,'gz'=2] {'gy'}, dimensions={0} | all-to-all | bytes 1441792 | tf_op jit(solution)/shard_map/all_to_all | solution.py:322
  59.7 2.0 %shard_map.62 = (f32[5,16,128]{2,1,0:T(8,128)}, f32[5,16,128]{2,1,0:T(8,128)}, f32[2,16,128]{2,1,0:T(8,128)}) custom-call(s32[2]{0:T(128)} %shift_ref.3, s32[2]{0:T(128)} %frac_ref.3, f32[8,176,128]{2,1,0:T(8,128)} %all_to_all.10.got_ref), custom_call_target="tpu_custom_call" | custom-call | tf_op jit(solution)/shard_map/pallas_call | solution.py:323
  61.6 0.6 collective-permute-start.4
  62.2 3.5 %collective-permute-start.5 = (f32[5,16,128]{2,1,0:T(8,128)}, f32[5,16,128]{2,1,0:T(8,128)S(1)}, u32[]{:S(2)}, u32[]{:S(2)}) collective-permute-start(f32[5,16,128]{2,1,0:T(8,128)} %get-tuple-element.21), channel_id=1, source_target_pairs={{0,112},{16,0},{32,16},{48,32},{64,48},{80,64},{96,80},{112,96},{1... | collective-permute-start | bytes 122888 | tf_op jit(solution)/shard_map/ppermute | solution.py:327
  65.8 2.2 %collective-permute-done.4.low_ref = f32[5,16,128]{2,1,0:T(8,128)S(1)} collective-permute-done((f32[5,16,128]{2,1,0:T(8,128)}, f32[5,16,128]{2,1,0:T(8,128)S(1)}, u32[]{:S(2)}, u32[]{:S(2)}) %collective-permute-start.4) | collective-permute-done | bytes 40992 | tf_op jit(solution)/shard_map/ppermute | solution.py:326
  68.0 0.6 copy-done.4
  68.6 2.9 %shard_map.63 = (f32[19,8,8,128]{3,2,1,0:T(8,128)}, f32[8,8,128]{2,1,0:T(8,128)}) custom-call(f32[19,8,16,128]{3,2,1,0:T(8,128)} %get-tuple-element.17.relaxed_ref, f32[2,16,128]{2,1,0:T(8,128)} %get-tuple-element.19.rims_ref, f32[5,16,128]{2,1,0:T(8,128)} %copy-done.4, f32[5,16,128]{2,1,0:T(8,128)} %copy-done.5, f32[19,8,16,128]{3,2,1,0:T(8,128)} %bitcast.4), custom_call_target="tpu_custom_call" | custom-call | tf_op jit(solution)/shard_map/pallas_call | solution.py:331
  (13 shorter events, 0.0 us)
Async XLA Ops:
  0.6 13.5 %copy-start.6 = (s32[8,8,32]{2,1,0:T(8,128)S(1)}, s32[8,8,32]{2,1,0:T(8,128)}, u32[]{:S(2)}) copy-start(s32[8,8,32]{2,1,0:T(8,128)} %param.7) | copy-start | bytes 24580
  0.6 2.3 %collective-permute-start = (f32[19,8,8,128]{3,2,1,0:T(8,128)}, f32[19,8,8,128]{3,2,1,0:T(8,128)S(1)}, u32[]{:S(2)}, u32[]{:S(2)}) collective-permute-start(f32[19,8,8,128]{3,2,1,0:T(8,128)} %mine_ref.1), channel_id=1, source_target_pairs={{0,1},{1,0},{2,3},{3,2},{4,5},{5,4},{6,7},{7,6},{8,9},{9,8},{10,11... | collective-permute-start | bytes 1867784 | tf_op jit(solution)/shard_map/ppermute | solution.py:304
  3.0 0.8 %copy-start.1 = (f32[19,8,8,128]{3,2,1,0:T(8,128)}, f32[19,8,8,128]{3,2,1,0:T(8,128)S(1)}, u32[]{:S(2)}) copy-start(f32[19,8,8,128]{3,2,1,0:T(8,128)S(1)} %collective-permute-done.other_ref) | copy-start | bytes 1867780
  7.1 21.0 %all-to-all-start = ((f32[8,176,128]{2,1,0:T(8,128)}), f32[8,176,128]{2,1,0:T(8,128)S(1)}, u32[]{:S(2)}, u32[]{:S(2)}) async-start(f32[8,176,128]{2,1,0:T(8,128)} %get-tuple-element.13), calls=%async_computation | async-start | bytes 1441792 | tf_op jit(solution)/shard_map/all_to_all | solution.py:322
  14.1 1.3 %collective-permute-start.3 = (s32[8,8,32]{2,1,0:T(8,128)S(1)}, s32[8,8,32]{2,1,0:T(8,128)S(1)}, u32[]{:S(2)}, u32[]{:S(2)}) collective-permute-start(s32[8,8,32]{2,1,0:T(8,128)S(1)} %copy-done.6), channel_id=1, source_target_pairs={{0,1},{1,0},{2,3},{3,2},{4,5},{5,4},{6,7},{7,6},{8,9},{9,8},{10,11... | collective-permute-start | bytes 24584 | tf_op jit(solution)/shard_map/ppermute | solution.py:305
  28.1 0.9 %copy-start = (f32[8,176,128]{2,1,0:T(8,128)}, f32[8,176,128]{2,1,0:T(8,128)S(1)}, u32[]{:S(2)}) copy-start(f32[8,176,128]{2,1,0:T(8,128)S(1)} %all-to-all-done.got_ref) | copy-start | bytes 2162692
  31.0 6.8 %collective-permute-start.1 = (f32[5,16,128]{2,1,0:T(8,128)}, f32[5,16,128]{2,1,0:T(8,128)S(1)}, u32[]{:S(2)}, u32[]{:S(2)}) collective-permute-start(f32[5,16,128]{2,1,0:T(8,128)} %get-tuple-element.15), channel_id=1, source_target_pairs={{0,16},{16,32},{32,48},{48,64},{64,80},{80,96},{96,112},{112,0},{1... | collective-permute-start | bytes 122888 | tf_op jit(solution)/shard_map/ppermute | solution.py:326
  31.6 6.2 %collective-permute-start.2 = (f32[5,16,128]{2,1,0:T(8,128)}, f32[5,16,128]{2,1,0:T(8,128)S(1)}, u32[]{:S(2)}, u32[]{:S(2)}) collective-permute-start(f32[5,16,128]{2,1,0:T(8,128)} %get-tuple-element.16), channel_id=1, source_target_pairs={{0,112},{16,0},{32,16},{48,32},{64,48},{80,64},{96,80},{112,96},{1... | collective-permute-start | bytes 122888 | tf_op jit(solution)/shard_map/ppermute | solution.py:327
  37.7 0.6 copy-start.2
  37.8 0.6 copy-start.3
  61.6 6.3 %collective-permute-start.4 = (f32[5,16,128]{2,1,0:T(8,128)}, f32[5,16,128]{2,1,0:T(8,128)S(1)}, u32[]{:S(2)}, u32[]{:S(2)}) collective-permute-start(f32[5,16,128]{2,1,0:T(8,128)} %get-tuple-element.20), channel_id=1, source_target_pairs={{0,16},{16,32},{32,48},{48,64},{64,80},{80,96},{96,112},{112,0},{1... | collective-permute-start | bytes 122888 | tf_op jit(solution)/shard_map/ppermute | solution.py:326
  62.2 5.7 %collective-permute-start.5 = (f32[5,16,128]{2,1,0:T(8,128)}, f32[5,16,128]{2,1,0:T(8,128)S(1)}, u32[]{:S(2)}, u32[]{:S(2)}) collective-permute-start(f32[5,16,128]{2,1,0:T(8,128)} %get-tuple-element.21), channel_id=1, source_target_pairs={{0,112},{16,0},{32,16},{48,32},{64,48},{80,64},{96,80},{112,96},{1... | collective-permute-start | bytes 122888 | tf_op jit(solution)/shard_map/ppermute | solution.py:327
  67.9 0.6 copy-start.4
  68.0 0.6 copy-start.5

commit v7 on v4

--- a/solution.py
+++ b/solution.py
@@ -113,7 +113,8 @@
     member = links % 19
     by_member = (member[:, :, None, :] == jnp.arange(19, dtype=jnp.int32)[:, None]).astype(jnp.bfloat16)
     by_cell = (cell_y[:, :, :, None] == jnp.arange(row_span, dtype=jnp.int32)).astype(jnp.bfloat16)
-    return jnp.einsum("xzml,xzly->mxzy", by_member, by_cell, preferred_element_type=jnp.float32)
+    counts = jnp.einsum("xzml,xzly->mxzy", by_member, by_cell, preferred_element_type=jnp.float32)
+    return (counts > 0.5).astype(jnp.bfloat16)
 
 
 LANES = 128
@@ -147,7 +148,7 @@
     return me_y, (me_y + 1) % flow_cycle, (me_y - 1 + flow_cycle) % flow_cycle, lax.axis_index("gz")
 
 
-def _emit_relax(cells_of_x, slab_width, relaxed_ref, chunk_ref, depth):
+def _emit_relax(cells_of_x, slab_width, relaxed_ref, chunk_ref, depth, plane_done=None):
     lane = lax.broadcasted_iota(jnp.int32, (depth, LANES), 1)
     up_pack = jnp.zeros((depth, LANES), jnp.float32)
     down_pack = jnp.zeros((depth, LANES), jnp.float32)
@@ -156,6 +157,8 @@
         r = relax(cells_of_x(x))
         for m in range(19):
             relaxed_ref[m, x] = r[m]
+        if plane_done is not None:
+            plane_done(x)
         if x == slab_width - 1:
             top = corrected(r, upward, -1.0)
         if x == 0:
@@ -200,41 +203,89 @@
     result = [out[0]]
     for n in range(1, 19):
         source = n - 1 + 2 * (n % 2)
-        result.append(jnp.where(hits_ref[source, x] > 0.5, relaxed_ref[source, x], out[n]))
+        result.append(jnp.where(hits_ref[source, x].astype(jnp.float32) > 0.5, relaxed_ref[source, x], out[n]))
     return result
 
 
-def _first_kernel(mine_ref, other_ref, relaxed_ref, chunk_ref):
-    slab_width, half = mine_ref.shape[1], mine_ref.shape[2]
+class _Planes:
+    def __init__(self, src, dst, sems):
+        self.copies = [pltpu.make_async_copy(src.at[:, x], dst.at[:, x], sems.at[x]) for x in range(src.shape[1])]
+        self.waited = set()
+
+    def start(self, x=None):
+        for i, c in enumerate(self.copies):
+            if x is None or i == x:
+                c.start()
+
+    def need(self, *planes):
+        for x in planes:
+            if 0 <= x < len(self.copies) and x not in self.waited:
+                self.copies[x].wait()
+                self.waited.add(x)
+
+    def finish(self):
+        self.need(*range(len(self.copies)))
+
+
+def _first_kernel(mine_hbm, other_hbm, relaxed_hbm, chunk_ref, mine_v, other_v, rel_v, sems):
+    slab_width, half = mine_v.shape[1], mine_v.shape[2]
     depth = 2 * half
     lower = jnp.full((half, LANES), _positions()[3], jnp.int32) == 0
+    mine = _Planes(mine_hbm, mine_v, sems.at[0])
+    other = _Planes(other_hbm, other_v, sems.at[1])
+    out = _Planes(rel_v, relaxed_hbm, sems.at[2])
+    mine.start()
+    other.start()
 
     def cells(x):
-        out = []
+        mine.need(x)
+        other.need(x)
+        res = []
         for m in range(19):
-            a, b = mine_ref[m, x], other_ref[m, x]
-            out.append(jnp.concatenate([jnp.where(lower, a, b), jnp.where(lower, b, a)], axis=0))
-        return out
-
-    _emit_relax(cells, slab_width, relaxed_ref, chunk_ref, depth)
-
-
-def _middle_kernel(relaxed_ref, rims_ref, low_ref, high_ref, hits_ref, next_ref, chunk_ref):
-    slab_width, depth = relaxed_ref.shape[1], relaxed_ref.shape[2]
-    cells = lambda x: _streamed(x, slab_width, relaxed_ref, rims_ref, low_ref, high_ref, hits_ref, depth)
-    _emit_relax(cells, slab_width, next_ref, chunk_ref, depth)
-
-
-def _last_kernel(relaxed_ref, rims_ref, low_ref, high_ref, hits_ref, out_ref, density_ref):
-    slab_width, depth = relaxed_ref.shape[1], relaxed_ref.shape[2]
+            a, b = mine_v[m, x], other_v[m, x]
+            res.append(jnp.concatenate([jnp.where(lower, a, b), jnp.where(lower, b, a)], axis=0))
+        return res
+
+    _emit_relax(cells, slab_width, rel_v, chunk_ref, depth, plane_done=out.start)
+    out.finish()
+
+
+def _middle_kernel(relaxed_hbm, hits_hbm, rims_ref, low_ref, high_ref, next_hbm, chunk_ref, rel_v, hits_v, out_v, sems):
+    slab_width, depth = rel_v.shape[1], rel_v.shape[2]
+    rel = _Planes(relaxed_hbm, rel_v, sems.at[0])
+    hit = _Planes(hits_hbm, hits_v, sems.at[1])
+    out = _Planes(out_v, next_hbm, sems.at[2])
+    rel.start()
+    hit.start()
+
+    def cells(x):
+        rel.need(x - 1, x, x + 1)
+        hit.need(x)
+        return _streamed(x, slab_width, rel_v, rims_ref, low_ref, high_ref, hits_v, depth)
+
+    _emit_relax(cells, slab_width, out_v, chunk_ref, depth, plane_done=out.start)
+    out.finish()
+
+
+def _last_kernel(relaxed_hbm, hits_hbm, rims_ref, low_ref, high_ref, out_hbm, density_ref, rel_v, hits_v, out_v, sems):
+    slab_width, depth = rel_v.shape[1], rel_v.shape[2]
     half = depth // 2
     lower = jnp.full((half, LANES), _positions()[3], jnp.int32) == 0
+    rel = _Planes(relaxed_hbm, rel_v, sems.at[0])
+    hit = _Planes(hits_hbm, hits_v, sems.at[1])
+    out = _Planes(out_v, out_hbm, sems.at[2])
+    rel.start()
+    hit.start()
     for x in range(slab_width):
-        cells = _streamed(x, slab_width, relaxed_ref, rims_ref, low_ref, high_ref, hits_ref, depth)
+        rel.need(x - 1, x, x + 1)
+        hit.need(x)
+        cells = _streamed(x, slab_width, rel_v, rims_ref, low_ref, high_ref, hits_v, depth)
         mine = [jnp.where(lower, c[:half], c[half:]) for c in cells]
         for m in range(19):
-            out_ref[m, x] = mine[m]
+            out_v[m, x] = mine[m]
+        out.start(x)
         density_ref[x] = total_density(mine)
+    out.finish()
 
 
 def _window_kernel(section, shift_ref, frac_ref, got_ref, low_ref, high_ref, rims_ref):
@@ -280,12 +331,19 @@
     return pl.BlockSpec(memory_space=pltpu.SMEM)
 
 
-def _call(kernel, n_smem, n_vmem, out_shapes):
+def _any():
+    return pl.BlockSpec(memory_space=pl.ANY)
+
+
+def _call(kernel, in_kinds, out_shapes, out_kinds=None, scratch=()):
+    kinds = {"s": _smem, "v": _vmem, "a": _any}
+    out_kinds = out_kinds or "v" * len(out_shapes)
     return pl.pallas_call(
         kernel,
         out_shape=out_shapes,
-        in_specs=[_smem()] * n_smem + [_vmem()] * n_vmem,
-        out_specs=tuple(_vmem() for _ in out_shapes),
+        in_specs=[kinds[k]() for k in in_kinds],
+        out_specs=tuple(kinds[k]() for k in out_kinds),
+        scratch_shapes=list(scratch),
     )
 
 
@@ -313,18 +371,31 @@
     own = jax.ShapeDtypeStruct((n_members, slab_width, half_depth, row_span), f32)
     density = jax.ShapeDtypeStruct((slab_width, half_depth, row_span), f32)
 
-    relaxed, chunks = _call(_first_kernel, 0, 2, (full, chunk))(populations, other_states)
+    half_full = (n_members, slab_width, half_depth, row_span)
+    dma = pltpu.SemaphoreType.DMA((3, slab_width))
+    relaxed, chunks = _call(
+        _first_kernel, "aa", (full, chunk), "av",
+        (pltpu.VMEM(half_full, f32), pltpu.VMEM(half_full, f32), pltpu.VMEM(full.shape, f32), dma),
+    )(populations, other_states)
+    stream_scratch = (
+        pltpu.VMEM(full.shape, f32), pltpu.VMEM(full.shape, jnp.bfloat16), pltpu.VMEM(full.shape, f32), dma
+    )
     for section in range(STEPS):
         got = lax.all_to_all(chunks, "gy", 0, 0, tiled=True)
-        low_send, high_send, rim_pair = _call(functools.partial(_window_kernel, section), 2, 1, (ghost, ghost, rims))(
+        low_send, high_send, rim_pair = _call(functools.partial(_window_kernel, section), "ssv", (ghost, ghost, rims))(
             le_shift, le_frac, got
         )
         low_ghost = lax.ppermute(low_send, "gx", [(i, (i + 1) % slab_cycle) for i in range(slab_cycle)])
         high_ghost = lax.ppermute(high_send, "gx", [(i, (i - 1) % slab_cycle) for i in range(slab_cycle)])
         if section + 1 < STEPS:
-            relaxed, chunks = _call(_middle_kernel, 0, 5, (full, chunk))(relaxed, rim_pair, low_ghost, high_ghost, hits)
+            relaxed, chunks = _call(_middle_kernel, "aavvv", (full, chunk), "av", stream_scratch)(
+                relaxed, hits, rim_pair, low_ghost, high_ghost
+            )
         else:
-            final, dens = _call(_last_kernel, 0, 5, (own, density))(relaxed, rim_pair, low_ghost, high_ghost, hits)
+            last_scratch = stream_scratch[:2] + (pltpu.VMEM(own.shape, f32), dma)
+            final, dens = _call(_last_kernel, "aavvv", (own, density), "av", last_scratch)(
+                relaxed, hits, rim_pair, low_ghost, high_ghost
+            )
     return (final, dens)
 
 

time: 71.9 us -> 75.2 us (1.046)
  Pallas kernels: 14.5 us -> 18.7 us
  local copies, waits for them, and re-layouts: 4.22 us -> 2.95 us
  other arithmetic: 0.08 us -> 1.24 us
    pallas_call x5, Pallas kernels: 14.5 us -> 18.7 us  [the longest x1 5.94 us: _per_device(): _call(_middle_kernel, 'aavvv', (full, chunk), 'av', stream_scratch)]
    all_to_all x1, waiting for transfers between devices: 12.6 us -> 11.3 us  [_per_device(): got = lax.all_to_all(chunks, 'gy', 0, 0, tiled=True)]
    dot_general x1 -> x0, local copies, waits for them, and re-layouts: 1.28 us -> none  [link_hits(): jnp.einsum('xzml,xzly->mxzy', by_member, by_cell, preferred_element_type=...]
    convert_element_type x0 -> x1, other arithmetic: none -> 1.15 us  [link_hits(): return (counts > 0.5).astype(jnp.bfloat16)]
    ppermute x2, waiting for transfers between devices: 2.19 us -> 3.22 us  [_per_device(): lax.ppermute(low_send, 'gx', [(i, (i + 1) % slab_cycle) for i in range(sl...]
    ppermute x2, starting transfers between devices: 7.06 us -> 6.04 us  [_per_device(): lax.ppermute(high_send, 'gx', [(i, (i - 1) % slab_cycle) for i in range(s...]
    ppermute x2, starting transfers between devices: 1.21 us -> 2.23 us  [_per_device(): lax.ppermute(low_send, 'gx', [(i, (i + 1) % slab_cycle) for i in range(sl...]
  transfers between devices with their start and end apart: 7 -> 7, of which waited for: 4 -> 5; matrix products, arithmetic and copies ran while one was open for 4% -> 3% of each run, Pallas kernels for 0% -> 0%
where the time goes in v7:
time: 75.2 us; the launch traced here: 74.7 us
  Pallas kernels  18.7 us (25%)
  waiting for transfers between devices  17.9 us (24%)
  blocking collectives  16.4 us (22%)
  starting transfers between devices  15.5 us (21%)
  local copies, waits for them, and re-layouts  2.95 us (4%)
  matrix products  1.35 us (2%)
  other arithmetic  1.24 us (2%)
    all_to_all x1, blocking collectives, _per_device(): got = lax.all_to_all(chunks, 'gy', 0, 0, tiled=True)  16.4 us
    all_to_all x1, waiting for transfers between devices, _per_device(): got = lax.all_to_all(chunks, 'gy', 0, 0, tiled=True)  11.3 us
    all_to_all x1, starting transfers between devices, _per_device(): got = lax.all_to_all(chunks, 'gy', 0, 0, tiled=True)  7.05 us
    ppermute x2, starting transfers between devices, _per_device(): lax.ppermute(high_send, 'gx', [(i, (i - 1) % slab_cycle) for i in range(s...  6.04 us
    pallas_call x1, Pallas kernels, _per_device(): _call(_middle_kernel, 'aavvv', (full, chunk), 'av', stream_scratch)  5.94 us
    pallas_call x1, Pallas kernels, _per_device(): _call(_last_kernel, 'aavvv', (own, density), 'av', last_scratch)  4.56 us
    pallas_call x1, Pallas kernels, _per_device(): _call(_first_kernel, 'aa', (full, chunk), 'av', (pltpu.VMEM(half_full, f3...  4.23 us
    pallas_call x2, Pallas kernels, _per_device(): _call(functools.partial(_window_kernel, section), 'ssv', (ghost, ghost, r...  3.93 us
  transfers between devices with their start and end apart: 7, of which 5 were waited for; matrix products, arithmetic and copies ran while one was open for 3% of the time, Pallas kernels for 0%

profile of v7, /device:TPU:0, one launch (start us, length us, event | category | flops | bytes accessed | tf_op | source)
XLA Modules:
  0.0 74.7 jit_solution(364218830332369332)
XLA Ops:
  0.6 0.1 collective-permute-start
  0.7 2.2 %collective-permute-done.other_hbm = f32[19,8,8,128]{3,2,1,0:T(8,128)S(1)} collective-permute-done((f32[19,8,8,128]{3,2,1,0:T(8,128)}, f32[19,8,8,128]{3,2,1,0:T(8,128)S(1)}, u32[]{:S(2)}, u32[]{:S(2)}) %collective-permute-start) | collective-permute-done | bytes 622624 | tf_op jit(solution)/shard_map/ppermute | solution.py:358
  3.0 0.8 %copy-done.1 = f32[19,8,8,128]{3,2,1,0:T(8,128)} copy-done((f32[19,8,8,128]{3,2,1,0:T(8,128)}, f32[19,8,8,128]{3,2,1,0:T(8,128)S(1)}, u32[]{:S(2)}) %copy-start.1) | copy-done | bytes 622616
  3.8 4.2 %shard_map.59 = (f32[19,8,16,128]{3,2,1,0:T(8,128)}, f32[8,176,128]{2,1,0:T(8,128)}) custom-call(f32[19,8,8,128]{3,2,1,0:T(8,128)} %mine_hbm.1, f32[19,8,8,128]{3,2,1,0:T(8,128)} %copy-done.1), custom_call_target="tpu_custom_call" | custom-call | tf_op jit(solution)/shard_map/pallas_call | solution.py:376
  8.0 7.1 %all-to-all-start = ((f32[8,176,128]{2,1,0:T(8,128)}), f32[8,176,128]{2,1,0:T(8,128)S(1)}, u32[]{:S(2)}, u32[]{:S(2)}) async-start(f32[8,176,128]{2,1,0:T(8,128)} %get-tuple-element.13), calls=%async_computation | async-start | bytes 1441792 | tf_op jit(solution)/shard_map/all_to_all | solution.py:384
  15.1 0.1 collective-permute-start.1
  15.2 1.2 %collective-permute-done.1 = s32[8,8,32]{2,1,0:T(8,128)S(1)} collective-permute-done((s32[8,8,32]{2,1,0:T(8,128)S(1)}, s32[8,8,32]{2,1,0:T(8,128)S(1)}, u32[]{:S(2)}, u32[]{:S(2)}) %collective-permute-start.1) | collective-permute-done | bytes 8224 | tf_op jit(solution)/shard_map/ppermute | solution.py:359
  16.5 1.4 %fusion = f32[8,16,128,19]{2,3,1,0:T(8,128)S(1)} fusion(s32[8,16,32]{2,1,0:T(8,128)S(1)} %get-tuple-element.23, s32[8,16,32]{2,1,0:T(8,128)S(1)} %get-tuple-element.22), kind=kOutput, calls=%fused_computation.1 | convolution fusion | flops 20525056 | bytes 1277952 | tf_op jit(solution)/shard_map/xzml,xzly->mxzy/dot_general | solution.py:116
  17.8 11.3 %all-to-all-done.got_ref = f32[8,176,128]{2,1,0:T(8,128)S(1)} async-done(((f32[8,176,128]{2,1,0:T(8,128)}), f32[8,176,128]{2,1,0:T(8,128)S(1)}, u32[]{:S(2)}, u32[]{:S(2)}) %all-to-all-start) | async-done | bytes 720928 | tf_op jit(solution)/shard_map/all_to_all | solution.py:384
  29.1 0.9 %copy-done = f32[8,176,128]{2,1,0:T(8,128)} copy-done((f32[8,176,128]{2,1,0:T(8,128)}, f32[8,176,128]{2,1,0:T(8,128)S(1)}, u32[]{:S(2)}) %copy-start) | copy-done | bytes 720920
  30.0 2.0 %shard_map.60 = (f32[5,16,128]{2,1,0:T(8,128)}, f32[5,16,128]{2,1,0:T(8,128)}, f32[2,16,128]{2,1,0:T(8,128)}) custom-call(s32[2]{0:T(128)} %shift_ref.3, s32[2]{0:T(128)} %frac_ref.3, f32[8,176,128]{2,1,0:T(8,128)} %copy-done), custom_call_target="tpu_custom_call" | custom-call | tf_op jit(solution)/shard_map/pallas_call | solution.py:385
  31.9 0.6 collective-permute-start.2
  32.5 3.5 %collective-permute-start.3 = (f32[5,16,128]{2,1,0:T(8,128)}, f32[5,16,128]{2,1,0:T(8,128)S(1)}, u32[]{:S(2)}, u32[]{:S(2)}) collective-permute-start(f32[5,16,128]{2,1,0:T(8,128)} %get-tuple-element.16), channel_id=1, source_target_pairs={{0,112},{16,0},{32,16},{48,32},{64,48},{80,64},{96,80},{112,96},{1... | collective-permute-start | bytes 122888 | tf_op jit(solution)/shard_map/ppermute | solution.py:389
  36.1 1.2 %fusion.4.hits_hbm = bf16[19,8,16,128]{3,2,1,0:T(8,128)(2,1)} fusion(f32[8,16,128,19]{2,3,1,0:T(8,128)S(1)} %fusion), kind=kLoop, calls=%fused_computation.7 | loop fusion | flops 622592 | bytes 1867776 | tf_op jit(solution)/shard_map/convert_element_type | solution.py:117
  37.2 1.0 %collective-permute-done.2.low_ref = f32[5,16,128]{2,1,0:T(8,128)S(1)} collective-permute-done((f32[5,16,128]{2,1,0:T(8,128)}, f32[5,16,128]{2,1,0:T(8,128)S(1)}, u32[]{:S(2)}, u32[]{:S(2)}) %collective-permute-start.2) | collective-permute-done | bytes 40992 | tf_op jit(solution)/shard_map/ppermute | solution.py:388
  38.3 0.6 copy-done.2
  38.9 5.9 %shard_map.61 = (f32[19,8,16,128]{3,2,1,0:T(8,128)}, f32[8,176,128]{2,1,0:T(8,128)}) custom-call(f32[19,8,16,128]{3,2,1,0:T(8,128)} %get-tuple-element.12.relaxed_hbm, bf16[19,8,16,128]{3,2,1,0:T(8,128)(2,1)} %fusion.4.hits_hbm, f32[2,16,128]{2,1,0:T(8,128)} %get-tuple-element.14.rims_ref, f32[5,16,128]{2,1,0:T(8,128)} %copy-done.2, f32[5,16,128]{2,1,0:T(8,128)} %copy-done.4), custom_call_target="tpu_custom_call" | custom-call | tf_op jit(solution)/shard_map/pallas_call | solution.py:391
  44.8 16.4 %all_to_all.10.got_ref = f32[8,176,128]{2,1,0:T(8,128)} all-to-all(f32[8,176,128]{2,1,0:T(8,128)} %get-tuple-element.18), channel_id=1, replica_groups=mesh['gx'=8,'gy'=8,'gz'=2] {'gy'}, dimensions={0} | all-to-all | bytes 1441792 | tf_op jit(solution)/shard_map/all_to_all | solution.py:384
  61.2 2.0 %shard_map.62 = (f32[5,16,128]{2,1,0:T(8,128)}, f32[5,16,128]{2,1,0:T(8,128)}, f32[2,16,128]{2,1,0:T(8,128)}) custom-call(s32[2]{0:T(128)} %shift_ref.3, s32[2]{0:T(128)} %frac_ref.3, f32[8,176,128]{2,1,0:T(8,128)} %all_to_all.10.got_ref), custom_call_target="tpu_custom_call" | custom-call | tf_op jit(solution)/shard_map/pallas_call | solution.py:385
  63.2 1.6 %collective-permute-start.4 = (f32[5,16,128]{2,1,0:T(8,128)}, f32[5,16,128]{2,1,0:T(8,128)S(1)}, u32[]{:S(2)}, u32[]{:S(2)}) collective-permute-start(f32[5,16,128]{2,1,0:T(8,128)} %get-tuple-element.20), channel_id=1, source_target_pairs={{0,16},{16,32},{32,48},{48,64},{64,80},{80,96},{96,112},{112,0},{1... | collective-permute-start | bytes 122888 | tf_op jit(solution)/shard_map/ppermute | solution.py:388
  64.8 2.5 %collective-permute-start.5 = (f32[5,16,128]{2,1,0:T(8,128)}, f32[5,16,128]{2,1,0:T(8,128)S(1)}, u32[]{:S(2)}, u32[]{:S(2)}) collective-permute-start(f32[5,16,128]{2,1,0:T(8,128)} %get-tuple-element.21), channel_id=1, source_target_pairs={{0,112},{16,0},{32,16},{48,32},{64,48},{80,64},{96,80},{112,96},{1... | collective-permute-start | bytes 122888 | tf_op jit(solution)/shard_map/ppermute | solution.py:389
  67.3 2.2 %collective-permute-done.4.low_ref = f32[5,16,128]{2,1,0:T(8,128)S(1)} collective-permute-done((f32[5,16,128]{2,1,0:T(8,128)}, f32[5,16,128]{2,1,0:T(8,128)S(1)}, u32[]{:S(2)}, u32[]{:S(2)}) %collective-permute-start.4) | collective-permute-done | bytes 40992 | tf_op jit(solution)/shard_map/ppermute | solution.py:388
  69.5 0.6 copy-done.3
  70.1 4.6 %shard_map.63 = (f32[19,8,8,128]{3,2,1,0:T(8,128)}, f32[8,8,128]{2,1,0:T(8,128)}) custom-call(f32[19,8,16,128]{3,2,1,0:T(8,128)} %get-tuple-element.17.relaxed_hbm, bf16[19,8,16,128]{3,2,1,0:T(8,128)(2,1)} %fusion.4.hits_hbm, f32[2,16,128]{2,1,0:T(8,128)} %get-tuple-element.19.rims_ref, f32[5,16,128]{2,1,0:T(8,128)} %copy-done.3, f32[5,16,128]{2,1,0:T(8,128)} %copy-done.5), custom_call_target="tpu_custom_call" | custom-call | tf_op jit(solution)/shard_map/pallas_call | solution.py:396
  (13 shorter events, 0.1 us)
Async XLA Ops:
  0.6 14.5 %copy-start.6 = (s32[8,8,32]{2,1,0:T(8,128)S(1)}, s32[8,8,32]{2,1,0:T(8,128)}, u32[]{:S(2)}) copy-start(s32[8,8,32]{2,1,0:T(8,128)} %param.7) | copy-start | bytes 24580
  0.6 2.3 %collective-permute-start = (f32[19,8,8,128]{3,2,1,0:T(8,128)}, f32[19,8,8,128]{3,2,1,0:T(8,128)S(1)}, u32[]{:S(2)}, u32[]{:S(2)}) collective-permute-start(f32[19,8,8,128]{3,2,1,0:T(8,128)} %mine_hbm.1), channel_id=1, source_target_pairs={{0,1},{1,0},{2,3},{3,2},{4,5},{5,4},{6,7},{7,6},{8,9},{9,8},{10,11... | collective-permute-start | bytes 1867784 | tf_op jit(solution)/shard_map/ppermute | solution.py:358
  3.0 0.8 %copy-start.1 = (f32[19,8,8,128]{3,2,1,0:T(8,128)}, f32[19,8,8,128]{3,2,1,0:T(8,128)S(1)}, u32[]{:S(2)}) copy-start(f32[19,8,8,128]{3,2,1,0:T(8,128)S(1)} %collective-permute-done.other_hbm) | copy-start | bytes 1867780
  8.0 21.0 %all-to-all-start = ((f32[8,176,128]{2,1,0:T(8,128)}), f32[8,176,128]{2,1,0:T(8,128)S(1)}, u32[]{:S(2)}, u32[]{:S(2)}) async-start(f32[8,176,128]{2,1,0:T(8,128)} %get-tuple-element.13), calls=%async_computation | async-start | bytes 1441792 | tf_op jit(solution)/shard_map/all_to_all | solution.py:384
  15.1 1.3 %collective-permute-start.1 = (s32[8,8,32]{2,1,0:T(8,128)S(1)}, s32[8,8,32]{2,1,0:T(8,128)S(1)}, u32[]{:S(2)}, u32[]{:S(2)}) collective-permute-start(s32[8,8,32]{2,1,0:T(8,128)S(1)} %copy-done.6), channel_id=1, source_target_pairs={{0,1},{1,0},{2,3},{3,2},{4,5},{5,4},{6,7},{7,6},{8,9},{9,8},{10,11... | collective-permute-start | bytes 24584 | tf_op jit(solution)/shard_map/ppermute | solution.py:359
  29.1 0.9 %copy-start = (f32[8,176,128]{2,1,0:T(8,128)}, f32[8,176,128]{2,1,0:T(8,128)S(1)}, u32[]{:S(2)}) copy-start(f32[8,176,128]{2,1,0:T(8,128)S(1)} %all-to-all-done.got_ref) | copy-start | bytes 2162692
  31.9 6.3 %collective-permute-start.2 = (f32[5,16,128]{2,1,0:T(8,128)}, f32[5,16,128]{2,1,0:T(8,128)S(1)}, u32[]{:S(2)}, u32[]{:S(2)}) collective-permute-start(f32[5,16,128]{2,1,0:T(8,128)} %get-tuple-element.15), channel_id=1, source_target_pairs={{0,16},{16,32},{32,48},{48,64},{64,80},{80,96},{96,112},{112,0},{1... | collective-permute-start | bytes 122888 | tf_op jit(solution)/shard_map/ppermute | solution.py:388
  32.5 5.7 %collective-permute-start.3 = (f32[5,16,128]{2,1,0:T(8,128)}, f32[5,16,128]{2,1,0:T(8,128)S(1)}, u32[]{:S(2)}, u32[]{:S(2)}) collective-permute-start(f32[5,16,128]{2,1,0:T(8,128)} %get-tuple-element.16), channel_id=1, source_target_pairs={{0,112},{16,0},{32,16},{48,32},{64,48},{80,64},{96,80},{112,96},{1... | collective-permute-start | bytes 122888 | tf_op jit(solution)/shard_map/ppermute | solution.py:389
  38.3 0.6 copy-start.2
  38.3 0.6 copy-start.4
  63.2 6.3 %collective-permute-start.4 = (f32[5,16,128]{2,1,0:T(8,128)}, f32[5,16,128]{2,1,0:T(8,128)S(1)}, u32[]{:S(2)}, u32[]{:S(2)}) collective-permute-start(f32[5,16,128]{2,1,0:T(8,128)} %get-tuple-element.20), channel_id=1, source_target_pairs={{0,16},{16,32},{32,48},{48,64},{64,80},{80,96},{96,112},{112,0},{1... | collective-permute-start | bytes 122888 | tf_op jit(solution)/shard_map/ppermute | solution.py:388
  64.8 4.7 %collective-permute-start.5 = (f32[5,16,128]{2,1,0:T(8,128)}, f32[5,16,128]{2,1,0:T(8,128)S(1)}, u32[]{:S(2)}, u32[]{:S(2)}) collective-permute-start(f32[5,16,128]{2,1,0:T(8,128)} %get-tuple-element.21), channel_id=1, source_target_pairs={{0,112},{16,0},{32,16},{48,32},{64,48},{80,64},{96,80},{112,96},{1... | collective-permute-start | bytes 122888 | tf_op jit(solution)/shard_map/ppermute | solution.py:389
  69.5 0.6 copy-start.3
  69.5 0.6 copy-start.5

commit v8 on v4

--- a/solution.py
+++ b/solution.py
@@ -154,8 +154,11 @@
     top = bottom = None
     for x in range(slab_width):
         r = relax(cells_of_x(x))
-        for m in range(19):
-            relaxed_ref[m, x] = r[m]
+        if relaxed_ref is not None:
+            for m in range(19):
+                relaxed_ref[m, x] = r[m]
+        if chunk_ref is None:
+            continue
         if x == slab_width - 1:
             top = corrected(r, upward, -1.0)
         if x == 0:
@@ -166,6 +169,8 @@
         for i, m in enumerate(y_minus):
             k = i * slab_width + x
             down_pack = jnp.where(lane == k, _roll(r[m], k, 1), down_pack)
+    if chunk_ref is None:
+        return
     faces = jnp.concatenate([top.reshape(5 * depth, LANES), bottom.reshape(5 * depth, LANES)], axis=0)
     _, after, before, _ = _positions()
     to_next = jnp.full((depth, LANES), after, jnp.int32)
@@ -204,7 +209,8 @@
     return result
 
 
-def _first_kernel(mine_ref, other_ref, relaxed_ref, chunk_ref):
+def _first_kernel(mine_ref, other_ref, *outs):
+    relaxed_ref, chunk_ref = (outs[0], None) if outs[0].shape[0] == 19 else (None, outs[0])
     slab_width, half = mine_ref.shape[1], mine_ref.shape[2]
     depth = 2 * half
     lower = jnp.full((half, LANES), _positions()[3], jnp.int32) == 0
@@ -219,7 +225,8 @@
     _emit_relax(cells, slab_width, relaxed_ref, chunk_ref, depth)
 
 
-def _middle_kernel(relaxed_ref, rims_ref, low_ref, high_ref, hits_ref, next_ref, chunk_ref):
+def _middle_kernel(relaxed_ref, rims_ref, low_ref, high_ref, hits_ref, *outs):
+    next_ref, chunk_ref = (outs[0], None) if outs[0].shape[0] == 19 else (None, outs[0])
     slab_width, depth = relaxed_ref.shape[1], relaxed_ref.shape[2]
     cells = lambda x: _streamed(x, slab_width, relaxed_ref, rims_ref, low_ref, high_ref, hits_ref, depth)
     _emit_relax(cells, slab_width, next_ref, chunk_ref, depth)
@@ -285,7 +292,7 @@
         kernel,
         out_shape=out_shapes,
         in_specs=[_smem()] * n_smem + [_vmem()] * n_vmem,
-        out_specs=tuple(_vmem() for _ in out_shapes),
+        out_specs=tuple(_vmem() for _ in out_shapes) if isinstance(out_shapes, tuple) else _vmem(),
     )
 
 
@@ -313,7 +320,8 @@
     own = jax.ShapeDtypeStruct((n_members, slab_width, half_depth, row_span), f32)
     density = jax.ShapeDtypeStruct((slab_width, half_depth, row_span), f32)
 
-    relaxed, chunks = _call(_first_kernel, 0, 2, (full, chunk))(populations, other_states)
+    chunks = _call(_first_kernel, 0, 2, chunk)(populations, other_states)
+    relaxed = _call(_first_kernel, 0, 2, full)(populations, other_states)
     for section in range(STEPS):
         got = lax.all_to_all(chunks, "gy", 0, 0, tiled=True)
         low_send, high_send, rim_pair = _call(functools.partial(_window_kernel, section), 2, 1, (ghost, ghost, rims))(
@@ -322,7 +330,9 @@
         low_ghost = lax.ppermute(low_send, "gx", [(i, (i + 1) % slab_cycle) for i in range(slab_cycle)])
         high_ghost = lax.ppermute(high_send, "gx", [(i, (i - 1) % slab_cycle) for i in range(slab_cycle)])
         if section + 1 < STEPS:
-            relaxed, chunks = _call(_middle_kernel, 0, 5, (full, chunk))(relaxed, rim_pair, low_ghost, high_ghost, hits)
+            args = (relaxed, rim_pair, low_ghost, high_ghost, hits)
+            chunks = _call(_middle_kernel, 0, 5, chunk)(*args)
+            relaxed = _call(_middle_kernel, 0, 5, full)(*args)
         else:
             final, dens = _call(_last_kernel, 0, 5, (own, density))(relaxed, rim_pair, low_ghost, high_ghost, hits)
     return (final, dens)

time: 71.9 us -> 75.4 us (1.049)
  Pallas kernels: 14.5 us -> 20.1 us
  waiting for transfers between devices: 18.2 us -> 16.1 us
    pallas_call x2 -> x4, Pallas kernels: 7.65 us -> 13.2 us  [the longest x1 3.83 us: _per_device(): chunks = _call(_middle_kernel, 0, 5, chunk)(*args)]
    ppermute x2, waiting for transfers between devices: 2.19 us -> 0.01 us  [_per_device(): lax.ppermute(low_send, 'gx', [(i, (i + 1) % slab_cycle) for i in range(sl...]
  transfers between devices with their start and end apart: 7 -> 7, of which waited for: 4 -> 3; matrix products, arithmetic and copies ran while one was open for 4% -> 4% of each run, Pallas kernels for 0% -> 9%
where the time goes in v8:
time: 75.4 us; the launch traced here: 74.9 us
  Pallas kernels  20.1 us (27%)
  blocking collectives  16.9 us (22%)
  waiting for transfers between devices  16.1 us (21%)
  starting transfers between devices  15.5 us (21%)
  local copies, waits for them, and re-layouts  4.21 us (6%)
  matrix products  1.34 us (2%)
    all_to_all x1, blocking collectives, _per_device(): got = lax.all_to_all(chunks, 'gy', 0, 0, tiled=True)  16.9 us
    all_to_all x1, waiting for transfers between devices, _per_device(): got = lax.all_to_all(chunks, 'gy', 0, 0, tiled=True)  12.6 us
    ppermute x2, starting transfers between devices, _per_device(): lax.ppermute(high_send, 'gx', [(i, (i - 1) % slab_cycle) for i in range(s...  7.68 us
    all_to_all x1, starting transfers between devices, _per_device(): got = lax.all_to_all(chunks, 'gy', 0, 0, tiled=True)  7.04 us
    pallas_call x2, Pallas kernels, _per_device(): _call(functools.partial(_window_kernel, section), 2, 1, (ghost, ghost, ri...  3.94 us
    pallas_call x1, Pallas kernels, _per_device(): chunks = _call(_middle_kernel, 0, 5, chunk)(*args)  3.83 us
    pallas_call x1, Pallas kernels, _per_device(): relaxed = _call(_middle_kernel, 0, 5, full)(*args)  3.58 us
    pallas_call x1, Pallas kernels, _per_device(): relaxed = _call(_first_kernel, 0, 2, full)(populations, other_states)  2.99 us
  transfers between devices with their start and end apart: 7, of which 3 were waited for; matrix products, arithmetic and copies ran while one was open for 4% of the time, Pallas kernels for 9%

profile of v8, /device:TPU:0, one launch (start us, length us, event | category | flops | bytes accessed | tf_op | source)
XLA Modules:
  0.0 74.9 jit_solution(14439111433001754060)
XLA Ops:
  0.6 0.1 collective-permute-start
  0.7 2.2 %collective-permute-done.other_ref = f32[19,8,8,128]{3,2,1,0:T(8,128)S(1)} collective-permute-done((f32[19,8,8,128]{3,2,1,0:T(8,128)}, f32[19,8,8,128]{3,2,1,0:T(8,128)S(1)}, u32[]{:S(2)}, u32[]{:S(2)}) %collective-permute-start) | collective-permute-done | bytes 622624 | tf_op jit(solution)/shard_map/ppermute | solution.py:307
  3.0 0.8 %copy-done.1 = f32[19,8,8,128]{3,2,1,0:T(8,128)} copy-done((f32[19,8,8,128]{3,2,1,0:T(8,128)}, f32[19,8,8,128]{3,2,1,0:T(8,128)S(1)}, u32[]{:S(2)}) %copy-start.1) | copy-done | bytes 622616
  3.8 2.8 %shard_map.60 = f32[8,176,128]{2,1,0:T(8,128)} custom-call(f32[19,8,8,128]{3,2,1,0:T(8,128)} %mine_ref.3, f32[19,8,8,128]{3,2,1,0:T(8,128)} %copy-done.1), custom_call_target="tpu_custom_call" | custom-call | tf_op jit(solution)/shard_map/pallas_call | solution.py:323
  6.6 7.0 %all-to-all-start = ((f32[8,176,128]{2,1,0:T(8,128)}), f32[8,176,128]{2,1,0:T(8,128)S(1)}, u32[]{:S(2)}, u32[]{:S(2)}) async-start(f32[8,176,128]{2,1,0:T(8,128)} %shard_map.60), calls=%async_computation | async-start | bytes 1441792 | tf_op jit(solution)/shard_map/all_to_all | solution.py:326
  13.7 0.1 collective-permute-start.3
  13.8 1.2 %collective-permute-done.3 = s32[8,8,32]{2,1,0:T(8,128)S(1)} collective-permute-done((s32[8,8,32]{2,1,0:T(8,128)S(1)}, s32[8,8,32]{2,1,0:T(8,128)S(1)}, u32[]{:S(2)}, u32[]{:S(2)}) %collective-permute-start.3) | collective-permute-done | bytes 8224 | tf_op jit(solution)/shard_map/ppermute | solution.py:308
  15.0 0.1 add_select_fusion
  15.0 12.6 %all-to-all-done.got_ref = f32[8,176,128]{2,1,0:T(8,128)S(1)} async-done(((f32[8,176,128]{2,1,0:T(8,128)}), f32[8,176,128]{2,1,0:T(8,128)S(1)}, u32[]{:S(2)}, u32[]{:S(2)}) %all-to-all-start) | async-done | bytes 720928 | tf_op jit(solution)/shard_map/all_to_all | solution.py:326
  27.7 0.9 %copy-done = f32[8,176,128]{2,1,0:T(8,128)} copy-done((f32[8,176,128]{2,1,0:T(8,128)}, f32[8,176,128]{2,1,0:T(8,128)S(1)}, u32[]{:S(2)}) %copy-start) | copy-done | bytes 720920
  28.5 2.0 %shard_map.61 = (f32[5,16,128]{2,1,0:T(8,128)}, f32[5,16,128]{2,1,0:T(8,128)}, f32[2,16,128]{2,1,0:T(8,128)}) custom-call(s32[2]{0:T(128)} %shift_ref.3, s32[2]{0:T(128)} %frac_ref.3, f32[8,176,128]{2,1,0:T(8,128)} %copy-done), custom_call_target="tpu_custom_call" | custom-call | tf_op jit(solution)/shard_map/pallas_call | solution.py:327
  30.5 0.6 collective-permute-start.1
  31.1 3.5 %collective-permute-start.2 = (f32[5,16,128]{2,1,0:T(8,128)}, f32[5,16,128]{2,1,0:T(8,128)S(1)}, u32[]{:S(2)}, u32[]{:S(2)}) collective-permute-start(f32[5,16,128]{2,1,0:T(8,128)} %get-tuple-element.10), channel_id=1, source_target_pairs={{0,112},{16,0},{32,16},{48,32},{64,48},{80,64},{96,80},{112,96},{1... | collective-permute-start | bytes 122888 | tf_op jit(solution)/shard_map/ppermute | solution.py:331
  34.6 1.3 %fusion = f32[8,16,128,19]{2,3,1,0:T(8,128)S(1)} fusion(s32[8,16,32]{2,1,0:T(8,128)S(1)} %get-tuple-element.15, s32[8,16,32]{2,1,0:T(8,128)S(1)} %get-tuple-element.14), kind=kOutput, calls=%fused_computation.1 | convolution fusion | flops 20525056 | bytes 1277952 | tf_op jit(solution)/shard_map/xzml,xzly->mxzy/dot_general | solution.py:116
  36.0 1.3 %copy.8 = f32[8,16,128,19]{2,1,0,3:T(8,128)} copy(f32[8,16,128,19]{2,3,1,0:T(8,128)S(1)} %fusion) | data formatting | bytes 2490368 | tf_op jit(solution)/shard_map/xzml,xzly->mxzy/dot_general | solution.py:116
  37.3 3.0 %shard_map.59.relaxed_ref = f32[19,8,16,128]{3,2,1,0:T(8,128)} custom-call(f32[19,8,8,128]{3,2,1,0:T(8,128)} %mine_ref.3, f32[19,8,8,128]{3,2,1,0:T(8,128)} %copy-done.1), custom_call_target="tpu_custom_call" | custom-call | tf_op jit(solution)/shard_map/pallas_call | solution.py:324
  40.3 0.6 copy-done.2
  40.9 3.8 %shard_map.63 = f32[8,176,128]{2,1,0:T(8,128)} custom-call(f32[19,8,16,128]{3,2,1,0:T(8,128)} %shard_map.59.relaxed_ref, f32[2,16,128]{2,1,0:T(8,128)} %get-tuple-element.8.rims_ref, f32[5,16,128]{2,1,0:T(8,128)} %copy-done.2, f32[5,16,128]{2,1,0:T(8,128)} %copy-done.3, f32[19,8,16,128]{3,2,1,0:T(8,128)} %bitcast.3), custom_call_target="tpu_custom_call" | custom-call | tf_op jit(solution)/shard_map/pallas_call | solution.py:334
  44.7 16.9 %all_to_all.10.got_ref = f32[8,176,128]{2,1,0:T(8,128)} all-to-all(f32[8,176,128]{2,1,0:T(8,128)} %shard_map.63), channel_id=1, replica_groups=mesh['gx'=8,'gy'=8,'gz'=2] {'gy'}, dimensions={0} | all-to-all | bytes 1441792 | tf_op jit(solution)/shard_map/all_to_all | solution.py:326
  61.7 2.0 %shard_map.64 = (f32[5,16,128]{2,1,0:T(8,128)}, f32[5,16,128]{2,1,0:T(8,128)}, f32[2,16,128]{2,1,0:T(8,128)}) custom-call(s32[2]{0:T(128)} %shift_ref.3, s32[2]{0:T(128)} %frac_ref.3, f32[8,176,128]{2,1,0:T(8,128)} %all_to_all.10.got_ref), custom_call_target="tpu_custom_call" | custom-call | tf_op jit(solution)/shard_map/pallas_call | solution.py:327
  63.6 4.1 %collective-permute-start.5 = (f32[5,16,128]{2,1,0:T(8,128)}, f32[5,16,128]{2,1,0:T(8,128)S(1)}, u32[]{:S(2)}, u32[]{:S(2)}) collective-permute-start(f32[5,16,128]{2,1,0:T(8,128)} %get-tuple-element.13), channel_id=1, source_target_pairs={{0,112},{16,0},{32,16},{48,32},{64,48},{80,64},{96,80},{112,96},{1... | collective-permute-start | bytes 122888 | tf_op jit(solution)/shard_map/ppermute | solution.py:331
  67.8 3.6 %shard_map.62.relaxed_ref = f32[19,8,16,128]{3,2,1,0:T(8,128)} custom-call(f32[19,8,16,128]{3,2,1,0:T(8,128)} %shard_map.59.relaxed_ref, f32[2,16,128]{2,1,0:T(8,128)} %get-tuple-element.8.rims_ref, f32[5,16,128]{2,1,0:T(8,128)} %copy-done.2, f32[5,16,128]{2,1,0:T(8,128)} %copy-done.3, f32[19,8,16,128]{3,2,1,0:T(8,128)} %bitcast.4), custom_call_target="tpu_custom_call" | custom-call | tf_op jit(solution)/shard_map/pallas_call | solution.py:335
  71.4 0.6 copy-done.4
  72.0 2.9 %shard_map.65 = (f32[19,8,8,128]{3,2,1,0:T(8,128)}, f32[8,8,128]{2,1,0:T(8,128)}) custom-call(f32[19,8,16,128]{3,2,1,0:T(8,128)} %shard_map.62.relaxed_ref, f32[2,16,128]{2,1,0:T(8,128)} %get-tuple-element.11.rims_ref, f32[5,16,128]{2,1,0:T(8,128)} %copy-done.4, f32[5,16,128]{2,1,0:T(8,128)} %copy-done.5, f32[19,8,16,128]{3,2,1,0:T(8,128)} %bitcast.5), custom_call_target="tpu_custom_call" | custom-call | tf_op jit(solution)/shard_map/pallas_call | solution.py:337
  (15 shorter events, 0.1 us)
Async XLA Ops:
  0.6 13.0 %copy-start.6 = (s32[8,8,32]{2,1,0:T(8,128)S(1)}, s32[8,8,32]{2,1,0:T(8,128)}, u32[]{:S(2)}) copy-start(s32[8,8,32]{2,1,0:T(8,128)} %param.7) | copy-start | bytes 24580
  0.6 2.3 %collective-permute-start = (f32[19,8,8,128]{3,2,1,0:T(8,128)}, f32[19,8,8,128]{3,2,1,0:T(8,128)S(1)}, u32[]{:S(2)}, u32[]{:S(2)}) collective-permute-start(f32[19,8,8,128]{3,2,1,0:T(8,128)} %mine_ref.3), channel_id=1, source_target_pairs={{0,1},{1,0},{2,3},{3,2},{4,5},{5,4},{6,7},{7,6},{8,9},{9,8},{10,11... | collective-permute-start | bytes 1867784 | tf_op jit(solution)/shard_map/ppermute | solution.py:307
  3.0 0.8 %copy-start.1 = (f32[19,8,8,128]{3,2,1,0:T(8,128)}, f32[19,8,8,128]{3,2,1,0:T(8,128)S(1)}, u32[]{:S(2)}) copy-start(f32[19,8,8,128]{3,2,1,0:T(8,128)S(1)} %collective-permute-done.other_ref) | copy-start | bytes 1867780
  6.6 21.0 %all-to-all-start = ((f32[8,176,128]{2,1,0:T(8,128)}), f32[8,176,128]{2,1,0:T(8,128)S(1)}, u32[]{:S(2)}, u32[]{:S(2)}) async-start(f32[8,176,128]{2,1,0:T(8,128)} %shard_map.60), calls=%async_computation | async-start | bytes 1441792 | tf_op jit(solution)/shard_map/all_to_all | solution.py:326
  13.7 1.3 %collective-permute-start.3 = (s32[8,8,32]{2,1,0:T(8,128)S(1)}, s32[8,8,32]{2,1,0:T(8,128)S(1)}, u32[]{:S(2)}, u32[]{:S(2)}) collective-permute-start(s32[8,8,32]{2,1,0:T(8,128)S(1)} %copy-done.6), channel_id=1, source_target_pairs={{0,1},{1,0},{2,3},{3,2},{4,5},{5,4},{6,7},{7,6},{8,9},{9,8},{10,11... | collective-permute-start | bytes 24584 | tf_op jit(solution)/shard_map/ppermute | solution.py:308
  27.7 0.9 %copy-start = (f32[8,176,128]{2,1,0:T(8,128)}, f32[8,176,128]{2,1,0:T(8,128)S(1)}, u32[]{:S(2)}) copy-start(f32[8,176,128]{2,1,0:T(8,128)S(1)} %all-to-all-done.got_ref) | copy-start | bytes 2162692
  30.5 9.8 %collective-permute-start.1 = (f32[5,16,128]{2,1,0:T(8,128)}, f32[5,16,128]{2,1,0:T(8,128)S(1)}, u32[]{:S(2)}, u32[]{:S(2)}) collective-permute-start(f32[5,16,128]{2,1,0:T(8,128)} %get-tuple-element.9), channel_id=1, source_target_pairs={{0,16},{16,32},{32,48},{48,64},{64,80},{80,96},{96,112},{112,0},{1... | collective-permute-start | bytes 122888 | tf_op jit(solution)/shard_map/ppermute | solution.py:330
  31.1 9.2 %collective-permute-start.2 = (f32[5,16,128]{2,1,0:T(8,128)}, f32[5,16,128]{2,1,0:T(8,128)S(1)}, u32[]{:S(2)}, u32[]{:S(2)}) collective-permute-start(f32[5,16,128]{2,1,0:T(8,128)} %get-tuple-element.10), channel_id=1, source_target_pairs={{0,112},{16,0},{32,16},{48,32},{64,48},{80,64},{96,80},{112,96},{1... | collective-permute-start | bytes 122888 | tf_op jit(solution)/shard_map/ppermute | solution.py:331
  40.3 0.6 copy-start.2
  40.3 0.6 copy-start.3
  63.6 7.7 %collective-permute-start.4 = (f32[5,16,128]{2,1,0:T(8,128)}, f32[5,16,128]{2,1,0:T(8,128)S(1)}, u32[]{:S(2)}, u32[]{:S(2)}) collective-permute-start(f32[5,16,128]{2,1,0:T(8,128)} %get-tuple-element.12), channel_id=1, source_target_pairs={{0,16},{16,32},{32,48},{48,64},{64,80},{80,96},{96,112},{112,0},{1... | collective-permute-start | bytes 122888 | tf_op jit(solution)/shard_map/ppermute | solution.py:330
  63.6 7.7 %collective-permute-start.5 = (f32[5,16,128]{2,1,0:T(8,128)}, f32[5,16,128]{2,1,0:T(8,128)S(1)}, u32[]{:S(2)}, u32[]{:S(2)}) collective-permute-start(f32[5,16,128]{2,1,0:T(8,128)} %get-tuple-element.13), channel_id=1, source_target_pairs={{0,112},{16,0},{32,16},{48,32},{64,48},{80,64},{96,80},{112,96},{1... | collective-permute-start | bytes 122888 | tf_op jit(solution)/shard_map/ppermute | solution.py:331
  71.4 0.6 copy-start.4
  71.4 0.6 copy-start.5

commit v9 on v8

--- a/solution.py
+++ b/solution.py
@@ -113,7 +113,8 @@
     member = links % 19
     by_member = (member[:, :, None, :] == jnp.arange(19, dtype=jnp.int32)[:, None]).astype(jnp.bfloat16)
     by_cell = (cell_y[:, :, :, None] == jnp.arange(row_span, dtype=jnp.int32)).astype(jnp.bfloat16)
-    return jnp.einsum("xzml,xzly->mxzy", by_member, by_cell, preferred_element_type=jnp.float32)
+    counts = jnp.einsum("xzml,xzly->mxzy", by_member, by_cell, preferred_element_type=jnp.float32)
+    return (counts > 0.5).astype(jnp.bfloat16)
 
 
 LANES = 128
@@ -181,31 +182,45 @@
         chunk_ref[p, FACE_ROWS * depth :] = jnp.where(to_next == p, up_pack, jnp.where(to_prev == p, down_pack, 0.0))
 
 
-def _streamed(x, slab_width, relaxed_ref, rims_ref, low_ref, high_ref, hits_ref, depth):
-    lane = lax.broadcasted_iota(jnp.int32, (depth, LANES), 1)
+def _streamed(x, slab_width, relaxed_ref, rims_ref, low_ref, high_ref, hits_ref, depth, own=None):
+    rows = depth if own is None else depth // 2
+    part = (lambda ref, *idx: ref[idx]) if own is None else (lambda ref, *idx: ref[idx + (pl.ds(own, rows),)])
+    lower = None if own is None else jnp.full((rows, LANES), own, jnp.int32) == 0
+
+    def source(n, full):
+        step_x, step_y, _ = velocity_table[n]
+        get = (lambda ref, *idx: ref[idx]) if full else part
+        width = depth if full else rows
+        lane = lax.broadcasted_iota(jnp.int32, (width, LANES), 1)
+        xs = x - step_x
+        if xs < 0:
+            return get(low_ref, upward.index(n))
+        if xs >= slab_width:
+            return get(high_ref, downward.index(n))
+        t = get(relaxed_ref, n, xs)
+        if step_y == 1:
+            k = y_plus.index(n) * slab_width + xs
+            t = jnp.where(lane == 0, _roll(get(rims_ref, 0), LANES - k, 1), _roll(t, 1, 1))
+        elif step_y == -1:
+            k = y_minus.index(n) * slab_width + xs
+            t = jnp.where(lane == LANES - 1, _roll(get(rims_ref, 1), LANES - 1 - k, 1), _roll(t, LANES - 1, 1))
+        return t
+
     out = []
     for n in range(19):
-        step_x, step_y, step_z = velocity_table[n]
-        xs = x - step_x
-        if xs < 0:
-            t = low_ref[upward.index(n)]
-        elif xs >= slab_width:
-            t = high_ref[downward.index(n)]
-        else:
-            t = relaxed_ref[n, xs]
-            if step_y == 1:
-                k = y_plus.index(n) * slab_width + xs
-                t = jnp.where(lane == 0, _roll(rims_ref[0], LANES - k, 1), _roll(t, 1, 1))
-            elif step_y == -1:
-                k = y_minus.index(n) * slab_width + xs
-                t = jnp.where(lane == LANES - 1, _roll(rims_ref[1], LANES - 1 - k, 1), _roll(t, LANES - 1, 1))
-        if step_z != 0:
-            t = _z_roll(t, step_z)
+        step_z = velocity_table[n][2]
+        if step_z == 0:
+            out.append(source(n, own is None))
+            continue
+        t = _z_roll(source(n, True), step_z)
+        if own is not None:
+            t = jnp.where(lower, t[:rows], t[rows:])
         out.append(t)
     result = [out[0]]
     for n in range(1, 19):
-        source = n - 1 + 2 * (n % 2)
-        result.append(jnp.where(hits_ref[source, x] > 0.5, relaxed_ref[source, x], out[n]))
+        src = n - 1 + 2 * (n % 2)
+        hit = part(hits_ref, src, x).astype(jnp.float32) > 0.5
+        result.append(jnp.where(hit, part(relaxed_ref, src, x), out[n]))
     return result
 
 
@@ -236,9 +251,9 @@
     slab_width, depth = relaxed_ref.shape[1], relaxed_ref.shape[2]
     half = depth // 2
     lower = jnp.full((half, LANES), _positions()[3], jnp.int32) == 0
+    own = pl.multiple_of(_positions()[3] * half, half)
     for x in range(slab_width):
-        cells = _streamed(x, slab_width, relaxed_ref, rims_ref, low_ref, high_ref, hits_ref, depth)
-        mine = [jnp.where(lower, c[:half], c[half:]) for c in cells]
+        mine = _streamed(x, slab_width, relaxed_ref, rims_ref, low_ref, high_ref, hits_ref, depth, own=own)
         for m in range(19):
             out_ref[m, x] = mine[m]
         density_ref[x] = total_density(mine)

time: 75.4 us -> 73.2 us (0.971)
  waiting for transfers between devices: 16.1 us -> 14.7 us
  local copies, waits for them, and re-layouts: 4.21 us -> 2.93 us
  other arithmetic: 0.08 us -> 1.23 us
    all_to_all x1, waiting for transfers between devices: 12.6 us -> 11.3 us  [_per_device(): got = lax.all_to_all(chunks, 'gy', 0, 0, tiled=True)]
    dot_general x1 -> x0, local copies, waits for them, and re-layouts: 1.29 us -> none  [link_hits(): jnp.einsum('xzml,xzly->mxzy', by_member, by_cell, preferred_element_type=...]
    convert_element_type x0 -> x1, other arithmetic: none -> 1.15 us  [link_hits(): return (counts > 0.5).astype(jnp.bfloat16)]
where the time goes in v9:
time: 73.2 us; the launch traced here: 72.8 us
  Pallas kernels  19.4 us (27%)
  blocking collectives  16.9 us (23%)
  starting transfers between devices  15.5 us (21%)
  waiting for transfers between devices  14.7 us (20%)
  local copies, waits for them, and re-layouts  2.93 us (4%)
  matrix products  1.35 us (2%)
  other arithmetic  1.23 us (2%)
    all_to_all x1, blocking collectives, _per_device(): got = lax.all_to_all(chunks, 'gy', 0, 0, tiled=True)  16.9 us
    all_to_all x1, waiting for transfers between devices, _per_device(): got = lax.all_to_all(chunks, 'gy', 0, 0, tiled=True)  11.3 us
    ppermute x2, starting transfers between devices, _per_device(): lax.ppermute(high_send, 'gx', [(i, (i - 1) % slab_cycle) for i in range(s...  7.68 us
    all_to_all x1, starting transfers between devices, _per_device(): got = lax.all_to_all(chunks, 'gy', 0, 0, tiled=True)  7.04 us
    pallas_call x2, Pallas kernels, _per_device(): _call(functools.partial(_window_kernel, section), 2, 1, (ghost, ghost, ri...  3.94 us
    pallas_call x1, Pallas kernels, _per_device(): chunks = _call(_middle_kernel, 0, 5, chunk)(*args)  3.6 us
    pallas_call x1, Pallas kernels, _per_device(): relaxed = _call(_middle_kernel, 0, 5, full)(*args)  3.4 us
    pallas_call x1, Pallas kernels, _per_device(): relaxed = _call(_first_kernel, 0, 2, full)(populations, other_states)  3.02 us
  transfers between devices with their start and end apart: 7, of which 3 were waited for; matrix products, arithmetic and copies ran while one was open for 4% of the time, Pallas kernels for 9%

profile of v9, /device:TPU:0, one launch (start us, length us, event | category | flops | bytes accessed | tf_op | source)
XLA Modules:
  0.0 72.8 jit_solution(18381246765197456504)
XLA Ops:
  0.6 0.1 collective-permute-start
  0.7 2.2 %collective-permute-done.other_ref = f32[19,8,8,128]{3,2,1,0:T(8,128)S(1)} collective-permute-done((f32[19,8,8,128]{3,2,1,0:T(8,128)}, f32[19,8,8,128]{3,2,1,0:T(8,128)S(1)}, u32[]{:S(2)}, u32[]{:S(2)}) %collective-permute-start) | collective-permute-done | bytes 622624 | tf_op jit(solution)/shard_map/ppermute | solution.py:322
  3.0 0.8 %copy-done.1 = f32[19,8,8,128]{3,2,1,0:T(8,128)} copy-done((f32[19,8,8,128]{3,2,1,0:T(8,128)}, f32[19,8,8,128]{3,2,1,0:T(8,128)S(1)}, u32[]{:S(2)}) %copy-start.1) | copy-done | bytes 622616
  3.8 2.8 %shard_map.60 = f32[8,176,128]{2,1,0:T(8,128)} custom-call(f32[19,8,8,128]{3,2,1,0:T(8,128)} %mine_ref.3, f32[19,8,8,128]{3,2,1,0:T(8,128)} %copy-done.1), custom_call_target="tpu_custom_call" | custom-call | tf_op jit(solution)/shard_map/pallas_call | solution.py:338
  6.6 7.0 %all-to-all-start = ((f32[8,176,128]{2,1,0:T(8,128)}), f32[8,176,128]{2,1,0:T(8,128)S(1)}, u32[]{:S(2)}, u32[]{:S(2)}) async-start(f32[8,176,128]{2,1,0:T(8,128)} %shard_map.60), calls=%async_computation | async-start | bytes 1441792 | tf_op jit(solution)/shard_map/all_to_all | solution.py:341
  13.7 0.1 collective-permute-start.3
  13.8 1.2 %collective-permute-done.3 = s32[8,8,32]{2,1,0:T(8,128)S(1)} collective-permute-done((s32[8,8,32]{2,1,0:T(8,128)S(1)}, s32[8,8,32]{2,1,0:T(8,128)S(1)}, u32[]{:S(2)}, u32[]{:S(2)}) %collective-permute-start.3) | collective-permute-done | bytes 8224 | tf_op jit(solution)/shard_map/ppermute | solution.py:323
  15.0 0.1 add_select_fusion
  15.0 1.4 %fusion = f32[8,16,128,19]{2,3,1,0:T(8,128)S(1)} fusion(s32[8,16,32]{2,1,0:T(8,128)S(1)} %get-tuple-element.15, s32[8,16,32]{2,1,0:T(8,128)S(1)} %get-tuple-element.14), kind=kOutput, calls=%fused_computation.1 | convolution fusion | flops 20525056 | bytes 1277952 | tf_op jit(solution)/shard_map/xzml,xzly->mxzy/dot_general | solution.py:116
  16.4 11.3 %all-to-all-done.got_ref = f32[8,176,128]{2,1,0:T(8,128)S(1)} async-done(((f32[8,176,128]{2,1,0:T(8,128)}), f32[8,176,128]{2,1,0:T(8,128)S(1)}, u32[]{:S(2)}, u32[]{:S(2)}) %all-to-all-start) | async-done | bytes 720928 | tf_op jit(solution)/shard_map/all_to_all | solution.py:341
  27.7 0.9 %copy-done = f32[8,176,128]{2,1,0:T(8,128)} copy-done((f32[8,176,128]{2,1,0:T(8,128)}, f32[8,176,128]{2,1,0:T(8,128)S(1)}, u32[]{:S(2)}) %copy-start) | copy-done | bytes 720920
  28.5 2.0 %shard_map.61 = (f32[5,16,128]{2,1,0:T(8,128)}, f32[5,16,128]{2,1,0:T(8,128)}, f32[2,16,128]{2,1,0:T(8,128)}) custom-call(s32[2]{0:T(128)} %shift_ref.3, s32[2]{0:T(128)} %frac_ref.3, f32[8,176,128]{2,1,0:T(8,128)} %copy-done), custom_call_target="tpu_custom_call" | custom-call | tf_op jit(solution)/shard_map/pallas_call | solution.py:342
  30.5 0.6 collective-permute-start.1
  31.1 3.5 %collective-permute-start.2 = (f32[5,16,128]{2,1,0:T(8,128)}, f32[5,16,128]{2,1,0:T(8,128)S(1)}, u32[]{:S(2)}, u32[]{:S(2)}) collective-permute-start(f32[5,16,128]{2,1,0:T(8,128)} %get-tuple-element.10), channel_id=1, source_target_pairs={{0,112},{16,0},{32,16},{48,32},{64,48},{80,64},{96,80},{112,96},{1... | collective-permute-start | bytes 122888 | tf_op jit(solution)/shard_map/ppermute | solution.py:346
  34.6 1.1 %fusion.4.hits_ref = bf16[19,8,16,128]{3,2,1,0:T(8,128)(2,1)} fusion(f32[8,16,128,19]{2,3,1,0:T(8,128)S(1)} %fusion), kind=kLoop, calls=%fused_computation.7 | loop fusion | flops 622592 | bytes 1867776 | tf_op jit(solution)/shard_map/convert_element_type | solution.py:117
  35.8 3.0 %shard_map.59.relaxed_ref = f32[19,8,16,128]{3,2,1,0:T(8,128)} custom-call(f32[19,8,8,128]{3,2,1,0:T(8,128)} %mine_ref.3, f32[19,8,8,128]{3,2,1,0:T(8,128)} %copy-done.1), custom_call_target="tpu_custom_call" | custom-call | tf_op jit(solution)/shard_map/pallas_call | solution.py:339
  38.8 0.6 copy-done.2
  39.4 3.6 %shard_map.63 = f32[8,176,128]{2,1,0:T(8,128)} custom-call(f32[19,8,16,128]{3,2,1,0:T(8,128)} %shard_map.59.relaxed_ref, f32[2,16,128]{2,1,0:T(8,128)} %get-tuple-element.8.rims_ref, f32[5,16,128]{2,1,0:T(8,128)} %copy-done.2, f32[5,16,128]{2,1,0:T(8,128)} %copy-done.3, bf16[19,8,16,128]{3,2,1,0:T(8,128)(2,1)} %fusion.4.hits_ref), custom_call_target="tpu_custom_call" | custom-call | tf_op jit(solution)/shard_map/pallas_call | solution.py:349
  43.0 16.9 %all_to_all.10.got_ref = f32[8,176,128]{2,1,0:T(8,128)} all-to-all(f32[8,176,128]{2,1,0:T(8,128)} %shard_map.63), channel_id=1, replica_groups=mesh['gx'=8,'gy'=8,'gz'=2] {'gy'}, dimensions={0} | all-to-all | bytes 1441792 | tf_op jit(solution)/shard_map/all_to_all | solution.py:341
  60.0 2.0 %shard_map.64 = (f32[5,16,128]{2,1,0:T(8,128)}, f32[5,16,128]{2,1,0:T(8,128)}, f32[2,16,128]{2,1,0:T(8,128)}) custom-call(s32[2]{0:T(128)} %shift_ref.3, s32[2]{0:T(128)} %frac_ref.3, f32[8,176,128]{2,1,0:T(8,128)} %all_to_all.10.got_ref), custom_call_target="tpu_custom_call" | custom-call | tf_op jit(solution)/shard_map/pallas_call | solution.py:342
  62.0 4.1 %collective-permute-start.5 = (f32[5,16,128]{2,1,0:T(8,128)}, f32[5,16,128]{2,1,0:T(8,128)S(1)}, u32[]{:S(2)}, u32[]{:S(2)}) collective-permute-start(f32[5,16,128]{2,1,0:T(8,128)} %get-tuple-element.13), channel_id=1, source_target_pairs={{0,112},{16,0},{32,16},{48,32},{64,48},{80,64},{96,80},{112,96},{1... | collective-permute-start | bytes 122888 | tf_op jit(solution)/shard_map/ppermute | solution.py:346
  66.1 3.4 %shard_map.62.relaxed_ref = f32[19,8,16,128]{3,2,1,0:T(8,128)} custom-call(f32[19,8,16,128]{3,2,1,0:T(8,128)} %shard_map.59.relaxed_ref, f32[2,16,128]{2,1,0:T(8,128)} %get-tuple-element.8.rims_ref, f32[5,16,128]{2,1,0:T(8,128)} %copy-done.2, f32[5,16,128]{2,1,0:T(8,128)} %copy-done.3, bf16[19,8,16,128]{3,2,1,0:T(8,128)(2,1)} %fusion.4.hits_ref), custom_call_target="tpu_custom_call" | custom-call | tf_op jit(solution)/shard_map/pallas_call | solution.py:350
  69.5 0.6 copy-done.4
  70.1 2.6 %shard_map.65 = (f32[19,8,8,128]{3,2,1,0:T(8,128)}, f32[8,8,128]{2,1,0:T(8,128)}) custom-call(f32[19,8,16,128]{3,2,1,0:T(8,128)} %shard_map.62.relaxed_ref, f32[2,16,128]{2,1,0:T(8,128)} %get-tuple-element.11.rims_ref, f32[5,16,128]{2,1,0:T(8,128)} %copy-done.4, f32[5,16,128]{2,1,0:T(8,128)} %copy-done.5, bf16[19,8,16,128]{3,2,1,0:T(8,128)(2,1)} %fusion.4.hits_ref), custom_call_target="tpu_custom_call" | custom-call | tf_op jit(solution)/shard_map/pallas_call | solution.py:352
  (15 shorter events, 0.0 us)
Async XLA Ops:
  0.6 13.0 %copy-start.6 = (s32[8,8,32]{2,1,0:T(8,128)S(1)}, s32[8,8,32]{2,1,0:T(8,128)}, u32[]{:S(2)}) copy-start(s32[8,8,32]{2,1,0:T(8,128)} %param.7) | copy-start | bytes 24580
  0.6 2.3 %collective-permute-start = (f32[19,8,8,128]{3,2,1,0:T(8,128)}, f32[19,8,8,128]{3,2,1,0:T(8,128)S(1)}, u32[]{:S(2)}, u32[]{:S(2)}) collective-permute-start(f32[19,8,8,128]{3,2,1,0:T(8,128)} %mine_ref.3), channel_id=1, source_target_pairs={{0,1},{1,0},{2,3},{3,2},{4,5},{5,4},{6,7},{7,6},{8,9},{9,8},{10,11... | collective-permute-start | bytes 1867784 | tf_op jit(solution)/shard_map/ppermute | solution.py:322
  3.0 0.8 %copy-start.1 = (f32[19,8,8,128]{3,2,1,0:T(8,128)}, f32[19,8,8,128]{3,2,1,0:T(8,128)S(1)}, u32[]{:S(2)}) copy-start(f32[19,8,8,128]{3,2,1,0:T(8,128)S(1)} %collective-permute-done.other_ref) | copy-start | bytes 1867780
  6.6 21.0 %all-to-all-start = ((f32[8,176,128]{2,1,0:T(8,128)}), f32[8,176,128]{2,1,0:T(8,128)S(1)}, u32[]{:S(2)}, u32[]{:S(2)}) async-start(f32[8,176,128]{2,1,0:T(8,128)} %shard_map.60), calls=%async_computation | async-start | bytes 1441792 | tf_op jit(solution)/shard_map/all_to_all | solution.py:341
  13.7 1.3 %collective-permute-start.3 = (s32[8,8,32]{2,1,0:T(8,128)S(1)}, s32[8,8,32]{2,1,0:T(8,128)S(1)}, u32[]{:S(2)}, u32[]{:S(2)}) collective-permute-start(s32[8,8,32]{2,1,0:T(8,128)S(1)} %copy-done.6), channel_id=1, source_target_pairs={{0,1},{1,0},{2,3},{3,2},{4,5},{5,4},{6,7},{7,6},{8,9},{9,8},{10,11... | collective-permute-start | bytes 24584 | tf_op jit(solution)/shard_map/ppermute | solution.py:323
  27.7 0.9 %copy-start = (f32[8,176,128]{2,1,0:T(8,128)}, f32[8,176,128]{2,1,0:T(8,128)S(1)}, u32[]{:S(2)}) copy-start(f32[8,176,128]{2,1,0:T(8,128)S(1)} %all-to-all-done.got_ref) | copy-start | bytes 2162692
  30.5 8.3 %collective-permute-start.1 = (f32[5,16,128]{2,1,0:T(8,128)}, f32[5,16,128]{2,1,0:T(8,128)S(1)}, u32[]{:S(2)}, u32[]{:S(2)}) collective-permute-start(f32[5,16,128]{2,1,0:T(8,128)} %get-tuple-element.9), channel_id=1, source_target_pairs={{0,16},{16,32},{32,48},{48,64},{64,80},{80,96},{96,112},{112,0},{1... | collective-permute-start | bytes 122888 | tf_op jit(solution)/shard_map/ppermute | solution.py:345
  31.1 7.7 %collective-permute-start.2 = (f32[5,16,128]{2,1,0:T(8,128)}, f32[5,16,128]{2,1,0:T(8,128)S(1)}, u32[]{:S(2)}, u32[]{:S(2)}) collective-permute-start(f32[5,16,128]{2,1,0:T(8,128)} %get-tuple-element.10), channel_id=1, source_target_pairs={{0,112},{16,0},{32,16},{48,32},{64,48},{80,64},{96,80},{112,96},{1... | collective-permute-start | bytes 122888 | tf_op jit(solution)/shard_map/ppermute | solution.py:346
  38.8 0.6 copy-start.2
  38.8 0.6 copy-start.3
  62.0 7.5 %collective-permute-start.4 = (f32[5,16,128]{2,1,0:T(8,128)}, f32[5,16,128]{2,1,0:T(8,128)S(1)}, u32[]{:S(2)}, u32[]{:S(2)}) collective-permute-start(f32[5,16,128]{2,1,0:T(8,128)} %get-tuple-element.12), channel_id=1, source_target_pairs={{0,16},{16,32},{32,48},{48,64},{64,80},{80,96},{96,112},{112,0},{1... | collective-permute-start | bytes 122888 | tf_op jit(solution)/shard_map/ppermute | solution.py:345
  62.0 7.5 %collective-permute-start.5 = (f32[5,16,128]{2,1,0:T(8,128)}, f32[5,16,128]{2,1,0:T(8,128)S(1)}, u32[]{:S(2)}, u32[]{:S(2)}) collective-permute-start(f32[5,16,128]{2,1,0:T(8,128)} %get-tuple-element.13), channel_id=1, source_target_pairs={{0,112},{16,0},{32,16},{48,32},{64,48},{80,64},{96,80},{112,96},{1... | collective-permute-start | bytes 122888 | tf_op jit(solution)/shard_map/ppermute | solution.py:346
  69.5 0.6 copy-start.4
  69.5 0.6 copy-start.5

commit v10 on v9

--- a/solution.py
+++ b/solution.py
@@ -172,14 +172,17 @@
             down_pack = jnp.where(lane == k, _roll(r[m], k, 1), down_pack)
     if chunk_ref is None:
         return
-    faces = jnp.concatenate([top.reshape(5 * depth, LANES), bottom.reshape(5 * depth, LANES)], axis=0)
-    _, after, before, _ = _positions()
-    to_next = jnp.full((depth, LANES), after, jnp.int32)
-    to_prev = jnp.full((depth, LANES), before, jnp.int32)
+    half = depth // 2
     peers = chunk_ref.shape[0]
-    for p in range(peers):
-        chunk_ref[p, : FACE_ROWS * depth] = faces
-        chunk_ref[p, FACE_ROWS * depth :] = jnp.where(to_next == p, up_pack, jnp.where(to_prev == p, down_pack, 0.0))
+    for h in range(2):
+        rows = slice(h * half, (h + 1) * half)
+        faces = jnp.concatenate(
+            [top[:, rows].reshape(5 * half, LANES), bottom[:, rows].reshape(5 * half, LANES)], axis=0
+        )
+        for p in range(peers):
+            chunk_ref[p, h, : FACE_ROWS * half] = faces
+            chunk_ref[p, h, FACE_ROWS * half : (FACE_ROWS + 1) * half] = up_pack[rows]
+            chunk_ref[p, h, (FACE_ROWS + 1) * half :] = down_pack[rows]
 
 
 def _streamed(x, slab_width, relaxed_ref, rims_ref, low_ref, high_ref, hits_ref, depth, own=None):
@@ -240,6 +243,27 @@
     _emit_relax(cells, slab_width, relaxed_ref, chunk_ref, depth)
 
 
+def _half_kernel(mine_ref, half_ref):
+    slab_width, half = mine_ref.shape[1], mine_ref.shape[2]
+    lane = lax.broadcasted_iota(jnp.int32, (half, LANES), 1)
+    up_pack = jnp.zeros((half, LANES), jnp.float32)
+    down_pack = jnp.zeros((half, LANES), jnp.float32)
+    for x in range(slab_width):
+        r = relax([mine_ref[m, x] for m in range(19)])
+        if x == slab_width - 1:
+            half_ref[: 5 * half] = corrected(r, upward, -1.0).reshape(5 * half, LANES)
+        if x == 0:
+            half_ref[5 * half : FACE_ROWS * half] = corrected(r, downward, 1.0).reshape(5 * half, LANES)
+        for i, m in enumerate(y_plus):
+            k = i * slab_width + x
+            up_pack = jnp.where(lane == k, _roll(r[m], k + 1, 1), up_pack)
+        for i, m in enumerate(y_minus):
+            k = i * slab_width + x
+            down_pack = jnp.where(lane == k, _roll(r[m], k, 1), down_pack)
+    half_ref[FACE_ROWS * half : (FACE_ROWS + 1) * half] = up_pack
+    half_ref[(FACE_ROWS + 1) * half :] = down_pack
+
+
 def _middle_kernel(relaxed_ref, rims_ref, low_ref, high_ref, hits_ref, *outs):
     next_ref, chunk_ref = (outs[0], None) if outs[0].shape[0] == 19 else (None, outs[0])
     slab_width, depth = relaxed_ref.shape[1], relaxed_ref.shape[2]
@@ -260,8 +284,13 @@
 
 
 def _window_kernel(section, shift_ref, frac_ref, got_ref, low_ref, high_ref, rims_ref):
-    peers, _, lanes = got_ref.shape
+    peers, _, _, lanes = got_ref.shape
     depth = low_ref.shape[1]
+    half = depth // 2
+
+    def tile(block, row0):
+        return jnp.concatenate([got_ref[block, 0, pl.ds(row0, half), :], got_ref[block, 1, pl.ds(row0, half), :]], axis=0)
+
     me_y, after, before, _ = _positions()
     offset = shift_ref[section]
     fraction = jnp.full((depth, lanes), frac_ref[section], jnp.int32).astype(jnp.float32) / 256.0
@@ -276,22 +305,22 @@
         off = start % lanes
         after = (block + 1) % peers
         shift = (lanes - off) % lanes
-        first = pltpu.roll(got_ref[block, pl.ds(row0, depth), :], shift, 1)
-        second = pltpu.roll(got_ref[after, pl.ds(row0, depth), :], shift, 1)
+        first = pltpu.roll(tile(block, row0), shift, 1)
+        second = pltpu.roll(tile(after, row0), shift, 1)
         return jnp.where(lane < lanes - off, first, second)
 
     for i, m in enumerate(upward):
         step_y = velocity_table[m][1]
-        row0 = i * depth
+        row0 = i * half
         a = anchor - offset - step_y
         low_ref[i] = keep * window(row0, a) + fraction * window(row0, a - 1)
     for i, m in enumerate(downward):
         step_y = velocity_table[m][1]
-        row0 = (5 + i) * depth
+        row0 = (5 + i) * half
         c = anchor + offset - step_y
         high_ref[i] = fraction * window(row0, c + 1) + keep * window(row0, c)
-    rims_ref[0] = got_ref[before, pl.ds(FACE_ROWS * depth, depth), :]
-    rims_ref[1] = got_ref[after, pl.ds(FACE_ROWS * depth, depth), :]
+    rims_ref[0] = tile(before, FACE_ROWS * half)
+    rims_ref[1] = tile(after, (FACE_ROWS + 1) * half)
 
 
 def _vmem():
@@ -329,13 +358,17 @@
 
     f32 = jnp.float32
     full = jax.ShapeDtypeStruct((n_members, slab_width, depth, row_span), f32)
-    chunk = jax.ShapeDtypeStruct((flow_cycle, (FACE_ROWS + 1) * depth, row_span), f32)
+    chunk = jax.ShapeDtypeStruct((flow_cycle, 2, (FACE_ROWS + 2) * half_depth, row_span), f32)
     ghost = jax.ShapeDtypeStruct((5, depth, row_span), f32)
     rims = jax.ShapeDtypeStruct((2, depth, row_span), f32)
     own = jax.ShapeDtypeStruct((n_members, slab_width, half_depth, row_span), f32)
     density = jax.ShapeDtypeStruct((slab_width, half_depth, row_span), f32)
 
-    chunks = _call(_first_kernel, 0, 2, chunk)(populations, other_states)
+    half_rows = (FACE_ROWS + 2) * half_depth
+    mine_half = _call(_half_kernel, 0, 1, jax.ShapeDtypeStruct((half_rows, row_span), f32))(populations)
+    other_half = lax.ppermute(mine_half, "gz", [(0, 1), (1, 0)])
+    both = jnp.where(me_z == 0, jnp.stack([mine_half, other_half]), jnp.stack([other_half, mine_half]))
+    chunks = jnp.broadcast_to(both[None], (flow_cycle,) + both.shape)
     relaxed = _call(_first_kernel, 0, 2, full)(populations, other_states)
     for section in range(STEPS):
         got = lax.all_to_all(chunks, "gy", 0, 0, tiled=True)

time: 73.2 us -> 74.3 us (1.015)
  other arithmetic: 1.23 us -> 2.11 us
  blocking collectives: 16.9 us -> 17.7 us
    ppermute x1, waiting for transfers between devices: 2.25 us -> 0.01 us  [_per_device(): other_states = lax.ppermute(populations, 'gz', [(0, 1), (1, 0)])]
    ppermute x0 -> x1, waiting for transfers between devices: none -> 1.44 us  [_per_device(): other_half = lax.ppermute(mine_half, 'gz', [(0, 1), (1, 0)])]
    broadcast_in_dim x0 -> x1, local copies, waits for them, and re-layouts: none -> 0.97 us  [_per_device(): chunks = jnp.broadcast_to(both[None], (flow_cycle,) + both.shape)]
    select_n x0 -> x1, other arithmetic: none -> 0.88 us  [_per_device(): jnp.where(me_z == 0, jnp.stack([mine_half, other_half]), jnp.stack([other...]
    unnamed x14, local copies, waits for them, and re-layouts: 2.93 us -> 2.13 us
  transfers between devices with their start and end apart: 7 -> 8, of which waited for: 3 -> 3; matrix products, arithmetic and copies ran while one was open for 4% -> 4% of each run, Pallas kernels for 9% -> 11%
where the time goes in v10:
time: 74.3 us; the launch traced here: 73.8 us
  Pallas kernels  18.8 us (25%)
  blocking collectives  17.7 us (24%)
  starting transfers between devices  15.9 us (21%)
  waiting for transfers between devices  14.1 us (19%)
  local copies, waits for them, and re-layouts  3.1 us (4%)
  other arithmetic  2.11 us (3%)
  matrix products  1.35 us (2%)
    all_to_all x1, blocking collectives, _per_device(): got = lax.all_to_all(chunks, 'gy', 0, 0, tiled=True)  17.7 us
    all_to_all x1, waiting for transfers between devices, _per_device(): got = lax.all_to_all(chunks, 'gy', 0, 0, tiled=True)  12 us
    ppermute x2, starting transfers between devices, _per_device(): lax.ppermute(high_send, 'gx', [(i, (i - 1) % slab_cycle) for i in range(s...  7.68 us
    all_to_all x1, starting transfers between devices, _per_device(): got = lax.all_to_all(chunks, 'gy', 0, 0, tiled=True)  7.04 us
    pallas_call x2, Pallas kernels, _per_device(): _call(functools.partial(_window_kernel, section), 2, 1, (ghost, ghost, ri...  3.99 us
    pallas_call x1, Pallas kernels, _per_device(): chunks = _call(_middle_kernel, 0, 5, chunk)(*args)  3.65 us
    pallas_call x1, Pallas kernels, _per_device(): relaxed = _call(_middle_kernel, 0, 5, full)(*args)  3.41 us
    pallas_call x1, Pallas kernels, _per_device(): relaxed = _call(_first_kernel, 0, 2, full)(populations, other_states)  3.02 us
  transfers between devices with their start and end apart: 8, of which 3 were waited for; matrix products, arithmetic and copies ran while one was open for 4% of the time, Pallas kernels for 11%

profile of v10, /device:TPU:0, one launch (start us, length us, event | category | flops | bytes accessed | tf_op | source)
XLA Modules:
  0.0 73.8 jit_solution(7515389277907111951)
XLA Ops:
  0.7 2.1 %shard_map.60 = f32[96,128]{1,0:T(8,128)} custom-call(f32[19,8,8,128]{3,2,1,0:T(8,128)} %mine_ref.3), custom_call_target="tpu_custom_call" | custom-call | tf_op jit(solution)/shard_map/pallas_call | solution.py:368
  2.7 1.4 %collective-permute-done.1 = f32[96,128]{1,0:T(8,128)S(1)} collective-permute-done((f32[96,128]{1,0:T(8,128)}, f32[96,128]{1,0:T(8,128)S(1)}, u32[]{:S(2)}, u32[]{:S(2)}) %collective-permute-start.1) | collective-permute-done | bytes 49184 | tf_op jit(solution)/shard_map/ppermute | solution.py:369
  4.2 0.9 %maximum_select_fusion = f32[2,96,128]{2,1,0:T(8,128)S(1)} fusion(f32[1,96,128]{2,1,0:T(8,128)S(1)} %bitcast.5, f32[1,96,128]{2,1,0:T(8,128)} %bitcast.4, pred[]{:T(512)S(6)} %eq.16), kind=kLoop, calls=%fused_computation.8 | loop fusion | flops 73728 | bytes 196609 | tf_op jit(solution)/shard_map/jit(_where)/select_n | solution.py:370
  5.1 1.0 %broadcast_in_dim.2 = f32[8,2,96,128]{3,2,1,0:T(8,128)} broadcast(f32[2,96,128]{2,1,0:T(8,128)S(1)} %maximum_select_fusion), dimensions={1,2,3} | broadcast | bytes 884736 | tf_op jit(solution)/shard_map/broadcast_in_dim | solution.py:371
  6.0 7.0 %all-to-all-start = ((f32[8,2,96,128]{3,2,1,0:T(8,128)}), f32[8,2,96,128]{3,2,1,0:T(8,128)S(1)}, u32[]{:S(2)}, u32[]{:S(2)}) async-start(f32[8,2,96,128]{3,2,1,0:T(8,128)} %broadcast_in_dim.2), calls=%async_computation | async-start | bytes 1572864 | tf_op jit(solution)/shard_map/all_to_all | solution.py:374
  13.1 0.1 collective-permute-start.4
  13.2 0.5 collective-permute-start
  13.7 0.7 collective-permute-done.4
  14.5 1.4 %fusion = f32[8,16,128,19]{2,3,1,0:T(8,128)S(1)} fusion(s32[8,16,32]{2,1,0:T(8,128)S(1)} %get-tuple-element.15, s32[8,16,32]{2,1,0:T(8,128)S(1)} %get-tuple-element.14), kind=kOutput, calls=%fused_computation.1 | convolution fusion | flops 20525056 | bytes 1277952 | tf_op jit(solution)/shard_map/xzml,xzly->mxzy/dot_general | solution.py:116
  15.8 12.0 %all-to-all-done.got_ref = f32[8,2,96,128]{3,2,1,0:T(8,128)S(1)} async-done(((f32[8,2,96,128]{3,2,1,0:T(8,128)}), f32[8,2,96,128]{3,2,1,0:T(8,128)S(1)}, u32[]{:S(2)}, u32[]{:S(2)}) %all-to-all-start) | async-done | bytes 786464 | tf_op jit(solution)/shard_map/all_to_all | solution.py:374
  27.8 0.9 %copy-done = f32[8,2,96,128]{3,2,1,0:T(8,128)} copy-done((f32[8,2,96,128]{3,2,1,0:T(8,128)}, f32[8,2,96,128]{3,2,1,0:T(8,128)S(1)}, u32[]{:S(2)}) %copy-start) | copy-done | bytes 786456
  28.7 2.0 %shard_map.61 = (f32[5,16,128]{2,1,0:T(8,128)}, f32[5,16,128]{2,1,0:T(8,128)}, f32[2,16,128]{2,1,0:T(8,128)}) custom-call(s32[2]{0:T(128)} %shift_ref.3, s32[2]{0:T(128)} %frac_ref.3, f32[8,2,96,128]{3,2,1,0:T(8,128)} %copy-done), custom_call_target="tpu_custom_call" | custom-call | tf_op jit(solution)/shard_map/pallas_call | solution.py:375
  30.7 0.6 collective-permute-start.2
  31.3 3.5 %collective-permute-start.3 = (f32[5,16,128]{2,1,0:T(8,128)}, f32[5,16,128]{2,1,0:T(8,128)S(1)}, u32[]{:S(2)}, u32[]{:S(2)}) collective-permute-start(f32[5,16,128]{2,1,0:T(8,128)} %get-tuple-element.10), channel_id=1, source_target_pairs={{0,112},{16,0},{32,16},{48,32},{64,48},{80,64},{96,80},{112,96},{1... | collective-permute-start | bytes 122888 | tf_op jit(solution)/shard_map/ppermute | solution.py:379
  34.8 1.1 %fusion.4.hits_ref = bf16[19,8,16,128]{3,2,1,0:T(8,128)(2,1)} fusion(f32[8,16,128,19]{2,3,1,0:T(8,128)S(1)} %fusion), kind=kLoop, calls=%fused_computation.7 | loop fusion | flops 622592 | bytes 1867776 | tf_op jit(solution)/shard_map/convert_element_type | solution.py:117
  36.0 3.0 %shard_map.59.relaxed_ref = f32[19,8,16,128]{3,2,1,0:T(8,128)} custom-call(f32[19,8,8,128]{3,2,1,0:T(8,128)} %mine_ref.3, f32[19,8,8,128]{3,2,1,0:T(8,128)} %collective-permute-done.other_ref), custom_call_target="tpu_custom_call" | custom-call | tf_op jit(solution)/shard_map/pallas_call | solution.py:372
  39.0 0.6 copy-done.2
  39.6 3.7 %shard_map.63 = f32[8,2,96,128]{3,2,1,0:T(8,128)} custom-call(f32[19,8,16,128]{3,2,1,0:T(8,128)} %shard_map.59.relaxed_ref, f32[2,16,128]{2,1,0:T(8,128)} %get-tuple-element.8.rims_ref, f32[5,16,128]{2,1,0:T(8,128)} %copy-done.2, f32[5,16,128]{2,1,0:T(8,128)} %copy-done.3, bf16[19,8,16,128]{3,2,1,0:T(8,128)(2,1)} %fusion.4.hits_ref), custom_call_target="tpu_custom_call" | custom-call | tf_op jit(solution)/shard_map/pallas_call | solution.py:382
  43.3 17.7 %all_to_all.10.got_ref = f32[8,2,96,128]{3,2,1,0:T(8,128)} all-to-all(f32[8,2,96,128]{3,2,1,0:T(8,128)} %shard_map.63), channel_id=1, replica_groups=mesh['gx'=8,'gy'=8,'gz'=2] {'gy'}, dimensions={0} | all-to-all | bytes 1572864 | tf_op jit(solution)/shard_map/all_to_all | solution.py:374
  60.9 2.0 %shard_map.64 = (f32[5,16,128]{2,1,0:T(8,128)}, f32[5,16,128]{2,1,0:T(8,128)}, f32[2,16,128]{2,1,0:T(8,128)}) custom-call(s32[2]{0:T(128)} %shift_ref.3, s32[2]{0:T(128)} %frac_ref.3, f32[8,2,96,128]{3,2,1,0:T(8,128)} %all_to_all.10.got_ref), custom_call_target="tpu_custom_call" | custom-call | tf_op jit(solution)/shard_map/pallas_call | solution.py:375
  62.9 4.1 %collective-permute-start.6 = (f32[5,16,128]{2,1,0:T(8,128)}, f32[5,16,128]{2,1,0:T(8,128)S(1)}, u32[]{:S(2)}, u32[]{:S(2)}) collective-permute-start(f32[5,16,128]{2,1,0:T(8,128)} %get-tuple-element.13), channel_id=1, source_target_pairs={{0,112},{16,0},{32,16},{48,32},{64,48},{80,64},{96,80},{112,96},{1... | collective-permute-start | bytes 122888 | tf_op jit(solution)/shard_map/ppermute | solution.py:379
  67.1 3.4 %shard_map.62.relaxed_ref = f32[19,8,16,128]{3,2,1,0:T(8,128)} custom-call(f32[19,8,16,128]{3,2,1,0:T(8,128)} %shard_map.59.relaxed_ref, f32[2,16,128]{2,1,0:T(8,128)} %get-tuple-element.8.rims_ref, f32[5,16,128]{2,1,0:T(8,128)} %copy-done.2, f32[5,16,128]{2,1,0:T(8,128)} %copy-done.3, bf16[19,8,16,128]{3,2,1,0:T(8,128)(2,1)} %fusion.4.hits_ref), custom_call_target="tpu_custom_call" | custom-call | tf_op jit(solution)/shard_map/pallas_call | solution.py:383
  70.5 0.6 copy-done.4
  71.1 2.6 %shard_map.65 = (f32[19,8,8,128]{3,2,1,0:T(8,128)}, f32[8,8,128]{2,1,0:T(8,128)}) custom-call(f32[19,8,16,128]{3,2,1,0:T(8,128)} %shard_map.62.relaxed_ref, f32[2,16,128]{2,1,0:T(8,128)} %get-tuple-element.11.rims_ref, f32[5,16,128]{2,1,0:T(8,128)} %copy-done.4, f32[5,16,128]{2,1,0:T(8,128)} %copy-done.5, bf16[19,8,16,128]{3,2,1,0:T(8,128)(2,1)} %fusion.4.hits_ref), custom_call_target="tpu_custom_call" | custom-call | tf_op jit(solution)/shard_map/pallas_call | solution.py:385
  (19 shorter events, 0.1 us)
Async XLA Ops:
  0.6 12.6 %copy-start.1 = (f32[19,8,8,128]{3,2,1,0:T(8,128)S(1)}, f32[19,8,8,128]{3,2,1,0:T(8,128)}, u32[]{:S(2)}) copy-start(f32[19,8,8,128]{3,2,1,0:T(8,128)} %mine_ref.3) | copy-start | bytes 1867780
  0.6 12.4 %copy-start.6 = (s32[8,8,32]{2,1,0:T(8,128)S(1)}, s32[8,8,32]{2,1,0:T(8,128)}, u32[]{:S(2)}) copy-start(s32[8,8,32]{2,1,0:T(8,128)} %param.7) | copy-start | bytes 24580
  2.7 1.4 %collective-permute-start.1 = (f32[96,128]{1,0:T(8,128)}, f32[96,128]{1,0:T(8,128)S(1)}, u32[]{:S(2)}, u32[]{:S(2)}) collective-permute-start(f32[96,128]{1,0:T(8,128)} %shard_map.60), channel_id=1, source_target_pairs={{0,1},{1,0},{2,3},{3,2},{4,5},{5,4},{6,7},{7,6},{8,9},{9,8},{10,11... | collective-permute-start | bytes 147464 | tf_op jit(solution)/shard_map/ppermute | solution.py:369
  6.0 21.8 %all-to-all-start = ((f32[8,2,96,128]{3,2,1,0:T(8,128)}), f32[8,2,96,128]{3,2,1,0:T(8,128)S(1)}, u32[]{:S(2)}, u32[]{:S(2)}) async-start(f32[8,2,96,128]{3,2,1,0:T(8,128)} %broadcast_in_dim.2), calls=%async_computation | async-start | bytes 1572864 | tf_op jit(solution)/shard_map/all_to_all | solution.py:374
  13.1 1.3 %collective-permute-start.4 = (s32[8,8,32]{2,1,0:T(8,128)S(1)}, s32[8,8,32]{2,1,0:T(8,128)S(1)}, u32[]{:S(2)}, u32[]{:S(2)}) collective-permute-start(s32[8,8,32]{2,1,0:T(8,128)S(1)} %copy-done.6), channel_id=1, source_target_pairs={{0,1},{1,0},{2,3},{3,2},{4,5},{5,4},{6,7},{7,6},{8,9},{9,8},{10,11... | collective-permute-start | bytes 24584 | tf_op jit(solution)/shard_map/ppermute | solution.py:352
  13.2 22.8 %collective-permute-start = (f32[19,8,8,128]{3,2,1,0:T(8,128)S(1)}, f32[19,8,8,128]{3,2,1,0:T(8,128)}, u32[]{:S(2)}, u32[]{:S(2)}) collective-permute-start(f32[19,8,8,128]{3,2,1,0:T(8,128)S(1)} %copy-done.1), channel_id=1, source_target_pairs={{0,1},{1,0},{2,3},{3,2},{4,5},{5,4},{6,7},{7,6},{8,9},{9,8},{10,11... | collective-permute-start | bytes 1867784 | tf_op jit(solution)/shard_map/ppermute | solution.py:351
  27.8 0.9 %copy-start = (f32[8,2,96,128]{3,2,1,0:T(8,128)}, f32[8,2,96,128]{3,2,1,0:T(8,128)S(1)}, u32[]{:S(2)}) copy-start(f32[8,2,96,128]{3,2,1,0:T(8,128)S(1)} %all-to-all-done.got_ref) | copy-start | bytes 2359300
  30.7 8.3 %collective-permute-start.2 = (f32[5,16,128]{2,1,0:T(8,128)}, f32[5,16,128]{2,1,0:T(8,128)S(1)}, u32[]{:S(2)}, u32[]{:S(2)}) collective-permute-start(f32[5,16,128]{2,1,0:T(8,128)} %get-tuple-element.9), channel_id=1, source_target_pairs={{0,16},{16,32},{32,48},{48,64},{64,80},{80,96},{96,112},{112,0},{1... | collective-permute-start | bytes 122888 | tf_op jit(solution)/shard_map/ppermute | solution.py:378
  31.3 7.7 %collective-permute-start.3 = (f32[5,16,128]{2,1,0:T(8,128)}, f32[5,16,128]{2,1,0:T(8,128)S(1)}, u32[]{:S(2)}, u32[]{:S(2)}) collective-permute-start(f32[5,16,128]{2,1,0:T(8,128)} %get-tuple-element.10), channel_id=1, source_target_pairs={{0,112},{16,0},{32,16},{48,32},{64,48},{80,64},{96,80},{112,96},{1... | collective-permute-start | bytes 122888 | tf_op jit(solution)/shard_map/ppermute | solution.py:379
  39.0 0.6 copy-start.2
  39.0 0.6 copy-start.3
  62.9 7.6 %collective-permute-start.5 = (f32[5,16,128]{2,1,0:T(8,128)}, f32[5,16,128]{2,1,0:T(8,128)S(1)}, u32[]{:S(2)}, u32[]{:S(2)}) collective-permute-start(f32[5,16,128]{2,1,0:T(8,128)} %get-tuple-element.12), channel_id=1, source_target_pairs={{0,16},{16,32},{32,48},{48,64},{64,80},{80,96},{96,112},{112,0},{1... | collective-permute-start | bytes 122888 | tf_op jit(solution)/shard_map/ppermute | solution.py:378
  62.9 7.6 %collective-permute-start.6 = (f32[5,16,128]{2,1,0:T(8,128)}, f32[5,16,128]{2,1,0:T(8,128)S(1)}, u32[]{:S(2)}, u32[]{:S(2)}) collective-permute-start(f32[5,16,128]{2,1,0:T(8,128)} %get-tuple-element.13), channel_id=1, source_target_pairs={{0,112},{16,0},{32,16},{48,32},{64,48},{80,64},{96,80},{112,96},{1... | collective-permute-start | bytes 122888 | tf_op jit(solution)/shard_map/ppermute | solution.py:379
  70.5 0.6 copy-start.4
  70.5 0.6 copy-start.5

commit v11 on v9

--- a/solution.py
+++ b/solution.py
@@ -148,17 +148,21 @@
     return me_y, (me_y + 1) % flow_cycle, (me_y - 1 + flow_cycle) % flow_cycle, lax.axis_index("gz")
 
 
-def _emit_relax(cells_of_x, slab_width, relaxed_ref, chunk_ref, depth):
+def _emit_relax(cells_of_x, slab_width, relaxed_ref, chunk_ref, depth, planes=None, packs_in=None, packs_ref=None):
     lane = lax.broadcasted_iota(jnp.int32, (depth, LANES), 1)
-    up_pack = jnp.zeros((depth, LANES), jnp.float32)
-    down_pack = jnp.zeros((depth, LANES), jnp.float32)
+    if packs_in is None:
+        up_pack = jnp.zeros((depth, LANES), jnp.float32)
+        down_pack = jnp.zeros((depth, LANES), jnp.float32)
+    else:
+        up_pack, down_pack = packs_in[0], packs_in[1]
     top = bottom = None
-    for x in range(slab_width):
+    packing = chunk_ref is not None or packs_ref is not None
+    for x in range(slab_width) if planes is None else planes:
         r = relax(cells_of_x(x))
         if relaxed_ref is not None:
             for m in range(19):
                 relaxed_ref[m, x] = r[m]
-        if chunk_ref is None:
+        if not packing:
             continue
         if x == slab_width - 1:
             top = corrected(r, upward, -1.0)
@@ -170,6 +174,9 @@
         for i, m in enumerate(y_minus):
             k = i * slab_width + x
             down_pack = jnp.where(lane == k, _roll(r[m], k, 1), down_pack)
+    if packs_ref is not None:
+        packs_ref[0] = up_pack
+        packs_ref[1] = down_pack
     if chunk_ref is None:
         return
     faces = jnp.concatenate([top.reshape(5 * depth, LANES), bottom.reshape(5 * depth, LANES)], axis=0)
@@ -247,16 +254,56 @@
     _emit_relax(cells, slab_width, next_ref, chunk_ref, depth)
 
 
-def _last_kernel(relaxed_ref, rims_ref, low_ref, high_ref, hits_ref, out_ref, density_ref):
+def _interior_kernel(relaxed_ref, rims_ref, hits_ref, packs_ref):
+    slab_width, depth = relaxed_ref.shape[1], relaxed_ref.shape[2]
+    cells = lambda x: _streamed(x, slab_width, relaxed_ref, rims_ref, None, None, hits_ref, depth)
+    _emit_relax(cells, slab_width, None, None, depth, planes=range(1, slab_width - 1), packs_ref=packs_ref)
+
+
+def _boundary_kernel(relaxed_ref, rims_ref, low_ref, high_ref, hits_ref, packs_ref, chunk_ref):
+    slab_width, depth = relaxed_ref.shape[1], relaxed_ref.shape[2]
+    cells = lambda x: _streamed(x, slab_width, relaxed_ref, rims_ref, low_ref, high_ref, hits_ref, depth)
+    _emit_relax(cells, slab_width, None, chunk_ref, depth, planes=(0, slab_width - 1), packs_in=packs_ref)
+
+
+def _last_planes(planes, relaxed_ref, rims_ref, low_ref, high_ref, hits_ref, put):
     slab_width, depth = relaxed_ref.shape[1], relaxed_ref.shape[2]
     half = depth // 2
-    lower = jnp.full((half, LANES), _positions()[3], jnp.int32) == 0
     own = pl.multiple_of(_positions()[3] * half, half)
-    for x in range(slab_width):
+    for slot, x in enumerate(planes):
         mine = _streamed(x, slab_width, relaxed_ref, rims_ref, low_ref, high_ref, hits_ref, depth, own=own)
+        put(slot, x, mine)
+
+
+def _last_interior(relaxed_ref, rims_ref, hits_ref, out_ref, density_ref):
+    slab_width = relaxed_ref.shape[1]
+
+    def put(slot, x, mine):
         for m in range(19):
             out_ref[m, x] = mine[m]
         density_ref[x] = total_density(mine)
+
+    _last_planes(range(1, slab_width - 1), relaxed_ref, rims_ref, None, None, hits_ref, put)
+
+
+def _last_boundary(relaxed_ref, rims_ref, low_ref, high_ref, hits_ref, out_in, dens_in, out_hbm, dens_hbm, out_v, dens_v, sems):
+    slab_width = relaxed_ref.shape[1]
+    planes = (0, slab_width - 1)
+
+    def put(slot, x, mine):
+        for m in range(19):
+            out_v[m, slot] = mine[m]
+        dens_v[slot] = total_density(mine)
+
+    _last_planes(planes, relaxed_ref, rims_ref, low_ref, high_ref, hits_ref, put)
+    copies = []
+    for slot, x in enumerate(planes):
+        copies.append(pltpu.make_async_copy(out_v.at[:, slot], out_hbm.at[:, x], sems.at[0, slot]))
+        copies.append(pltpu.make_async_copy(dens_v.at[slot], dens_hbm.at[x], sems.at[1, slot]))
+    for c in copies:
+        c.start()
+    for c in copies:
+        c.wait()
 
 
 def _window_kernel(section, shift_ref, frac_ref, got_ref, low_ref, high_ref, rims_ref):
@@ -346,10 +393,23 @@
         high_ghost = lax.ppermute(high_send, "gx", [(i, (i - 1) % slab_cycle) for i in range(slab_cycle)])
         if section + 1 < STEPS:
             args = (relaxed, rim_pair, low_ghost, high_ghost, hits)
-            chunks = _call(_middle_kernel, 0, 5, chunk)(*args)
+            packs = _call(_interior_kernel, 0, 3, rims)(relaxed, rim_pair, hits)
+            chunks = _call(_boundary_kernel, 0, 6, chunk)(relaxed, rim_pair, low_ghost, high_ghost, hits, packs)
             relaxed = _call(_middle_kernel, 0, 5, full)(*args)
         else:
-            final, dens = _call(_last_kernel, 0, 5, (own, density))(relaxed, rim_pair, low_ghost, high_ghost, hits)
+            part, part_dens = _call(_last_interior, 0, 3, (own, density))(relaxed, rim_pair, hits)
+            final, dens = pl.pallas_call(
+                _last_boundary,
+                out_shape=(own, density),
+                in_specs=[_vmem()] * 5 + [pl.BlockSpec(memory_space=pl.ANY)] * 2,
+                out_specs=(pl.BlockSpec(memory_space=pl.ANY), pl.BlockSpec(memory_space=pl.ANY)),
+                scratch_shapes=[
+                    pltpu.VMEM((n_members, 2, half_depth, row_span), f32),
+                    pltpu.VMEM((2, half_depth, row_span), f32),
+                    pltpu.SemaphoreType.DMA((2, 2)),
+                ],
+                input_output_aliases={5: 0, 6: 1},
+            )(relaxed, rim_pair, low_ghost, high_ghost, hits, part, part_dens)
     return (final, dens)
 
 

time: 73.2 us -> 78.2 us (1.068)
  Pallas kernels: 19.4 us -> 23.7 us
    pallas_call x2 -> x4, Pallas kernels: 6.24 us -> 10.5 us  [the longest x1 2.89 us: _per_device(): packs = _call(_interior_kernel, 0, 3, rims)(relaxed, rim_pair, hits)]
  transfers between devices with their start and end apart: 7 -> 7, of which waited for: 3 -> 3; matrix products, arithmetic and copies ran while one was open for 4% -> 3% of each run, Pallas kernels for 9% -> 15%
where the time goes in v11:
time: 78.2 us; the launch traced here: 77.7 us
  Pallas kernels  23.7 us (30%)
  blocking collectives  16.9 us (22%)
  starting transfers between devices  15.5 us (20%)
  waiting for transfers between devices  14.7 us (19%)
  local copies, waits for them, and re-layouts  3.57 us (5%)
  matrix products  1.35 us (2%)
  other arithmetic  1.24 us (2%)
    all_to_all x1, blocking collectives, _per_device(): got = lax.all_to_all(chunks, 'gy', 0, 0, tiled=True)  16.9 us
    all_to_all x1, waiting for transfers between devices, _per_device(): got = lax.all_to_all(chunks, 'gy', 0, 0, tiled=True)  11.3 us
    ppermute x2, starting transfers between devices, _per_device(): lax.ppermute(high_send, 'gx', [(i, (i - 1) % slab_cycle) for i in range(s...  7.68 us
    all_to_all x1, starting transfers between devices, _per_device(): got = lax.all_to_all(chunks, 'gy', 0, 0, tiled=True)  7.04 us
    pallas_call x2, Pallas kernels, _per_device(): _call(functools.partial(_window_kernel, section), 2, 1, (ghost, ghost, ri...  3.94 us
    unnamed x14, local copies, waits for them, and re-layouts  3.57 us
    pallas_call x1, Pallas kernels, _per_device(): relaxed = _call(_middle_kernel, 0, 5, full)(*args)  3.41 us
    pallas_call x1, Pallas kernels, _per_device(): relaxed = _call(_first_kernel, 0, 2, full)(populations, other_states)  3.02 us
  transfers between devices with their start and end apart: 7, of which 3 were waited for; matrix products, arithmetic and copies ran while one was open for 3% of the time, Pallas kernels for 15%

profile of v11, /device:TPU:0, one launch (start us, length us, event | category | flops | bytes accessed | tf_op | source)
XLA Modules:
  0.0 77.7 jit_solution(13196132621069470248)
XLA Ops:
  0.7 2.2 %collective-permute-done.other_ref = f32[19,8,8,128]{3,2,1,0:T(8,128)S(1)} collective-permute-done((f32[19,8,8,128]{3,2,1,0:T(8,128)}, f32[19,8,8,128]{3,2,1,0:T(8,128)S(1)}, u32[]{:S(2)}, u32[]{:S(2)}) %collective-permute-start) | collective-permute-done | bytes 622624 | tf_op jit(solution)/shard_map/ppermute | solution.py:369
  3.0 0.8 %copy-done.1 = f32[19,8,8,128]{3,2,1,0:T(8,128)} copy-done((f32[19,8,8,128]{3,2,1,0:T(8,128)}, f32[19,8,8,128]{3,2,1,0:T(8,128)S(1)}, u32[]{:S(2)}) %copy-start.1) | copy-done | bytes 622616
  3.8 2.8 %shard_map.60 = f32[8,176,128]{2,1,0:T(8,128)} custom-call(f32[19,8,8,128]{3,2,1,0:T(8,128)} %mine_ref.3, f32[19,8,8,128]{3,2,1,0:T(8,128)} %copy-done.1), custom_call_target="tpu_custom_call" | custom-call | tf_op jit(solution)/shard_map/pallas_call | solution.py:385
  6.6 7.0 %all-to-all-start = ((f32[8,176,128]{2,1,0:T(8,128)}), f32[8,176,128]{2,1,0:T(8,128)S(1)}, u32[]{:S(2)}, u32[]{:S(2)}) async-start(f32[8,176,128]{2,1,0:T(8,128)} %shard_map.60), calls=%async_computation | async-start | bytes 1441792 | tf_op jit(solution)/shard_map/all_to_all | solution.py:388
  13.8 1.2 %collective-permute-done.3 = s32[8,8,32]{2,1,0:T(8,128)S(1)} collective-permute-done((s32[8,8,32]{2,1,0:T(8,128)S(1)}, s32[8,8,32]{2,1,0:T(8,128)S(1)}, u32[]{:S(2)}, u32[]{:S(2)}) %collective-permute-start.3) | collective-permute-done | bytes 8224 | tf_op jit(solution)/shard_map/ppermute | solution.py:370
  15.1 1.4 %fusion = f32[8,16,128,19]{2,3,1,0:T(8,128)S(1)} fusion(s32[8,16,32]{2,1,0:T(8,128)S(1)} %get-tuple-element.19, s32[8,16,32]{2,1,0:T(8,128)S(1)} %get-tuple-element.18), kind=kOutput, calls=%fused_computation.1 | convolution fusion | flops 20525056 | bytes 1277952 | tf_op jit(solution)/shard_map/xzml,xzly->mxzy/dot_general | solution.py:116
  16.4 11.3 %all-to-all-done.got_ref = f32[8,176,128]{2,1,0:T(8,128)S(1)} async-done(((f32[8,176,128]{2,1,0:T(8,128)}), f32[8,176,128]{2,1,0:T(8,128)S(1)}, u32[]{:S(2)}, u32[]{:S(2)}) %all-to-all-start) | async-done | bytes 720928 | tf_op jit(solution)/shard_map/all_to_all | solution.py:388
  27.7 0.9 %copy-done = f32[8,176,128]{2,1,0:T(8,128)} copy-done((f32[8,176,128]{2,1,0:T(8,128)}, f32[8,176,128]{2,1,0:T(8,128)S(1)}, u32[]{:S(2)}) %copy-start) | copy-done | bytes 720920
  28.6 2.0 %shard_map.61 = (f32[5,16,128]{2,1,0:T(8,128)}, f32[5,16,128]{2,1,0:T(8,128)}, f32[2,16,128]{2,1,0:T(8,128)}) custom-call(s32[2]{0:T(128)} %shift_ref.3, s32[2]{0:T(128)} %frac_ref.3, f32[8,176,128]{2,1,0:T(8,128)} %copy-done), custom_call_target="tpu_custom_call" | custom-call | tf_op jit(solution)/shard_map/pallas_call | solution.py:389
  30.5 0.6 collective-permute-start.1
  31.1 3.5 %collective-permute-start.2 = (f32[5,16,128]{2,1,0:T(8,128)}, f32[5,16,128]{2,1,0:T(8,128)S(1)}, u32[]{:S(2)}, u32[]{:S(2)}) collective-permute-start(f32[5,16,128]{2,1,0:T(8,128)} %get-tuple-element.12), channel_id=1, source_target_pairs={{0,112},{16,0},{32,16},{48,32},{64,48},{80,64},{96,80},{112,96},{1... | collective-permute-start | bytes 122888 | tf_op jit(solution)/shard_map/ppermute | solution.py:393
  34.7 1.2 %fusion.4.hits_ref = bf16[19,8,16,128]{3,2,1,0:T(8,128)(2,1)} fusion(f32[8,16,128,19]{2,3,1,0:T(8,128)S(1)} %fusion), kind=kLoop, calls=%fused_computation.7 | loop fusion | flops 622592 | bytes 1867776 | tf_op jit(solution)/shard_map/convert_element_type | solution.py:117
  35.8 3.0 %shard_map.59.relaxed_ref = f32[19,8,16,128]{3,2,1,0:T(8,128)} custom-call(f32[19,8,8,128]{3,2,1,0:T(8,128)} %mine_ref.3, f32[19,8,8,128]{3,2,1,0:T(8,128)} %copy-done.1), custom_call_target="tpu_custom_call" | custom-call | tf_op jit(solution)/shard_map/pallas_call | solution.py:386
  38.8 2.9 %shard_map.63.packs_ref = f32[2,16,128]{2,1,0:T(8,128)} custom-call(f32[19,8,16,128]{3,2,1,0:T(8,128)} %shard_map.59.relaxed_ref, f32[2,16,128]{2,1,0:T(8,128)} %get-tuple-element.10.rims_ref, bf16[19,8,16,128]{3,2,1,0:T(8,128)(2,1)} %fusion.4.hits_ref), custom_call_target="tpu_custom_call" | custom-call | tf_op jit(solution)/shard_map/pallas_call | solution.py:396
  41.8 0.6 copy-done.2
  42.4 0.6 copy-done.3
  43.0 2.8 %shard_map.64 = f32[8,176,128]{2,1,0:T(8,128)} custom-call(f32[19,8,16,128]{3,2,1,0:T(8,128)} %shard_map.59.relaxed_ref, f32[2,16,128]{2,1,0:T(8,128)} %get-tuple-element.10.rims_ref, f32[5,16,128]{2,1,0:T(8,128)} %copy-done.2, f32[5,16,128]{2,1,0:T(8,128)} %copy-done.3, bf16[19,8,16,128]{3,2,1,0:T(8,128)(2,1)} %fusion.4.hits_ref, ...), custom_call_target="tpu_custom_call" | custom-call | tf_op jit(solution)/shard_map/pallas_call | solution.py:397
  45.7 16.9 %all_to_all.10.got_ref = f32[8,176,128]{2,1,0:T(8,128)} all-to-all(f32[8,176,128]{2,1,0:T(8,128)} %shard_map.64), channel_id=1, replica_groups=mesh['gx'=8,'gy'=8,'gz'=2] {'gy'}, dimensions={0} | all-to-all | bytes 1441792 | tf_op jit(solution)/shard_map/all_to_all | solution.py:388
  62.7 2.0 %shard_map.65 = (f32[5,16,128]{2,1,0:T(8,128)}, f32[5,16,128]{2,1,0:T(8,128)}, f32[2,16,128]{2,1,0:T(8,128)}) custom-call(s32[2]{0:T(128)} %shift_ref.3, s32[2]{0:T(128)} %frac_ref.3, f32[8,176,128]{2,1,0:T(8,128)} %all_to_all.10.got_ref), custom_call_target="tpu_custom_call" | custom-call | tf_op jit(solution)/shard_map/pallas_call | solution.py:389
  64.6 4.1 %collective-permute-start.5 = (f32[5,16,128]{2,1,0:T(8,128)}, f32[5,16,128]{2,1,0:T(8,128)S(1)}, u32[]{:S(2)}, u32[]{:S(2)}) collective-permute-start(f32[5,16,128]{2,1,0:T(8,128)} %get-tuple-element.15), channel_id=1, source_target_pairs={{0,112},{16,0},{32,16},{48,32},{64,48},{80,64},{96,80},{112,96},{1... | collective-permute-start | bytes 122888 | tf_op jit(solution)/shard_map/ppermute | solution.py:393
  68.8 3.4 %shard_map.62.relaxed_ref = f32[19,8,16,128]{3,2,1,0:T(8,128)} custom-call(f32[19,8,16,128]{3,2,1,0:T(8,128)} %shard_map.59.relaxed_ref, f32[2,16,128]{2,1,0:T(8,128)} %get-tuple-element.10.rims_ref, f32[5,16,128]{2,1,0:T(8,128)} %copy-done.2, f32[5,16,128]{2,1,0:T(8,128)} %copy-done.3, bf16[19,8,16,128]{3,2,1,0:T(8,128)(2,1)} %fusion.4.hits_ref), custom_call_target="tpu_custom_call" | custom-call | tf_op jit(solution)/shard_map/pallas_call | solution.py:398
  72.2 2.5 %shard_map.66 = (f32[19,8,8,128]{3,2,1,0:T(8,128)}, f32[8,8,128]{2,1,0:T(8,128)}) custom-call(f32[19,8,16,128]{3,2,1,0:T(8,128)} %shard_map.62.relaxed_ref, f32[2,16,128]{2,1,0:T(8,128)} %get-tuple-element.13.rims_ref, bf16[19,8,16,128]{3,2,1,0:T(8,128)(2,1)} %fusion.4.hits_ref), custom_call_target="tpu_custom_call" | custom-call | tf_op jit(solution)/shard_map/pallas_call | solution.py:400
  74.8 0.6 copy-done.4
  75.4 2.3 %shard_map.67 = (f32[19,8,8,128]{3,2,1,0:T(8,128)}, f32[8,8,128]{2,1,0:T(8,128)}) custom-call(f32[19,8,16,128]{3,2,1,0:T(8,128)} %shard_map.62.relaxed_ref, f32[2,16,128]{2,1,0:T(8,128)} %get-tuple-element.13.rims_ref, f32[5,16,128]{2,1,0:T(8,128)} %copy-done.4, f32[5,16,128]{2,1,0:T(8,128)} %copy-done.5, ...), custom_call_target="tpu_custom_call", output_to_operand_aliasing={{0}: (5, {}), {1}: (6, {})} | custom-call | tf_op jit(solution)/shard_map/pallas_call | solution.py:401
  (17 shorter events, 0.3 us)
Async XLA Ops:
  0.6 13.1 %copy-start.6 = (s32[8,8,32]{2,1,0:T(8,128)S(1)}, s32[8,8,32]{2,1,0:T(8,128)}, u32[]{:S(2)}) copy-start(s32[8,8,32]{2,1,0:T(8,128)} %param.7) | copy-start | bytes 24580
  0.6 2.3 %collective-permute-start = (f32[19,8,8,128]{3,2,1,0:T(8,128)}, f32[19,8,8,128]{3,2,1,0:T(8,128)S(1)}, u32[]{:S(2)}, u32[]{:S(2)}) collective-permute-start(f32[19,8,8,128]{3,2,1,0:T(8,128)} %mine_ref.3), channel_id=1, source_target_pairs={{0,1},{1,0},{2,3},{3,2},{4,5},{5,4},{6,7},{7,6},{8,9},{9,8},{10,11... | collective-permute-start | bytes 1867784 | tf_op jit(solution)/shard_map/ppermute | solution.py:369
  3.0 0.8 %copy-start.1 = (f32[19,8,8,128]{3,2,1,0:T(8,128)}, f32[19,8,8,128]{3,2,1,0:T(8,128)S(1)}, u32[]{:S(2)}) copy-start(f32[19,8,8,128]{3,2,1,0:T(8,128)S(1)} %collective-permute-done.other_ref) | copy-start | bytes 1867780
  6.6 21.0 %all-to-all-start = ((f32[8,176,128]{2,1,0:T(8,128)}), f32[8,176,128]{2,1,0:T(8,128)S(1)}, u32[]{:S(2)}, u32[]{:S(2)}) async-start(f32[8,176,128]{2,1,0:T(8,128)} %shard_map.60), calls=%async_computation | async-start | bytes 1441792 | tf_op jit(solution)/shard_map/all_to_all | solution.py:388
  13.7 1.3 %collective-permute-start.3 = (s32[8,8,32]{2,1,0:T(8,128)S(1)}, s32[8,8,32]{2,1,0:T(8,128)S(1)}, u32[]{:S(2)}, u32[]{:S(2)}) collective-permute-start(s32[8,8,32]{2,1,0:T(8,128)S(1)} %copy-done.6), channel_id=1, source_target_pairs={{0,1},{1,0},{2,3},{3,2},{4,5},{5,4},{6,7},{7,6},{8,9},{9,8},{10,11... | collective-permute-start | bytes 24584 | tf_op jit(solution)/shard_map/ppermute | solution.py:370
  27.7 0.9 %copy-start = (f32[8,176,128]{2,1,0:T(8,128)}, f32[8,176,128]{2,1,0:T(8,128)S(1)}, u32[]{:S(2)}) copy-start(f32[8,176,128]{2,1,0:T(8,128)S(1)} %all-to-all-done.got_ref) | copy-start | bytes 2162692
  30.5 11.2 %collective-permute-start.1 = (f32[5,16,128]{2,1,0:T(8,128)}, f32[5,16,128]{2,1,0:T(8,128)S(1)}, u32[]{:S(2)}, u32[]{:S(2)}) collective-permute-start(f32[5,16,128]{2,1,0:T(8,128)} %get-tuple-element.11), channel_id=1, source_target_pairs={{0,16},{16,32},{32,48},{48,64},{64,80},{80,96},{96,112},{112,0},{1... | collective-permute-start | bytes 122888 | tf_op jit(solution)/shard_map/ppermute | solution.py:392
  31.1 10.6 %collective-permute-start.2 = (f32[5,16,128]{2,1,0:T(8,128)}, f32[5,16,128]{2,1,0:T(8,128)S(1)}, u32[]{:S(2)}, u32[]{:S(2)}) collective-permute-start(f32[5,16,128]{2,1,0:T(8,128)} %get-tuple-element.12), channel_id=1, source_target_pairs={{0,112},{16,0},{32,16},{48,32},{64,48},{80,64},{96,80},{112,96},{1... | collective-permute-start | bytes 122888 | tf_op jit(solution)/shard_map/ppermute | solution.py:393
  41.7 0.6 copy-start.2
  42.4 0.6 copy-start.3
  64.6 10.1 %collective-permute-start.4 = (f32[5,16,128]{2,1,0:T(8,128)}, f32[5,16,128]{2,1,0:T(8,128)S(1)}, u32[]{:S(2)}, u32[]{:S(2)}) collective-permute-start(f32[5,16,128]{2,1,0:T(8,128)} %get-tuple-element.14), channel_id=1, source_target_pairs={{0,16},{16,32},{32,48},{48,64},{64,80},{80,96},{96,112},{112,0},{1... | collective-permute-start | bytes 122888 | tf_op jit(solution)/shard_map/ppermute | solution.py:392
  64.6 10.1 %collective-permute-start.5 = (f32[5,16,128]{2,1,0:T(8,128)}, f32[5,16,128]{2,1,0:T(8,128)S(1)}, u32[]{:S(2)}, u32[]{:S(2)}) collective-permute-start(f32[5,16,128]{2,1,0:T(8,128)} %get-tuple-element.15), channel_id=1, source_target_pairs={{0,112},{16,0},{32,16},{48,32},{64,48},{80,64},{96,80},{112,96},{1... | collective-permute-start | bytes 122888 | tf_op jit(solution)/shard_map/ppermute | solution.py:393
  74.7 0.6 copy-start.4
  74.8 0.6 copy-start.5

commit v12 on v9

--- a/solution.py
+++ b/solution.py
@@ -113,8 +113,9 @@
     member = links % 19
     by_member = (member[:, :, None, :] == jnp.arange(19, dtype=jnp.int32)[:, None]).astype(jnp.bfloat16)
     by_cell = (cell_y[:, :, :, None] == jnp.arange(row_span, dtype=jnp.int32)).astype(jnp.bfloat16)
-    counts = jnp.einsum("xzml,xzly->mxzy", by_member, by_cell, preferred_element_type=jnp.float32)
-    return (counts > 0.5).astype(jnp.bfloat16)
+    counts = jnp.einsum("xzml,xzly->xzym", by_member, by_cell, preferred_element_type=jnp.float32)
+    bits = jnp.left_shift(1, jnp.arange(19, dtype=jnp.int32))
+    return jnp.sum(jnp.where(counts > 0.5, bits, 0), axis=-1, dtype=jnp.int32)
 
 
 LANES = 128
@@ -219,7 +220,7 @@
     result = [out[0]]
     for n in range(1, 19):
         src = n - 1 + 2 * (n % 2)
-        hit = part(hits_ref, src, x).astype(jnp.float32) > 0.5
+        hit = jnp.bitwise_and(jnp.right_shift(part(hits_ref, x), src), 1) != 0
         result.append(jnp.where(hit, part(relaxed_ref, src, x), out[n]))
     return result
 
@@ -259,8 +260,8 @@
         density_ref[x] = total_density(mine)
 
 
-def _window_kernel(section, shift_ref, frac_ref, got_ref, low_ref, high_ref, rims_ref):
-    peers, _, lanes = got_ref.shape
+def _window_kernel(section, shift_ref, frac_ref, got_hbm, low_ref, high_ref, rims_ref, faces_v, rim_v, sems):
+    peers, _, lanes = got_hbm.shape
     depth = low_ref.shape[1]
     me_y, after, before, _ = _positions()
     offset = shift_ref[section]
@@ -269,29 +270,48 @@
     flow_cells = peers * lanes
     anchor = me_y * lanes
     lane = lax.broadcasted_iota(jnp.int32, (depth, lanes), 1)
-
-    def window(row0, start):
+    face_rows = 5 * depth
+    firsts = [
+        ((anchor - offset - 2 + 2 * flow_cells) % flow_cells) // lanes,
+        ((anchor + offset - 1 + flow_cells) % flow_cells) // lanes,
+    ]
+    copies = []
+    for f in range(2):
+        for b in range(3):
+            block = (firsts[f] + b) % peers
+            copies.append(
+                pltpu.make_async_copy(
+                    got_hbm.at[block, pl.ds(f * face_rows, face_rows)], faces_v.at[f, b], sems.at[f * 3 + b]
+                )
+            )
+    rim_rows = pl.ds(FACE_ROWS * depth, depth)
+    copies.append(pltpu.make_async_copy(got_hbm.at[before, rim_rows], rim_v.at[0], sems.at[6]))
+    copies.append(pltpu.make_async_copy(got_hbm.at[after, rim_rows], rim_v.at[1], sems.at[7]))
+    for c in copies:
+        c.start()
+    for c in copies:
+        c.wait()
+
+    def window(f, row0, start):
         start = (start + 2 * flow_cells) % flow_cells
         block = start // lanes
         off = start % lanes
-        after = (block + 1) % peers
+        near = (block - firsts[f] + peers) % peers
         shift = (lanes - off) % lanes
-        first = pltpu.roll(got_ref[block, pl.ds(row0, depth), :], shift, 1)
-        second = pltpu.roll(got_ref[after, pl.ds(row0, depth), :], shift, 1)
+        first = pltpu.roll(faces_v[f, near, pl.ds(row0, depth), :], shift, 1)
+        second = pltpu.roll(faces_v[f, near + 1, pl.ds(row0, depth), :], shift, 1)
         return jnp.where(lane < lanes - off, first, second)
 
     for i, m in enumerate(upward):
         step_y = velocity_table[m][1]
-        row0 = i * depth
         a = anchor - offset - step_y
-        low_ref[i] = keep * window(row0, a) + fraction * window(row0, a - 1)
+        low_ref[i] = keep * window(0, i * depth, a) + fraction * window(0, i * depth, a - 1)
     for i, m in enumerate(downward):
         step_y = velocity_table[m][1]
-        row0 = (5 + i) * depth
         c = anchor + offset - step_y
-        high_ref[i] = fraction * window(row0, c + 1) + keep * window(row0, c)
-    rims_ref[0] = got_ref[before, pl.ds(FACE_ROWS * depth, depth), :]
-    rims_ref[1] = got_ref[after, pl.ds(FACE_ROWS * depth, depth), :]
+        high_ref[i] = fraction * window(1, i * depth, c + 1) + keep * window(1, i * depth, c)
+    rims_ref[0] = rim_v[0]
+    rims_ref[1] = rim_v[1]
 
 
 def _vmem():
@@ -339,9 +359,17 @@
     relaxed = _call(_first_kernel, 0, 2, full)(populations, other_states)
     for section in range(STEPS):
         got = lax.all_to_all(chunks, "gy", 0, 0, tiled=True)
-        low_send, high_send, rim_pair = _call(functools.partial(_window_kernel, section), 2, 1, (ghost, ghost, rims))(
-            le_shift, le_frac, got
-        )
+        low_send, high_send, rim_pair = pl.pallas_call(
+            functools.partial(_window_kernel, section),
+            out_shape=(ghost, ghost, rims),
+            in_specs=[_smem(), _smem(), pl.BlockSpec(memory_space=pl.ANY)],
+            out_specs=(_vmem(), _vmem(), _vmem()),
+            scratch_shapes=[
+                pltpu.VMEM((2, 3, 5 * depth, row_span), f32),
+                pltpu.VMEM((2, depth, row_span), f32),
+                pltpu.SemaphoreType.DMA((8,)),
+            ],
+        )(le_shift, le_frac, got)
         low_ghost = lax.ppermute(low_send, "gx", [(i, (i + 1) % slab_cycle) for i in range(slab_cycle)])
         high_ghost = lax.ppermute(high_send, "gx", [(i, (i - 1) % slab_cycle) for i in range(slab_cycle)])
         if section + 1 < STEPS:

time: 73.2 us -> 73.9 us (level)
    convert_element_type x1 -> x0, other arithmetic: 1.15 us -> none  [link_hits(): return (counts > 0.5).astype(jnp.bfloat16)]
    reduce_sum x0 -> x1, other arithmetic: none -> 1.04 us  [link_hits(): return jnp.sum(jnp.where(counts > 0.5, bits, 0), axis=-1, dtype=jnp.int32)]
    pallas_call x2, Pallas kernels: 3.94 us -> 4.91 us  [_per_device(): pl.pallas_call(functools.partial(_window_kernel, section), out_shape=(gho...]
  transfers between devices with their start and end apart: 7 -> 7, of which waited for: 3 -> 3; matrix products, arithmetic and copies ran while one was open for 4% -> 3% of each run, Pallas kernels for 9% -> 9%
where the time goes in v12:
time: 73.9 us; the launch traced here: 73.4 us
  Pallas kernels  19.9 us (27%)
  blocking collectives  17 us (23%)
  starting transfers between devices  15.6 us (21%)
  waiting for transfers between devices  15 us (20%)
  local copies, waits for them, and re-layouts  2.94 us (4%)
  other arithmetic  1.12 us (2%)
  matrix products  1.07 us (1%)
  between operations  0.74 us (1%)
    all_to_all x1, blocking collectives, _per_device(): got = lax.all_to_all(chunks, 'gy', 0, 0, tiled=True)  17 us
    all_to_all x1, waiting for transfers between devices, _per_device(): got = lax.all_to_all(chunks, 'gy', 0, 0, tiled=True)  11.5 us
    ppermute x2, starting transfers between devices, _per_device(): lax.ppermute(high_send, 'gx', [(i, (i - 1) % slab_cycle) for i in range(s...  7.68 us
    all_to_all x1, starting transfers between devices, _per_device(): got = lax.all_to_all(chunks, 'gy', 0, 0, tiled=True)  7.04 us
    pallas_call x2, Pallas kernels, _per_device(): pl.pallas_call(functools.partial(_window_kernel, section), out_shape=(gho...  4.91 us
    pallas_call x1, Pallas kernels, _per_device(): chunks = _call(_middle_kernel, 0, 5, chunk)(*args)  3.46 us
    pallas_call x1, Pallas kernels, _per_device(): relaxed = _call(_middle_kernel, 0, 5, full)(*args)  3.26 us
    pallas_call x1, Pallas kernels, _per_device(): relaxed = _call(_first_kernel, 0, 2, full)(populations, other_states)  3.01 us
  transfers between devices with their start and end apart: 7, of which 3 were waited for; matrix products, arithmetic and copies ran while one was open for 3% of the time, Pallas kernels for 9%

profile of v12, /device:TPU:0, one launch (start us, length us, event | category | flops | bytes accessed | tf_op | source)
XLA Modules:
  0.0 73.4 jit_solution(4455295808227958605)
XLA Ops:
  0.6 0.1 collective-permute-start
  0.7 2.2 %collective-permute-done.other_ref = f32[19,8,8,128]{3,2,1,0:T(8,128)S(1)} collective-permute-done((f32[19,8,8,128]{3,2,1,0:T(8,128)}, f32[19,8,8,128]{3,2,1,0:T(8,128)S(1)}, u32[]{:S(2)}, u32[]{:S(2)}) %collective-permute-start) | collective-permute-done | bytes 622624 | tf_op jit(solution)/shard_map/ppermute | solution.py:342
  3.0 0.8 %copy-done.1 = f32[19,8,8,128]{3,2,1,0:T(8,128)} copy-done((f32[19,8,8,128]{3,2,1,0:T(8,128)}, f32[19,8,8,128]{3,2,1,0:T(8,128)S(1)}, u32[]{:S(2)}) %copy-start.1) | copy-done | bytes 622616
  3.8 2.8 %shard_map.60 = f32[8,176,128]{2,1,0:T(8,128)} custom-call(f32[19,8,8,128]{3,2,1,0:T(8,128)} %mine_ref.3, f32[19,8,8,128]{3,2,1,0:T(8,128)} %copy-done.1), custom_call_target="tpu_custom_call" | custom-call | tf_op jit(solution)/shard_map/pallas_call | solution.py:358
  6.6 7.0 %all-to-all-start = ((f32[8,176,128]{2,1,0:T(8,128)}), f32[8,176,128]{2,1,0:T(8,128)S(1)}, u32[]{:S(2)}, u32[]{:S(2)}) async-start(f32[8,176,128]{2,1,0:T(8,128)} %shard_map.60), calls=%async_computation | async-start | bytes 1441792 | tf_op jit(solution)/shard_map/all_to_all | solution.py:361
  13.7 0.1 collective-permute-start.3
  13.8 1.2 %collective-permute-done.3 = s32[8,8,32]{2,1,0:T(8,128)S(1)} collective-permute-done((s32[8,8,32]{2,1,0:T(8,128)S(1)}, s32[8,8,32]{2,1,0:T(8,128)S(1)}, u32[]{:S(2)}, u32[]{:S(2)}) %collective-permute-start.3) | collective-permute-done | bytes 8224 | tf_op jit(solution)/shard_map/ppermute | solution.py:343
  14.9 0.1 add_select_fusion
  15.0 1.1 %fusion.1 = u16[8,128,19]{1,2,0:T(8,128)(2,1)S(1)} fusion(s32[8,16,32]{2,1,0:T(8,128)S(1)} %get-tuple-element.15, s32[8,16,32]{2,1,0:T(8,128)S(1)} %get-tuple-element.14), kind=kOutput, calls=%fused_computation.6 | convolution fusion | flops 22062080 | bytes 71680 | tf_op jit(solution)/shard_map/xzml,xzly->xzym/dot_general | solution.py:116
  16.1 11.5 %all-to-all-done.got_hbm = f32[8,176,128]{2,1,0:T(8,128)S(1)} async-done(((f32[8,176,128]{2,1,0:T(8,128)}), f32[8,176,128]{2,1,0:T(8,128)S(1)}, u32[]{:S(2)}, u32[]{:S(2)}) %all-to-all-start) | async-done | bytes 720928 | tf_op jit(solution)/shard_map/all_to_all | solution.py:361
  27.6 0.9 %copy-done = f32[8,176,128]{2,1,0:T(8,128)} copy-done((f32[8,176,128]{2,1,0:T(8,128)}, f32[8,176,128]{2,1,0:T(8,128)S(1)}, u32[]{:S(2)}) %copy-start) | copy-done | bytes 720920
  28.5 2.5 %shard_map.61 = (f32[5,16,128]{2,1,0:T(8,128)}, f32[5,16,128]{2,1,0:T(8,128)}, f32[2,16,128]{2,1,0:T(8,128)}) custom-call(s32[2]{0:T(128)} %shift_ref.3, s32[2]{0:T(128)} %frac_ref.3, f32[8,176,128]{2,1,0:T(8,128)} %copy-done), custom_call_target="tpu_custom_call" | custom-call | tf_op jit(solution)/shard_map/pallas_call | solution.py:362
  31.0 0.7 collective-permute-start.1
  31.6 3.6 %collective-permute-start.2 = (f32[5,16,128]{2,1,0:T(8,128)}, f32[5,16,128]{2,1,0:T(8,128)S(1)}, u32[]{:S(2)}, u32[]{:S(2)}) collective-permute-start(f32[5,16,128]{2,1,0:T(8,128)} %get-tuple-element.10), channel_id=1, source_target_pairs={{0,112},{16,0},{32,16},{48,32},{64,48},{80,64},{96,80},{112,96},{1... | collective-permute-start | bytes 122888 | tf_op jit(solution)/shard_map/ppermute | solution.py:374
  35.2 1.0 %select_reduce_fusion.hits_ref = s32[8,16,128]{2,1,0:T(8,128)} fusion(s32[19]{0:T(128)S(1)} %iota_shift-left_fusion, u16[8,128,19]{1,2,0:T(8,128)(2,1)S(1)} %fusion.1), kind=kLoop, calls=%fused_computation.4 | loop fusion | flops 1851392 | bytes 104524 | tf_op jit(solution)/shard_map/reduce_sum | solution.py:118
  36.2 3.0 %shard_map.59.relaxed_ref = f32[19,8,16,128]{3,2,1,0:T(8,128)} custom-call(f32[19,8,8,128]{3,2,1,0:T(8,128)} %mine_ref.3, f32[19,8,8,128]{3,2,1,0:T(8,128)} %copy-done.1), custom_call_target="tpu_custom_call" | custom-call | tf_op jit(solution)/shard_map/pallas_call | solution.py:359
  39.3 0.6 copy-done.2
  39.9 3.5 %shard_map.63 = f32[8,176,128]{2,1,0:T(8,128)} custom-call(f32[19,8,16,128]{3,2,1,0:T(8,128)} %shard_map.59.relaxed_ref, f32[2,16,128]{2,1,0:T(8,128)} %get-tuple-element.8.rims_ref, f32[5,16,128]{2,1,0:T(8,128)} %copy-done.2, f32[5,16,128]{2,1,0:T(8,128)} %copy-done.3, s32[8,16,128]{2,1,0:T(8,128)} %select_reduce_fusion.hits_ref), custom_call_target="tpu_custom_call" | custom-call | tf_op jit(solution)/shard_map/pallas_call | solution.py:377
  43.3 17.0 %all_to_all.10.got_hbm = f32[8,176,128]{2,1,0:T(8,128)} all-to-all(f32[8,176,128]{2,1,0:T(8,128)} %shard_map.63), channel_id=1, replica_groups=mesh['gx'=8,'gy'=8,'gz'=2] {'gy'}, dimensions={0} | all-to-all | bytes 1441792 | tf_op jit(solution)/shard_map/all_to_all | solution.py:361
  60.3 2.5 %shard_map.64 = (f32[5,16,128]{2,1,0:T(8,128)}, f32[5,16,128]{2,1,0:T(8,128)}, f32[2,16,128]{2,1,0:T(8,128)}) custom-call(s32[2]{0:T(128)} %shift_ref.3, s32[2]{0:T(128)} %frac_ref.3, f32[8,176,128]{2,1,0:T(8,128)} %all_to_all.10.got_hbm), custom_call_target="tpu_custom_call" | custom-call | tf_op jit(solution)/shard_map/pallas_call | solution.py:362
  62.9 4.1 %collective-permute-start.5 = (f32[5,16,128]{2,1,0:T(8,128)}, f32[5,16,128]{2,1,0:T(8,128)S(1)}, u32[]{:S(2)}, u32[]{:S(2)}) collective-permute-start(f32[5,16,128]{2,1,0:T(8,128)} %get-tuple-element.13), channel_id=1, source_target_pairs={{0,112},{16,0},{32,16},{48,32},{64,48},{80,64},{96,80},{112,96},{1... | collective-permute-start | bytes 122888 | tf_op jit(solution)/shard_map/ppermute | solution.py:374
  67.0 3.3 %shard_map.62.relaxed_ref = f32[19,8,16,128]{3,2,1,0:T(8,128)} custom-call(f32[19,8,16,128]{3,2,1,0:T(8,128)} %shard_map.59.relaxed_ref, f32[2,16,128]{2,1,0:T(8,128)} %get-tuple-element.8.rims_ref, f32[5,16,128]{2,1,0:T(8,128)} %copy-done.2, f32[5,16,128]{2,1,0:T(8,128)} %copy-done.3, s32[8,16,128]{2,1,0:T(8,128)} %select_reduce_fusion.hits_ref), custom_call_target="tpu_custom_call" | custom-call | tf_op jit(solution)/shard_map/pallas_call | solution.py:378
  70.3 0.6 copy-done.4
  70.9 2.5 %shard_map.65 = (f32[19,8,8,128]{3,2,1,0:T(8,128)}, f32[8,8,128]{2,1,0:T(8,128)}) custom-call(f32[19,8,16,128]{3,2,1,0:T(8,128)} %shard_map.62.relaxed_ref, f32[2,16,128]{2,1,0:T(8,128)} %get-tuple-element.11.rims_ref, f32[5,16,128]{2,1,0:T(8,128)} %copy-done.4, f32[5,16,128]{2,1,0:T(8,128)} %copy-done.5, s32[8,16,128]{2,1,0:T(8,128)} %select_reduce_fusion.hits_ref), custom_call_target="tpu_custom_call" | custom-call | tf_op jit(solution)/shard_map/pallas_call | solution.py:380
  (16 shorter events, 0.1 us)
Async XLA Ops:
  0.6 13.0 %copy-start.6 = (s32[8,8,32]{2,1,0:T(8,128)S(1)}, s32[8,8,32]{2,1,0:T(8,128)}, u32[]{:S(2)}) copy-start(s32[8,8,32]{2,1,0:T(8,128)} %param.7) | copy-start | bytes 24580
  0.6 2.3 %collective-permute-start = (f32[19,8,8,128]{3,2,1,0:T(8,128)}, f32[19,8,8,128]{3,2,1,0:T(8,128)S(1)}, u32[]{:S(2)}, u32[]{:S(2)}) collective-permute-start(f32[19,8,8,128]{3,2,1,0:T(8,128)} %mine_ref.3), channel_id=1, source_target_pairs={{0,1},{1,0},{2,3},{3,2},{4,5},{5,4},{6,7},{7,6},{8,9},{9,8},{10,11... | collective-permute-start | bytes 1867784 | tf_op jit(solution)/shard_map/ppermute | solution.py:342
  3.0 0.8 %copy-start.1 = (f32[19,8,8,128]{3,2,1,0:T(8,128)}, f32[19,8,8,128]{3,2,1,0:T(8,128)S(1)}, u32[]{:S(2)}) copy-start(f32[19,8,8,128]{3,2,1,0:T(8,128)S(1)} %collective-permute-done.other_ref) | copy-start | bytes 1867780
  6.6 21.0 %all-to-all-start = ((f32[8,176,128]{2,1,0:T(8,128)}), f32[8,176,128]{2,1,0:T(8,128)S(1)}, u32[]{:S(2)}, u32[]{:S(2)}) async-start(f32[8,176,128]{2,1,0:T(8,128)} %shard_map.60), calls=%async_computation | async-start | bytes 1441792 | tf_op jit(solution)/shard_map/all_to_all | solution.py:361
  13.7 1.3 %collective-permute-start.3 = (s32[8,8,32]{2,1,0:T(8,128)S(1)}, s32[8,8,32]{2,1,0:T(8,128)S(1)}, u32[]{:S(2)}, u32[]{:S(2)}) collective-permute-start(s32[8,8,32]{2,1,0:T(8,128)S(1)} %copy-done.6), channel_id=1, source_target_pairs={{0,1},{1,0},{2,3},{3,2},{4,5},{5,4},{6,7},{7,6},{8,9},{9,8},{10,11... | collective-permute-start | bytes 24584 | tf_op jit(solution)/shard_map/ppermute | solution.py:343
  27.6 0.9 %copy-start = (f32[8,176,128]{2,1,0:T(8,128)}, f32[8,176,128]{2,1,0:T(8,128)S(1)}, u32[]{:S(2)}) copy-start(f32[8,176,128]{2,1,0:T(8,128)S(1)} %all-to-all-done.got_hbm) | copy-start | bytes 2162692
  31.0 8.3 %collective-permute-start.1 = (f32[5,16,128]{2,1,0:T(8,128)}, f32[5,16,128]{2,1,0:T(8,128)S(1)}, u32[]{:S(2)}, u32[]{:S(2)}) collective-permute-start(f32[5,16,128]{2,1,0:T(8,128)} %get-tuple-element.9), channel_id=1, source_target_pairs={{0,16},{16,32},{32,48},{48,64},{64,80},{80,96},{96,112},{112,0},{1... | collective-permute-start | bytes 122888 | tf_op jit(solution)/shard_map/ppermute | solution.py:373
  31.6 7.6 %collective-permute-start.2 = (f32[5,16,128]{2,1,0:T(8,128)}, f32[5,16,128]{2,1,0:T(8,128)S(1)}, u32[]{:S(2)}, u32[]{:S(2)}) collective-permute-start(f32[5,16,128]{2,1,0:T(8,128)} %get-tuple-element.10), channel_id=1, source_target_pairs={{0,112},{16,0},{32,16},{48,32},{64,48},{80,64},{96,80},{112,96},{1... | collective-permute-start | bytes 122888 | tf_op jit(solution)/shard_map/ppermute | solution.py:374
  39.2 0.6 copy-start.2
  39.3 0.6 copy-start.3
  62.8 7.5 %collective-permute-start.4 = (f32[5,16,128]{2,1,0:T(8,128)}, f32[5,16,128]{2,1,0:T(8,128)S(1)}, u32[]{:S(2)}, u32[]{:S(2)}) collective-permute-start(f32[5,16,128]{2,1,0:T(8,128)} %get-tuple-element.12), channel_id=1, source_target_pairs={{0,16},{16,32},{32,48},{48,64},{64,80},{80,96},{96,112},{112,0},{1... | collective-permute-start | bytes 122888 | tf_op jit(solution)/shard_map/ppermute | solution.py:373
  62.9 7.4 %collective-permute-start.5 = (f32[5,16,128]{2,1,0:T(8,128)}, f32[5,16,128]{2,1,0:T(8,128)S(1)}, u32[]{:S(2)}, u32[]{:S(2)}) collective-permute-start(f32[5,16,128]{2,1,0:T(8,128)} %get-tuple-element.13), channel_id=1, source_target_pairs={{0,112},{16,0},{32,16},{48,32},{64,48},{80,64},{96,80},{112,96},{1... | collective-permute-start | bytes 122888 | tf_op jit(solution)/shard_map/ppermute | solution.py:374
  70.3 0.6 copy-start.4
  70.3 0.6 copy-start.5

commit v13 on v9

--- a/solution.py
+++ b/solution.py
@@ -113,8 +113,9 @@
     member = links % 19
     by_member = (member[:, :, None, :] == jnp.arange(19, dtype=jnp.int32)[:, None]).astype(jnp.bfloat16)
     by_cell = (cell_y[:, :, :, None] == jnp.arange(row_span, dtype=jnp.int32)).astype(jnp.bfloat16)
-    counts = jnp.einsum("xzml,xzly->mxzy", by_member, by_cell, preferred_element_type=jnp.float32)
-    return (counts > 0.5).astype(jnp.bfloat16)
+    counts = jnp.einsum("xzml,xzly->xzym", by_member, by_cell, preferred_element_type=jnp.float32)
+    bits = jnp.left_shift(1, jnp.arange(19, dtype=jnp.int32))
+    return jnp.sum(jnp.where(counts > 0.5, bits, 0), axis=-1, dtype=jnp.int32)
 
 
 LANES = 128
@@ -219,7 +220,7 @@
     result = [out[0]]
     for n in range(1, 19):
         src = n - 1 + 2 * (n % 2)
-        hit = part(hits_ref, src, x).astype(jnp.float32) > 0.5
+        hit = jnp.bitwise_and(jnp.right_shift(part(hits_ref, x), src), 1) != 0
         result.append(jnp.where(hit, part(relaxed_ref, src, x), out[n]))
     return result
 

time: 73.2 us -> 72.6 us (level)
    convert_element_type x1 -> x0, other arithmetic: 1.15 us -> none  [link_hits(): return (counts > 0.5).astype(jnp.bfloat16)]
    reduce_sum x0 -> x1, other arithmetic: none -> 1.04 us  [link_hits(): return jnp.sum(jnp.where(counts > 0.5, bits, 0), axis=-1, dtype=jnp.int32)]
  transfers between devices with their start and end apart: 7 -> 7, of which waited for: 3 -> 3; matrix products, arithmetic and copies ran while one was open for 4% -> 3% of each run, Pallas kernels for 9% -> 9%
where the time goes in v13:
time: 72.6 us; the launch traced here: 72.2 us
  Pallas kernels  18.9 us (26%)
  blocking collectives  16.9 us (23%)
  starting transfers between devices  15.5 us (21%)
  waiting for transfers between devices  15 us (21%)
  local copies, waits for them, and re-layouts  2.94 us (4%)
  other arithmetic  1.12 us (2%)
  matrix products  1.07 us (1%)
    all_to_all x1, blocking collectives, _per_device(): got = lax.all_to_all(chunks, 'gy', 0, 0, tiled=True)  16.9 us
    all_to_all x1, waiting for transfers between devices, _per_device(): got = lax.all_to_all(chunks, 'gy', 0, 0, tiled=True)  11.5 us
    ppermute x2, starting transfers between devices, _per_device(): lax.ppermute(high_send, 'gx', [(i, (i - 1) % slab_cycle) for i in range(s...  7.68 us
    all_to_all x1, starting transfers between devices, _per_device(): got = lax.all_to_all(chunks, 'gy', 0, 0, tiled=True)  7.04 us
    pallas_call x2, Pallas kernels, _per_device(): _call(functools.partial(_window_kernel, section), 2, 1, (ghost, ghost, ri...  3.94 us
    pallas_call x1, Pallas kernels, _per_device(): chunks = _call(_middle_kernel, 0, 5, chunk)(*args)  3.46 us
    pallas_call x1, Pallas kernels, _per_device(): relaxed = _call(_middle_kernel, 0, 5, full)(*args)  3.26 us
    pallas_call x1, Pallas kernels, _per_device(): relaxed = _call(_first_kernel, 0, 2, full)(populations, other_states)  3.01 us
  transfers between devices with their start and end apart: 7, of which 3 were waited for; matrix products, arithmetic and copies ran while one was open for 3% of the time, Pallas kernels for 9%

profile of v13, /device:TPU:0, one launch (start us, length us, event | category | flops | bytes accessed | tf_op | source)
XLA Modules:
  0.0 72.2 jit_solution(16573001343497234329)
XLA Ops:
  0.6 0.1 collective-permute-start
  0.7 2.2 %collective-permute-done.other_ref = f32[19,8,8,128]{3,2,1,0:T(8,128)S(1)} collective-permute-done((f32[19,8,8,128]{3,2,1,0:T(8,128)}, f32[19,8,8,128]{3,2,1,0:T(8,128)S(1)}, u32[]{:S(2)}, u32[]{:S(2)}) %collective-permute-start) | collective-permute-done | bytes 622624 | tf_op jit(solution)/shard_map/ppermute | solution.py:323
  3.0 0.8 %copy-done.1 = f32[19,8,8,128]{3,2,1,0:T(8,128)} copy-done((f32[19,8,8,128]{3,2,1,0:T(8,128)}, f32[19,8,8,128]{3,2,1,0:T(8,128)S(1)}, u32[]{:S(2)}) %copy-start.1) | copy-done | bytes 622616
  3.8 2.8 %shard_map.60 = f32[8,176,128]{2,1,0:T(8,128)} custom-call(f32[19,8,8,128]{3,2,1,0:T(8,128)} %mine_ref.3, f32[19,8,8,128]{3,2,1,0:T(8,128)} %copy-done.1), custom_call_target="tpu_custom_call" | custom-call | tf_op jit(solution)/shard_map/pallas_call | solution.py:339
  6.6 7.0 %all-to-all-start = ((f32[8,176,128]{2,1,0:T(8,128)}), f32[8,176,128]{2,1,0:T(8,128)S(1)}, u32[]{:S(2)}, u32[]{:S(2)}) async-start(f32[8,176,128]{2,1,0:T(8,128)} %shard_map.60), calls=%async_computation | async-start | bytes 1441792 | tf_op jit(solution)/shard_map/all_to_all | solution.py:342
  13.7 0.1 collective-permute-start.3
  13.8 1.2 %collective-permute-done.3 = s32[8,8,32]{2,1,0:T(8,128)S(1)} collective-permute-done((s32[8,8,32]{2,1,0:T(8,128)S(1)}, s32[8,8,32]{2,1,0:T(8,128)S(1)}, u32[]{:S(2)}, u32[]{:S(2)}) %collective-permute-start.3) | collective-permute-done | bytes 8224 | tf_op jit(solution)/shard_map/ppermute | solution.py:324
  14.9 0.1 add_select_fusion
  15.0 1.1 %fusion.1 = u16[8,128,19]{1,2,0:T(8,128)(2,1)S(1)} fusion(s32[8,16,32]{2,1,0:T(8,128)S(1)} %get-tuple-element.15, s32[8,16,32]{2,1,0:T(8,128)S(1)} %get-tuple-element.14), kind=kOutput, calls=%fused_computation.6 | convolution fusion | flops 22062080 | bytes 71680 | tf_op jit(solution)/shard_map/xzml,xzly->xzym/dot_general | solution.py:116
  16.1 11.5 %all-to-all-done.got_ref = f32[8,176,128]{2,1,0:T(8,128)S(1)} async-done(((f32[8,176,128]{2,1,0:T(8,128)}), f32[8,176,128]{2,1,0:T(8,128)S(1)}, u32[]{:S(2)}, u32[]{:S(2)}) %all-to-all-start) | async-done | bytes 720928 | tf_op jit(solution)/shard_map/all_to_all | solution.py:342
  27.6 0.9 %copy-done = f32[8,176,128]{2,1,0:T(8,128)} copy-done((f32[8,176,128]{2,1,0:T(8,128)}, f32[8,176,128]{2,1,0:T(8,128)S(1)}, u32[]{:S(2)}) %copy-start) | copy-done | bytes 720920
  28.5 2.0 %shard_map.61 = (f32[5,16,128]{2,1,0:T(8,128)}, f32[5,16,128]{2,1,0:T(8,128)}, f32[2,16,128]{2,1,0:T(8,128)}) custom-call(s32[2]{0:T(128)} %shift_ref.3, s32[2]{0:T(128)} %frac_ref.3, f32[8,176,128]{2,1,0:T(8,128)} %copy-done), custom_call_target="tpu_custom_call" | custom-call | tf_op jit(solution)/shard_map/pallas_call | solution.py:343
  30.5 0.6 collective-permute-start.1
  31.1 3.5 %collective-permute-start.2 = (f32[5,16,128]{2,1,0:T(8,128)}, f32[5,16,128]{2,1,0:T(8,128)S(1)}, u32[]{:S(2)}, u32[]{:S(2)}) collective-permute-start(f32[5,16,128]{2,1,0:T(8,128)} %get-tuple-element.10), channel_id=1, source_target_pairs={{0,112},{16,0},{32,16},{48,32},{64,48},{80,64},{96,80},{112,96},{1... | collective-permute-start | bytes 122888 | tf_op jit(solution)/shard_map/ppermute | solution.py:347
  34.6 1.0 %select_reduce_fusion.hits_ref = s32[8,16,128]{2,1,0:T(8,128)} fusion(s32[19]{0:T(128)S(1)} %iota_shift-left_fusion, u16[8,128,19]{1,2,0:T(8,128)(2,1)S(1)} %fusion.1), kind=kLoop, calls=%fused_computation.4 | loop fusion | flops 1851392 | bytes 104524 | tf_op jit(solution)/shard_map/reduce_sum | solution.py:118
  35.7 3.0 %shard_map.59.relaxed_ref = f32[19,8,16,128]{3,2,1,0:T(8,128)} custom-call(f32[19,8,8,128]{3,2,1,0:T(8,128)} %mine_ref.3, f32[19,8,8,128]{3,2,1,0:T(8,128)} %copy-done.1), custom_call_target="tpu_custom_call" | custom-call | tf_op jit(solution)/shard_map/pallas_call | solution.py:340
  38.7 0.6 copy-done.2
  39.3 3.5 %shard_map.63 = f32[8,176,128]{2,1,0:T(8,128)} custom-call(f32[19,8,16,128]{3,2,1,0:T(8,128)} %shard_map.59.relaxed_ref, f32[2,16,128]{2,1,0:T(8,128)} %get-tuple-element.8.rims_ref, f32[5,16,128]{2,1,0:T(8,128)} %copy-done.2, f32[5,16,128]{2,1,0:T(8,128)} %copy-done.3, s32[8,16,128]{2,1,0:T(8,128)} %select_reduce_fusion.hits_ref), custom_call_target="tpu_custom_call" | custom-call | tf_op jit(solution)/shard_map/pallas_call | solution.py:350
  42.8 16.9 %all_to_all.10.got_ref = f32[8,176,128]{2,1,0:T(8,128)} all-to-all(f32[8,176,128]{2,1,0:T(8,128)} %shard_map.63), channel_id=1, replica_groups=mesh['gx'=8,'gy'=8,'gz'=2] {'gy'}, dimensions={0} | all-to-all | bytes 1441792 | tf_op jit(solution)/shard_map/all_to_all | solution.py:342
  59.7 2.0 %shard_map.64 = (f32[5,16,128]{2,1,0:T(8,128)}, f32[5,16,128]{2,1,0:T(8,128)}, f32[2,16,128]{2,1,0:T(8,128)}) custom-call(s32[2]{0:T(128)} %shift_ref.3, s32[2]{0:T(128)} %frac_ref.3, f32[8,176,128]{2,1,0:T(8,128)} %all_to_all.10.got_ref), custom_call_target="tpu_custom_call" | custom-call | tf_op jit(solution)/shard_map/pallas_call | solution.py:343
  61.7 4.1 %collective-permute-start.5 = (f32[5,16,128]{2,1,0:T(8,128)}, f32[5,16,128]{2,1,0:T(8,128)S(1)}, u32[]{:S(2)}, u32[]{:S(2)}) collective-permute-start(f32[5,16,128]{2,1,0:T(8,128)} %get-tuple-element.13), channel_id=1, source_target_pairs={{0,112},{16,0},{32,16},{48,32},{64,48},{80,64},{96,80},{112,96},{1... | collective-permute-start | bytes 122888 | tf_op jit(solution)/shard_map/ppermute | solution.py:347
  65.8 3.3 %shard_map.62.relaxed_ref = f32[19,8,16,128]{3,2,1,0:T(8,128)} custom-call(f32[19,8,16,128]{3,2,1,0:T(8,128)} %shard_map.59.relaxed_ref, f32[2,16,128]{2,1,0:T(8,128)} %get-tuple-element.8.rims_ref, f32[5,16,128]{2,1,0:T(8,128)} %copy-done.2, f32[5,16,128]{2,1,0:T(8,128)} %copy-done.3, s32[8,16,128]{2,1,0:T(8,128)} %select_reduce_fusion.hits_ref), custom_call_target="tpu_custom_call" | custom-call | tf_op jit(solution)/shard_map/pallas_call | solution.py:351
  69.1 0.6 copy-done.4
  69.7 2.5 %shard_map.65 = (f32[19,8,8,128]{3,2,1,0:T(8,128)}, f32[8,8,128]{2,1,0:T(8,128)}) custom-call(f32[19,8,16,128]{3,2,1,0:T(8,128)} %shard_map.62.relaxed_ref, f32[2,16,128]{2,1,0:T(8,128)} %get-tuple-element.11.rims_ref, f32[5,16,128]{2,1,0:T(8,128)} %copy-done.4, f32[5,16,128]{2,1,0:T(8,128)} %copy-done.5, s32[8,16,128]{2,1,0:T(8,128)} %select_reduce_fusion.hits_ref), custom_call_target="tpu_custom_call" | custom-call | tf_op jit(solution)/shard_map/pallas_call | solution.py:353
  (16 shorter events, 0.1 us)
Async XLA Ops:
  0.6 13.0 %copy-start.6 = (s32[8,8,32]{2,1,0:T(8,128)S(1)}, s32[8,8,32]{2,1,0:T(8,128)}, u32[]{:S(2)}) copy-start(s32[8,8,32]{2,1,0:T(8,128)} %param.7) | copy-start | bytes 24580
  0.6 2.3 %collective-permute-start = (f32[19,8,8,128]{3,2,1,0:T(8,128)}, f32[19,8,8,128]{3,2,1,0:T(8,128)S(1)}, u32[]{:S(2)}, u32[]{:S(2)}) collective-permute-start(f32[19,8,8,128]{3,2,1,0:T(8,128)} %mine_ref.3), channel_id=1, source_target_pairs={{0,1},{1,0},{2,3},{3,2},{4,5},{5,4},{6,7},{7,6},{8,9},{9,8},{10,11... | collective-permute-start | bytes 1867784 | tf_op jit(solution)/shard_map/ppermute | solution.py:323
  3.0 0.8 %copy-start.1 = (f32[19,8,8,128]{3,2,1,0:T(8,128)}, f32[19,8,8,128]{3,2,1,0:T(8,128)S(1)}, u32[]{:S(2)}) copy-start(f32[19,8,8,128]{3,2,1,0:T(8,128)S(1)} %collective-permute-done.other_ref) | copy-start | bytes 1867780
  6.6 21.0 %all-to-all-start = ((f32[8,176,128]{2,1,0:T(8,128)}), f32[8,176,128]{2,1,0:T(8,128)S(1)}, u32[]{:S(2)}, u32[]{:S(2)}) async-start(f32[8,176,128]{2,1,0:T(8,128)} %shard_map.60), calls=%async_computation | async-start | bytes 1441792 | tf_op jit(solution)/shard_map/all_to_all | solution.py:342
  13.7 1.3 %collective-permute-start.3 = (s32[8,8,32]{2,1,0:T(8,128)S(1)}, s32[8,8,32]{2,1,0:T(8,128)S(1)}, u32[]{:S(2)}, u32[]{:S(2)}) collective-permute-start(s32[8,8,32]{2,1,0:T(8,128)S(1)} %copy-done.6), channel_id=1, source_target_pairs={{0,1},{1,0},{2,3},{3,2},{4,5},{5,4},{6,7},{7,6},{8,9},{9,8},{10,11... | collective-permute-start | bytes 24584 | tf_op jit(solution)/shard_map/ppermute | solution.py:324
  27.6 0.9 %copy-start = (f32[8,176,128]{2,1,0:T(8,128)}, f32[8,176,128]{2,1,0:T(8,128)S(1)}, u32[]{:S(2)}) copy-start(f32[8,176,128]{2,1,0:T(8,128)S(1)} %all-to-all-done.got_ref) | copy-start | bytes 2162692
  30.5 8.2 %collective-permute-start.1 = (f32[5,16,128]{2,1,0:T(8,128)}, f32[5,16,128]{2,1,0:T(8,128)S(1)}, u32[]{:S(2)}, u32[]{:S(2)}) collective-permute-start(f32[5,16,128]{2,1,0:T(8,128)} %get-tuple-element.9), channel_id=1, source_target_pairs={{0,16},{16,32},{32,48},{48,64},{64,80},{80,96},{96,112},{112,0},{1... | collective-permute-start | bytes 122888 | tf_op jit(solution)/shard_map/ppermute | solution.py:346
  31.1 7.6 %collective-permute-start.2 = (f32[5,16,128]{2,1,0:T(8,128)}, f32[5,16,128]{2,1,0:T(8,128)S(1)}, u32[]{:S(2)}, u32[]{:S(2)}) collective-permute-start(f32[5,16,128]{2,1,0:T(8,128)} %get-tuple-element.10), channel_id=1, source_target_pairs={{0,112},{16,0},{32,16},{48,32},{64,48},{80,64},{96,80},{112,96},{1... | collective-permute-start | bytes 122888 | tf_op jit(solution)/shard_map/ppermute | solution.py:347
  38.7 0.6 copy-start.2
  38.7 0.6 copy-start.3
  61.7 7.4 %collective-permute-start.4 = (f32[5,16,128]{2,1,0:T(8,128)}, f32[5,16,128]{2,1,0:T(8,128)S(1)}, u32[]{:S(2)}, u32[]{:S(2)}) collective-permute-start(f32[5,16,128]{2,1,0:T(8,128)} %get-tuple-element.12), channel_id=1, source_target_pairs={{0,16},{16,32},{32,48},{48,64},{64,80},{80,96},{96,112},{112,0},{1... | collective-permute-start | bytes 122888 | tf_op jit(solution)/shard_map/ppermute | solution.py:346
  61.7 7.4 %collective-permute-start.5 = (f32[5,16,128]{2,1,0:T(8,128)}, f32[5,16,128]{2,1,0:T(8,128)S(1)}, u32[]{:S(2)}, u32[]{:S(2)}) collective-permute-start(f32[5,16,128]{2,1,0:T(8,128)} %get-tuple-element.13), channel_id=1, source_target_pairs={{0,112},{16,0},{32,16},{48,32},{64,48},{80,64},{96,80},{112,96},{1... | collective-permute-start | bytes 122888 | tf_op jit(solution)/shard_map/ppermute | solution.py:347
  69.1 0.6 copy-start.4
  69.1 0.6 copy-start.5

commit v14 on v13

--- a/solution.py
+++ b/solution.py
@@ -149,7 +149,7 @@
     return me_y, (me_y + 1) % flow_cycle, (me_y - 1 + flow_cycle) % flow_cycle, lax.axis_index("gz")
 
 
-def _emit_relax(cells_of_x, slab_width, relaxed_ref, chunk_ref, depth):
+def _emit_relax(cells_of_x, slab_width, relaxed_ref, chunk_ref, depth, mix=None):
     lane = lax.broadcasted_iota(jnp.int32, (depth, LANES), 1)
     up_pack = jnp.zeros((depth, LANES), jnp.float32)
     down_pack = jnp.zeros((depth, LANES), jnp.float32)
@@ -173,14 +173,48 @@
             down_pack = jnp.where(lane == k, _roll(r[m], k, 1), down_pack)
     if chunk_ref is None:
         return
-    faces = jnp.concatenate([top.reshape(5 * depth, LANES), bottom.reshape(5 * depth, LANES)], axis=0)
-    _, after, before, _ = _positions()
-    to_next = jnp.full((depth, LANES), after, jnp.int32)
-    to_prev = jnp.full((depth, LANES), before, jnp.int32)
+    _write_shares(chunk_ref, top, bottom, up_pack, down_pack, mix, depth)
+
+
+def _write_shares(chunk_ref, top, bottom, up_pack, down_pack, mix, depth):
+    shift_ref, frac_ref, section = mix
     peers = chunk_ref.shape[0]
+    flow_cells = peers * LANES
+    me_y, after, before, _ = _positions()
+    offset = shift_ref[section]
+    shape = (depth, LANES)
+    lane = lax.broadcasted_iota(jnp.int32, shape, 1)
+    fraction = jnp.full(shape, frac_ref[section], jnp.int32).astype(jnp.float32) / 256.0
+    keep = 1.0 - fraction
+    here = jnp.full(shape, me_y, jnp.int32)
+
+    def rolled(tile, rel):
+        off = (rel + 2 * flow_cells) % LANES
+        return pltpu.roll(tile, (LANES - off) % LANES, 1), off
+
+    def share(r, off, rel, p):
+        start = (p * LANES + rel + 2 * flow_cells) % flow_cells
+        block = jnp.full(shape, start // LANES, jnp.int32)
+        first = lane < LANES - off
+        mine = jnp.where(first, block, (block + 1) % peers) == here
+        return jnp.where(mine, r, 0.0)
+
+    lows, highs = [], []
+    for i, m in enumerate(upward):
+        rel = -offset - velocity_table[m][1]
+        lows.append((rolled(top[i], rel), rel, rolled(top[i], rel - 1), rel - 1))
+    for i, m in enumerate(downward):
+        rel = offset - velocity_table[m][1]
+        highs.append((rolled(bottom[i], rel + 1), rel + 1, rolled(bottom[i], rel), rel))
     for p in range(peers):
-        chunk_ref[p, : FACE_ROWS * depth] = faces
-        chunk_ref[p, FACE_ROWS * depth :] = jnp.where(to_next == p, up_pack, jnp.where(to_prev == p, down_pack, 0.0))
+        for i, ((ra, oa), a, (rb, ob), b) in enumerate(lows):
+            chunk_ref[p, pl.ds(i * depth, depth)] = keep * share(ra, oa, a, p) + fraction * share(rb, ob, b, p)
+        for i, ((rc, oc), c, (rd, od), d) in enumerate(highs):
+            chunk_ref[p, pl.ds((5 + i) * depth, depth)] = fraction * share(rc, oc, c, p) + keep * share(rd, od, d, p)
+        up = jnp.full(shape, after, jnp.int32) == p
+        down = jnp.full(shape, before, jnp.int32) == p
+        chunk_ref[p, pl.ds(FACE_ROWS * depth, depth)] = jnp.where(up, up_pack, 0.0)
+        chunk_ref[p, pl.ds((FACE_ROWS + 1) * depth, depth)] = jnp.where(down, down_pack, 0.0)
 
 
 def _streamed(x, slab_width, relaxed_ref, rims_ref, low_ref, high_ref, hits_ref, depth, own=None):
@@ -225,7 +259,7 @@
     return result
 
 
-def _first_kernel(mine_ref, other_ref, *outs):
+def _first_kernel(section, shift_ref, frac_ref, mine_ref, other_ref, *outs):
     relaxed_ref, chunk_ref = (outs[0], None) if outs[0].shape[0] == 19 else (None, outs[0])
     slab_width, half = mine_ref.shape[1], mine_ref.shape[2]
     depth = 2 * half
@@ -238,14 +272,14 @@
             out.append(jnp.concatenate([jnp.where(lower, a, b), jnp.where(lower, b, a)], axis=0))
         return out
 
-    _emit_relax(cells, slab_width, relaxed_ref, chunk_ref, depth)
-
-
-def _middle_kernel(relaxed_ref, rims_ref, low_ref, high_ref, hits_ref, *outs):
+    _emit_relax(cells, slab_width, relaxed_ref, chunk_ref, depth, mix=(shift_ref, frac_ref, section))
+
+
+def _middle_kernel(section, shift_ref, frac_ref, relaxed_ref, rims_ref, low_ref, high_ref, hits_ref, *outs):
     next_ref, chunk_ref = (outs[0], None) if outs[0].shape[0] == 19 else (None, outs[0])
     slab_width, depth = relaxed_ref.shape[1], relaxed_ref.shape[2]
     cells = lambda x: _streamed(x, slab_width, relaxed_ref, rims_ref, low_ref, high_ref, hits_ref, depth)
-    _emit_relax(cells, slab_width, next_ref, chunk_ref, depth)
+    _emit_relax(cells, slab_width, next_ref, chunk_ref, depth, mix=(shift_ref, frac_ref, section))
 
 
 def _last_kernel(relaxed_ref, rims_ref, low_ref, high_ref, hits_ref, out_ref, density_ref):
@@ -260,41 +294,6 @@
         density_ref[x] = total_density(mine)
 
 
-def _window_kernel(section, shift_ref, frac_ref, got_ref, low_ref, high_ref, rims_ref):
-    peers, _, lanes = got_ref.shape
-    depth = low_ref.shape[1]
-    me_y, after, before, _ = _positions()
-    offset = shift_ref[section]
-    fraction = jnp.full((depth, lanes), frac_ref[section], jnp.int32).astype(jnp.float32) / 256.0
-    keep = 1.0 - fraction
-    flow_cells = peers * lanes
-    anchor = me_y * lanes
-    lane = lax.broadcasted_iota(jnp.int32, (depth, lanes), 1)
-
-    def window(row0, start):
-        start = (start + 2 * flow_cells) % flow_cells
-        block = start // lanes
-        off = start % lanes
-        after = (block + 1) % peers
-        shift = (lanes - off) % lanes
-        first = pltpu.roll(got_ref[block, pl.ds(row0, depth), :], shift, 1)
-        second = pltpu.roll(got_ref[after, pl.ds(row0, depth), :], shift, 1)
-        return jnp.where(lane < lanes - off, first, second)
-
-    for i, m in enumerate(upward):
-        step_y = velocity_table[m][1]
-        row0 = i * depth
-        a = anchor - offset - step_y
-        low_ref[i] = keep * window(row0, a) + fraction * window(row0, a - 1)
-    for i, m in enumerate(downward):
-        step_y = velocity_table[m][1]
-        row0 = (5 + i) * depth
-        c = anchor + offset - step_y
-        high_ref[i] = fraction * window(row0, c + 1) + keep * window(row0, c)
-    rims_ref[0] = got_ref[before, pl.ds(FACE_ROWS * depth, depth), :]
-    rims_ref[1] = got_ref[after, pl.ds(FACE_ROWS * depth, depth), :]
-
-
 def _vmem():
     return pl.BlockSpec(memory_space=pltpu.VMEM)
 
@@ -330,25 +329,27 @@
 
     f32 = jnp.float32
     full = jax.ShapeDtypeStruct((n_members, slab_width, depth, row_span), f32)
-    chunk = jax.ShapeDtypeStruct((flow_cycle, (FACE_ROWS + 1) * depth, row_span), f32)
-    ghost = jax.ShapeDtypeStruct((5, depth, row_span), f32)
-    rims = jax.ShapeDtypeStruct((2, depth, row_span), f32)
+    chunk = jax.ShapeDtypeStruct((flow_cycle, (FACE_ROWS + 2) * depth, row_span), f32)
     own = jax.ShapeDtypeStruct((n_members, slab_width, half_depth, row_span), f32)
     density = jax.ShapeDtypeStruct((slab_width, half_depth, row_span), f32)
 
-    chunks = _call(_first_kernel, 0, 2, chunk)(populations, other_states)
-    relaxed = _call(_first_kernel, 0, 2, full)(populations, other_states)
+    first_kernel = functools.partial(_first_kernel, 0)
+    chunks = _call(first_kernel, 2, 2, chunk)(le_shift, le_frac, populations, other_states)
+    relaxed = _call(first_kernel, 2, 2, full)(le_shift, le_frac, populations, other_states)
     for section in range(STEPS):
         got = lax.all_to_all(chunks, "gy", 0, 0, tiled=True)
-        low_send, high_send, rim_pair = _call(functools.partial(_window_kernel, section), 2, 1, (ghost, ghost, rims))(
-            le_shift, le_frac, got
-        )
+        total = jnp.sum(got, axis=0)
+        face_rows = 5 * depth
+        low_send = total[:face_rows].reshape(5, depth, row_span)
+        high_send = total[face_rows : 2 * face_rows].reshape(5, depth, row_span)
+        rim_pair = total[2 * face_rows :].reshape(2, depth, row_span)
         low_ghost = lax.ppermute(low_send, "gx", [(i, (i + 1) % slab_cycle) for i in range(slab_cycle)])
         high_ghost = lax.ppermute(high_send, "gx", [(i, (i - 1) % slab_cycle) for i in range(slab_cycle)])
         if section + 1 < STEPS:
-            args = (relaxed, rim_pair, low_ghost, high_ghost, hits)
-            chunks = _call(_middle_kernel, 0, 5, chunk)(*args)
-            relaxed = _call(_middle_kernel, 0, 5, full)(*args)
+            args = (le_shift, le_frac, relaxed, rim_pair, low_ghost, high_ghost, hits)
+            middle_kernel = functools.partial(_middle_kernel, section + 1)
+            chunks = _call(middle_kernel, 2, 5, chunk)(*args)
+            relaxed = _call(middle_kernel, 2, 5, full)(*args)
         else:
             final, dens = _call(_last_kernel, 0, 5, (own, density))(relaxed, rim_pair, low_ghost, high_ghost, hits)
     return (final, dens)

time: 72.6 us -> 71.6 us (0.986)
  Pallas kernels: 18.9 us -> 15.8 us
    pallas_call x6 -> x4, Pallas kernels: 16.5 us -> 13.4 us  [the longest x1 3.84 us: _per_device(): chunks = _call(middle_kernel, 2, 5, chunk)(*args)]
    slice x0 -> x4, local copies, waits for them, and re-layouts: none -> 1.22 us  [the longest x2 1.21 us: _per_device(): rim_pair = total[2 * face_rows:].reshape(2, depth, row_span)]
    unnamed x14 -> x12, local copies, waits for them, and re-layouts: 2.94 us -> 2.05 us
  transfers between devices with their start and end apart: 7 -> 7, of which waited for: 3 -> 3; matrix products, arithmetic and copies ran while one was open for 3% -> 5% of each run, Pallas kernels for 9% -> 9%
where the time goes in v14:
time: 71.6 us; the launch traced here: 71.2 us
  blocking collectives  17.6 us (25%)
  starting transfers between devices  15.8 us (22%)
  Pallas kernels  15.8 us (22%)
  waiting for transfers between devices  15.7 us (22%)
  local copies, waits for them, and re-layouts  3.28 us (5%)
  other arithmetic  1.21 us (2%)
  matrix products  1.07 us (1%)
  between operations  0.74 us (1%)
    all_to_all x1, blocking collectives, _per_device(): got = lax.all_to_all(chunks, 'gy', 0, 0, tiled=True)  17.6 us
    all_to_all x1, waiting for transfers between devices, _per_device(): got = lax.all_to_all(chunks, 'gy', 0, 0, tiled=True)  12.2 us
    ppermute x2, starting transfers between devices, _per_device(): lax.ppermute(high_send, 'gx', [(i, (i - 1) % slab_cycle) for i in range(s...  7.68 us
    all_to_all x1, starting transfers between devices, _per_device(): got = lax.all_to_all(chunks, 'gy', 0, 0, tiled=True)  7.17 us
    pallas_call x1, Pallas kernels, _per_device(): chunks = _call(middle_kernel, 2, 5, chunk)(*args)  3.84 us
    pallas_call x1, Pallas kernels, _per_device(): relaxed = _call(middle_kernel, 2, 5, full)(*args)  3.29 us
    pallas_call x1, Pallas kernels, _per_device(): _call(first_kernel, 2, 2, chunk)  3.19 us
    pallas_call x1, Pallas kernels, _per_device(): _call(first_kernel, 2, 2, full)  3.03 us
  transfers between devices with their start and end apart: 7, of which 3 were waited for; matrix products, arithmetic and copies ran while one was open for 5% of the time, Pallas kernels for 9%

profile of v14, /device:TPU:0, one launch (start us, length us, event | category | flops | bytes accessed | tf_op | source)
XLA Modules:
  0.0 71.2 jit_solution(7736716994833188353)
XLA Ops:
  0.6 0.1 collective-permute-start
  0.7 2.2 %collective-permute-done.other_ref = f32[19,8,8,128]{3,2,1,0:T(8,128)S(1)} collective-permute-done((f32[19,8,8,128]{3,2,1,0:T(8,128)}, f32[19,8,8,128]{3,2,1,0:T(8,128)S(1)}, u32[]{:S(2)}, u32[]{:S(2)}) %collective-permute-start) | collective-permute-done | bytes 622624 | tf_op jit(solution)/shard_map/ppermute | solution.py:322
  3.0 0.8 %copy-done = f32[19,8,8,128]{3,2,1,0:T(8,128)} copy-done((f32[19,8,8,128]{3,2,1,0:T(8,128)}, f32[19,8,8,128]{3,2,1,0:T(8,128)S(1)}, u32[]{:S(2)}) %copy-start) | copy-done | bytes 622616
  3.8 3.2 %shard_map.60 = f32[8,192,128]{2,1,0:T(8,128)} custom-call(s32[2]{0:T(128)} %shift_ref.7, s32[2]{0:T(128)} %frac_ref.7, f32[19,8,8,128]{3,2,1,0:T(8,128)} %mine_ref.3, f32[19,8,8,128]{3,2,1,0:T(8,128)} %copy-done), custom_call_target="tpu_custom_call" | custom-call | tf_op jit(solution)/shard_map/pallas_call | solution.py:337
  7.0 7.2 %all-to-all-start = ((f32[8,192,128]{2,1,0:T(8,128)}), f32[8,192,128]{2,1,0:T(8,128)S(1)}, u32[]{:S(2)}, u32[]{:S(2)}) async-start(f32[8,192,128]{2,1,0:T(8,128)} %shard_map.60), calls=%async_computation | async-start | bytes 1572864 | tf_op jit(solution)/shard_map/all_to_all | solution.py:340
  14.2 0.1 collective-permute-start.3
  14.3 1.2 %collective-permute-done.3 = s32[8,8,32]{2,1,0:T(8,128)S(1)} collective-permute-done((s32[8,8,32]{2,1,0:T(8,128)S(1)}, s32[8,8,32]{2,1,0:T(8,128)S(1)}, u32[]{:S(2)}, u32[]{:S(2)}) %collective-permute-start.3) | collective-permute-done | bytes 8224 | tf_op jit(solution)/shard_map/ppermute | solution.py:323
  15.5 0.1 add_select_fusion
  15.5 1.1 %fusion.1 = u16[8,128,19]{1,2,0:T(8,128)(2,1)S(1)} fusion(s32[8,16,32]{2,1,0:T(8,128)S(1)} %get-tuple-element.7, s32[8,16,32]{2,1,0:T(8,128)S(1)} %get-tuple-element.6), kind=kOutput, calls=%fused_computation.6 | convolution fusion | flops 22062080 | bytes 71680 | tf_op jit(solution)/shard_map/xzml,xzly->xzym/dot_general | solution.py:116
  16.6 12.2 %all-to-all-done = f32[8,192,128]{2,1,0:T(8,128)S(1)} async-done(((f32[8,192,128]{2,1,0:T(8,128)}), f32[8,192,128]{2,1,0:T(8,128)S(1)}, u32[]{:S(2)}, u32[]{:S(2)}) %all-to-all-start) | async-done | bytes 786464 | tf_op jit(solution)/shard_map/all_to_all | solution.py:340
  28.9 0.7 collective-permute-start.1
  29.6 3.6 %collective-permute-start.2 = (f32[5,16,128]{2,1,0:T(8,128)S(1)}, f32[5,16,128]{2,1,0:T(8,128)S(1)}, u32[]{:S(2)}, u32[]{:S(2)}) collective-permute-start(f32[5,16,128]{2,1,0:T(8,128)S(1)} %bitcast.9), channel_id=1, source_target_pairs={{0,112},{16,0},{32,16},{48,32},{64,48},{80,64},{96,80},{112,96},{1... | collective-permute-start | bytes 122888 | tf_op jit(solution)/shard_map/ppermute | solution.py:347
  33.1 1.0 %select_reduce_fusion.hits_ref = s32[8,16,128]{2,1,0:T(8,128)} fusion(s32[19]{0:T(128)S(1)} %iota_shift-left_fusion, u16[8,128,19]{1,2,0:T(8,128)(2,1)S(1)} %fusion.1), kind=kLoop, calls=%fused_computation.4 | loop fusion | flops 1851392 | bytes 104524 | tf_op jit(solution)/shard_map/reduce_sum | solution.py:118
  34.2 3.0 %shard_map.59.relaxed_ref = f32[19,8,16,128]{3,2,1,0:T(8,128)} custom-call(s32[2]{0:T(128)} %shift_ref.7, s32[2]{0:T(128)} %frac_ref.7, f32[19,8,8,128]{3,2,1,0:T(8,128)} %mine_ref.3, f32[19,8,8,128]{3,2,1,0:T(8,128)} %copy-done), custom_call_target="tpu_custom_call" | custom-call | tf_op jit(solution)/shard_map/pallas_call | solution.py:338
  37.2 0.6 slice.24
  37.8 0.6 copy-done.1
  38.4 3.8 %shard_map.62 = f32[8,192,128]{2,1,0:T(8,128)} custom-call(s32[2]{0:T(128)} %shift_ref.7, s32[2]{0:T(128)} %frac_ref.7, f32[19,8,16,128]{3,2,1,0:T(8,128)} %shard_map.59.relaxed_ref, f32[2,16,128]{2,1,0:T(8,128)} %bitcast.6, f32[5,16,128]{2,1,0:T(8,128)} %copy-done.1, f32[5,16,128]{2,1,0:T(8,128)} %copy-done.2, s32[8,16,128]{2,1,0:T(8,128)} %select_reduce_fusion.hits_ref), custom_call_target="tpu_custom_call" | custom-call | tf_op jit(solution)/shard_map/pallas_call | solution.py:351
  42.3 17.6 %all_to_all.10 = f32[8,192,128]{2,1,0:T(8,128)S(1)} all-to-all(f32[8,192,128]{2,1,0:T(8,128)} %shard_map.62), channel_id=1, replica_groups=mesh['gx'=8,'gy'=8,'gz'=2] {'gy'}, dimensions={0} | all-to-all | bytes 1572864 | tf_op jit(solution)/shard_map/all_to_all | solution.py:340
  60.0 0.1 collective-permute-start.4
  60.1 4.1 %collective-permute-start.5 = (f32[5,16,128]{2,1,0:T(8,128)S(1)}, f32[5,16,128]{2,1,0:T(8,128)S(1)}, u32[]{:S(2)}, u32[]{:S(2)}) collective-permute-start(f32[5,16,128]{2,1,0:T(8,128)S(1)} %bitcast.10), channel_id=1, source_target_pairs={{0,112},{16,0},{32,16},{48,32},{64,48},{80,64},{96,80},{112,96},{1... | collective-permute-start | bytes 122888 | tf_op jit(solution)/shard_map/ppermute | solution.py:347
  64.2 3.3 %shard_map.61.relaxed_ref = f32[19,8,16,128]{3,2,1,0:T(8,128)} custom-call(s32[2]{0:T(128)} %shift_ref.7, s32[2]{0:T(128)} %frac_ref.7, f32[19,8,16,128]{3,2,1,0:T(8,128)} %shard_map.59.relaxed_ref, f32[2,16,128]{2,1,0:T(8,128)} %bitcast.7, f32[5,16,128]{2,1,0:T(8,128)} %copy-done.1, f32[5,16,128]{2,1,0:T(8,128)} %copy-done.2, ...), custom_call_target="tpu_custom_call" | custom-call | tf_op jit(solution)/shard_map/pallas_call | solution.py:352
  67.5 0.6 slice.27
  68.1 0.6 copy-done.3
  68.7 2.5 %shard_map.63 = (f32[19,8,8,128]{3,2,1,0:T(8,128)}, f32[8,8,128]{2,1,0:T(8,128)}) custom-call(f32[19,8,16,128]{3,2,1,0:T(8,128)} %shard_map.61.relaxed_ref, f32[2,16,128]{2,1,0:T(8,128)} %bitcast.8, f32[5,16,128]{2,1,0:T(8,128)} %copy-done.3, f32[5,16,128]{2,1,0:T(8,128)} %copy-done.4, s32[8,16,128]{2,1,0:T(8,128)} %select_reduce_fusion.hits_ref), custom_call_target="tpu_custom_call" | custom-call | tf_op jit(solution)/shard_map/pallas_call | solution.py:354
  (18 shorter events, 0.1 us)
Async XLA Ops:
  0.6 2.3 %collective-permute-start = (f32[19,8,8,128]{3,2,1,0:T(8,128)}, f32[19,8,8,128]{3,2,1,0:T(8,128)S(1)}, u32[]{:S(2)}, u32[]{:S(2)}) collective-permute-start(f32[19,8,8,128]{3,2,1,0:T(8,128)} %mine_ref.3), channel_id=1, source_target_pairs={{0,1},{1,0},{2,3},{3,2},{4,5},{5,4},{6,7},{7,6},{8,9},{9,8},{10,11... | collective-permute-start | bytes 1867784 | tf_op jit(solution)/shard_map/ppermute | solution.py:322
  3.0 0.8 %copy-start = (f32[19,8,8,128]{3,2,1,0:T(8,128)}, f32[19,8,8,128]{3,2,1,0:T(8,128)S(1)}, u32[]{:S(2)}) copy-start(f32[19,8,8,128]{3,2,1,0:T(8,128)S(1)} %collective-permute-done.other_ref) | copy-start | bytes 1867780
  7.0 7.2 %copy-start.5 = (s32[8,8,32]{2,1,0:T(8,128)S(1)}, s32[8,8,32]{2,1,0:T(8,128)}, u32[]{:S(2)}) copy-start(s32[8,8,32]{2,1,0:T(8,128)} %param.7) | copy-start | bytes 24580
  7.0 21.9 %all-to-all-start = ((f32[8,192,128]{2,1,0:T(8,128)}), f32[8,192,128]{2,1,0:T(8,128)S(1)}, u32[]{:S(2)}, u32[]{:S(2)}) async-start(f32[8,192,128]{2,1,0:T(8,128)} %shard_map.60), calls=%async_computation | async-start | bytes 1572864 | tf_op jit(solution)/shard_map/all_to_all | solution.py:340
  14.2 1.3 %collective-permute-start.3 = (s32[8,8,32]{2,1,0:T(8,128)S(1)}, s32[8,8,32]{2,1,0:T(8,128)S(1)}, u32[]{:S(2)}, u32[]{:S(2)}) collective-permute-start(s32[8,8,32]{2,1,0:T(8,128)S(1)} %copy-done.5), channel_id=1, source_target_pairs={{0,1},{1,0},{2,3},{3,2},{4,5},{5,4},{6,7},{7,6},{8,9},{9,8},{10,11... | collective-permute-start | bytes 24584 | tf_op jit(solution)/shard_map/ppermute | solution.py:323
  28.9 8.9 %collective-permute-start.1 = (f32[5,16,128]{2,1,0:T(8,128)S(1)}, f32[5,16,128]{2,1,0:T(8,128)S(1)}, u32[]{:S(2)}, u32[]{:S(2)}) collective-permute-start(f32[5,16,128]{2,1,0:T(8,128)S(1)} %bitcast.11), channel_id=1, source_target_pairs={{0,16},{16,32},{32,48},{48,64},{64,80},{80,96},{96,112},{112,0},{1... | collective-permute-start | bytes 122888 | tf_op jit(solution)/shard_map/ppermute | solution.py:346
  29.6 8.2 %collective-permute-start.2 = (f32[5,16,128]{2,1,0:T(8,128)S(1)}, f32[5,16,128]{2,1,0:T(8,128)S(1)}, u32[]{:S(2)}, u32[]{:S(2)}) collective-permute-start(f32[5,16,128]{2,1,0:T(8,128)S(1)} %bitcast.9), channel_id=1, source_target_pairs={{0,112},{16,0},{32,16},{48,32},{64,48},{80,64},{96,80},{112,96},{1... | collective-permute-start | bytes 122888 | tf_op jit(solution)/shard_map/ppermute | solution.py:347
  37.8 0.6 copy-start.1
  37.8 0.6 copy-start.2
  60.0 8.1 %collective-permute-start.4 = (f32[5,16,128]{2,1,0:T(8,128)S(1)}, f32[5,16,128]{2,1,0:T(8,128)S(1)}, u32[]{:S(2)}, u32[]{:S(2)}) collective-permute-start(f32[5,16,128]{2,1,0:T(8,128)S(1)} %bitcast.12), channel_id=1, source_target_pairs={{0,16},{16,32},{32,48},{48,64},{64,80},{80,96},{96,112},{112,0},{1... | collective-permute-start | bytes 122888 | tf_op jit(solution)/shard_map/ppermute | solution.py:346
  60.1 8.0 %collective-permute-start.5 = (f32[5,16,128]{2,1,0:T(8,128)S(1)}, f32[5,16,128]{2,1,0:T(8,128)S(1)}, u32[]{:S(2)}, u32[]{:S(2)}) collective-permute-start(f32[5,16,128]{2,1,0:T(8,128)S(1)} %bitcast.10), channel_id=1, source_target_pairs={{0,112},{16,0},{32,16},{48,32},{64,48},{80,64},{96,80},{112,96},{1... | collective-permute-start | bytes 122888 | tf_op jit(solution)/shard_map/ppermute | solution.py:347
  68.1 0.6 copy-start.3
  68.1 0.6 copy-start.4

commit v15 on v14

--- a/solution.py
+++ b/solution.py
@@ -213,8 +213,7 @@
             chunk_ref[p, pl.ds((5 + i) * depth, depth)] = fraction * share(rc, oc, c, p) + keep * share(rd, od, d, p)
         up = jnp.full(shape, after, jnp.int32) == p
         down = jnp.full(shape, before, jnp.int32) == p
-        chunk_ref[p, pl.ds(FACE_ROWS * depth, depth)] = jnp.where(up, up_pack, 0.0)
-        chunk_ref[p, pl.ds((FACE_ROWS + 1) * depth, depth)] = jnp.where(down, down_pack, 0.0)
+        chunk_ref[p, pl.ds(FACE_ROWS * depth, depth)] = jnp.where(up, up_pack, jnp.where(down, down_pack, 0.0))
 
 
 def _streamed(x, slab_width, relaxed_ref, rims_ref, low_ref, high_ref, hits_ref, depth, own=None):
@@ -329,7 +328,7 @@
 
     f32 = jnp.float32
     full = jax.ShapeDtypeStruct((n_members, slab_width, depth, row_span), f32)
-    chunk = jax.ShapeDtypeStruct((flow_cycle, (FACE_ROWS + 2) * depth, row_span), f32)
+    chunk = jax.ShapeDtypeStruct((flow_cycle, (FACE_ROWS + 1) * depth, row_span), f32)
     own = jax.ShapeDtypeStruct((n_members, slab_width, half_depth, row_span), f32)
     density = jax.ShapeDtypeStruct((slab_width, half_depth, row_span), f32)
 
@@ -338,11 +337,17 @@
     relaxed = _call(first_kernel, 2, 2, full)(le_shift, le_frac, populations, other_states)
     for section in range(STEPS):
         got = lax.all_to_all(chunks, "gy", 0, 0, tiled=True)
-        total = jnp.sum(got, axis=0)
         face_rows = 5 * depth
+        total = jnp.sum(got[:, : 2 * face_rows], axis=0)
         low_send = total[:face_rows].reshape(5, depth, row_span)
-        high_send = total[face_rows : 2 * face_rows].reshape(5, depth, row_span)
-        rim_pair = total[2 * face_rows :].reshape(2, depth, row_span)
+        high_send = total[face_rows:].reshape(5, depth, row_span)
+        rim_rows = got[:, 2 * face_rows :]
+        rim_pair = jnp.stack(
+            [
+                lax.dynamic_index_in_dim(rim_rows, (me_y - 1 + flow_cycle) % flow_cycle, 0, keepdims=False),
+                lax.dynamic_index_in_dim(rim_rows, (me_y + 1) % flow_cycle, 0, keepdims=False),
+            ]
+        )
         low_ghost = lax.ppermute(low_send, "gx", [(i, (i + 1) % slab_cycle) for i in range(slab_cycle)])
         high_ghost = lax.ppermute(high_send, "gx", [(i, (i - 1) % slab_cycle) for i in range(slab_cycle)])
         if section + 1 < STEPS:

time: 71.6 us -> 65.8 us (0.919)
  blocking collectives: 17.6 us -> 0 us
  waiting for transfers between devices: 15.7 us -> 23 us
  starting transfers between devices: 15.8 us -> 19.2 us
  other arithmetic: 1.21 us -> 2.41 us
    all_to_all x1 -> x0, blocking collectives: 17.6 us -> none  [_per_device(): got = lax.all_to_all(chunks, 'gy', 0, 0, tiled=True)]
    all_to_all x1 -> x2, waiting for transfers between devices: 12.2 us -> 16.9 us  [_per_device(): got = lax.all_to_all(chunks, 'gy', 0, 0, tiled=True)]
    all_to_all x1 -> x2, starting transfers between devices: 7.17 us -> 10.6 us  [_per_device(): got = lax.all_to_all(chunks, 'gy', 0, 0, tiled=True)]
    ppermute x2, waiting for transfers between devices: 0.01 us -> 2.7 us  [_per_device(): lax.ppermute(low_send, 'gx', [(i, (i + 1) % slab_cycle) for i in range(sl...]
    unnamed x12, local copies, waits for them, and re-layouts: 2.05 us -> 3.27 us
    another operation x0 -> x2, other arithmetic: none -> 1.21 us  [_per_device(): jnp.stack([lax.dynamic_index_in_dim(rim_rows, (me_y - 1 + flow_cycle) % f...]
    slice x4, local copies, waits for them, and re-layouts: 1.22 us -> 0.03 us  [the longest x2 0.02 us: _per_device(): high_send = total[face_rows:].reshape(5, depth, row_span)]
  transfers between devices with their start and end apart: 7 -> 8, of which waited for: 3 -> 6; matrix products, arithmetic and copies ran while one was open for 5% -> 5% of each run, Pallas kernels for 9% -> 10%
where the time goes in v15:
time: 65.8 us; the launch traced here: 65.4 us
  waiting for transfers between devices  23 us (35%)
  starting transfers between devices  19.2 us (29%)
  Pallas kernels  15.8 us (24%)
  local copies, waits for them, and re-layouts  3.31 us (5%)
  other arithmetic  2.41 us (4%)
  matrix products  1.07 us (2%)
  between operations  0.75 us (1%)
    all_to_all x2, waiting for transfers between devices, _per_device(): got = lax.all_to_all(chunks, 'gy', 0, 0, tiled=True)  16.9 us
    all_to_all x2, starting transfers between devices, _per_device(): got = lax.all_to_all(chunks, 'gy', 0, 0, tiled=True)  10.6 us
    ppermute x2, starting transfers between devices, _per_device(): lax.ppermute(high_send, 'gx', [(i, (i - 1) % slab_cycle) for i in range(s...  7.21 us
    pallas_call x1, Pallas kernels, _per_device(): chunks = _call(middle_kernel, 2, 5, chunk)(*args)  3.81 us
    pallas_call x1, Pallas kernels, _per_device(): relaxed = _call(middle_kernel, 2, 5, full)(*args)  3.3 us
    unnamed x12, local copies, waits for them, and re-layouts  3.27 us
    pallas_call x1, Pallas kernels, _per_device(): _call(first_kernel, 2, 2, chunk)  3.16 us
    pallas_call x1, Pallas kernels, _per_device(): _call(first_kernel, 2, 2, full)  3.03 us
  transfers between devices with their start and end apart: 8, of which 6 were waited for; matrix products, arithmetic and copies ran while one was open for 5% of the time, Pallas kernels for 10%

profile of v15, /device:TPU:0, one launch (start us, length us, event | category | flops | bytes accessed | tf_op | source)
XLA Modules:
  0.0 65.4 jit_solution(17020246239273544198)
XLA Ops:
  0.7 2.2 %collective-permute-done.other_ref = f32[19,8,8,128]{3,2,1,0:T(8,128)S(1)} collective-permute-done((f32[19,8,8,128]{3,2,1,0:T(8,128)}, f32[19,8,8,128]{3,2,1,0:T(8,128)S(1)}, u32[]{:S(2)}, u32[]{:S(2)}) %collective-permute-start) | collective-permute-done | bytes 622624 | tf_op jit(solution)/shard_map/ppermute | solution.py:321
  3.0 0.8 %copy-done = f32[19,8,8,128]{3,2,1,0:T(8,128)} copy-done((f32[19,8,8,128]{3,2,1,0:T(8,128)}, f32[19,8,8,128]{3,2,1,0:T(8,128)S(1)}, u32[]{:S(2)}) %copy-start) | copy-done | bytes 622616
  3.8 3.2 %shard_map.60 = f32[8,176,128]{2,1,0:T(8,128)} custom-call(s32[2]{0:T(128)} %shift_ref.7, s32[2]{0:T(128)} %frac_ref.7, f32[19,8,8,128]{3,2,1,0:T(8,128)} %mine_ref.3, f32[19,8,8,128]{3,2,1,0:T(8,128)} %copy-done), custom_call_target="tpu_custom_call" | custom-call | tf_op jit(solution)/shard_map/pallas_call | solution.py:336
  7.0 7.0 %all-to-all-start = ((f32[8,176,128]{2,1,0:T(8,128)}), f32[8,176,128]{2,1,0:T(8,128)S(1)}, u32[]{:S(2)}, u32[]{:S(2)}) async-start(f32[8,176,128]{2,1,0:T(8,128)} %shard_map.60), calls=%async_computation | async-start | bytes 1441792 | tf_op jit(solution)/shard_map/all_to_all | solution.py:339
  14.2 1.2 %collective-permute-done.3 = s32[8,8,32]{2,1,0:T(8,128)S(1)} collective-permute-done((s32[8,8,32]{2,1,0:T(8,128)S(1)}, s32[8,8,32]{2,1,0:T(8,128)S(1)}, u32[]{:S(2)}, u32[]{:S(2)}) %collective-permute-start.3) | collective-permute-done | bytes 8224 | tf_op jit(solution)/shard_map/ppermute | solution.py:322
  15.4 1.1 %fusion.1 = u16[8,128,19]{1,2,0:T(8,128)(2,1)S(1)} fusion(s32[8,16,32]{2,1,0:T(8,128)S(1)} %get-tuple-element.9, s32[8,16,32]{2,1,0:T(8,128)S(1)} %get-tuple-element.8), kind=kOutput, calls=%fused_computation.6 | convolution fusion | flops 22062080 | bytes 71680 | tf_op jit(solution)/shard_map/xzml,xzly->xzym/dot_general | solution.py:116
  16.5 1.0 %select_reduce_fusion.hits_ref = s32[8,16,128]{2,1,0:T(8,128)} fusion(s32[19]{0:T(128)S(1)} %iota_shift-left_fusion, u16[8,128,19]{1,2,0:T(8,128)(2,1)S(1)} %fusion.1), kind=kLoop, calls=%fused_computation.4 | loop fusion | flops 1851392 | bytes 104524 | tf_op jit(solution)/shard_map/reduce_sum | solution.py:118
  17.5 3.0 %shard_map.59.relaxed_ref = f32[19,8,16,128]{3,2,1,0:T(8,128)} custom-call(s32[2]{0:T(128)} %shift_ref.7, s32[2]{0:T(128)} %frac_ref.7, f32[19,8,8,128]{3,2,1,0:T(8,128)} %mine_ref.3, f32[19,8,8,128]{3,2,1,0:T(8,128)} %copy-done), custom_call_target="tpu_custom_call" | custom-call | tf_op jit(solution)/shard_map/pallas_call | solution.py:337
  20.5 7.5 %all-to-all-done = f32[8,176,128]{2,1,0:T(8,128)S(1)} async-done(((f32[8,176,128]{2,1,0:T(8,128)}), f32[8,176,128]{2,1,0:T(8,128)S(1)}, u32[]{:S(2)}, u32[]{:S(2)}) %all-to-all-start) | async-done | bytes 720928 | tf_op jit(solution)/shard_map/all_to_all | solution.py:339
  28.1 0.7 %collective-permute-start.1 = (f32[5,16,128]{2,1,0:T(8,128)S(1)}, f32[5,16,128]{2,1,0:T(8,128)S(1)}, u32[]{:S(2)}, u32[]{:S(2)}) collective-permute-start(f32[5,16,128]{2,1,0:T(8,128)S(1)} %bitcast.7), channel_id=1, source_target_pairs={{0,16},{16,32},{32,48},{48,64},{64,80},{80,96},{96,112},{112,0},{1... | collective-permute-start | bytes 122888 | tf_op jit(solution)/shard_map/ppermute | solution.py:351
  28.7 3.6 %collective-permute-start.2 = (f32[5,16,128]{2,1,0:T(8,128)S(1)}, f32[5,16,128]{2,1,0:T(8,128)S(1)}, u32[]{:S(2)}, u32[]{:S(2)}) collective-permute-start(f32[5,16,128]{2,1,0:T(8,128)S(1)} %bitcast.5), channel_id=1, source_target_pairs={{0,112},{16,0},{32,16},{48,32},{64,48},{80,64},{96,80},{112,96},{1... | collective-permute-start | bytes 122888 | tf_op jit(solution)/shard_map/ppermute | solution.py:352
  32.3 0.6 pad_maximum_fusion.rims_ref
  32.9 1.3 %collective-permute-done.1.low_ref = f32[5,16,128]{2,1,0:T(8,128)S(1)} collective-permute-done((f32[5,16,128]{2,1,0:T(8,128)S(1)}, f32[5,16,128]{2,1,0:T(8,128)S(1)}, u32[]{:S(2)}, u32[]{:S(2)}) %collective-permute-start.1) | collective-permute-done | bytes 40992 | tf_op jit(solution)/shard_map/ppermute | solution.py:351
  34.2 0.6 copy-done.1
  34.9 0.6 copy-done.2
  35.5 3.8 %shard_map.62 = f32[8,176,128]{2,1,0:T(8,128)} custom-call(s32[2]{0:T(128)} %shift_ref.7, s32[2]{0:T(128)} %frac_ref.7, f32[19,8,16,128]{3,2,1,0:T(8,128)} %shard_map.59.relaxed_ref, f32[2,16,128]{2,1,0:T(8,128)} %pad_maximum_fusion.rims_ref, f32[5,16,128]{2,1,0:T(8,128)} %copy-done.1, f32[5,16,128]{2,1,0:T(8,128)} %copy-done.2, ...), custom_call_target="tpu_custom_call" | custom-call | tf_op jit(solution)/shard_map/pallas_call | solution.py:356
  39.3 3.5 %all-to-all-start.1 = ((f32[8,176,128]{2,1,0:T(8,128)}), f32[8,176,128]{2,1,0:T(8,128)S(1)}, u32[]{:S(2)}, u32[]{:S(2)}) async-start(f32[8,176,128]{2,1,0:T(8,128)} %shard_map.62), calls=%async_computation.1 | async-start | bytes 1441792 | tf_op jit(solution)/shard_map/all_to_all | solution.py:339
  42.8 3.3 %shard_map.61.relaxed_ref = f32[19,8,16,128]{3,2,1,0:T(8,128)} custom-call(s32[2]{0:T(128)} %shift_ref.7, s32[2]{0:T(128)} %frac_ref.7, f32[19,8,16,128]{3,2,1,0:T(8,128)} %shard_map.59.relaxed_ref, f32[2,16,128]{2,1,0:T(8,128)} %pad_maximum_fusion.rims_ref, f32[5,16,128]{2,1,0:T(8,128)} %copy-done.1, f32[5,16,128]{2,1,0:T(8,128)} %copy-done.2, ...), custom_call_target="tpu_custom_call" | custom-call | tf_op jit(solution)/shard_map/pallas_call | solution.py:357
  46.1 9.4 %all-to-all-done.1 = f32[8,176,128]{2,1,0:T(8,128)S(1)} async-done(((f32[8,176,128]{2,1,0:T(8,128)}), f32[8,176,128]{2,1,0:T(8,128)S(1)}, u32[]{:S(2)}, u32[]{:S(2)}) %all-to-all-start.1) | async-done | bytes 720928 | tf_op jit(solution)/shard_map/all_to_all | solution.py:339
  56.1 3.7 %collective-permute-start.5 = (f32[5,16,128]{2,1,0:T(8,128)S(1)}, f32[5,16,128]{2,1,0:T(8,128)S(1)}, u32[]{:S(2)}, u32[]{:S(2)}) collective-permute-start(f32[5,16,128]{2,1,0:T(8,128)S(1)} %bitcast.4), channel_id=1, source_target_pairs={{0,112},{16,0},{32,16},{48,32},{64,48},{80,64},{96,80},{112,96},{1... | collective-permute-start | bytes 122888 | tf_op jit(solution)/shard_map/ppermute | solution.py:352
  59.8 0.6 pad_maximum_fusion.1.rims_ref
  60.4 1.4 %collective-permute-done.4.low_ref = f32[5,16,128]{2,1,0:T(8,128)S(1)} collective-permute-done((f32[5,16,128]{2,1,0:T(8,128)S(1)}, f32[5,16,128]{2,1,0:T(8,128)S(1)}, u32[]{:S(2)}, u32[]{:S(2)}) %collective-permute-start.4) | collective-permute-done | bytes 40992 | tf_op jit(solution)/shard_map/ppermute | solution.py:351
  62.4 0.6 copy-done.4
  63.0 2.5 %shard_map.63 = (f32[19,8,8,128]{3,2,1,0:T(8,128)}, f32[8,8,128]{2,1,0:T(8,128)}) custom-call(f32[19,8,16,128]{3,2,1,0:T(8,128)} %shard_map.61.relaxed_ref, f32[2,16,128]{2,1,0:T(8,128)} %pad_maximum_fusion.1.rims_ref, f32[5,16,128]{2,1,0:T(8,128)} %copy-done.3, f32[5,16,128]{2,1,0:T(8,128)} %copy-done.4, s32[8,16,128]{2,1,0:T(8,128)} %select_reduce_fusion.hits_ref), custom_call_target="tpu_custom_call" | custom-call | tf_op jit(solution)/shard_map/pallas_call | solution.py:359
  (23 shorter events, 1.5 us)
Async XLA Ops:
  0.6 13.4 %copy-start.5 = (s32[8,8,32]{2,1,0:T(8,128)S(1)}, s32[8,8,32]{2,1,0:T(8,128)}, u32[]{:S(2)}) copy-start(s32[8,8,32]{2,1,0:T(8,128)} %param.7) | copy-start | bytes 24580
  0.6 2.3 %collective-permute-start = (f32[19,8,8,128]{3,2,1,0:T(8,128)}, f32[19,8,8,128]{3,2,1,0:T(8,128)S(1)}, u32[]{:S(2)}, u32[]{:S(2)}) collective-permute-start(f32[19,8,8,128]{3,2,1,0:T(8,128)} %mine_ref.3), channel_id=1, source_target_pairs={{0,1},{1,0},{2,3},{3,2},{4,5},{5,4},{6,7},{7,6},{8,9},{9,8},{10,11... | collective-permute-start | bytes 1867784 | tf_op jit(solution)/shard_map/ppermute | solution.py:321
  3.0 0.8 %copy-start = (f32[19,8,8,128]{3,2,1,0:T(8,128)}, f32[19,8,8,128]{3,2,1,0:T(8,128)S(1)}, u32[]{:S(2)}) copy-start(f32[19,8,8,128]{3,2,1,0:T(8,128)S(1)} %collective-permute-done.other_ref) | copy-start | bytes 1867780
  7.0 21.0 %all-to-all-start = ((f32[8,176,128]{2,1,0:T(8,128)}), f32[8,176,128]{2,1,0:T(8,128)S(1)}, u32[]{:S(2)}, u32[]{:S(2)}) async-start(f32[8,176,128]{2,1,0:T(8,128)} %shard_map.60), calls=%async_computation | async-start | bytes 1441792 | tf_op jit(solution)/shard_map/all_to_all | solution.py:339
  14.0 1.3 %collective-permute-start.3 = (s32[8,8,32]{2,1,0:T(8,128)S(1)}, s32[8,8,32]{2,1,0:T(8,128)S(1)}, u32[]{:S(2)}, u32[]{:S(2)}) collective-permute-start(s32[8,8,32]{2,1,0:T(8,128)S(1)} %copy-done.5), channel_id=1, source_target_pairs={{0,1},{1,0},{2,3},{3,2},{4,5},{5,4},{6,7},{7,6},{8,9},{9,8},{10,11... | collective-permute-start | bytes 24584 | tf_op jit(solution)/shard_map/ppermute | solution.py:322
  28.1 6.2 %collective-permute-start.1 = (f32[5,16,128]{2,1,0:T(8,128)S(1)}, f32[5,16,128]{2,1,0:T(8,128)S(1)}, u32[]{:S(2)}, u32[]{:S(2)}) collective-permute-start(f32[5,16,128]{2,1,0:T(8,128)S(1)} %bitcast.7), channel_id=1, source_target_pairs={{0,16},{16,32},{32,48},{48,64},{64,80},{80,96},{96,112},{112,0},{1... | collective-permute-start | bytes 122888 | tf_op jit(solution)/shard_map/ppermute | solution.py:351
  28.7 5.5 %collective-permute-start.2 = (f32[5,16,128]{2,1,0:T(8,128)S(1)}, f32[5,16,128]{2,1,0:T(8,128)S(1)}, u32[]{:S(2)}, u32[]{:S(2)}) collective-permute-start(f32[5,16,128]{2,1,0:T(8,128)S(1)} %bitcast.5), channel_id=1, source_target_pairs={{0,112},{16,0},{32,16},{48,32},{64,48},{80,64},{96,80},{112,96},{1... | collective-permute-start | bytes 122888 | tf_op jit(solution)/shard_map/ppermute | solution.py:352
  34.2 0.6 copy-start.1
  34.9 0.6 copy-start.2
  39.3 16.2 %all-to-all-start.1 = ((f32[8,176,128]{2,1,0:T(8,128)}), f32[8,176,128]{2,1,0:T(8,128)S(1)}, u32[]{:S(2)}, u32[]{:S(2)}) async-start(f32[8,176,128]{2,1,0:T(8,128)} %shard_map.62), calls=%async_computation.1 | async-start | bytes 1441792 | tf_op jit(solution)/shard_map/all_to_all | solution.py:339
  55.6 6.2 %collective-permute-start.4 = (f32[5,16,128]{2,1,0:T(8,128)S(1)}, f32[5,16,128]{2,1,0:T(8,128)S(1)}, u32[]{:S(2)}, u32[]{:S(2)}) collective-permute-start(f32[5,16,128]{2,1,0:T(8,128)S(1)} %bitcast.6), channel_id=1, source_target_pairs={{0,16},{16,32},{32,48},{48,64},{64,80},{80,96},{96,112},{112,0},{1... | collective-permute-start | bytes 122888 | tf_op jit(solution)/shard_map/ppermute | solution.py:351
  56.1 5.6 %collective-permute-start.5 = (f32[5,16,128]{2,1,0:T(8,128)S(1)}, f32[5,16,128]{2,1,0:T(8,128)S(1)}, u32[]{:S(2)}, u32[]{:S(2)}) collective-permute-start(f32[5,16,128]{2,1,0:T(8,128)S(1)} %bitcast.4), channel_id=1, source_target_pairs={{0,112},{16,0},{32,16},{48,32},{64,48},{80,64},{96,80},{112,96},{1... | collective-permute-start | bytes 122888 | tf_op jit(solution)/shard_map/ppermute | solution.py:352
  61.7 0.6 copy-start.3
  62.4 0.6 copy-start.4

commit v16 on v15

--- a/solution.py
+++ b/solution.py
@@ -154,8 +154,17 @@
     up_pack = jnp.zeros((depth, LANES), jnp.float32)
     down_pack = jnp.zeros((depth, LANES), jnp.float32)
     top = bottom = None
+    edge_only = relaxed_ref is None and chunk_ref is not None
+    edges = [jnp.zeros((depth, LANES), jnp.float32) for _ in range(19)]
     for x in range(slab_width):
-        r = relax(cells_of_x(x))
+        cells = cells_of_x(x)
+        if edge_only and 0 < x < slab_width - 1:
+            low_lane, high_lane = 2 * (x - 1), 2 * (x - 1) + 1
+            for m in range(19):
+                t = jnp.where(lane == low_lane, _roll(cells[m], low_lane, 1), edges[m])
+                edges[m] = jnp.where(lane == high_lane, _roll(cells[m], high_lane + 1, 1), t)
+            continue
+        r = relax(cells)
         if relaxed_ref is not None:
             for m in range(19):
                 relaxed_ref[m, x] = r[m]
@@ -173,6 +182,16 @@
             down_pack = jnp.where(lane == k, _roll(r[m], k, 1), down_pack)
     if chunk_ref is None:
         return
+    if edge_only:
+        packed = relax(edges)
+        for x in range(1, slab_width - 1):
+            low_lane, high_lane = 2 * (x - 1), 2 * (x - 1) + 1
+            for i, m in enumerate(y_plus):
+                k = i * slab_width + x
+                up_pack = jnp.where(lane == k, _roll(packed[m], k - high_lane, 1), up_pack)
+            for i, m in enumerate(y_minus):
+                k = i * slab_width + x
+                down_pack = jnp.where(lane == k, _roll(packed[m], k - low_lane, 1), down_pack)
     _write_shares(chunk_ref, top, bottom, up_pack, down_pack, mix, depth)
 
 

time: 65.8 us -> 66.1 us (level)
  no operation moved by 1% of the time
where the time goes in v16:
time: 66.1 us; the launch traced here: 65.7 us
  waiting for transfers between devices  23 us (35%)
  starting transfers between devices  19.2 us (29%)
  Pallas kernels  16 us (24%)
  local copies, waits for them, and re-layouts  3.31 us (5%)
  other arithmetic  2.41 us (4%)
  matrix products  1.07 us (2%)
  between operations  0.75 us (1%)
    all_to_all x2, waiting for transfers between devices, _per_device(): got = lax.all_to_all(chunks, 'gy', 0, 0, tiled=True)  16.9 us
    all_to_all x2, starting transfers between devices, _per_device(): got = lax.all_to_all(chunks, 'gy', 0, 0, tiled=True)  10.6 us
    ppermute x2, starting transfers between devices, _per_device(): lax.ppermute(high_send, 'gx', [(i, (i - 1) % slab_cycle) for i in range(s...  7.21 us
    pallas_call x1, Pallas kernels, _per_device(): chunks = _call(middle_kernel, 2, 5, chunk)(*args)  3.89 us
    pallas_call x1, Pallas kernels, _per_device(): _call(first_kernel, 2, 2, chunk)  3.35 us
    pallas_call x1, Pallas kernels, _per_device(): relaxed = _call(middle_kernel, 2, 5, full)(*args)  3.3 us
    unnamed x12, local copies, waits for them, and re-layouts  3.27 us
    pallas_call x1, Pallas kernels, _per_device(): _call(first_kernel, 2, 2, full)  3.03 us
  transfers between devices with their start and end apart: 8, of which 6 were waited for; matrix products, arithmetic and copies ran while one was open for 5% of the time, Pallas kernels for 10%

profile of v16, /device:TPU:0, one launch (start us, length us, event | category | flops | bytes accessed | tf_op | source)
XLA Modules:
  0.0 65.7 jit_solution(2101698759632629407)
XLA Ops:
  0.7 2.2 %collective-permute-done.other_ref = f32[19,8,8,128]{3,2,1,0:T(8,128)S(1)} collective-permute-done((f32[19,8,8,128]{3,2,1,0:T(8,128)}, f32[19,8,8,128]{3,2,1,0:T(8,128)S(1)}, u32[]{:S(2)}, u32[]{:S(2)}) %collective-permute-start) | collective-permute-done | bytes 622624 | tf_op jit(solution)/shard_map/ppermute | solution.py:340
  3.0 0.8 %copy-done = f32[19,8,8,128]{3,2,1,0:T(8,128)} copy-done((f32[19,8,8,128]{3,2,1,0:T(8,128)}, f32[19,8,8,128]{3,2,1,0:T(8,128)S(1)}, u32[]{:S(2)}) %copy-start) | copy-done | bytes 622616
  3.8 3.4 %shard_map.60 = f32[8,176,128]{2,1,0:T(8,128)} custom-call(s32[2]{0:T(128)} %shift_ref.7, s32[2]{0:T(128)} %frac_ref.7, f32[19,8,8,128]{3,2,1,0:T(8,128)} %mine_ref.3, f32[19,8,8,128]{3,2,1,0:T(8,128)} %copy-done), custom_call_target="tpu_custom_call" | custom-call | tf_op jit(solution)/shard_map/pallas_call | solution.py:355
  7.2 7.0 %all-to-all-start = ((f32[8,176,128]{2,1,0:T(8,128)}), f32[8,176,128]{2,1,0:T(8,128)S(1)}, u32[]{:S(2)}, u32[]{:S(2)}) async-start(f32[8,176,128]{2,1,0:T(8,128)} %shard_map.60), calls=%async_computation | async-start | bytes 1441792 | tf_op jit(solution)/shard_map/all_to_all | solution.py:358
  14.3 1.2 %collective-permute-done.3 = s32[8,8,32]{2,1,0:T(8,128)S(1)} collective-permute-done((s32[8,8,32]{2,1,0:T(8,128)S(1)}, s32[8,8,32]{2,1,0:T(8,128)S(1)}, u32[]{:S(2)}, u32[]{:S(2)}) %collective-permute-start.3) | collective-permute-done | bytes 8224 | tf_op jit(solution)/shard_map/ppermute | solution.py:341
  15.6 1.1 %fusion.1 = u16[8,128,19]{1,2,0:T(8,128)(2,1)S(1)} fusion(s32[8,16,32]{2,1,0:T(8,128)S(1)} %get-tuple-element.9, s32[8,16,32]{2,1,0:T(8,128)S(1)} %get-tuple-element.8), kind=kOutput, calls=%fused_computation.6 | convolution fusion | flops 22062080 | bytes 71680 | tf_op jit(solution)/shard_map/xzml,xzly->xzym/dot_general | solution.py:116
  16.7 1.0 %select_reduce_fusion.hits_ref = s32[8,16,128]{2,1,0:T(8,128)} fusion(s32[19]{0:T(128)S(1)} %iota_shift-left_fusion, u16[8,128,19]{1,2,0:T(8,128)(2,1)S(1)} %fusion.1), kind=kLoop, calls=%fused_computation.4 | loop fusion | flops 1851392 | bytes 104524 | tf_op jit(solution)/shard_map/reduce_sum | solution.py:118
  17.7 3.0 %shard_map.59.relaxed_ref = f32[19,8,16,128]{3,2,1,0:T(8,128)} custom-call(s32[2]{0:T(128)} %shift_ref.7, s32[2]{0:T(128)} %frac_ref.7, f32[19,8,8,128]{3,2,1,0:T(8,128)} %mine_ref.3, f32[19,8,8,128]{3,2,1,0:T(8,128)} %copy-done), custom_call_target="tpu_custom_call" | custom-call | tf_op jit(solution)/shard_map/pallas_call | solution.py:356
  20.7 7.5 %all-to-all-done = f32[8,176,128]{2,1,0:T(8,128)S(1)} async-done(((f32[8,176,128]{2,1,0:T(8,128)}), f32[8,176,128]{2,1,0:T(8,128)S(1)}, u32[]{:S(2)}, u32[]{:S(2)}) %all-to-all-start) | async-done | bytes 720928 | tf_op jit(solution)/shard_map/all_to_all | solution.py:358
  28.2 0.7 %collective-permute-start.1 = (f32[5,16,128]{2,1,0:T(8,128)S(1)}, f32[5,16,128]{2,1,0:T(8,128)S(1)}, u32[]{:S(2)}, u32[]{:S(2)}) collective-permute-start(f32[5,16,128]{2,1,0:T(8,128)S(1)} %bitcast.7), channel_id=1, source_target_pairs={{0,16},{16,32},{32,48},{48,64},{64,80},{80,96},{96,112},{112,0},{1... | collective-permute-start | bytes 122888 | tf_op jit(solution)/shard_map/ppermute | solution.py:370
  28.9 3.6 %collective-permute-start.2 = (f32[5,16,128]{2,1,0:T(8,128)S(1)}, f32[5,16,128]{2,1,0:T(8,128)S(1)}, u32[]{:S(2)}, u32[]{:S(2)}) collective-permute-start(f32[5,16,128]{2,1,0:T(8,128)S(1)} %bitcast.5), channel_id=1, source_target_pairs={{0,112},{16,0},{32,16},{48,32},{64,48},{80,64},{96,80},{112,96},{1... | collective-permute-start | bytes 122888 | tf_op jit(solution)/shard_map/ppermute | solution.py:371
  32.5 0.6 pad_maximum_fusion.rims_ref
  33.1 1.3 %collective-permute-done.1.low_ref = f32[5,16,128]{2,1,0:T(8,128)S(1)} collective-permute-done((f32[5,16,128]{2,1,0:T(8,128)S(1)}, f32[5,16,128]{2,1,0:T(8,128)S(1)}, u32[]{:S(2)}, u32[]{:S(2)}) %collective-permute-start.1) | collective-permute-done | bytes 40992 | tf_op jit(solution)/shard_map/ppermute | solution.py:370
  34.4 0.6 copy-done.1
  35.0 0.6 copy-done.2
  35.7 3.9 %shard_map.62 = f32[8,176,128]{2,1,0:T(8,128)} custom-call(s32[2]{0:T(128)} %shift_ref.7, s32[2]{0:T(128)} %frac_ref.7, f32[19,8,16,128]{3,2,1,0:T(8,128)} %shard_map.59.relaxed_ref, f32[2,16,128]{2,1,0:T(8,128)} %pad_maximum_fusion.rims_ref, f32[5,16,128]{2,1,0:T(8,128)} %copy-done.1, f32[5,16,128]{2,1,0:T(8,128)} %copy-done.2, ...), custom_call_target="tpu_custom_call" | custom-call | tf_op jit(solution)/shard_map/pallas_call | solution.py:375
  39.6 3.5 %all-to-all-start.1 = ((f32[8,176,128]{2,1,0:T(8,128)}), f32[8,176,128]{2,1,0:T(8,128)S(1)}, u32[]{:S(2)}, u32[]{:S(2)}) async-start(f32[8,176,128]{2,1,0:T(8,128)} %shard_map.62), calls=%async_computation.1 | async-start | bytes 1441792 | tf_op jit(solution)/shard_map/all_to_all | solution.py:358
  43.1 3.3 %shard_map.61.relaxed_ref = f32[19,8,16,128]{3,2,1,0:T(8,128)} custom-call(s32[2]{0:T(128)} %shift_ref.7, s32[2]{0:T(128)} %frac_ref.7, f32[19,8,16,128]{3,2,1,0:T(8,128)} %shard_map.59.relaxed_ref, f32[2,16,128]{2,1,0:T(8,128)} %pad_maximum_fusion.rims_ref, f32[5,16,128]{2,1,0:T(8,128)} %copy-done.1, f32[5,16,128]{2,1,0:T(8,128)} %copy-done.2, ...), custom_call_target="tpu_custom_call" | custom-call | tf_op jit(solution)/shard_map/pallas_call | solution.py:376
  46.4 9.4 %all-to-all-done.1 = f32[8,176,128]{2,1,0:T(8,128)S(1)} async-done(((f32[8,176,128]{2,1,0:T(8,128)}), f32[8,176,128]{2,1,0:T(8,128)S(1)}, u32[]{:S(2)}, u32[]{:S(2)}) %all-to-all-start.1) | async-done | bytes 720928 | tf_op jit(solution)/shard_map/all_to_all | solution.py:358
  56.4 3.7 %collective-permute-start.5 = (f32[5,16,128]{2,1,0:T(8,128)S(1)}, f32[5,16,128]{2,1,0:T(8,128)S(1)}, u32[]{:S(2)}, u32[]{:S(2)}) collective-permute-start(f32[5,16,128]{2,1,0:T(8,128)S(1)} %bitcast.4), channel_id=1, source_target_pairs={{0,112},{16,0},{32,16},{48,32},{64,48},{80,64},{96,80},{112,96},{1... | collective-permute-start | bytes 122888 | tf_op jit(solution)/shard_map/ppermute | solution.py:371
  60.1 0.6 pad_maximum_fusion.1.rims_ref
  60.7 1.4 %collective-permute-done.4.low_ref = f32[5,16,128]{2,1,0:T(8,128)S(1)} collective-permute-done((f32[5,16,128]{2,1,0:T(8,128)S(1)}, f32[5,16,128]{2,1,0:T(8,128)S(1)}, u32[]{:S(2)}, u32[]{:S(2)}) %collective-permute-start.4) | collective-permute-done | bytes 40992 | tf_op jit(solution)/shard_map/ppermute | solution.py:370
  62.6 0.6 copy-done.4
  63.2 2.5 %shard_map.63 = (f32[19,8,8,128]{3,2,1,0:T(8,128)}, f32[8,8,128]{2,1,0:T(8,128)}) custom-call(f32[19,8,16,128]{3,2,1,0:T(8,128)} %shard_map.61.relaxed_ref, f32[2,16,128]{2,1,0:T(8,128)} %pad_maximum_fusion.1.rims_ref, f32[5,16,128]{2,1,0:T(8,128)} %copy-done.3, f32[5,16,128]{2,1,0:T(8,128)} %copy-done.4, s32[8,16,128]{2,1,0:T(8,128)} %select_reduce_fusion.hits_ref), custom_call_target="tpu_custom_call" | custom-call | tf_op jit(solution)/shard_map/pallas_call | solution.py:378
  (23 shorter events, 1.5 us)
Async XLA Ops:
  0.6 13.6 %copy-start.5 = (s32[8,8,32]{2,1,0:T(8,128)S(1)}, s32[8,8,32]{2,1,0:T(8,128)}, u32[]{:S(2)}) copy-start(s32[8,8,32]{2,1,0:T(8,128)} %param.7) | copy-start | bytes 24580
  0.6 2.3 %collective-permute-start = (f32[19,8,8,128]{3,2,1,0:T(8,128)}, f32[19,8,8,128]{3,2,1,0:T(8,128)S(1)}, u32[]{:S(2)}, u32[]{:S(2)}) collective-permute-start(f32[19,8,8,128]{3,2,1,0:T(8,128)} %mine_ref.3), channel_id=1, source_target_pairs={{0,1},{1,0},{2,3},{3,2},{4,5},{5,4},{6,7},{7,6},{8,9},{9,8},{10,11... | collective-permute-start | bytes 1867784 | tf_op jit(solution)/shard_map/ppermute | solution.py:340
  3.0 0.8 %copy-start = (f32[19,8,8,128]{3,2,1,0:T(8,128)}, f32[19,8,8,128]{3,2,1,0:T(8,128)S(1)}, u32[]{:S(2)}) copy-start(f32[19,8,8,128]{3,2,1,0:T(8,128)S(1)} %collective-permute-done.other_ref) | copy-start | bytes 1867780
  7.2 21.0 %all-to-all-start = ((f32[8,176,128]{2,1,0:T(8,128)}), f32[8,176,128]{2,1,0:T(8,128)S(1)}, u32[]{:S(2)}, u32[]{:S(2)}) async-start(f32[8,176,128]{2,1,0:T(8,128)} %shard_map.60), calls=%async_computation | async-start | bytes 1441792 | tf_op jit(solution)/shard_map/all_to_all | solution.py:358
  14.2 1.3 %collective-permute-start.3 = (s32[8,8,32]{2,1,0:T(8,128)S(1)}, s32[8,8,32]{2,1,0:T(8,128)S(1)}, u32[]{:S(2)}, u32[]{:S(2)}) collective-permute-start(s32[8,8,32]{2,1,0:T(8,128)S(1)} %copy-done.5), channel_id=1, source_target_pairs={{0,1},{1,0},{2,3},{3,2},{4,5},{5,4},{6,7},{7,6},{8,9},{9,8},{10,11... | collective-permute-start | bytes 24584 | tf_op jit(solution)/shard_map/ppermute | solution.py:341
  28.2 6.2 %collective-permute-start.1 = (f32[5,16,128]{2,1,0:T(8,128)S(1)}, f32[5,16,128]{2,1,0:T(8,128)S(1)}, u32[]{:S(2)}, u32[]{:S(2)}) collective-permute-start(f32[5,16,128]{2,1,0:T(8,128)S(1)} %bitcast.7), channel_id=1, source_target_pairs={{0,16},{16,32},{32,48},{48,64},{64,80},{80,96},{96,112},{112,0},{1... | collective-permute-start | bytes 122888 | tf_op jit(solution)/shard_map/ppermute | solution.py:370
  28.9 5.5 %collective-permute-start.2 = (f32[5,16,128]{2,1,0:T(8,128)S(1)}, f32[5,16,128]{2,1,0:T(8,128)S(1)}, u32[]{:S(2)}, u32[]{:S(2)}) collective-permute-start(f32[5,16,128]{2,1,0:T(8,128)S(1)} %bitcast.5), channel_id=1, source_target_pairs={{0,112},{16,0},{32,16},{48,32},{64,48},{80,64},{96,80},{112,96},{1... | collective-permute-start | bytes 122888 | tf_op jit(solution)/shard_map/ppermute | solution.py:371
  34.4 0.6 copy-start.1
  35.0 0.6 copy-start.2
  39.6 16.2 %all-to-all-start.1 = ((f32[8,176,128]{2,1,0:T(8,128)}), f32[8,176,128]{2,1,0:T(8,128)S(1)}, u32[]{:S(2)}, u32[]{:S(2)}) async-start(f32[8,176,128]{2,1,0:T(8,128)} %shard_map.62), calls=%async_computation.1 | async-start | bytes 1441792 | tf_op jit(solution)/shard_map/all_to_all | solution.py:358
  55.8 6.2 %collective-permute-start.4 = (f32[5,16,128]{2,1,0:T(8,128)S(1)}, f32[5,16,128]{2,1,0:T(8,128)S(1)}, u32[]{:S(2)}, u32[]{:S(2)}) collective-permute-start(f32[5,16,128]{2,1,0:T(8,128)S(1)} %bitcast.6), channel_id=1, source_target_pairs={{0,16},{16,32},{32,48},{48,64},{64,80},{80,96},{96,112},{112,0},{1... | collective-permute-start | bytes 122888 | tf_op jit(solution)/shard_map/ppermute | solution.py:370
  56.4 5.6 %collective-permute-start.5 = (f32[5,16,128]{2,1,0:T(8,128)S(1)}, f32[5,16,128]{2,1,0:T(8,128)S(1)}, u32[]{:S(2)}, u32[]{:S(2)}) collective-permute-start(f32[5,16,128]{2,1,0:T(8,128)S(1)} %bitcast.4), channel_id=1, source_target_pairs={{0,112},{16,0},{32,16},{48,32},{64,48},{80,64},{96,80},{112,96},{1... | collective-permute-start | bytes 122888 | tf_op jit(solution)/shard_map/ppermute | solution.py:371
  62.0 0.6 copy-start.3
  62.6 0.6 copy-start.4
